TPU v7x, 32 devices: a whole 2x2x4 slice. The times are simulated.
32 devices in a mesh: groups: 2 (over y), pairs: 4 (over z), mp: 4 (over x, core).
Axes of the slice: x: 2, y: 2, z: 4, core: 2. Of those that a mesh axis runs over, the one named last changes fastest.
Arguments:
- tokens: bfloat16 [512, 768], P(('groups', 'pairs'), 'mp'), parts along dimension 0, may hold values from -6 to 6
- pair_list: int32 [16, 2], P(('groups', 'pairs')), parts along dimension 0, may hold values from 0 to 7, as said below
- confidence: float32 [16, 64], P(('groups', 'pairs')), parts along dimension 0, may hold values from 0.1 to 10
- gain_self: float32 [768], replicated, may hold values from 0.1 to 1.9
- gain_query: float32 [768], replicated, may hold values from 0.1 to 1.9
- gain_context: float32 [768], replicated, may hold values from 0.1 to 1.9
- gain_mlp: float32 [768], replicated, may hold values from 0.1 to 1.9
- self_qkv: bfloat16 [3, 768, 768], P(None, None, 'mp'), may hold values from -1 to 1
- self_out: bfloat16 [768, 768], P('mp'), may hold values from -0.21875 to 0.21875
- cross_query: bfloat16 [768, 768], P(None, 'mp'), may hold values from -1 to 1
- cross_kv: bfloat16 [2, 768, 768], P(None, None, 'mp'), may hold values from -1 to 1
- cross_out: bfloat16 [768, 768], P('mp'), may hold values from -0.21875 to 0.21875
- mlp_up: bfloat16 [768, 3072], P(None, 'mp'), may hold values from -0.21875 to 0.21875
- mlp_down: bfloat16 [3072, 768], P('mp'), may hold values from -0.109375 to 0.109375
Outputs:
- image_features: bfloat16 [512, 768], P(('groups', 'pairs'), 'mp'), parts along dimension 0
There are 2 independent parts, one for each index of `groups`. A program takes and returns all parts, laid end to end along the dimension named above; an argument that names none is the same for every part. Nothing has to cross between parts.
Inputs may be any that keep to these rules, and one draw needn't show every extreme that they name: `pair_list`: in each block of 2 consecutive pairs the 4 images named are distinct and have distinct owners, the owner of image i being i // 2; the images of each owner are named in exactly 4 blocks; some images are named by no pair.
All inputs are finite; a program needn't handle non-finite values.
Results may differ from a plain program's by a relative error of at most 0.012.
Values may be sent and summed in bfloat16 or wider, within the bound.
No kernel may reach another device: no remote copies, remote signals or barrier semaphores. Data moves between devices by JAX's collectives and lax.ppermute only.
A program may use at most 64 MiB of HBM per device.

v0:
```python
import jax
import jax.numpy as jnp
from jax import lax
from jax.sharding import PartitionSpec as P

HEAD = 64
TOKS = 32


EPSILON = 1e-06


def layer_norm(values, gain):
    center = values - jnp.mean(values, axis=-1, keepdims=True)
    spread = jnp.mean(center * center, axis=-1, keepdims=True)
    return (center * lax.rsqrt(spread + EPSILON) * gain).astype(jnp.bfloat16)


def attend(query, keys, values, views_n):
    rows_n, width = query.shape
    heads_n = width // HEAD
    qh = query.reshape(views_n, TOKS, heads_n, HEAD)
    kh = keys.reshape(views_n, TOKS, heads_n, HEAD)
    vh = values.reshape(views_n, TOKS, heads_n, HEAD)
    scores = jnp.einsum("vqhc,vkhc->vhqk", qh, kh, preferred_element_type=jnp.float32) * HEAD ** (
        -0.5
    )
    probs = jax.nn.softmax(scores, axis=-1).astype(jnp.bfloat16)
    mixed = jnp.einsum("vhqk,vkhc->vqhc", probs, vh, preferred_element_type=jnp.float32)
    return mixed.astype(jnp.bfloat16).reshape(rows_n, width)


def partner(values):
    shape = values.shape
    paired = values.reshape((shape[0] // 2, 2) + shape[1:])
    return jnp.flip(paired, axis=1).reshape(shape)


def summed_full(term):
    return lax.psum(term.astype(jnp.bfloat16), "mp").astype(jnp.float32)


def per_device(
    tokens,
    pair_list,
    confidence,
    gain_self,
    gain_query,
    gain_context,
    gain_mlp,
    self_qkv,
    self_out,
    cross_query,
    cross_kv,
    cross_out,
    mlp_up,
    mlp_down,
):
    quarter = tokens.shape[1]
    img_dev = tokens.shape[0] // TOKS
    pair_dev = pair_list.shape[0]
    views_n = 2 * pair_dev
    owners_n = lax.axis_size("pairs")
    own = lax.axis_index("pairs")
    table = lax.all_gather(pair_list, "pairs", axis=0, tiled=True).reshape(owners_n, views_n)
    wanted = jnp.where(table // img_dev == own, table % img_dev, -1)
    chosen = jnp.max(wanted, axis=1)
    images = tokens.reshape(img_dev, TOKS, quarter)
    picked = jnp.take(images, jnp.maximum(chosen, 0), axis=0)
    outgoing = jnp.where((chosen >= 0)[:, None, None], picked, jnp.zeros_like(picked))
    arrived = lax.all_to_all(outgoing, "pairs", split_axis=0, concat_axis=0, tiled=True)
    source = pair_list.reshape(views_n) // img_dev
    slices = jnp.take(arrived, source, axis=0)
    start = lax.all_gather(slices, "mp", axis=2, tiled=True)
    width = start.shape[2]
    rows_n = views_n * TOKS
    begin = start.astype(jnp.float32).reshape(rows_n, width)
    context = layer_norm(partner(start.astype(jnp.float32)), gain_context).reshape(rows_n, width)
    offset = lax.axis_index("mp") * quarter
    normed = layer_norm(begin, gain_self)
    qkv = jnp.einsum("rd,kdc->krc", normed, self_qkv, preferred_element_type=jnp.float32).astype(
        jnp.bfloat16
    )
    term = jnp.dot(
        attend(qkv[0], qkv[1], qkv[2], views_n), self_out, preferred_element_type=jnp.float32
    )
    resid = begin + summed_full(term)
    normed = layer_norm(resid, gain_query)
    query = jnp.dot(normed, cross_query, preferred_element_type=jnp.float32).astype(jnp.bfloat16)
    keyval = jnp.einsum(
        "rd,kdc->krc", context, cross_kv, preferred_element_type=jnp.float32
    ).astype(jnp.bfloat16)
    term = jnp.dot(
        attend(query, keyval[0], keyval[1], views_n), cross_out, preferred_element_type=jnp.float32
    )
    resid = resid + summed_full(term)
    normed = layer_norm(resid, gain_mlp)
    hidden = jax.nn.gelu(
        jnp.dot(normed, mlp_up, preferred_element_type=jnp.float32), approximate=False
    )
    term = jnp.dot(hidden.astype(jnp.bfloat16), mlp_down, preferred_element_type=jnp.float32)
    resid = resid + summed_full(term)
    final = lax.dynamic_slice_in_dim(resid, offset, quarter, 1)
    conf = confidence.reshape(views_n, TOKS)
    weighted = (final.reshape(views_n, TOKS, quarter) * conf[:, :, None]).reshape(
        views_n, TOKS * quarter
    )
    route = (source[None, :] == jnp.arange(owners_n)[:, None]).astype(jnp.float32)
    back = jnp.dot(route, weighted, precision=lax.Precision.HIGHEST).astype(jnp.bfloat16)
    back_weight = jnp.dot(route, conf, precision=lax.Precision.HIGHEST).astype(jnp.bfloat16)
    got_feat, got_weight = (
        lax.all_to_all(
            back.reshape(owners_n, TOKS, quarter), "pairs", split_axis=0, concat_axis=0, tiled=True
        ),
        lax.all_to_all(back_weight, "pairs", split_axis=0, concat_axis=0, tiled=True),
    )
    owner_match = chosen[None, :] == jnp.arange(img_dev)[:, None]
    numer = jnp.einsum(
        "ij,jtc->itc",
        owner_match.astype(jnp.bfloat16),
        got_feat,
        preferred_element_type=jnp.float32,
    )
    denom = jnp.dot(
        owner_match.astype(jnp.float32),
        got_weight.astype(jnp.float32),
        precision=lax.Precision.HIGHEST,
    )
    result = numer / jnp.maximum(denom, 1.0)[:, :, None]
    return result.astype(jnp.bfloat16).reshape(img_dev * TOKS, quarter)


def solution(mesh):
    return jax.shard_map(
        per_device,
        mesh=mesh,
        in_specs=(
            P(("groups", "pairs"), "mp"),
            P(("groups", "pairs"), None),
            P(("groups", "pairs"), None),
            P(),
            P(),
            P(),
            P(),
            P(None, None, "mp"),
            P("mp", None),
            P(None, "mp"),
            P(None, None, "mp"),
            P("mp", None),
            P(None, "mp"),
            P("mp", None),
        ),
        out_specs=P(("groups", "pairs"), "mp"),
        check_vma=False,
    )
```

profile of v0, /device:TPU:0, one launch (start us, length us, event | category | flops | bytes accessed | tf_op | source)
XLA Modules:
  0.0 180.7 jit_solution(869110114710449456)
XLA Ops:
  6.5 13.0 %all-gather = s32[4,2,2]{2,1,0:T(2,128)S(1)} all-gather(s32[1,2,2]{2,1,0:T(2,128)} %bitcast.90), channel_id=1, replica_groups=mesh['groups'=2,'pairs'=4,'mp'=4] {'pairs'}, dimensions={0}, use_global_device_ids=true | all-gather | bytes 80 | tf_op jit(solution)/shard_map/all_gather | solution.py:65
  19.7 0.1 reduce_max.36
  19.9 0.5 copy-done.11
  20.4 1.3 gather_fusion
  21.7 0.7 select_select_fusion
  22.4 3.3 %all-to-all-start = ((bf16[4,32,192]{2,1,0:T(8,128)(2,1)}), bf16[4,32,192]{2,1,0:T(8,128)(2,1)S(1)}, u32[]{:S(2)}, u32[]{:S(2)}) async-start(bf16[4,32,192]{2,1,0:T(8,128)(2,1)} %select_select_fusion), calls=%async_computation | async-start | bytes 131072 | tf_op jit(solution)/shard_map/all_to_all | solution.py:71
  25.7 0.8 reshape.277
  26.5 0.8 reshape.275
  27.3 0.5 compare_and_fusion
  27.8 3.6 %all-to-all-done = bf16[4,32,192]{2,1,0:T(8,128)(2,1)S(1)} async-done(((bf16[4,32,192]{2,1,0:T(8,128)(2,1)}), bf16[4,32,192]{2,1,0:T(8,128)(2,1)S(1)}, u32[]{:S(2)}, u32[]{:S(2)}) %all-to-all-start) | async-done | bytes 49184 | tf_op jit(solution)/shard_map/all_to_all | solution.py:71
  31.4 0.5 gather_fusion.1
  32.0 0.2 copy.73
  32.2 8.6 %all_gather.7 = bf16[4,32,768]{1,0,2:T(4,128)(2,1)S(1)} all-gather(bf16[4,32,192]{1,0,2:T(4,128)(2,1)S(1)} %copy.73), channel_id=1, replica_groups=mesh['groups'=2,'pairs'=4,'mp'=4] {'mp'}, dimensions={2}, use_global_device_ids=true | all-gather | bytes 245760 | tf_op jit(solution)/shard_map/all_gather | solution.py:74
  40.8 0.8 convert_reduce_fusion
  41.6 0.4 copy.74
  42.1 0.8 multiply_reduce_fusion.1
  42.9 0.7 div.88
  43.6 1.3 convert_element_type.84
  44.9 7.5 %rev.4 = f32[2,2,32,768]{2,1,0,3:T(2,128)S(1)} reverse(f32[2,2,32,768]{2,1,0,3:T(2,128)} %bitcast.83), dimensions={1} | reverse | bytes 786432 | tf_op jit(solution)/shard_map/jit(_flip)/rev | solution.py:36
  52.4 0.8 reduce_sum.93
  53.2 1.1 multiply_reduce_fusion
  54.4 0.6 copy.83
  55.2 0.8 fusion.18
  56.0 1.6 fusion.122
  57.6 0.1 reshape.312
  57.7 0.1 reshape.313
  57.9 0.2 convolution_multiply_fusion.1
  58.2 0.1 reshape.311
  58.4 0.3 fusion.6
  58.6 0.1 copy.82
  58.7 0.1 reshape.279
  58.9 0.9 convolution_convert_fusion.3
  59.9 0.1 fusion.15
  60.1 0.3 fusion.123
  60.5 0.1 reshape.316
  60.6 0.1 reshape.314
  60.7 28.6 %all-reduce.4.cloned.1.call-done = bf16[128,768]{1,0:T(8,128)(2,1)} async-done(((bf16[128,768]{1,0:T(8,128)(2,1)}), bf16[128,768]{1,0:T(8,128)(2,1)}) %all-reduce.4.cloned.1.call-update) | async-done | bytes 196624 | tf_op jit(solution)/shard_map/psum | solution.py:40
  89.3 1.0 fusion.77
  90.4 1.1 multiply_reduce_fusion.3
  91.5 0.3 convolution_convert_fusion.6
  91.8 0.1 reshape.315
  92.0 0.2 convolution_multiply_fusion
  92.3 0.3 fusion.7
  92.7 0.1 reshape.283
  92.8 0.9 convolution_convert_fusion.2
  93.9 31.7 %all-reduce.6.cloned.1.call-done = bf16[128,768]{1,0:T(8,128)(2,1)} async-done(((bf16[128,768]{1,0:T(8,128)(2,1)}), bf16[128,768]{1,0:T(8,128)(2,1)}) %all-reduce.6.cloned.1.call-update) | async-done | bytes 196624 | tf_op jit(solution)/shard_map/psum | solution.py:40
  125.6 1.1 fusion.117
  126.7 0.2 multiply_reduce_fusion.2
  126.9 2.1 %convolution_convert_fusion.1 = bf16[128,768]{1,0:T(8,128)(2,1)} fusion(bf16[768,768]{1,0:T(8,128)(2,1)S(1)} %copy-done, bf16[768,768]{1,0:T(8,128)(2,1)S(1)} %copy-done.13, f32[128,768]{1,0:T(8,128)S(1)} %get-tuple-element.6, f32[768]{0:T(1024)S(1)} %copy-done.14, f32[128]{0:T(128)S(1)} %add_rsqrt_fusion.2, f32[128]{0:T(128)S(1)} %broadcast_multiply_fusion.2), kind=kOutput, calls=%fused_computation.9 | convolution fusion | flops 308871168 | bytes 2953216 | tf_op jit(solution)/shard_map/dot_general | solution.py:101
  129.1 0.1 fusion.9
  129.2 0.6 copy.94
  129.8 4.6 %all-to-all-start.2 = ((bf16[4,1,32]{2,1,0:T(2,128)(2,1)}), bf16[4,1,32]{2,1,0:T(2,128)(2,1)S(1)}, u32[]{:S(2)}, u32[]{:S(2)}) async-start(bf16[4,1,32]{2,1,0:T(2,128)(2,1)} %copy.94), calls=%async_computation.2 | async-start | bytes 4096 | tf_op jit(solution)/shard_map/all_to_all | solution.py:115
  134.5 0.1 mul.147
  134.6 26.3 %all-reduce.8.cloned.1.call-done = bf16[128,768]{1,0:T(8,128)(2,1)} async-done(((bf16[128,768]{1,0:T(8,128)(2,1)}), bf16[128,768]{1,0:T(8,128)(2,1)}) %all-reduce.8.cloned.1.call-update) | async-done | bytes 196624 | tf_op jit(solution)/shard_map/psum | solution.py:40
  160.9 1.0 dynamic-slice_add_fusion
  161.9 0.1 reshape.284
  162.1 0.2 convolution_convert_fusion
  162.3 0.7 reshape.285
  163.0 4.6 %all-to-all-start.1 = ((bf16[4,32,192]{2,1,0:T(8,128)(2,1)}), bf16[4,32,192]{2,1,0:T(8,128)(2,1)S(1)}, u32[]{:S(2)}, u32[]{:S(2)}) async-start(bf16[4,32,192]{2,1,0:T(8,128)(2,1)} %reshape.285), calls=%async_computation.1 | async-start | bytes 131072 | tf_op jit(solution)/shard_map/all_to_all | solution.py:112
  167.6 0.1 convolution_maximum_fusion
  167.7 0.1 copy.95
  167.8 5.5 %all-to-all-done.1 = bf16[4,32,192]{2,1,0:T(8,128)(2,1)S(1)} async-done(((bf16[4,32,192]{2,1,0:T(8,128)(2,1)}), bf16[4,32,192]{2,1,0:T(8,128)(2,1)S(1)}, u32[]{:S(2)}, u32[]{:S(2)}) %all-to-all-start.1) | async-done | bytes 49184 | tf_op jit(solution)/shard_map/all_to_all | solution.py:112
  173.4 0.2 fusion.8
  173.5 0.6 copy.96
  (65 shorter events, 1.3 us)
Async XLA Ops:
  6.5 120.3 %copy-start = (bf16[768,768]{1,0:T(8,128)(2,1)S(1)}, bf16[768,768]{1,0:T(8,128)(2,1)}, u32[]{:S(2)}) copy-start(bf16[768,768]{1,0:T(8,128)(2,1)} %param.27) | copy-start | bytes 3538948
  19.8 0.5 copy-start.11
  22.4 9.0 %all-to-all-start = ((bf16[4,32,192]{2,1,0:T(8,128)(2,1)}), bf16[4,32,192]{2,1,0:T(8,128)(2,1)S(1)}, u32[]{:S(2)}, u32[]{:S(2)}) async-start(bf16[4,32,192]{2,1,0:T(8,128)(2,1)} %select_select_fusion), calls=%async_computation | async-start | bytes 131072 | tf_op jit(solution)/shard_map/all_to_all | solution.py:71
  25.7 63.6 %all-reduce.4.cloned.1.call-start = ((), (), s32[]{:S(2)}) async-start(), calls=%async_computation.3 | async-start | bytes 393216 | tf_op jit(solution)/shard_map/psum | solution.py:40
  53.2 1.9 %copy-start.6 = (f32[768]{0:T(1024)S(1)}, f32[768]{0:T(1024)}, u32[]{:S(2)}) copy-start(f32[768]{0:T(1024)} %param.17) | copy-start | bytes 9220
  57.6 1.3 copy-start.3
  57.9 2.0 %copy-start.7 = (f32[768]{0:T(1024)S(1)}, f32[768]{0:T(1024)}, u32[]{:S(2)}) copy-start(f32[768]{0:T(1024)} %param.19) | copy-start | bytes 9220
  58.2 1.9 %copy-start.2 = (bf16[2,768,192]{1,2,0:T(8,128)(2,1)S(1)}, bf16[2,768,192]{1,2,0:T(8,128)(2,1)}, u32[]{:S(2)}) copy-start(bf16[2,768,192]{1,2,0:T(8,128)(2,1)} %param.24) | copy-start | bytes 1769476
  59.8 65.8 %all-reduce.6.cloned.1.call-start = ((), (), s32[]{:S(2)}) async-start(), calls=%async_computation.4 | async-start | bytes 393216 | tf_op jit(solution)/shard_map/psum | solution.py:40
  60.1 31.4 %copy-start.4 = (bf16[768,192]{0,1:T(8,128)(2,1)S(1)}, bf16[768,192]{0,1:T(8,128)(2,1)}, u32[]{:S(2)}) copy-start(bf16[768,192]{0,1:T(8,128)(2,1)} %param.23) | copy-start | bytes 884740
  60.1 31.4 %copy-start.8 = (f32[768]{0:T(1024)S(1)}, f32[768]{0:T(1024)}, u32[]{:S(2)}) copy-start(f32[768]{0:T(1024)} %param.18) | copy-start | bytes 9220
  91.5 1.3 copy-start.5
  92.0 1.8 copy-start.9
  92.0 33.6 %copy-start.1 = (bf16[128,768]{1,0:T(8,128)(2,1)S(1)}, bf16[128,768]{1,0:T(8,128)(2,1)}, u32[]{:S(2)}) copy-start(bf16[128,768]{1,0:T(8,128)(2,1)} %all-reduce.4.cloned.1.call-done) | copy-start | bytes 589828
  92.6 34.3 %copy-start.14 = (f32[768]{0:T(1024)S(1)}, f32[768]{0:T(1024)}, u32[]{:S(2)}) copy-start(f32[768]{0:T(1024)} %param.20) | copy-start | bytes 9220
  93.7 67.2 %all-reduce.8.cloned.1.call-start = ((), (), s32[]{:S(2)}) async-start(), calls=%async_computation.5 | async-start | bytes 393216 | tf_op jit(solution)/shard_map/psum | solution.py:40
  93.9 33.0 %copy-start.13 = (bf16[768,768]{1,0:T(8,128)(2,1)S(1)}, bf16[768,768]{1,0:T(8,128)(2,1)}, u32[]{:S(2)}) copy-start(bf16[768,768]{1,0:T(8,128)(2,1)} %param.26) | copy-start | bytes 3538948
  126.9 2.2 %copy-start.10 = (s32[4]{0:T(128)S(1)}, s32[4]{0:T(128)}, u32[]{:S(2)}) copy-start(s32[4]{0:T(128)} %get-tuple-element.8) | copy-start | bytes 52
  129.1 38.6 %copy-start.12 = (s32[4]{0:T(128)S(1)}, s32[4]{0:T(128)}, u32[]{:S(2)}) copy-start(s32[4]{0:T(128)} %copy-done.11) | copy-start | bytes 52
  129.8 33.2 %all-to-all-start.2 = ((bf16[4,1,32]{2,1,0:T(2,128)(2,1)}), bf16[4,1,32]{2,1,0:T(2,128)(2,1)S(1)}, u32[]{:S(2)}, u32[]{:S(2)}) async-start(bf16[4,1,32]{2,1,0:T(2,128)(2,1)} %copy.94), calls=%async_computation.2 | async-start | bytes 4096 | tf_op jit(solution)/shard_map/all_to_all | solution.py:115
  163.0 10.3 %all-to-all-start.1 = ((bf16[4,32,192]{2,1,0:T(8,128)(2,1)}), bf16[4,32,192]{2,1,0:T(8,128)(2,1)S(1)}, u32[]{:S(2)}, u32[]{:S(2)}) async-start(bf16[4,32,192]{2,1,0:T(8,128)(2,1)} %reshape.285), calls=%async_computation.1 | async-start | bytes 131072 | tf_op jit(solution)/shard_map/all_to_all | solution.py:112
Sparse Core Ops, SparseCore 0:
  59.9 29.3 all-reduce.3
  93.8 31.7 all-reduce.5
  129.2 31.6 all-reduce.7
where the time goes:
time: 181 us
  waiting for transfers between devices  95.8 us (53%)
  blocking collectives  21.6 us (12%)
  local copies, waits for them, and re-layouts  17.5 us (10%)
  between operations  13.6 us (8%)
  starting transfers between devices  12.6 us (7%)
  other arithmetic  12 us (7%)
  matrix products  7.72 us (4%)
    psum x3, waiting for transfers between devices, summed_full(): return lax.psum(term.astype(jnp.bfloat16), 'mp').astype(jnp.float32)  86.6 us
    all_gather x1, blocking collectives, per_device(): lax.all_gather(pair_list, 'pairs', axis=0, tiled=True)  13 us
    all_gather x1, blocking collectives, per_device(): start = lax.all_gather(slices, 'mp', axis=2, tiled=True)  8.6 us
    rev x2, local copies, waits for them, and re-layouts, partner(): return jnp.flip(paired, axis=1).reshape(shape)  8.14 us
    all_to_all x1, waiting for transfers between devices, per_device(): lax.all_to_all(back.reshape(owners_n, TOKS, quarter), 'pairs', split_axis...  5.53 us
    all_to_all x1, starting transfers between devices, per_device(): lax.all_to_all(back_weight, 'pairs', split_axis=0, concat_axis=0, tiled=T...  4.6 us
    all_to_all x1, starting transfers between devices, per_device(): lax.all_to_all(back.reshape(owners_n, TOKS, quarter), 'pairs', split_axis...  4.6 us
    reduce_sum x4, other arithmetic, layer_norm(): center = values - jnp.mean(values, axis=-1, keepdims=True)  3.78 us
  transfers between devices with their start and end apart: 6, of which 5 were waited for; matrix products, arithmetic and copies ran while one was open for 3% of the time, Pallas kernels for 0%

commit v1 on v0

v1 whole, which is shorter than its diff:
```python
import jax
import jax.numpy as jnp
from jax import lax
from jax.sharding import PartitionSpec as P

HEAD = 64
TOKS = 32


EPSILON = 1e-06


def layer_norm(values, gain):
    center = values - jnp.mean(values, axis=-1, keepdims=True)
    spread = jnp.mean(center * center, axis=-1, keepdims=True)
    return (center * lax.rsqrt(spread + EPSILON) * gain).astype(jnp.bfloat16)


def attend(query, keys, values, views_n):
    rows_n, width = query.shape
    heads_n = width // HEAD
    qh = query.reshape(views_n, TOKS, heads_n, HEAD)
    kh = keys.reshape(views_n, TOKS, heads_n, HEAD)
    vh = values.reshape(views_n, TOKS, heads_n, HEAD)
    scores = jnp.einsum("vqhc,vkhc->vhqk", qh, kh, preferred_element_type=jnp.float32) * HEAD ** (
        -0.5
    )
    probs = jax.nn.softmax(scores, axis=-1).astype(jnp.bfloat16)
    mixed = jnp.einsum("vhqk,vkhc->vqhc", probs, vh, preferred_element_type=jnp.float32)
    return mixed.astype(jnp.bfloat16).reshape(rows_n, width)


def swap(values, pairs):
    return lax.ppermute(values, "mp", pairs)


def mp_pairs(bit):
    n = 4
    return [(i, i ^ bit) for i in range(n)]


def mp_allreduce(term):
    if lax.axis_size("mp") != 4:
        return lax.psum(term.astype(jnp.float32), "mp")
    core = lax.axis_index("mp") % 2
    rows_n = term.shape[0]
    halves = term.reshape(2, rows_n // 2, term.shape[1])
    keep = jnp.where(core == 0, halves[0], halves[1])
    send = jnp.where(core == 0, halves[1], halves[0])
    got = swap(send, mp_pairs(1))
    chip_sum = (keep.astype(jnp.float32) + got.astype(jnp.float32)).astype(jnp.bfloat16)
    other = swap(chip_sum, mp_pairs(2))
    total = chip_sum.astype(jnp.float32) + other.astype(jnp.float32)
    rest = swap(total, mp_pairs(1))
    first = jnp.where(core == 0, total, rest)
    second = jnp.where(core == 0, rest, total)
    return jnp.concatenate([first, second], axis=0)


def mp_reduce_cols(term):
    if lax.axis_size("mp") != 4:
        full = lax.psum(term.astype(jnp.float32), "mp")
        quarter = term.shape[1] // lax.axis_size("mp")
        return lax.dynamic_slice_in_dim(full, lax.axis_index("mp") * quarter, quarter, 1)
    index = lax.axis_index("mp")
    core = index % 2
    chip = index // 2
    rows_n, width = term.shape
    parts = term.reshape(rows_n, 2, 2, width // 4)
    keep = jnp.where(core == 0, parts[:, :, 0], parts[:, :, 1])
    send = jnp.where(core == 0, parts[:, :, 1], parts[:, :, 0])
    got = swap(send, mp_pairs(1))
    both = keep.astype(jnp.float32) + got.astype(jnp.float32)
    mine = jnp.where(chip == 0, both[:, 0], both[:, 1])
    theirs = jnp.where(chip == 0, both[:, 1], both[:, 0])
    other = swap(theirs, mp_pairs(2))
    return mine + other


def mp_gather_cols(part):
    if lax.axis_size("mp") != 4:
        return lax.all_gather(part, "mp", axis=2, tiled=True)
    index = lax.axis_index("mp")
    core = index % 2
    chip = index // 2
    got = swap(part, mp_pairs(1))
    pair = jnp.where(
        core == 0, jnp.concatenate([part, got], axis=2), jnp.concatenate([got, part], axis=2)
    )
    other = swap(pair, mp_pairs(2))
    return jnp.where(
        chip == 0, jnp.concatenate([pair, other], axis=2), jnp.concatenate([other, pair], axis=2)
    )


def per_device(
    tokens,
    pair_list,
    confidence,
    gain_self,
    gain_query,
    gain_context,
    gain_mlp,
    self_qkv,
    self_out,
    cross_query,
    cross_kv,
    cross_out,
    mlp_up,
    mlp_down,
):
    quarter = tokens.shape[1]
    img_dev = tokens.shape[0] // TOKS
    pair_dev = pair_list.shape[0]
    views_n = 2 * pair_dev
    owners_n = lax.axis_size("pairs")
    every = lax.all_gather(tokens, "pairs", axis=0, tiled=True).reshape(
        owners_n * img_dev, TOKS, quarter
    )
    ids = pair_list.reshape(views_n)
    slices = jnp.take(every, ids, axis=0)
    start = mp_gather_cols(slices)
    width = start.shape[2]
    rows_n = views_n * TOKS
    flipped = start.reshape(pair_dev, 2, TOKS, width)
    flipped = jnp.concatenate([flipped[:, 1:], flipped[:, :1]], axis=1)
    begin = start.astype(jnp.float32).reshape(rows_n, width)
    context = layer_norm(flipped.astype(jnp.float32), gain_context).reshape(rows_n, width)
    normed = layer_norm(begin, gain_self)
    qkv = jnp.einsum("rd,kdc->krc", normed, self_qkv, preferred_element_type=jnp.float32).astype(
        jnp.bfloat16
    )
    term = jnp.dot(
        attend(qkv[0], qkv[1], qkv[2], views_n), self_out, preferred_element_type=jnp.float32
    )
    resid = begin + mp_allreduce(term.astype(jnp.bfloat16))
    normed = layer_norm(resid, gain_query)
    query = jnp.dot(normed, cross_query, preferred_element_type=jnp.float32).astype(jnp.bfloat16)
    keyval = jnp.einsum(
        "rd,kdc->krc", context, cross_kv, preferred_element_type=jnp.float32
    ).astype(jnp.bfloat16)
    term = jnp.dot(
        attend(query, keyval[0], keyval[1], views_n), cross_out, preferred_element_type=jnp.float32
    )
    resid = resid + mp_allreduce(term.astype(jnp.bfloat16))
    normed = layer_norm(resid, gain_mlp)
    hidden = jax.nn.gelu(
        jnp.dot(normed, mlp_up, preferred_element_type=jnp.float32), approximate=False
    )
    term = jnp.dot(hidden.astype(jnp.bfloat16), mlp_down, preferred_element_type=jnp.float32)
    offset = lax.axis_index("mp") * quarter
    final = lax.dynamic_slice_in_dim(resid, offset, quarter, 1) + mp_reduce_cols(
        term.astype(jnp.bfloat16)
    )
    conf = confidence.reshape(views_n, TOKS)
    weighted = (final.reshape(views_n, TOKS, quarter) * conf[:, :, None]).reshape(
        views_n, TOKS * quarter
    )
    source = ids // img_dev
    slot = (ids % img_dev + 1).astype(jnp.float32)
    route = (source[None, :] == jnp.arange(owners_n)[:, None]).astype(jnp.float32)
    back = jnp.dot(route, weighted, precision=lax.Precision.HIGHEST)
    back_weight = jnp.dot(route, conf, precision=lax.Precision.HIGHEST)
    back_slot = jnp.dot(route, slot[:, None], precision=lax.Precision.HIGHEST)
    pad = jnp.zeros((owners_n, 128 - TOKS - 1), jnp.float32)
    payload = jnp.concatenate([back, back_weight, back_slot, pad], axis=1).astype(jnp.bfloat16)
    got = lax.all_to_all(payload, "pairs", split_axis=0, concat_axis=0, tiled=True).astype(
        jnp.float32
    )
    feat = got[:, : TOKS * quarter].reshape(owners_n, TOKS, quarter)
    got_weight = got[:, TOKS * quarter : TOKS * quarter + TOKS]
    got_slot = got[:, TOKS * quarter + TOKS]
    owner_match = (got_slot[None, :] == (jnp.arange(img_dev) + 1)[:, None].astype(jnp.float32)).astype(
        jnp.float32
    )
    numer = jnp.einsum("ij,jtc->itc", owner_match, feat, precision=lax.Precision.HIGHEST)
    denom = jnp.dot(owner_match, got_weight, precision=lax.Precision.HIGHEST)
    result = numer / jnp.maximum(denom, 1.0)[:, :, None]
    return result.astype(jnp.bfloat16).reshape(img_dev * TOKS, quarter)


def solution(mesh):
    return jax.shard_map(
        per_device,
        mesh=mesh,
        in_specs=(
            P(("groups", "pairs"), "mp"),
            P(("groups", "pairs"), None),
            P(("groups", "pairs"), None),
            P(),
            P(),
            P(),
            P(),
            P(None, None, "mp"),
            P("mp", None),
            P(None, "mp"),
            P(None, None, "mp"),
            P("mp", None),
            P(None, "mp"),
            P("mp", None),
        ),
        out_specs=P(("groups", "pairs"), "mp"),
        check_vma=False,
    )
```

time: 181 us -> 69.4 us (0.38)
  waiting for transfers between devices: 95.8 us -> 24.7 us
  between operations: 13.6 us -> 0.62 us
  local copies, waits for them, and re-layouts: 17.5 us -> 7.6 us
  other arithmetic: 12 us -> 4.32 us
  blocking collectives: 21.6 us -> 15.3 us
  matrix products: 7.72 us -> 4.83 us
    psum x3 -> x0, waiting for transfers between devices: 86.6 us -> none  [summed_full(): return lax.psum(term.astype(jnp.bfloat16), 'mp').astype(jnp.float32)]
    ppermute x0 -> x10, waiting for transfers between devices: none -> 19 us  [swap(): return lax.ppermute(values, 'mp', pairs)]
    rev x2 -> x0, local copies, waits for them, and re-layouts: 8.14 us -> none  [partner(): return jnp.flip(paired, axis=1).reshape(shape)]
    all_to_all x3 -> x1, starting transfers between devices: 12.5 us -> 4.97 us  [per_device(): lax.all_to_all(payload, 'pairs', split_axis=0, concat_axis=0, tiled=True)]
    ppermute x0 -> x10, starting transfers between devices: none -> 6.86 us  [swap(): return lax.ppermute(values, 'mp', pairs)]
    all_gather x2 -> x1, blocking collectives: 21.6 us -> 15.3 us  [per_device(): lax.all_gather(tokens, 'pairs', axis=0, tiled=True)]
    all_to_all x3 -> x1, waiting for transfers between devices: 9.14 us -> 5.7 us  [per_device(): lax.all_to_all(payload, 'pairs', split_axis=0, concat_axis=0, tiled=True)]
    reduce_sum x4, other arithmetic: 3.78 us -> 0.52 us  [layer_norm(): center = values - jnp.mean(values, axis=-1, keepdims=True)]
  transfers between devices with their start and end apart: 6 -> 11, of which waited for: 5 -> 11; matrix products, arithmetic and copies ran while one was open for 3% -> 4% of each run, Pallas kernels for 0% -> 0%
where the time goes in v1:
time: 69.4 us; the launch traced here: 69.1 us
  waiting for transfers between devices  24.7 us (36%)
  blocking collectives  15.3 us (22%)
  starting transfers between devices  11.8 us (17%)
  local copies, waits for them, and re-layouts  7.6 us (11%)
  matrix products  4.83 us (7%)
  other arithmetic  4.32 us (6%)
    ppermute x10, waiting for transfers between devices, swap(): return lax.ppermute(values, 'mp', pairs)  19 us
    all_gather x1, blocking collectives, per_device(): lax.all_gather(tokens, 'pairs', axis=0, tiled=True)  15.3 us
    ppermute x10, starting transfers between devices, swap(): return lax.ppermute(values, 'mp', pairs)  6.86 us
    all_to_all x1, waiting for transfers between devices, per_device(): lax.all_to_all(payload, 'pairs', split_axis=0, concat_axis=0, tiled=True)  5.7 us
    all_to_all x1, starting transfers between devices, per_device(): lax.all_to_all(payload, 'pairs', split_axis=0, concat_axis=0, tiled=True)  4.97 us
    unnamed x29, local copies, waits for them, and re-layouts  1.71 us
    reshape x2, local copies, waits for them, and re-layouts, per_device(): ids = pair_list.reshape(views_n)  1.61 us
    dot_general x1, matrix products, per_device(): jnp.dot(hidden.astype(jnp.bfloat16), mlp_down, preferred_element_type=jnp...  1.45 us
  transfers between devices with their start and end apart: 11, of which 11 were waited for; matrix products, arithmetic and copies ran while one was open for 4% of the time, Pallas kernels for 0%

profile of v1, /device:TPU:0, one launch (start us, length us, event | category | flops | bytes accessed | tf_op | source)
XLA Modules:
  0.0 69.1 jit_solution(16886699572011220582)
XLA Ops:
  0.0 0.9 %reshape.280 = s32[4,1]{0,1:T(1,128)S(1)} reshape(s32[2,2]{1,0:T(2,128)} %param.15) | data formatting | bytes 32 | tf_op jit(solution)/shard_map/reshape | solution.py:120
  0.9 0.8 %reshape.278 = s32[4]{0:T(128)S(1)} reshape(s32[2,2]{1,0:T(2,128)} %param.15) | data formatting | bytes 32 | tf_op jit(solution)/shard_map/reshape | solution.py:120
  1.6 15.3 %all_gather.3 = bf16[256,192]{1,0:T(8,128)(2,1)S(1)} all-gather(bf16[64,192]{1,0:T(8,128)(2,1)} %param.14), channel_id=1, replica_groups=mesh['groups'=2,'pairs'=4,'mp'=4] {'pairs'}, dimensions={0}, use_global_device_ids=true | all-gather | bytes 122880 | tf_op jit(solution)/shard_map/all_gather | solution.py:117
  16.9 0.6 gather_fusion
  17.6 0.7 compare_and_fusion
  18.6 0.2 collective-permute-done
  18.9 1.6 %collective-permute-start.1 = (bf16[4,32,384]{2,1,0:T(8,128)(2,1)S(1)}, bf16[4,32,384]{2,1,0:T(8,128)(2,1)S(1)}, u32[]{:S(2)}, u32[]{:S(2)}) collective-permute-start(bf16[4,32,384]{2,1,0:T(8,128)(2,1)S(1)} %maximum_select_fusion.3), channel_id=1, source_target_pairs={{0,2},{1,3},{2,0},{3,1},{4,6},{5,7},{6,4},{7,5},{8,10},{9,11},{10,... | collective-permute-start | bytes 294920 | tf_op jit(solution)/shard_map/ppermute | solution.py:34
  20.7 3.2 %collective-permute-done.1 = bf16[4,32,384]{2,1,0:T(8,128)(2,1)S(1)} collective-permute-done((bf16[4,32,384]{2,1,0:T(8,128)(2,1)S(1)}, bf16[4,32,384]{2,1,0:T(8,128)(2,1)S(1)}, u32[]{:S(2)}, u32[]{:S(2)}) %collective-permute-start.1) | collective-permute-done | bytes 98336 | tf_op jit(solution)/shard_map/ppermute | solution.py:34
  24.2 0.2 multiply_reduce_fusion.2
  24.6 0.1 convert_reduce_fusion
  24.7 0.2 fusion.15
  24.9 0.5 fusion.33
  25.5 0.1 reshape.306
  25.6 0.1 reshape.308
  25.8 0.1 reshape.307
  25.9 0.2 convolution_multiply_fusion.1
  26.2 0.3 fusion.7
  26.6 0.1 reshape.281
  26.7 0.1 copy-done.2
  26.9 0.2 convolution_convert_fusion.3
  27.2 0.1 fusion.23
  27.3 0.3 copy-done.1
  27.6 0.3 fusion.149
  27.9 0.5 collective-permute-done.2
  28.5 1.6 %collective-permute-start.3 = (bf16[64,768]{1,0:T(8,128)(2,1)S(1)}, bf16[64,768]{1,0:T(8,128)(2,1)S(1)}, u32[]{:S(2)}, u32[]{:S(2)}) collective-permute-start(bf16[64,768]{1,0:T(8,128)(2,1)S(1)} %add_convert_fusion.1), channel_id=1, source_target_pairs={{0,2},{1,3},{2,0},{3,1},{4,6},{5,7},{6,4},{7,5},{8,10},{9,11},{10,... | collective-permute-start | bytes 294920 | tf_op jit(solution)/shard_map/ppermute | solution.py:34
  30.1 3.3 %collective-permute-done.3 = bf16[64,768]{1,0:T(8,128)(2,1)S(1)} collective-permute-done((bf16[64,768]{1,0:T(8,128)(2,1)S(1)}, bf16[64,768]{1,0:T(8,128)(2,1)S(1)}, u32[]{:S(2)}, u32[]{:S(2)}) %collective-permute-start.3) | collective-permute-done | bytes 98336 | tf_op jit(solution)/shard_map/ppermute | solution.py:34
  33.6 0.1 reshape.309
  33.7 0.1 reshape.311
  33.8 1.1 %collective-permute-done.4 = f32[64,768]{1,0:T(8,128)S(1)} collective-permute-done((f32[64,768]{1,0:T(8,128)S(1)}, f32[64,768]{1,0:T(8,128)S(1)}, u32[]{:S(2)}, u32[]{:S(2)}) %collective-permute-start.4) | collective-permute-done | bytes 196640 | tf_op jit(solution)/shard_map/ppermute | solution.py:34
  35.0 0.1 fusion.141
  35.1 0.2 multiply_reduce_fusion.1
  35.4 0.3 convolution_convert_fusion.6
  35.7 0.1 reshape.310
  35.8 0.2 convolution_multiply_fusion
  36.2 0.3 fusion.8
  36.5 0.1 reshape.283
  36.7 0.1 copy-done.3
  36.8 0.2 convolution_convert_fusion.2
  37.0 0.2 collective-permute-start.5
  37.2 1.2 %collective-permute-done.5 = bf16[64,768]{1,0:T(8,128)(2,1)S(1)} collective-permute-done((bf16[64,768]{1,0:T(8,128)(2,1)S(1)}, bf16[64,768]{1,0:T(8,128)(2,1)S(1)}, u32[]{:S(2)}, u32[]{:S(2)}) %collective-permute-start.5) | collective-permute-done | bytes 98336 | tf_op jit(solution)/shard_map/ppermute | solution.py:34
  38.4 1.6 %collective-permute-start.6 = (bf16[64,768]{1,0:T(8,128)(2,1)S(1)}, bf16[64,768]{1,0:T(8,128)(2,1)S(1)}, u32[]{:S(2)}, u32[]{:S(2)}) collective-permute-start(bf16[64,768]{1,0:T(8,128)(2,1)S(1)} %add_convert_fusion), channel_id=1, source_target_pairs={{0,2},{1,3},{2,0},{3,1},{4,6},{5,7},{6,4},{7,5},{8,10},{9,11},{10,... | collective-permute-start | bytes 294920 | tf_op jit(solution)/shard_map/ppermute | solution.py:34
  40.3 3.1 %collective-permute-done.6 = bf16[64,768]{1,0:T(8,128)(2,1)S(1)} collective-permute-done((bf16[64,768]{1,0:T(8,128)(2,1)S(1)}, bf16[64,768]{1,0:T(8,128)(2,1)S(1)}, u32[]{:S(2)}, u32[]{:S(2)}) %collective-permute-start.6) | collective-permute-done | bytes 98336 | tf_op jit(solution)/shard_map/ppermute | solution.py:34
  43.5 1.4 %collective-permute-done.7 = f32[64,768]{1,0:T(8,128)S(1)} collective-permute-done((f32[64,768]{1,0:T(8,128)S(1)}, f32[64,768]{1,0:T(8,128)S(1)}, u32[]{:S(2)}, u32[]{:S(2)}) %collective-permute-start.7) | collective-permute-done | bytes 196640 | tf_op jit(solution)/shard_map/ppermute | solution.py:34
  44.9 0.1 fusion.142
  45.1 0.2 multiply_reduce_fusion
  45.3 1.5 %convolution_convert_fusion.1 = bf16[128,768]{1,0:T(8,128)(2,1)S(1)} fusion(bf16[768,768]{1,0:T(8,128)(2,1)S(1)} %copy-done, bf16[768,768]{1,0:T(8,128)(2,1)S(1)} %copy-done.6, f32[128,768]{1,0:T(8,128)S(1)} %get-tuple-element.6, f32[768]{0:T(1024)S(1)} %copy-done.11, f32[128]{0:T(128)S(1)} %add_rsqrt_fusion.1, f32[128]{0:T(128)S(1)} %broadcast_multiply_fusion.1), kind=kOutput, calls=%fused_computation.7 | convolution fusion | flops 308871168 | bytes 2953216 | tf_op jit(solution)/shard_map/dot_general | solution.py:150
  46.8 0.2 copy.88
  47.2 0.2 collective-permute-start.8
  47.4 0.1 fusion.12
  47.7 1.0 %collective-permute-done.8 = bf16[128,2,192]{2,0,1:T(8,128)(2,1)S(1)} collective-permute-done((bf16[128,2,192]{2,0,1:T(8,128)(2,1)S(1)}, bf16[128,2,192]{2,0,1:T(8,128)(2,1)S(1)}, u32[]{:S(2)}, u32[]{:S(2)}) %collective-permute-start.8) | collective-permute-done | bytes 98336 | tf_op jit(solution)/shard_map/ppermute | solution.py:34
  48.7 1.6 %collective-permute-start.9 = (f32[128,192]{1,0:T(8,128)S(1)}, f32[128,192]{1,0:T(8,128)S(1)}, u32[]{:S(2)}, u32[]{:S(2)}) collective-permute-start(f32[128,192]{1,0:T(8,128)S(1)} %select_bitcast_fusion), channel_id=1, source_target_pairs={{0,2},{1,3},{2,0},{3,1},{4,6},{5,7},{6,4},{7,5},{8,10},{9,11},{10,... | collective-permute-start | bytes 294920 | tf_op jit(solution)/shard_map/ppermute | solution.py:34
  50.3 0.1 fusion.10
  50.4 3.9 %collective-permute-done.9 = f32[128,192]{1,0:T(8,128)S(1)} collective-permute-done((f32[128,192]{1,0:T(8,128)S(1)}, f32[128,192]{1,0:T(8,128)S(1)}, u32[]{:S(2)}, u32[]{:S(2)}) %collective-permute-start.9) | collective-permute-done | bytes 98336 | tf_op jit(solution)/shard_map/ppermute | solution.py:34
  54.5 0.2 fusion.2
  54.9 0.5 broadcast.282
  55.4 0.7 reduce.2
  56.1 0.7 %reshape.313 = bf16[4,2,3136]{2,1,0:T(2,128)(2,1)} reshape(bf16[4,6272]{1,0:T(4,128)(2,1)S(1)} %reduce.2) | data formatting | bytes 100352
  56.8 5.0 %all-to-all-start = ((bf16[4,2,3136]{2,1,0:T(2,128)(2,1)}), bf16[4,2,3136]{2,1,0:T(2,128)(2,1)S(1)}, u32[]{:S(2)}, u32[]{:S(2)}) async-start(bf16[4,2,3136]{2,1,0:T(2,128)(2,1)} %reshape.313), calls=%async_computation | async-start | bytes 102400 | tf_op jit(solution)/shard_map/all_to_all | solution.py:167
  61.8 5.7 %all-to-all-done = bf16[4,2,3136]{2,1,0:T(2,128)(2,1)S(1)} async-done(((bf16[4,2,3136]{2,1,0:T(2,128)(2,1)}), bf16[4,2,3136]{2,1,0:T(2,128)(2,1)S(1)}, u32[]{:S(2)}, u32[]{:S(2)}) %all-to-all-start) | async-done | bytes 50208 | tf_op jit(solution)/shard_map/all_to_all | solution.py:167
  67.5 0.1 reshape.314
  67.7 0.2 convert_reduce_fusion.1
  68.0 0.2 convolution_maximum_fusion
  68.3 0.2 fusion.9
  68.5 0.6 copy.95
  (86 shorter events, 3.4 us)
Async XLA Ops:
  0.0 45.3 %copy-start = (bf16[768,768]{1,0:T(8,128)(2,1)S(1)}, bf16[768,768]{1,0:T(8,128)(2,1)}, u32[]{:S(2)}) copy-start(bf16[768,768]{1,0:T(8,128)(2,1)} %param.27) | copy-start | bytes 3538948
  17.5 1.3 %collective-permute-start = (bf16[4,32,192]{2,1,0:T(8,128)(2,1)S(1)}, bf16[4,32,192]{2,1,0:T(8,128)(2,1)S(1)}, u32[]{:S(2)}, u32[]{:S(2)}) collective-permute-start(bf16[4,32,192]{2,1,0:T(8,128)(2,1)S(1)} %broadcast_select_fusion.6), channel_id=1, source_target_pairs={{0,1},{1,0},{2,3},{3,2},{4,5},{5,4},{6,7},{7,6},{8,9},{9,8},{10,11... | collective-permute-start | bytes 147464 | tf_op jit(solution)/shard_map/ppermute | solution.py:34
  18.9 5.1 %collective-permute-start.1 = (bf16[4,32,384]{2,1,0:T(8,128)(2,1)S(1)}, bf16[4,32,384]{2,1,0:T(8,128)(2,1)S(1)}, u32[]{:S(2)}, u32[]{:S(2)}) collective-permute-start(bf16[4,32,384]{2,1,0:T(8,128)(2,1)S(1)} %maximum_select_fusion.3), channel_id=1, source_target_pairs={{0,2},{1,3},{2,0},{3,1},{4,6},{5,7},{6,4},{7,5},{8,10},{9,11},{10,... | collective-permute-start | bytes 294920 | tf_op jit(solution)/shard_map/ppermute | solution.py:34
  20.6 4.3 %copy-start.7 = (bf16[3,768,192]{1,2,0:T(8,128)(2,1)S(1)}, bf16[3,768,192]{1,2,0:T(8,128)(2,1)}, u32[]{:S(2)}) copy-start(bf16[3,768,192]{1,2,0:T(8,128)(2,1)} %param.21) | copy-start | bytes 2654212
  20.6 4.3 %copy-start.9 = (f32[768]{0:T(1024)S(1)}, f32[768]{0:T(1024)}, u32[]{:S(2)}) copy-start(f32[768]{0:T(1024)} %param.17) | copy-start | bytes 9220
  25.9 1.0 %copy-start.2 = (bf16[192,768]{1,0:T(8,128)(2,1)S(1)}, bf16[192,768]{1,0:T(8,128)(2,1)}, u32[]{:S(2)}) copy-start(bf16[192,768]{1,0:T(8,128)(2,1)} %param.22) | copy-start | bytes 884740
  26.2 1.0 %copy-start.4 = (f32[768]{0:T(1024)S(1)}, f32[768]{0:T(1024)}, u32[]{:S(2)}) copy-start(f32[768]{0:T(1024)} %param.19) | copy-start | bytes 9220
  26.5 1.1 %copy-start.1 = (bf16[2,768,192]{1,2,0:T(8,128)(2,1)S(1)}, bf16[2,768,192]{1,2,0:T(8,128)(2,1)}, u32[]{:S(2)}) copy-start(bf16[2,768,192]{1,2,0:T(8,128)(2,1)} %param.24) | copy-start | bytes 1769476
  27.1 1.4 %collective-permute-start.2 = (bf16[64,768]{1,0:T(8,128)(2,1)S(1)}, bf16[64,768]{1,0:T(8,128)(2,1)S(1)}, u32[]{:S(2)}, u32[]{:S(2)}) collective-permute-start(bf16[64,768]{1,0:T(8,128)(2,1)S(1)} %broadcast_select_fusion.5), channel_id=1, source_target_pairs={{0,1},{1,0},{2,3},{3,2},{4,5},{5,4},{6,7},{7,6},{8,9},{9,8},{10,11... | collective-permute-start | bytes 294920 | tf_op jit(solution)/shard_map/ppermute | solution.py:34
  28.5 4.9 %collective-permute-start.3 = (bf16[64,768]{1,0:T(8,128)(2,1)S(1)}, bf16[64,768]{1,0:T(8,128)(2,1)S(1)}, u32[]{:S(2)}, u32[]{:S(2)}) collective-permute-start(bf16[64,768]{1,0:T(8,128)(2,1)S(1)} %add_convert_fusion.1), channel_id=1, source_target_pairs={{0,2},{1,3},{2,0},{3,1},{4,6},{5,7},{6,4},{7,5},{8,10},{9,11},{10,... | collective-permute-start | bytes 294920 | tf_op jit(solution)/shard_map/ppermute | solution.py:34
  33.4 1.5 %collective-permute-start.4 = (f32[64,768]{1,0:T(8,128)S(1)}, f32[64,768]{1,0:T(8,128)S(1)}, u32[]{:S(2)}, u32[]{:S(2)}) collective-permute-start(f32[64,768]{1,0:T(8,128)S(1)} %convert_add_fusion.3), channel_id=1, source_target_pairs={{0,1},{1,0},{2,3},{3,2},{4,5},{5,4},{6,7},{7,6},{8,9},{9,8},{10,11... | collective-permute-start | bytes 589832 | tf_op jit(solution)/shard_map/ppermute | solution.py:34
  33.5 1.8 %copy-start.8 = (bf16[768,192]{0,1:T(8,128)(2,1)S(1)}, bf16[768,192]{0,1:T(8,128)(2,1)}, u32[]{:S(2)}) copy-start(bf16[768,192]{0,1:T(8,128)(2,1)} %param.23) | copy-start | bytes 884740
  33.5 1.8 %copy-start.10 = (f32[768]{0:T(1024)S(1)}, f32[768]{0:T(1024)}, u32[]{:S(2)}) copy-start(f32[768]{0:T(1024)} %param.18) | copy-start | bytes 9220
  35.8 1.0 %copy-start.3 = (bf16[192,768]{1,0:T(8,128)(2,1)S(1)}, bf16[192,768]{1,0:T(8,128)(2,1)}, u32[]{:S(2)}) copy-start(bf16[192,768]{1,0:T(8,128)(2,1)} %param.25) | copy-start | bytes 884740
  36.1 3.8 %copy-start.5 = (f32[2,64]{1,0:T(2,128)S(1)}, f32[2,64]{1,0:T(2,128)}, u32[]{:S(2)}) copy-start(f32[2,64]{1,0:T(2,128)} %param.16) | copy-start | bytes 1540
  37.0 1.4 %collective-permute-start.5 = (bf16[64,768]{1,0:T(8,128)(2,1)S(1)}, bf16[64,768]{1,0:T(8,128)(2,1)S(1)}, u32[]{:S(2)}, u32[]{:S(2)}) collective-permute-start(bf16[64,768]{1,0:T(8,128)(2,1)S(1)} %broadcast_select_fusion.2), channel_id=1, source_target_pairs={{0,1},{1,0},{2,3},{3,2},{4,5},{5,4},{6,7},{7,6},{8,9},{9,8},{10,11... | collective-permute-start | bytes 294920 | tf_op jit(solution)/shard_map/ppermute | solution.py:34
  38.4 4.9 %collective-permute-start.6 = (bf16[64,768]{1,0:T(8,128)(2,1)S(1)}, bf16[64,768]{1,0:T(8,128)(2,1)S(1)}, u32[]{:S(2)}, u32[]{:S(2)}) collective-permute-start(bf16[64,768]{1,0:T(8,128)(2,1)S(1)} %add_convert_fusion), channel_id=1, source_target_pairs={{0,2},{1,3},{2,0},{3,1},{4,6},{5,7},{6,4},{7,5},{8,10},{9,11},{10,... | collective-permute-start | bytes 294920 | tf_op jit(solution)/shard_map/ppermute | solution.py:34
  43.4 1.5 %collective-permute-start.7 = (f32[64,768]{1,0:T(8,128)S(1)}, f32[64,768]{1,0:T(8,128)S(1)}, u32[]{:S(2)}, u32[]{:S(2)}) collective-permute-start(f32[64,768]{1,0:T(8,128)S(1)} %convert_add_fusion.2), channel_id=1, source_target_pairs={{0,1},{1,0},{2,3},{3,2},{4,5},{5,4},{6,7},{7,6},{8,9},{9,8},{10,11... | collective-permute-start | bytes 589832 | tf_op jit(solution)/shard_map/ppermute | solution.py:34
  43.5 1.8 %copy-start.6 = (bf16[768,768]{1,0:T(8,128)(2,1)S(1)}, bf16[768,768]{1,0:T(8,128)(2,1)}, u32[]{:S(2)}) copy-start(bf16[768,768]{1,0:T(8,128)(2,1)} %param.26) | copy-start | bytes 3538948
  43.5 1.8 %copy-start.11 = (f32[768]{0:T(1024)S(1)}, f32[768]{0:T(1024)}, u32[]{:S(2)}) copy-start(f32[768]{0:T(1024)} %param.20) | copy-start | bytes 9220
  47.2 1.4 %collective-permute-start.8 = (bf16[128,2,192]{2,0,1:T(8,128)(2,1)S(1)}, bf16[128,2,192]{2,0,1:T(8,128)(2,1)S(1)}, u32[]{:S(2)}, u32[]{:S(2)}) collective-permute-start(bf16[128,2,192]{2,0,1:T(8,128)(2,1)S(1)} %select_bitcast_fusion.1), channel_id=1, source_target_pairs={{0,1},{1,0},{2,3},{3,2},{4,5},{5,4},{6,7},{7,6},{8,9},{9,8},{10,11... | collective-permute-start | bytes 294920 | tf_op jit(solution)/shard_map/ppermute | solution.py:34
  48.7 5.6 %collective-permute-start.9 = (f32[128,192]{1,0:T(8,128)S(1)}, f32[128,192]{1,0:T(8,128)S(1)}, u32[]{:S(2)}, u32[]{:S(2)}) collective-permute-start(f32[128,192]{1,0:T(8,128)S(1)} %select_bitcast_fusion), channel_id=1, source_target_pairs={{0,2},{1,3},{2,0},{3,1},{4,6},{5,7},{6,4},{7,5},{8,10},{9,11},{10,... | collective-permute-start | bytes 294920 | tf_op jit(solution)/shard_map/ppermute | solution.py:34
  56.8 10.7 %all-to-all-start = ((bf16[4,2,3136]{2,1,0:T(2,128)(2,1)}), bf16[4,2,3136]{2,1,0:T(2,128)(2,1)S(1)}, u32[]{:S(2)}, u32[]{:S(2)}) async-start(bf16[4,2,3136]{2,1,0:T(2,128)(2,1)} %reshape.313), calls=%async_computation | async-start | bytes 102400 | tf_op jit(solution)/shard_map/all_to_all | solution.py:167

commit v2 on v1

--- a/solution.py
+++ b/solution.py
@@ -28,6 +28,13 @@
     probs = jax.nn.softmax(scores, axis=-1).astype(jnp.bfloat16)
     mixed = jnp.einsum("vhqk,vkhc->vqhc", probs, vh, preferred_element_type=jnp.float32)
     return mixed.astype(jnp.bfloat16).reshape(rows_n, width)
+
+
+SHIFTS_MAX = 8
+
+
+def pairs_shift(values, step, owners_n):
+    return lax.ppermute(values, "pairs", [(i, (i + step) % owners_n) for i in range(owners_n)])
 
 
 def swap(values, pairs):
@@ -114,11 +121,21 @@
     pair_dev = pair_list.shape[0]
     views_n = 2 * pair_dev
     owners_n = lax.axis_size("pairs")
-    every = lax.all_gather(tokens, "pairs", axis=0, tiled=True).reshape(
-        owners_n * img_dev, TOKS, quarter
-    )
+    own = lax.axis_index("pairs")
     ids = pair_list.reshape(views_n)
-    slices = jnp.take(every, ids, axis=0)
+    source = ids // img_dev
+    if owners_n <= SHIFTS_MAX:
+        every = jnp.concatenate(
+            [tokens] + [pairs_shift(tokens, step, owners_n) for step in range(1, owners_n)], axis=0
+        )
+        at = ((own - source) % owners_n) * img_dev + ids % img_dev
+        targets = (own + jnp.arange(owners_n)) % owners_n
+    else:
+        every = lax.all_gather(tokens, "pairs", axis=0, tiled=True)
+        at = ids
+        targets = jnp.arange(owners_n)
+    every = every.reshape(owners_n * img_dev, TOKS, quarter)
+    slices = jnp.take(every, at, axis=0)
     start = mp_gather_cols(slices)
     width = start.shape[2]
     rows_n = views_n * TOKS
@@ -156,17 +173,21 @@
     weighted = (final.reshape(views_n, TOKS, quarter) * conf[:, :, None]).reshape(
         views_n, TOKS * quarter
     )
-    source = ids // img_dev
     slot = (ids % img_dev + 1).astype(jnp.float32)
-    route = (source[None, :] == jnp.arange(owners_n)[:, None]).astype(jnp.float32)
+    route = (source[None, :] == targets[:, None]).astype(jnp.float32)
     back = jnp.dot(route, weighted, precision=lax.Precision.HIGHEST)
     back_weight = jnp.dot(route, conf, precision=lax.Precision.HIGHEST)
     back_slot = jnp.dot(route, slot[:, None], precision=lax.Precision.HIGHEST)
     pad = jnp.zeros((owners_n, 128 - TOKS - 1), jnp.float32)
     payload = jnp.concatenate([back, back_weight, back_slot, pad], axis=1).astype(jnp.bfloat16)
-    got = lax.all_to_all(payload, "pairs", split_axis=0, concat_axis=0, tiled=True).astype(
-        jnp.float32
-    )
+    if owners_n <= SHIFTS_MAX:
+        got = jnp.stack(
+            [payload[0]]
+            + [pairs_shift(payload[step], step, owners_n) for step in range(1, owners_n)]
+        )
+    else:
+        got = lax.all_to_all(payload, "pairs", split_axis=0, concat_axis=0, tiled=True)
+    got = got.astype(jnp.float32)
     feat = got[:, : TOKS * quarter].reshape(owners_n, TOKS, quarter)
     got_weight = got[:, TOKS * quarter : TOKS * quarter + TOKS]
     got_slot = got[:, TOKS * quarter + TOKS]

time: 69.4 us -> 59.6 us (0.86)
  blocking collectives: 15.3 us -> 0 us
  starting transfers between devices: 11.8 us -> 16.1 us
  local copies, waits for them, and re-layouts: 7.6 us -> 6.39 us
  waiting for transfers between devices: 24.7 us -> 25.9 us
  matrix products: 4.83 us -> 5.71 us
    all_gather x1 -> x0, blocking collectives: 15.3 us -> none  [per_device(): lax.all_gather(tokens, 'pairs', axis=0, tiled=True)]
    ppermute x0 -> x6, starting transfers between devices: none -> 9.27 us  [pairs_shift(): lax.ppermute(values, 'pairs', [(i, (i + step) % owners_n) for i in range(...]
    ppermute x0 -> x6, waiting for transfers between devices: none -> 6.27 us  [pairs_shift(): lax.ppermute(values, 'pairs', [(i, (i + step) % owners_n) for i in range(...]
    all_to_all x1 -> x0, waiting for transfers between devices: 5.7 us -> none  [per_device(): lax.all_to_all(payload, 'pairs', split_axis=0, concat_axis=0, tiled=True)]
    all_to_all x1 -> x0, starting transfers between devices: 4.97 us -> none  [per_device(): lax.all_to_all(payload, 'pairs', split_axis=0, concat_axis=0, tiled=True)]
    unnamed x29 -> x24, local copies, waits for them, and re-layouts: 1.71 us -> 0.82 us
  transfers between devices with their start and end apart: 11 -> 16, of which waited for: 11 -> 15; matrix products, arithmetic and copies ran while one was open for 4% -> 7% of each run, Pallas kernels for 0% -> 0%
where the time goes in v2:
time: 59.6 us; the launch traced here: 59.3 us
  waiting for transfers between devices  25.9 us (43%)
  starting transfers between devices  16.1 us (27%)
  local copies, waits for them, and re-layouts  6.39 us (11%)
  matrix products  5.71 us (10%)
  other arithmetic  4.62 us (8%)
  between operations  0.63 us (1%)
    ppermute x10, waiting for transfers between devices, swap(): return lax.ppermute(values, 'mp', pairs)  19.6 us
    ppermute x6, starting transfers between devices, pairs_shift(): lax.ppermute(values, 'pairs', [(i, (i + step) % owners_n) for i in range(...  9.27 us
    ppermute x10, starting transfers between devices, swap(): return lax.ppermute(values, 'mp', pairs)  6.86 us
    ppermute x6, waiting for transfers between devices, pairs_shift(): lax.ppermute(values, 'pairs', [(i, (i + step) % owners_n) for i in range(...  6.27 us
    dot_general x1, matrix products, per_device(): jnp.dot(hidden.astype(jnp.bfloat16), mlp_down, preferred_element_type=jnp...  2.14 us
    reshape x2, local copies, waits for them, and re-layouts, per_device(): ids = pair_list.reshape(views_n)  1.52 us
  transfers between devices with their start and end apart: 16, of which 15 were waited for; matrix products, arithmetic and copies ran while one was open for 7% of the time, Pallas kernels for 0%

profile of v2, /device:TPU:0, one launch (start us, length us, event | category | flops | bytes accessed | tf_op | source)
XLA Modules:
  0.0 59.3 jit_solution(1516193516099292751)
XLA Ops:
  0.0 5.0 %collective-permute-start.2 = (bf16[64,192]{1,0:T(8,128)(2,1)}, bf16[64,192]{1,0:T(8,128)(2,1)S(1)}, u32[]{:S(2)}, u32[]{:S(2)}) collective-permute-start(bf16[64,192]{1,0:T(8,128)(2,1)} %param.14), channel_id=1, source_target_pairs={{0,12},{4,0},{8,4},{12,8},{1,13},{5,1},{9,5},{13,9},{2,14},{6,2},{... | collective-permute-start | bytes 73736 | tf_op jit(solution)/shard_map/ppermute | solution.py:37
  5.1 1.0 %collective-permute-start = (bf16[64,192]{1,0:T(8,128)(2,1)}, bf16[64,192]{1,0:T(8,128)(2,1)S(1)}, u32[]{:S(2)}, u32[]{:S(2)}) collective-permute-start(bf16[64,192]{1,0:T(8,128)(2,1)} %param.14), channel_id=1, source_target_pairs={{0,4},{4,8},{8,12},{12,0},{1,5},{5,9},{9,13},{13,1},{2,6},{6,10},{... | collective-permute-start | bytes 73736 | tf_op jit(solution)/shard_map/ppermute | solution.py:37
  6.1 0.8 %reshape.359 = s32[4,1]{0,1:T(1,128)S(1)} reshape(s32[2,2]{1,0:T(2,128)} %param.15) | data formatting | bytes 32 | tf_op jit(solution)/shard_map/reshape | solution.py:125
  6.8 0.8 %reshape.357 = s32[4]{0:T(128)S(1)} reshape(s32[2,2]{1,0:T(2,128)} %param.15) | data formatting | bytes 32 | tf_op jit(solution)/shard_map/reshape | solution.py:125
  7.6 0.7 %compare_and_fusion = pred[2,2]{1,0:T(4,128)(4,1)S(1)} fusion(s32[2,2]{1,0:T(2,128)} %param.15, s32[]{:T(128)S(6)} %axis_index.15), kind=kLoop, calls=%fused_computation.166 | loop fusion | flops 156 | bytes 24 | tf_op jit(solution)/shard_map/jit(_take)/and | solution.py:138
  8.5 1.5 %collective-permute-done.1 = bf16[64,192]{1,0:T(8,128)(2,1)S(1)} collective-permute-done((bf16[64,192]{1,0:T(8,128)(2,1)}, bf16[64,192]{1,0:T(8,128)(2,1)S(1)}, u32[]{:S(2)}, u32[]{:S(2)}) %collective-permute-start.1) | collective-permute-done | bytes 24608 | tf_op jit(solution)/shard_map/ppermute | solution.py:37
  10.1 0.9 %collective-permute-done = bf16[64,192]{1,0:T(8,128)(2,1)S(1)} collective-permute-done((bf16[64,192]{1,0:T(8,128)(2,1)}, bf16[64,192]{1,0:T(8,128)(2,1)S(1)}, u32[]{:S(2)}, u32[]{:S(2)}) %collective-permute-start) | collective-permute-done | bytes 24608 | tf_op jit(solution)/shard_map/ppermute | solution.py:37
  11.0 0.8 %pad_maximum_fusion = bf16[256,192]{1,0:T(8,128)(2,1)S(1)} fusion(bf16[64,192]{1,0:T(8,128)(2,1)S(1)} %collective-permute-done.2, bf16[64,192]{1,0:T(8,128)(2,1)S(1)} %collective-permute-done.1, bf16[64,192]{1,0:T(8,128)(2,1)S(1)} %collective-permute-done, bf16[64,192]{1,0:T(8,128)(2,1)} %param.14), kind=kLoop, calls=%fused_computation.120 | loop fusion | flops 393216 | bytes 196608 | tf_op jit(solution)/shard_map/concatenate | solution.py:128
  11.8 0.6 gather_fusion
  12.6 1.1 %collective-permute-done.3 = bf16[4,32,192]{2,1,0:T(8,128)(2,1)S(1)} collective-permute-done((bf16[4,32,192]{2,1,0:T(8,128)(2,1)S(1)}, bf16[4,32,192]{2,1,0:T(8,128)(2,1)S(1)}, u32[]{:S(2)}, u32[]{:S(2)}) %collective-permute-start.3) | collective-permute-done | bytes 49184 | tf_op jit(solution)/shard_map/ppermute | solution.py:41
  13.8 1.6 %collective-permute-start.4 = (bf16[4,32,384]{2,1,0:T(8,128)(2,1)S(1)}, bf16[4,32,384]{2,1,0:T(8,128)(2,1)S(1)}, u32[]{:S(2)}, u32[]{:S(2)}) collective-permute-start(bf16[4,32,384]{2,1,0:T(8,128)(2,1)S(1)} %maximum_select_fusion.3), channel_id=1, source_target_pairs={{0,2},{1,3},{2,0},{3,1},{4,6},{5,7},{6,4},{7,5},{8,10},{9,11},{10,... | collective-permute-start | bytes 294920 | tf_op jit(solution)/shard_map/ppermute | solution.py:41
  15.6 3.1 %collective-permute-done.4 = bf16[4,32,384]{2,1,0:T(8,128)(2,1)S(1)} collective-permute-done((bf16[4,32,384]{2,1,0:T(8,128)(2,1)S(1)}, bf16[4,32,384]{2,1,0:T(8,128)(2,1)S(1)}, u32[]{:S(2)}, u32[]{:S(2)}) %collective-permute-start.4) | collective-permute-done | bytes 98336 | tf_op jit(solution)/shard_map/ppermute | solution.py:41
  18.9 0.2 multiply_reduce_fusion.2
  19.4 0.2 fusion.13
  19.7 0.5 fusion.31
  20.2 0.1 reshape.385
  20.3 0.1 reshape.387
  20.5 0.1 reshape.386
  20.6 0.2 convolution_multiply_fusion.1
  20.9 0.3 fusion.6
  21.3 0.1 reshape.360
  21.6 0.2 convolution_convert_fusion.3
  22.0 0.3 copy-done.1
  22.3 0.3 fusion.161
  22.7 0.5 collective-permute-done.5
  23.2 1.6 %collective-permute-start.6 = (bf16[64,768]{1,0:T(8,128)(2,1)S(1)}, bf16[64,768]{1,0:T(8,128)(2,1)S(1)}, u32[]{:S(2)}, u32[]{:S(2)}) collective-permute-start(bf16[64,768]{1,0:T(8,128)(2,1)S(1)} %add_convert_fusion.1), channel_id=1, source_target_pairs={{0,2},{1,3},{2,0},{3,1},{4,6},{5,7},{6,4},{7,5},{8,10},{9,11},{10,... | collective-permute-start | bytes 294920 | tf_op jit(solution)/shard_map/ppermute | solution.py:41
  24.8 3.3 %collective-permute-done.6 = bf16[64,768]{1,0:T(8,128)(2,1)S(1)} collective-permute-done((bf16[64,768]{1,0:T(8,128)(2,1)S(1)}, bf16[64,768]{1,0:T(8,128)(2,1)S(1)}, u32[]{:S(2)}, u32[]{:S(2)}) %collective-permute-start.6) | collective-permute-done | bytes 98336 | tf_op jit(solution)/shard_map/ppermute | solution.py:41
  28.3 0.1 reshape.388
  28.6 1.1 %collective-permute-done.7 = f32[64,768]{1,0:T(8,128)S(1)} collective-permute-done((f32[64,768]{1,0:T(8,128)S(1)}, f32[64,768]{1,0:T(8,128)S(1)}, u32[]{:S(2)}, u32[]{:S(2)}) %collective-permute-start.7) | collective-permute-done | bytes 196640 | tf_op jit(solution)/shard_map/ppermute | solution.py:41
  29.7 0.1 fusion.153
  29.9 0.2 multiply_reduce_fusion.1
  30.1 0.3 convolution_convert_fusion.6
  30.4 0.1 reshape.389
  30.6 0.2 convolution_multiply_fusion
  30.9 0.3 fusion.7
  31.3 0.1 reshape.362
  31.5 0.2 convolution_convert_fusion.2
  31.8 0.2 collective-permute-start.8
  32.0 1.2 %collective-permute-done.8 = bf16[64,768]{1,0:T(8,128)(2,1)S(1)} collective-permute-done((bf16[64,768]{1,0:T(8,128)(2,1)S(1)}, bf16[64,768]{1,0:T(8,128)(2,1)S(1)}, u32[]{:S(2)}, u32[]{:S(2)}) %collective-permute-start.8) | collective-permute-done | bytes 98336 | tf_op jit(solution)/shard_map/ppermute | solution.py:41
  33.2 1.6 %collective-permute-start.9 = (bf16[64,768]{1,0:T(8,128)(2,1)S(1)}, bf16[64,768]{1,0:T(8,128)(2,1)S(1)}, u32[]{:S(2)}, u32[]{:S(2)}) collective-permute-start(bf16[64,768]{1,0:T(8,128)(2,1)S(1)} %add_convert_fusion), channel_id=1, source_target_pairs={{0,2},{1,3},{2,0},{3,1},{4,6},{5,7},{6,4},{7,5},{8,10},{9,11},{10,... | collective-permute-start | bytes 294920 | tf_op jit(solution)/shard_map/ppermute | solution.py:41
  34.7 3.4 %collective-permute-done.9 = bf16[64,768]{1,0:T(8,128)(2,1)S(1)} collective-permute-done((bf16[64,768]{1,0:T(8,128)(2,1)S(1)}, bf16[64,768]{1,0:T(8,128)(2,1)S(1)}, u32[]{:S(2)}, u32[]{:S(2)}) %collective-permute-start.9) | collective-permute-done | bytes 98336 | tf_op jit(solution)/shard_map/ppermute | solution.py:41
  38.3 1.3 %collective-permute-done.10 = f32[64,768]{1,0:T(8,128)S(1)} collective-permute-done((f32[64,768]{1,0:T(8,128)S(1)}, f32[64,768]{1,0:T(8,128)S(1)}, u32[]{:S(2)}, u32[]{:S(2)}) %collective-permute-start.10) | collective-permute-done | bytes 196640 | tf_op jit(solution)/shard_map/ppermute | solution.py:41
  39.7 0.2 fusion.154
  39.8 0.2 multiply_reduce_fusion
  40.1 2.1 %convolution_convert_fusion.1 = bf16[128,768]{1,0:T(8,128)(2,1)S(1)} fusion(bf16[768,768]{1,0:T(8,128)(2,1)S(1)} %copy-done, bf16[768,768]{1,0:T(8,128)(2,1)S(1)} %copy-done.6, f32[128,768]{1,0:T(8,128)S(1)} %get-tuple-element.9, f32[768]{0:T(1024)} %param.20, f32[128]{0:T(128)S(1)} %add_rsqrt_fusion.1, f32[128]{0:T(128)S(1)} %broadcast_multiply_fusion.1), kind=kOutput, calls=%fused_computation.6 | convolution fusion | flops 308871168 | bytes 2953216 | tf_op jit(solution)/shard_map/dot_general | solution.py:167
  42.2 0.2 copy.42
  42.7 0.2 collective-permute-start.11
  42.9 0.2 convolution_convert_fusion.7
  43.3 0.8 %collective-permute-done.11 = bf16[128,2,192]{2,0,1:T(8,128)(2,1)S(1)} collective-permute-done((bf16[128,2,192]{2,0,1:T(8,128)(2,1)S(1)}, bf16[128,2,192]{2,0,1:T(8,128)(2,1)S(1)}, u32[]{:S(2)}, u32[]{:S(2)}) %collective-permute-start.11) | collective-permute-done | bytes 98336 | tf_op jit(solution)/shard_map/ppermute | solution.py:41
  44.1 1.6 %collective-permute-start.12 = (f32[128,192]{1,0:T(8,128)S(1)}, f32[128,192]{1,0:T(8,128)S(1)}, u32[]{:S(2)}, u32[]{:S(2)}) collective-permute-start(f32[128,192]{1,0:T(8,128)S(1)} %select_bitcast_fusion), channel_id=1, source_target_pairs={{0,2},{1,3},{2,0},{3,1},{4,6},{5,7},{6,4},{7,5},{8,10},{9,11},{10,... | collective-permute-start | bytes 294920 | tf_op jit(solution)/shard_map/ppermute | solution.py:41
  45.7 0.2 fusion.10
  46.0 3.8 %collective-permute-done.12 = f32[128,192]{1,0:T(8,128)S(1)} collective-permute-done((f32[128,192]{1,0:T(8,128)S(1)}, f32[128,192]{1,0:T(8,128)S(1)}, u32[]{:S(2)}, u32[]{:S(2)}) %collective-permute-start.12) | collective-permute-done | bytes 98336 | tf_op jit(solution)/shard_map/ppermute | solution.py:41
  50.0 0.3 convolution_convert_fusion
  50.4 0.2 slice_reduce_fusion.2
  50.6 0.6 %collective-permute-start.15 = (bf16[6272]{0:T(1024)(128)(2,1)S(1)}, bf16[6272]{0:T(1024)(128)(2,1)S(1)}, u32[]{:S(2)}, u32[]{:S(2)}) collective-permute-start(bf16[6272]{0:T(1024)(128)(2,1)S(1)} %get-tuple-element.6), channel_id=1, source_target_pairs={{0,12},{4,0},{8,4},{12,8},{1,13},{5,1},{9,5},{13,9},{2,14},{6,2},{... | collective-permute-start | bytes 37640 | tf_op jit(solution)/shard_map/ppermute | solution.py:37
  51.3 0.9 %collective-permute-start.14 = (bf16[6272]{0:T(1024)(128)(2,1)S(1)}, bf16[6272]{0:T(1024)(128)(2,1)S(1)}, u32[]{:S(2)}, u32[]{:S(2)}) collective-permute-start(bf16[6272]{0:T(1024)(128)(2,1)S(1)} %get-tuple-element.7), channel_id=1, source_target_pairs={{0,8},{4,12},{8,0},{12,4},{1,9},{5,13},{9,1},{13,5},{2,10},{6,14},... | collective-permute-start | bytes 37640 | tf_op jit(solution)/shard_map/ppermute | solution.py:37
  52.2 1.6 %collective-permute-start.13 = (bf16[6272]{0:T(1024)(128)(2,1)S(1)}, bf16[6272]{0:T(1024)(128)(2,1)S(1)}, u32[]{:S(2)}, u32[]{:S(2)}) collective-permute-start(bf16[6272]{0:T(1024)(128)(2,1)S(1)} %get-tuple-element.5), channel_id=1, source_target_pairs={{0,4},{4,8},{8,12},{12,0},{1,5},{5,9},{9,13},{13,1},{2,6},{6,10},{... | collective-permute-start | bytes 37640 | tf_op jit(solution)/shard_map/ppermute | solution.py:37
  53.8 0.6 collective-permute-done.15
  54.4 1.5 %collective-permute-done.14 = bf16[6272]{0:T(1024)(128)(2,1)S(1)} collective-permute-done((bf16[6272]{0:T(1024)(128)(2,1)S(1)}, bf16[6272]{0:T(1024)(128)(2,1)S(1)}, u32[]{:S(2)}, u32[]{:S(2)}) %collective-permute-start.14) | collective-permute-done | bytes 12576 | tf_op jit(solution)/shard_map/ppermute | solution.py:37
  55.9 1.8 %collective-permute-done.13 = bf16[6272]{0:T(1024)(128)(2,1)S(1)} collective-permute-done((bf16[6272]{0:T(1024)(128)(2,1)S(1)}, bf16[6272]{0:T(1024)(128)(2,1)S(1)}, u32[]{:S(2)}, u32[]{:S(2)}) %collective-permute-start.13) | collective-permute-done | bytes 12576 | tf_op jit(solution)/shard_map/ppermute | solution.py:37
  57.9 0.2 convert_reduce_fusion.1
  58.2 0.2 convolution_maximum_fusion
  58.5 0.2 fusion.8
  58.7 0.6 %copy.48 = bf16[2,32,192]{2,1,0:T(8,128)(2,1)} copy(bf16[2,32,192]{2,0,1:T(2,128)(2,1)S(1)} %fusion.8) | data formatting | bytes 49152 | tf_op jit(solution)/shard_map/convert_element_type | solution.py:200
  (94 shorter events, 4.2 us)
Async XLA Ops:
  0.0 40.0 %copy-start = (bf16[768,768]{1,0:T(8,128)(2,1)S(1)}, bf16[768,768]{1,0:T(8,128)(2,1)}, u32[]{:S(2)}) copy-start(bf16[768,768]{1,0:T(8,128)(2,1)} %param.27) | copy-start | bytes 3538948
  0.0 8.5 %collective-permute-start.2 = (bf16[64,192]{1,0:T(8,128)(2,1)}, bf16[64,192]{1,0:T(8,128)(2,1)S(1)}, u32[]{:S(2)}, u32[]{:S(2)}) collective-permute-start(bf16[64,192]{1,0:T(8,128)(2,1)} %param.14), channel_id=1, source_target_pairs={{0,12},{4,0},{8,4},{12,8},{1,13},{5,1},{9,5},{13,9},{2,14},{6,2},{... | collective-permute-start | bytes 73736 | tf_op jit(solution)/shard_map/ppermute | solution.py:37
  5.1 5.0 %collective-permute-start.1 = (bf16[64,192]{1,0:T(8,128)(2,1)}, bf16[64,192]{1,0:T(8,128)(2,1)S(1)}, u32[]{:S(2)}, u32[]{:S(2)}) collective-permute-start(bf16[64,192]{1,0:T(8,128)(2,1)} %param.14), channel_id=1, source_target_pairs={{0,8},{4,12},{8,0},{12,4},{1,9},{5,13},{9,1},{13,5},{2,10},{6,14},... | collective-permute-start | bytes 73736 | tf_op jit(solution)/shard_map/ppermute | solution.py:37
  5.1 5.9 %collective-permute-start = (bf16[64,192]{1,0:T(8,128)(2,1)}, bf16[64,192]{1,0:T(8,128)(2,1)S(1)}, u32[]{:S(2)}, u32[]{:S(2)}) collective-permute-start(bf16[64,192]{1,0:T(8,128)(2,1)} %param.14), channel_id=1, source_target_pairs={{0,4},{4,8},{8,12},{12,0},{1,5},{5,9},{9,13},{13,1},{2,6},{6,10},{... | collective-permute-start | bytes 73736 | tf_op jit(solution)/shard_map/ppermute | solution.py:37
  12.4 1.3 %collective-permute-start.3 = (bf16[4,32,192]{2,1,0:T(8,128)(2,1)S(1)}, bf16[4,32,192]{2,1,0:T(8,128)(2,1)S(1)}, u32[]{:S(2)}, u32[]{:S(2)}) collective-permute-start(bf16[4,32,192]{2,1,0:T(8,128)(2,1)S(1)} %broadcast_select_fusion.6), channel_id=1, source_target_pairs={{0,1},{1,0},{2,3},{3,2},{4,5},{5,4},{6,7},{7,6},{8,9},{9,8},{10,11... | collective-permute-start | bytes 147464 | tf_op jit(solution)/shard_map/ppermute | solution.py:41
  13.8 4.9 %collective-permute-start.4 = (bf16[4,32,384]{2,1,0:T(8,128)(2,1)S(1)}, bf16[4,32,384]{2,1,0:T(8,128)(2,1)S(1)}, u32[]{:S(2)}, u32[]{:S(2)}) collective-permute-start(bf16[4,32,384]{2,1,0:T(8,128)(2,1)S(1)} %maximum_select_fusion.3), channel_id=1, source_target_pairs={{0,2},{1,3},{2,0},{3,1},{4,6},{5,7},{6,4},{7,5},{8,10},{9,11},{10,... | collective-permute-start | bytes 294920 | tf_op jit(solution)/shard_map/ppermute | solution.py:41
  15.5 4.2 %copy-start.7 = (bf16[3,768,192]{1,2,0:T(8,128)(2,1)S(1)}, bf16[3,768,192]{1,2,0:T(8,128)(2,1)}, u32[]{:S(2)}) copy-start(bf16[3,768,192]{1,2,0:T(8,128)(2,1)} %param.21) | copy-start | bytes 2654212
  15.5 4.2 %copy-start.9 = (f32[768]{0:T(1024)S(1)}, f32[768]{0:T(1024)}, u32[]{:S(2)}) copy-start(f32[768]{0:T(1024)} %param.17) | copy-start | bytes 9220
  20.6 1.0 %copy-start.2 = (bf16[192,768]{1,0:T(8,128)(2,1)S(1)}, bf16[192,768]{1,0:T(8,128)(2,1)}, u32[]{:S(2)}) copy-start(bf16[192,768]{1,0:T(8,128)(2,1)} %param.22) | copy-start | bytes 884740
  20.9 1.0 %copy-start.4 = (f32[768]{0:T(1024)S(1)}, f32[768]{0:T(1024)}, u32[]{:S(2)}) copy-start(f32[768]{0:T(1024)} %param.19) | copy-start | bytes 9220
  21.2 1.1 %copy-start.1 = (bf16[2,768,192]{1,2,0:T(8,128)(2,1)S(1)}, bf16[2,768,192]{1,2,0:T(8,128)(2,1)}, u32[]{:S(2)}) copy-start(bf16[2,768,192]{1,2,0:T(8,128)(2,1)} %param.24) | copy-start | bytes 1769476
  21.8 1.4 %collective-permute-start.5 = (bf16[64,768]{1,0:T(8,128)(2,1)S(1)}, bf16[64,768]{1,0:T(8,128)(2,1)S(1)}, u32[]{:S(2)}, u32[]{:S(2)}) collective-permute-start(bf16[64,768]{1,0:T(8,128)(2,1)S(1)} %broadcast_select_fusion.5), channel_id=1, source_target_pairs={{0,1},{1,0},{2,3},{3,2},{4,5},{5,4},{6,7},{7,6},{8,9},{9,8},{10,11... | collective-permute-start | bytes 294920 | tf_op jit(solution)/shard_map/ppermute | solution.py:41
  23.2 4.9 %collective-permute-start.6 = (bf16[64,768]{1,0:T(8,128)(2,1)S(1)}, bf16[64,768]{1,0:T(8,128)(2,1)S(1)}, u32[]{:S(2)}, u32[]{:S(2)}) collective-permute-start(bf16[64,768]{1,0:T(8,128)(2,1)S(1)} %add_convert_fusion.1), channel_id=1, source_target_pairs={{0,2},{1,3},{2,0},{3,1},{4,6},{5,7},{6,4},{7,5},{8,10},{9,11},{10,... | collective-permute-start | bytes 294920 | tf_op jit(solution)/shard_map/ppermute | solution.py:41
  28.2 1.5 %collective-permute-start.7 = (f32[64,768]{1,0:T(8,128)S(1)}, f32[64,768]{1,0:T(8,128)S(1)}, u32[]{:S(2)}, u32[]{:S(2)}) collective-permute-start(f32[64,768]{1,0:T(8,128)S(1)} %convert_add_fusion.3), channel_id=1, source_target_pairs={{0,1},{1,0},{2,3},{3,2},{4,5},{5,4},{6,7},{7,6},{8,9},{9,8},{10,11... | collective-permute-start | bytes 589832 | tf_op jit(solution)/shard_map/ppermute | solution.py:41
  28.3 1.8 %copy-start.8 = (bf16[768,192]{0,1:T(8,128)(2,1)S(1)}, bf16[768,192]{0,1:T(8,128)(2,1)}, u32[]{:S(2)}) copy-start(bf16[768,192]{0,1:T(8,128)(2,1)} %param.23) | copy-start | bytes 884740
  28.3 1.8 %copy-start.10 = (f32[768]{0:T(1024)S(1)}, f32[768]{0:T(1024)}, u32[]{:S(2)}) copy-start(f32[768]{0:T(1024)} %param.18) | copy-start | bytes 9220
  30.6 1.0 %copy-start.3 = (bf16[192,768]{1,0:T(8,128)(2,1)S(1)}, bf16[192,768]{1,0:T(8,128)(2,1)}, u32[]{:S(2)}) copy-start(bf16[192,768]{1,0:T(8,128)(2,1)} %param.25) | copy-start | bytes 884740
  31.2 7.0 %copy-start.5 = (f32[2,64]{1,0:T(2,128)S(1)}, f32[2,64]{1,0:T(2,128)}, u32[]{:S(2)}) copy-start(f32[2,64]{1,0:T(2,128)} %param.16) | copy-start | bytes 1540
  31.8 1.4 %collective-permute-start.8 = (bf16[64,768]{1,0:T(8,128)(2,1)S(1)}, bf16[64,768]{1,0:T(8,128)(2,1)S(1)}, u32[]{:S(2)}, u32[]{:S(2)}) collective-permute-start(bf16[64,768]{1,0:T(8,128)(2,1)S(1)} %broadcast_select_fusion.2), channel_id=1, source_target_pairs={{0,1},{1,0},{2,3},{3,2},{4,5},{5,4},{6,7},{7,6},{8,9},{9,8},{10,11... | collective-permute-start | bytes 294920 | tf_op jit(solution)/shard_map/ppermute | solution.py:41
  33.2 4.9 %collective-permute-start.9 = (bf16[64,768]{1,0:T(8,128)(2,1)S(1)}, bf16[64,768]{1,0:T(8,128)(2,1)S(1)}, u32[]{:S(2)}, u32[]{:S(2)}) collective-permute-start(bf16[64,768]{1,0:T(8,128)(2,1)S(1)} %add_convert_fusion), channel_id=1, source_target_pairs={{0,2},{1,3},{2,0},{3,1},{4,6},{5,7},{6,4},{7,5},{8,10},{9,11},{10,... | collective-permute-start | bytes 294920 | tf_op jit(solution)/shard_map/ppermute | solution.py:41
  38.1 1.5 %collective-permute-start.10 = (f32[64,768]{1,0:T(8,128)S(1)}, f32[64,768]{1,0:T(8,128)S(1)}, u32[]{:S(2)}, u32[]{:S(2)}) collective-permute-start(f32[64,768]{1,0:T(8,128)S(1)} %convert_add_fusion.2), channel_id=1, source_target_pairs={{0,1},{1,0},{2,3},{3,2},{4,5},{5,4},{6,7},{7,6},{8,9},{9,8},{10,11... | collective-permute-start | bytes 589832 | tf_op jit(solution)/shard_map/ppermute | solution.py:41
  38.3 1.8 %copy-start.6 = (bf16[768,768]{1,0:T(8,128)(2,1)S(1)}, bf16[768,768]{1,0:T(8,128)(2,1)}, u32[]{:S(2)}) copy-start(bf16[768,768]{1,0:T(8,128)(2,1)} %param.26) | copy-start | bytes 3538948
  42.7 1.4 %collective-permute-start.11 = (bf16[128,2,192]{2,0,1:T(8,128)(2,1)S(1)}, bf16[128,2,192]{2,0,1:T(8,128)(2,1)S(1)}, u32[]{:S(2)}, u32[]{:S(2)}) collective-permute-start(bf16[128,2,192]{2,0,1:T(8,128)(2,1)S(1)} %select_bitcast_fusion.1), channel_id=1, source_target_pairs={{0,1},{1,0},{2,3},{3,2},{4,5},{5,4},{6,7},{7,6},{8,9},{9,8},{10,11... | collective-permute-start | bytes 294920 | tf_op jit(solution)/shard_map/ppermute | solution.py:41
  44.1 5.6 %collective-permute-start.12 = (f32[128,192]{1,0:T(8,128)S(1)}, f32[128,192]{1,0:T(8,128)S(1)}, u32[]{:S(2)}, u32[]{:S(2)}) collective-permute-start(f32[128,192]{1,0:T(8,128)S(1)} %select_bitcast_fusion), channel_id=1, source_target_pairs={{0,2},{1,3},{2,0},{3,1},{4,6},{5,7},{6,4},{7,5},{8,10},{9,11},{10,... | collective-permute-start | bytes 294920 | tf_op jit(solution)/shard_map/ppermute | solution.py:41
  50.6 3.8 %collective-permute-start.15 = (bf16[6272]{0:T(1024)(128)(2,1)S(1)}, bf16[6272]{0:T(1024)(128)(2,1)S(1)}, u32[]{:S(2)}, u32[]{:S(2)}) collective-permute-start(bf16[6272]{0:T(1024)(128)(2,1)S(1)} %get-tuple-element.6), channel_id=1, source_target_pairs={{0,12},{4,0},{8,4},{12,8},{1,13},{5,1},{9,5},{13,9},{2,14},{6,2},{... | collective-permute-start | bytes 37640 | tf_op jit(solution)/shard_map/ppermute | solution.py:37
  51.3 4.6 %collective-permute-start.14 = (bf16[6272]{0:T(1024)(128)(2,1)S(1)}, bf16[6272]{0:T(1024)(128)(2,1)S(1)}, u32[]{:S(2)}, u32[]{:S(2)}) collective-permute-start(bf16[6272]{0:T(1024)(128)(2,1)S(1)} %get-tuple-element.7), channel_id=1, source_target_pairs={{0,8},{4,12},{8,0},{12,4},{1,9},{5,13},{9,1},{13,5},{2,10},{6,14},... | collective-permute-start | bytes 37640 | tf_op jit(solution)/shard_map/ppermute | solution.py:37
  52.2 5.5 %collective-permute-start.13 = (bf16[6272]{0:T(1024)(128)(2,1)S(1)}, bf16[6272]{0:T(1024)(128)(2,1)S(1)}, u32[]{:S(2)}, u32[]{:S(2)}) collective-permute-start(bf16[6272]{0:T(1024)(128)(2,1)S(1)} %get-tuple-element.5), channel_id=1, source_target_pairs={{0,4},{4,8},{8,12},{12,0},{1,5},{5,9},{9,13},{13,1},{2,6},{6,10},{... | collective-permute-start | bytes 37640 | tf_op jit(solution)/shard_map/ppermute | solution.py:37

commit v3 on v2

--- a/solution.py
+++ b/solution.py
@@ -70,18 +70,44 @@
         quarter = term.shape[1] // lax.axis_size("mp")
         return lax.dynamic_slice_in_dim(full, lax.axis_index("mp") * quarter, quarter, 1)
     index = lax.axis_index("mp")
+    rows_n, width = term.shape
+    parts = term.reshape(rows_n, 4, width // 4)
+    total = jnp.take(parts, index, axis=1).astype(jnp.float32)
+    for bit in (1, 2, 3):
+        total = total + swap(jnp.take(parts, index ^ bit, axis=1), mp_pairs(bit)).astype(jnp.float32)
+    return total
+
+
+def gather_tokens(tokens, owners_n):
+    index = lax.axis_index("mp")
     core = index % 2
     chip = index // 2
-    rows_n, width = term.shape
-    parts = term.reshape(rows_n, 2, 2, width // 4)
-    keep = jnp.where(core == 0, parts[:, :, 0], parts[:, :, 1])
-    send = jnp.where(core == 0, parts[:, :, 1], parts[:, :, 0])
-    got = swap(send, mp_pairs(1))
-    both = keep.astype(jnp.float32) + got.astype(jnp.float32)
-    mine = jnp.where(chip == 0, both[:, 0], both[:, 1])
-    theirs = jnp.where(chip == 0, both[:, 1], both[:, 0])
-    other = swap(theirs, mp_pairs(2))
-    return mine + other
+    got = swap(tokens, mp_pairs(1))
+    half = jnp.where(
+        core == 0, jnp.concatenate([tokens, got], axis=1), jnp.concatenate([got, tokens], axis=1)
+    )
+    owners = []
+    for step in range(owners_n):
+        moved = []
+        for cross in (0, 2):
+            if step == 0 and cross == 0:
+                moved.append(half)
+                continue
+            perm = [
+                (p * 4 + m, ((p + step) % owners_n) * 4 + (m ^ cross))
+                for p in range(owners_n)
+                for m in range(4)
+            ]
+            moved.append(lax.ppermute(half, ("pairs", "mp"), perm))
+        mine, other = moved
+        owners.append(
+            jnp.where(
+                chip == 0,
+                jnp.concatenate([mine, other], axis=1),
+                jnp.concatenate([other, mine], axis=1),
+            )
+        )
+    return jnp.stack(owners)
 
 
 def mp_gather_cols(part):
@@ -124,19 +150,22 @@
     own = lax.axis_index("pairs")
     ids = pair_list.reshape(views_n)
     source = ids // img_dev
-    if owners_n <= SHIFTS_MAX:
-        every = jnp.concatenate(
-            [tokens] + [pairs_shift(tokens, step, owners_n) for step in range(1, owners_n)], axis=0
-        )
+    if owners_n <= SHIFTS_MAX and lax.axis_size("mp") == 4:
+        every = gather_tokens(tokens, owners_n)
         at = ((own - source) % owners_n) * img_dev + ids % img_dev
         targets = (own + jnp.arange(owners_n)) % owners_n
     else:
         every = lax.all_gather(tokens, "pairs", axis=0, tiled=True)
+        every = lax.all_gather(every, "mp", axis=1, tiled=True)
         at = ids
         targets = jnp.arange(owners_n)
-    every = every.reshape(owners_n * img_dev, TOKS, quarter)
-    slices = jnp.take(every, at, axis=0)
-    start = mp_gather_cols(slices)
+    every = every.reshape(owners_n * img_dev, TOKS * 4 * quarter)
+    pick = (at[:, None] == jnp.arange(owners_n * img_dev)[None, :]).astype(jnp.bfloat16)
+    start = (
+        jnp.dot(pick, every, preferred_element_type=jnp.float32)
+        .astype(jnp.bfloat16)
+        .reshape(views_n, TOKS, 4 * quarter)
+    )
     width = start.shape[2]
     rows_n = views_n * TOKS
     flipped = start.reshape(pair_dev, 2, TOKS, width)
@@ -180,7 +209,7 @@
     back_slot = jnp.dot(route, slot[:, None], precision=lax.Precision.HIGHEST)
     pad = jnp.zeros((owners_n, 128 - TOKS - 1), jnp.float32)
     payload = jnp.concatenate([back, back_weight, back_slot, pad], axis=1).astype(jnp.bfloat16)
-    if owners_n <= SHIFTS_MAX:
+    if owners_n <= SHIFTS_MAX and lax.axis_size("mp") == 4:
         got = jnp.stack(
             [payload[0]]
             + [pairs_shift(payload[step], step, owners_n) for step in range(1, owners_n)]

time: 59.6 us -> 58.6 us (0.983)
  starting transfers between devices: 16.1 us -> 20.7 us
  waiting for transfers between devices: 25.9 us -> 22.5 us
  other arithmetic: 4.62 us -> 3.42 us
  local copies, waits for them, and re-layouts: 6.39 us -> 5.68 us
    ppermute x0 -> x7, starting transfers between devices: none -> 12.4 us  [gather_tokens(): moved.append(lax.ppermute(half, ('pairs', 'mp'), perm))]
    ppermute x6 -> x3, starting transfers between devices: 9.27 us -> 4.1 us  [pairs_shift(): lax.ppermute(values, 'pairs', [(i, (i + step) % owners_n) for i in range(...]
    ppermute x0 -> x7, waiting for transfers between devices: none -> 4.66 us  [gather_tokens(): moved.append(lax.ppermute(half, ('pairs', 'mp'), perm))]
    ppermute x10, waiting for transfers between devices: 19.6 us -> 15.4 us  [swap(): return lax.ppermute(values, 'mp', pairs)]
    ppermute x6 -> x3, waiting for transfers between devices: 6.27 us -> 2.43 us  [pairs_shift(): lax.ppermute(values, 'pairs', [(i, (i + step) % owners_n) for i in range(...]
    ppermute x10, starting transfers between devices: 6.86 us -> 4.12 us  [swap(): return lax.ppermute(values, 'mp', pairs)]
    concatenate x1 -> x0, other arithmetic: 0.78 us -> none  [per_device(): jnp.concatenate([tokens] + [pairs_shift(tokens, step, owners_n) for step...]
    reshape x2 -> x1, local copies, waits for them, and re-layouts: 1.52 us -> 0.76 us  [per_device(): ids = pair_list.reshape(views_n)]
  transfers between devices with their start and end apart: 16 -> 20, of which waited for: 15 -> 16; matrix products, arithmetic and copies ran while one was open for 7% -> 5% of each run, Pallas kernels for 0% -> 0%
where the time goes in v3:
time: 58.6 us; the launch traced here: 58.3 us
  waiting for transfers between devices  22.5 us (38%)
  starting transfers between devices  20.7 us (35%)
  local copies, waits for them, and re-layouts  5.68 us (10%)
  matrix products  5.33 us (9%)
  other arithmetic  3.42 us (6%)
  between operations  0.67 us (1%)
    ppermute x10, waiting for transfers between devices, swap(): return lax.ppermute(values, 'mp', pairs)  15.4 us
    ppermute x7, starting transfers between devices, gather_tokens(): moved.append(lax.ppermute(half, ('pairs', 'mp'), perm))  12.4 us
    ppermute x7, waiting for transfers between devices, gather_tokens(): moved.append(lax.ppermute(half, ('pairs', 'mp'), perm))  4.66 us
    ppermute x10, starting transfers between devices, swap(): return lax.ppermute(values, 'mp', pairs)  4.12 us
    ppermute x3, starting transfers between devices, pairs_shift(): lax.ppermute(values, 'pairs', [(i, (i + step) % owners_n) for i in range(...  4.1 us
    ppermute x3, waiting for transfers between devices, pairs_shift(): lax.ppermute(values, 'pairs', [(i, (i + step) % owners_n) for i in range(...  2.43 us
    dot_general x1, matrix products, per_device(): jnp.dot(hidden.astype(jnp.bfloat16), mlp_down, preferred_element_type=jnp...  1.44 us
    unnamed x29, local copies, waits for them, and re-layouts  1.29 us
  transfers between devices with their start and end apart: 20, of which 16 were waited for; matrix products, arithmetic and copies ran while one was open for 5% of the time, Pallas kernels for 0%

profile of v3, /device:TPU:0, one launch (start us, length us, event | category | flops | bytes accessed | tf_op | source)
XLA Modules:
  0.0 58.3 jit_solution(9745122221731285665)
XLA Ops:
  0.0 0.5 collective-permute-start
  0.5 0.8 %reshape.507 = s32[4]{0:T(128)S(1)} reshape(s32[2,2]{1,0:T(2,128)} %param.17) | data formatting | bytes 32 | tf_op jit(solution)/shard_map/reshape | solution.py:151
  1.2 0.3 collective-permute-done
  1.5 0.9 %maximum_select_fusion.4 = bf16[64,384]{1,0:T(8,128)(2,1)S(1)} fusion(bf16[64,192]{1,0:T(8,128)(2,1)S(1)} %collective-permute-done, bf16[64,192]{1,0:T(8,128)(2,1)} %param.16, pred[]{:T(512)S(6)} %eq.77), kind=kLoop, calls=%fused_computation.134 | loop fusion | flops 221184 | bytes 98305 | tf_op jit(solution)/shard_map/jit(_where)/select_n | solution.py:86
  2.5 3.0 %collective-permute-start.2 = (bf16[64,384]{1,0:T(8,128)(2,1)S(1)}, bf16[64,384]{1,0:T(8,128)(2,1)S(1)}, u32[]{:S(2)}, u32[]{:S(2)}) collective-permute-start(bf16[64,384]{1,0:T(8,128)(2,1)S(1)} %maximum_select_fusion.4), channel_id=1, source_target_pairs={{0,4},{1,5},{2,6},{3,7},{4,8},{5,9},{6,10},{7,11},{8,12},{9,13},{1... | collective-permute-start | bytes 147464 | tf_op jit(solution)/shard_map/ppermute | solution.py:101
  5.4 2.5 %collective-permute-start.3 = (bf16[64,384]{1,0:T(8,128)(2,1)S(1)}, bf16[64,384]{1,0:T(8,128)(2,1)S(1)}, u32[]{:S(2)}, u32[]{:S(2)}) collective-permute-start(bf16[64,384]{1,0:T(8,128)(2,1)S(1)} %maximum_select_fusion.4), channel_id=1, source_target_pairs={{0,6},{1,7},{2,4},{3,5},{4,10},{5,11},{6,8},{7,9},{8,14},{9,15},{1... | collective-permute-start | bytes 147464 | tf_op jit(solution)/shard_map/ppermute | solution.py:101
  8.0 1.3 %collective-permute-start.4 = (bf16[64,384]{1,0:T(8,128)(2,1)S(1)}, bf16[64,384]{1,0:T(8,128)(2,1)S(1)}, u32[]{:S(2)}, u32[]{:S(2)}) collective-permute-start(bf16[64,384]{1,0:T(8,128)(2,1)S(1)} %maximum_select_fusion.4), channel_id=1, source_target_pairs={{0,8},{1,9},{2,10},{3,11},{4,12},{5,13},{6,14},{7,15},{8,0},{9,1},... | collective-permute-start | bytes 147464 | tf_op jit(solution)/shard_map/ppermute | solution.py:101
  9.3 1.7 %collective-permute-start.5 = (bf16[64,384]{1,0:T(8,128)(2,1)S(1)}, bf16[64,384]{1,0:T(8,128)(2,1)S(1)}, u32[]{:S(2)}, u32[]{:S(2)}) collective-permute-start(bf16[64,384]{1,0:T(8,128)(2,1)S(1)} %maximum_select_fusion.4), channel_id=1, source_target_pairs={{0,10},{1,11},{2,8},{3,9},{4,14},{5,15},{6,12},{7,13},{8,2},{9,3},... | collective-permute-start | bytes 147464 | tf_op jit(solution)/shard_map/ppermute | solution.py:101
  10.9 1.5 %collective-permute-start.1 = (bf16[64,384]{1,0:T(8,128)(2,1)S(1)}, bf16[64,384]{1,0:T(8,128)(2,1)S(1)}, u32[]{:S(2)}, u32[]{:S(2)}) collective-permute-start(bf16[64,384]{1,0:T(8,128)(2,1)S(1)} %maximum_select_fusion.4), channel_id=1, source_target_pairs={{0,2},{1,3},{2,0},{3,1},{4,6},{5,7},{6,4},{7,5},{8,10},{9,11},{10,... | collective-permute-start | bytes 147464 | tf_op jit(solution)/shard_map/ppermute | solution.py:101
  12.4 2.2 %collective-permute-start.6 = (bf16[64,384]{1,0:T(8,128)(2,1)S(1)}, bf16[64,384]{1,0:T(8,128)(2,1)S(1)}, u32[]{:S(2)}, u32[]{:S(2)}) collective-permute-start(bf16[64,384]{1,0:T(8,128)(2,1)S(1)} %maximum_select_fusion.4), channel_id=1, source_target_pairs={{0,12},{1,13},{2,14},{3,15},{4,0},{5,1},{6,2},{7,3},{8,4},{9,5},{1... | collective-permute-start | bytes 147464 | tf_op jit(solution)/shard_map/ppermute | solution.py:101
  14.7 0.3 collective-permute-start.7
  15.1 0.6 %collective-permute-done.5 = bf16[64,384]{1,0:T(8,128)(2,1)S(1)} collective-permute-done((bf16[64,384]{1,0:T(8,128)(2,1)S(1)}, bf16[64,384]{1,0:T(8,128)(2,1)S(1)}, u32[]{:S(2)}, u32[]{:S(2)}) %collective-permute-start.5) | collective-permute-done | bytes 49184 | tf_op jit(solution)/shard_map/ppermute | solution.py:101
  15.8 1.3 %collective-permute-done.6 = bf16[64,384]{1,0:T(8,128)(2,1)S(1)} collective-permute-done((bf16[64,384]{1,0:T(8,128)(2,1)S(1)}, bf16[64,384]{1,0:T(8,128)(2,1)S(1)}, u32[]{:S(2)}, u32[]{:S(2)}) %collective-permute-start.6) | collective-permute-done | bytes 49184 | tf_op jit(solution)/shard_map/ppermute | solution.py:101
  17.2 2.5 %collective-permute-done.7 = bf16[64,384]{1,0:T(8,128)(2,1)S(1)} collective-permute-done((bf16[64,384]{1,0:T(8,128)(2,1)S(1)}, bf16[64,384]{1,0:T(8,128)(2,1)S(1)}, u32[]{:S(2)}, u32[]{:S(2)}) %collective-permute-start.7) | collective-permute-done | bytes 49184 | tf_op jit(solution)/shard_map/ppermute | solution.py:101
  19.8 0.2 reshape.508
  19.9 0.3 convolution_convert_fusion
  20.6 0.2 multiply_reduce_fusion.2
  21.0 0.2 multiply_reduce_fusion.3
  21.2 0.3 copy-done.1
  21.6 0.5 fusion.25
  22.4 0.2 convolution_multiply_fusion.1
  22.9 0.3 fusion.6
  23.2 0.1 reshape.509
  23.4 0.2 convolution_convert_fusion.4
  23.9 0.3 copy-done.2
  24.2 0.3 fusion.148
  24.6 0.4 collective-permute-done.8
  25.0 0.6 %collective-permute-start.9 = (bf16[64,768]{1,0:T(8,128)(2,1)S(1)}, bf16[64,768]{1,0:T(8,128)(2,1)S(1)}, u32[]{:S(2)}, u32[]{:S(2)}) collective-permute-start(bf16[64,768]{1,0:T(8,128)(2,1)S(1)} %add_convert_fusion.1), channel_id=1, source_target_pairs={{0,2},{1,3},{2,0},{3,1},{4,6},{5,7},{6,4},{7,5},{8,10},{9,11},{10,... | collective-permute-start | bytes 294920 | tf_op jit(solution)/shard_map/ppermute | solution.py:41
  25.6 4.3 %collective-permute-done.9 = bf16[64,768]{1,0:T(8,128)(2,1)S(1)} collective-permute-done((bf16[64,768]{1,0:T(8,128)(2,1)S(1)}, bf16[64,768]{1,0:T(8,128)(2,1)S(1)}, u32[]{:S(2)}, u32[]{:S(2)}) %collective-permute-start.9) | collective-permute-done | bytes 98336 | tf_op jit(solution)/shard_map/ppermute | solution.py:41
  30.4 1.1 %collective-permute-done.10 = f32[64,768]{1,0:T(8,128)S(1)} collective-permute-done((f32[64,768]{1,0:T(8,128)S(1)}, f32[64,768]{1,0:T(8,128)S(1)}, u32[]{:S(2)}, u32[]{:S(2)}) %collective-permute-start.10) | collective-permute-done | bytes 196640 | tf_op jit(solution)/shard_map/ppermute | solution.py:41
  31.5 0.1 fusion.141
  31.6 0.2 multiply_reduce_fusion.1
  31.9 0.3 convolution_convert_fusion.7
  32.2 0.1 reshape.625
  32.3 0.2 convolution_multiply_fusion
  32.7 0.3 fusion.7
  33.0 0.1 reshape.511
  33.3 0.2 convolution_convert_fusion.3
  33.5 0.2 collective-permute-start.11
  33.8 1.1 %collective-permute-done.11 = bf16[64,768]{1,0:T(8,128)(2,1)S(1)} collective-permute-done((bf16[64,768]{1,0:T(8,128)(2,1)S(1)}, bf16[64,768]{1,0:T(8,128)(2,1)S(1)}, u32[]{:S(2)}, u32[]{:S(2)}) %collective-permute-start.11) | collective-permute-done | bytes 98336 | tf_op jit(solution)/shard_map/ppermute | solution.py:41
  34.9 0.6 %collective-permute-start.12 = (bf16[64,768]{1,0:T(8,128)(2,1)S(1)}, bf16[64,768]{1,0:T(8,128)(2,1)S(1)}, u32[]{:S(2)}, u32[]{:S(2)}) collective-permute-start(bf16[64,768]{1,0:T(8,128)(2,1)S(1)} %add_convert_fusion), channel_id=1, source_target_pairs={{0,2},{1,3},{2,0},{3,1},{4,6},{5,7},{6,4},{7,5},{8,10},{9,11},{10,... | collective-permute-start | bytes 294920 | tf_op jit(solution)/shard_map/ppermute | solution.py:41
  35.5 4.3 %collective-permute-done.12 = bf16[64,768]{1,0:T(8,128)(2,1)S(1)} collective-permute-done((bf16[64,768]{1,0:T(8,128)(2,1)S(1)}, bf16[64,768]{1,0:T(8,128)(2,1)S(1)}, u32[]{:S(2)}, u32[]{:S(2)}) %collective-permute-start.12) | collective-permute-done | bytes 98336 | tf_op jit(solution)/shard_map/ppermute | solution.py:41
  40.0 0.2 convolution_convert_fusion.8
  40.2 1.2 %collective-permute-done.13 = f32[64,768]{1,0:T(8,128)S(1)} collective-permute-done((f32[64,768]{1,0:T(8,128)S(1)}, f32[64,768]{1,0:T(8,128)S(1)}, u32[]{:S(2)}, u32[]{:S(2)}) %collective-permute-start.13) | collective-permute-done | bytes 196640 | tf_op jit(solution)/shard_map/ppermute | solution.py:41
  41.4 0.1 fusion.140
  41.6 0.2 multiply_reduce_fusion
  41.8 1.4 %convolution_convert_fusion.2 = bf16[128,768]{1,0:T(8,128)(2,1)S(1)} fusion(bf16[768,768]{1,0:T(8,128)(2,1)S(1)} %copy-done, bf16[768,768]{1,0:T(8,128)(2,1)S(1)} %copy-done.10, f32[128,768]{1,0:T(8,128)S(1)} %get-tuple-element.21, f32[768]{0:T(1024)S(1)} %copy-done.11, f32[128]{0:T(128)S(1)} %add_rsqrt_fusion.1, f32[128]{0:T(128)S(1)} %broadcast_multiply_fusion.1), kind=kOutput, calls=%fused_computation.6 | convolution fusion | flops 308871168 | bytes 2953216 | tf_op jit(solution)/shard_map/dot_general | solution.py:196
  43.3 0.2 copy.42
  43.6 0.2 collective-permute-start.14
  43.9 0.6 %collective-permute-start.15 = (bf16[128,192]{1,0:T(8,128)(2,1)S(1)}, bf16[128,192]{1,0:T(8,128)(2,1)S(1)}, u32[]{:S(2)}, u32[]{:S(2)}) collective-permute-start(bf16[128,192]{1,0:T(8,128)(2,1)S(1)} %select_bitcast_fusion.1), channel_id=1, source_target_pairs={{0,2},{1,3},{2,0},{3,1},{4,6},{5,7},{6,4},{7,5},{8,10},{9,11},{10,... | collective-permute-start | bytes 147464 | tf_op jit(solution)/shard_map/ppermute | solution.py:41
  44.7 1.2 %collective-permute-start.16 = (bf16[128,192]{1,0:T(8,128)(2,1)S(1)}, bf16[128,192]{1,0:T(8,128)(2,1)S(1)}, u32[]{:S(2)}, u32[]{:S(2)}) collective-permute-start(bf16[128,192]{1,0:T(8,128)(2,1)S(1)} %select_bitcast_fusion), channel_id=1, source_target_pairs={{0,3},{1,2},{2,1},{3,0},{4,7},{5,6},{6,5},{7,4},{8,11},{9,10},{10,... | collective-permute-start | bytes 147464 | tf_op jit(solution)/shard_map/ppermute | solution.py:41
  45.9 0.2 fusion.10
  46.5 2.4 %collective-permute-done.15 = bf16[128,192]{1,0:T(8,128)(2,1)S(1)} collective-permute-done((bf16[128,192]{1,0:T(8,128)(2,1)S(1)}, bf16[128,192]{1,0:T(8,128)(2,1)S(1)}, u32[]{:S(2)}, u32[]{:S(2)}) %collective-permute-start.15) | collective-permute-done | bytes 49184 | tf_op jit(solution)/shard_map/ppermute | solution.py:41
  48.9 0.3 collective-permute-done.16
  49.4 0.3 convolution_convert_fusion.1
  49.8 0.2 slice_reduce_fusion.2
  50.1 2.8 %collective-permute-start.18 = (bf16[6272]{0:T(1024)(128)(2,1)S(1)}, bf16[6272]{0:T(1024)(128)(2,1)S(1)}, u32[]{:S(2)}, u32[]{:S(2)}) collective-permute-start(bf16[6272]{0:T(1024)(128)(2,1)S(1)} %get-tuple-element.19), channel_id=1, source_target_pairs={{0,8},{4,12},{8,0},{12,4},{1,9},{5,13},{9,1},{13,5},{2,10},{6,14},... | collective-permute-start | bytes 37640 | tf_op jit(solution)/shard_map/ppermute | solution.py:37
  53.0 1.2 %collective-permute-start.19 = (bf16[6272]{0:T(1024)(128)(2,1)S(1)}, bf16[6272]{0:T(1024)(128)(2,1)S(1)}, u32[]{:S(2)}, u32[]{:S(2)}) collective-permute-start(bf16[6272]{0:T(1024)(128)(2,1)S(1)} %get-tuple-element.18), channel_id=1, source_target_pairs={{0,12},{4,0},{8,4},{12,8},{1,13},{5,1},{9,5},{13,9},{2,14},{6,2},{... | collective-permute-start | bytes 37640 | tf_op jit(solution)/shard_map/ppermute | solution.py:37
  54.2 1.5 %collective-permute-done.17 = bf16[6272]{0:T(1024)(128)(2,1)S(1)} collective-permute-done((bf16[6272]{0:T(1024)(128)(2,1)S(1)}, bf16[6272]{0:T(1024)(128)(2,1)S(1)}, u32[]{:S(2)}, u32[]{:S(2)}) %collective-permute-start.17) | collective-permute-done | bytes 12576 | tf_op jit(solution)/shard_map/ppermute | solution.py:37
  55.7 1.0 %collective-permute-done.19 = bf16[6272]{0:T(1024)(128)(2,1)S(1)} collective-permute-done((bf16[6272]{0:T(1024)(128)(2,1)S(1)}, bf16[6272]{0:T(1024)(128)(2,1)S(1)}, u32[]{:S(2)}, u32[]{:S(2)}) %collective-permute-start.19) | collective-permute-done | bytes 12576 | tf_op jit(solution)/shard_map/ppermute | solution.py:37
  56.7 0.2 convert_reduce_fusion
  57.0 0.2 convolution_maximum_fusion
  57.4 0.2 fusion.8
  57.7 0.6 %copy.50 = bf16[2,32,192]{2,1,0:T(8,128)(2,1)} copy(bf16[2,32,192]{2,0,1:T(2,128)(2,1)S(1)} %fusion.8) | data formatting | bytes 49152 | tf_op jit(solution)/shard_map/convert_element_type | solution.py:229
  (101 shorter events, 4.4 us)
Async XLA Ops:
  0.0 41.8 %copy-start = (bf16[768,768]{1,0:T(8,128)(2,1)S(1)}, bf16[768,768]{1,0:T(8,128)(2,1)}, u32[]{:S(2)}) copy-start(bf16[768,768]{1,0:T(8,128)(2,1)} %param.29) | copy-start | bytes 3538948
  0.0 1.5 %collective-permute-start = (bf16[64,192]{1,0:T(8,128)(2,1)}, bf16[64,192]{1,0:T(8,128)(2,1)S(1)}, u32[]{:S(2)}, u32[]{:S(2)}) collective-permute-start(bf16[64,192]{1,0:T(8,128)(2,1)} %param.16), channel_id=1, source_target_pairs={{0,1},{1,0},{2,3},{3,2},{4,5},{5,4},{6,7},{7,6},{8,9},{9,8},{10,11... | collective-permute-start | bytes 73736 | tf_op jit(solution)/shard_map/ppermute | solution.py:41
  2.5 10.0 %collective-permute-start.2 = (bf16[64,384]{1,0:T(8,128)(2,1)S(1)}, bf16[64,384]{1,0:T(8,128)(2,1)S(1)}, u32[]{:S(2)}, u32[]{:S(2)}) collective-permute-start(bf16[64,384]{1,0:T(8,128)(2,1)S(1)} %maximum_select_fusion.4), channel_id=1, source_target_pairs={{0,4},{1,5},{2,6},{3,7},{4,8},{5,9},{6,10},{7,11},{8,12},{9,13},{1... | collective-permute-start | bytes 147464 | tf_op jit(solution)/shard_map/ppermute | solution.py:101
  5.4 9.2 %collective-permute-start.3 = (bf16[64,384]{1,0:T(8,128)(2,1)S(1)}, bf16[64,384]{1,0:T(8,128)(2,1)S(1)}, u32[]{:S(2)}, u32[]{:S(2)}) collective-permute-start(bf16[64,384]{1,0:T(8,128)(2,1)S(1)} %maximum_select_fusion.4), channel_id=1, source_target_pairs={{0,6},{1,7},{2,4},{3,5},{4,10},{5,11},{6,8},{7,9},{8,14},{9,15},{1... | collective-permute-start | bytes 147464 | tf_op jit(solution)/shard_map/ppermute | solution.py:101
  8.0 7.1 %collective-permute-start.4 = (bf16[64,384]{1,0:T(8,128)(2,1)S(1)}, bf16[64,384]{1,0:T(8,128)(2,1)S(1)}, u32[]{:S(2)}, u32[]{:S(2)}) collective-permute-start(bf16[64,384]{1,0:T(8,128)(2,1)S(1)} %maximum_select_fusion.4), channel_id=1, source_target_pairs={{0,8},{1,9},{2,10},{3,11},{4,12},{5,13},{6,14},{7,15},{8,0},{9,1},... | collective-permute-start | bytes 147464 | tf_op jit(solution)/shard_map/ppermute | solution.py:101
  9.3 6.4 %collective-permute-start.5 = (bf16[64,384]{1,0:T(8,128)(2,1)S(1)}, bf16[64,384]{1,0:T(8,128)(2,1)S(1)}, u32[]{:S(2)}, u32[]{:S(2)}) collective-permute-start(bf16[64,384]{1,0:T(8,128)(2,1)S(1)} %maximum_select_fusion.4), channel_id=1, source_target_pairs={{0,10},{1,11},{2,8},{3,9},{4,14},{5,15},{6,12},{7,13},{8,2},{9,3},... | collective-permute-start | bytes 147464 | tf_op jit(solution)/shard_map/ppermute | solution.py:101
  10.9 4.9 %collective-permute-start.1 = (bf16[64,384]{1,0:T(8,128)(2,1)S(1)}, bf16[64,384]{1,0:T(8,128)(2,1)S(1)}, u32[]{:S(2)}, u32[]{:S(2)}) collective-permute-start(bf16[64,384]{1,0:T(8,128)(2,1)S(1)} %maximum_select_fusion.4), channel_id=1, source_target_pairs={{0,2},{1,3},{2,0},{3,1},{4,6},{5,7},{6,4},{7,5},{8,10},{9,11},{10,... | collective-permute-start | bytes 147464 | tf_op jit(solution)/shard_map/ppermute | solution.py:101
  12.4 4.7 %collective-permute-start.6 = (bf16[64,384]{1,0:T(8,128)(2,1)S(1)}, bf16[64,384]{1,0:T(8,128)(2,1)S(1)}, u32[]{:S(2)}, u32[]{:S(2)}) collective-permute-start(bf16[64,384]{1,0:T(8,128)(2,1)S(1)} %maximum_select_fusion.4), channel_id=1, source_target_pairs={{0,12},{1,13},{2,14},{3,15},{4,0},{5,1},{6,2},{7,3},{8,4},{9,5},{1... | collective-permute-start | bytes 147464 | tf_op jit(solution)/shard_map/ppermute | solution.py:101
  14.7 5.0 %collective-permute-start.7 = (bf16[64,384]{1,0:T(8,128)(2,1)S(1)}, bf16[64,384]{1,0:T(8,128)(2,1)S(1)}, u32[]{:S(2)}, u32[]{:S(2)}) collective-permute-start(bf16[64,384]{1,0:T(8,128)(2,1)S(1)} %maximum_select_fusion.4), channel_id=1, source_target_pairs={{0,14},{1,15},{2,12},{3,13},{4,2},{5,3},{6,0},{7,1},{8,6},{9,7},{1... | collective-permute-start | bytes 147464 | tf_op jit(solution)/shard_map/ppermute | solution.py:101
  20.4 1.2 %copy-start.1 = (bf16[3,768,192]{1,2,0:T(8,128)(2,1)S(1)}, bf16[3,768,192]{1,2,0:T(8,128)(2,1)}, u32[]{:S(2)}) copy-start(bf16[3,768,192]{1,2,0:T(8,128)(2,1)} %param.23) | copy-start | bytes 2654212
  20.4 1.2 %copy-start.6 = (f32[768]{0:T(1024)S(1)}, f32[768]{0:T(1024)}, u32[]{:S(2)}) copy-start(f32[768]{0:T(1024)} %param.19) | copy-start | bytes 9220
  22.4 1.0 %copy-start.3 = (bf16[192,768]{1,0:T(8,128)(2,1)S(1)}, bf16[192,768]{1,0:T(8,128)(2,1)}, u32[]{:S(2)}) copy-start(bf16[192,768]{1,0:T(8,128)(2,1)} %param.24) | copy-start | bytes 884740
  22.8 0.9 %copy-start.7 = (f32[768]{0:T(1024)S(1)}, f32[768]{0:T(1024)}, u32[]{:S(2)}) copy-start(f32[768]{0:T(1024)} %param.21) | copy-start | bytes 9220
  23.1 1.1 %copy-start.2 = (bf16[2,768,192]{1,2,0:T(8,128)(2,1)S(1)}, bf16[2,768,192]{1,2,0:T(8,128)(2,1)}, u32[]{:S(2)}) copy-start(bf16[2,768,192]{1,2,0:T(8,128)(2,1)} %param.26) | copy-start | bytes 1769476
  23.6 1.4 %collective-permute-start.8 = (bf16[64,768]{1,0:T(8,128)(2,1)S(1)}, bf16[64,768]{1,0:T(8,128)(2,1)S(1)}, u32[]{:S(2)}, u32[]{:S(2)}) collective-permute-start(bf16[64,768]{1,0:T(8,128)(2,1)S(1)} %broadcast_select_fusion.5), channel_id=1, source_target_pairs={{0,1},{1,0},{2,3},{3,2},{4,5},{5,4},{6,7},{7,6},{8,9},{9,8},{10,11... | collective-permute-start | bytes 294920 | tf_op jit(solution)/shard_map/ppermute | solution.py:41
  25.0 4.9 %collective-permute-start.9 = (bf16[64,768]{1,0:T(8,128)(2,1)S(1)}, bf16[64,768]{1,0:T(8,128)(2,1)S(1)}, u32[]{:S(2)}, u32[]{:S(2)}) collective-permute-start(bf16[64,768]{1,0:T(8,128)(2,1)S(1)} %add_convert_fusion.1), channel_id=1, source_target_pairs={{0,2},{1,3},{2,0},{3,1},{4,6},{5,7},{6,4},{7,5},{8,10},{9,11},{10,... | collective-permute-start | bytes 294920 | tf_op jit(solution)/shard_map/ppermute | solution.py:41
  30.0 1.5 %collective-permute-start.10 = (f32[64,768]{1,0:T(8,128)S(1)}, f32[64,768]{1,0:T(8,128)S(1)}, u32[]{:S(2)}, u32[]{:S(2)}) collective-permute-start(f32[64,768]{1,0:T(8,128)S(1)} %convert_add_fusion.1), channel_id=1, source_target_pairs={{0,1},{1,0},{2,3},{3,2},{4,5},{5,4},{6,7},{7,6},{8,9},{9,8},{10,11... | collective-permute-start | bytes 589832 | tf_op jit(solution)/shard_map/ppermute | solution.py:41
  30.3 1.5 %copy-start.4 = (bf16[768,192]{0,1:T(8,128)(2,1)S(1)}, bf16[768,192]{0,1:T(8,128)(2,1)}, u32[]{:S(2)}) copy-start(bf16[768,192]{0,1:T(8,128)(2,1)} %param.25) | copy-start | bytes 884740
  30.3 1.5 %copy-start.8 = (f32[768]{0:T(1024)S(1)}, f32[768]{0:T(1024)}, u32[]{:S(2)}) copy-start(f32[768]{0:T(1024)} %param.20) | copy-start | bytes 9220
  32.3 1.0 %copy-start.5 = (bf16[192,768]{1,0:T(8,128)(2,1)S(1)}, bf16[192,768]{1,0:T(8,128)(2,1)}, u32[]{:S(2)}) copy-start(bf16[192,768]{1,0:T(8,128)(2,1)} %param.27) | copy-start | bytes 884740
  32.7 1.1 %copy-start.9 = (f32[2,64]{1,0:T(2,128)S(1)}, f32[2,64]{1,0:T(2,128)}, u32[]{:S(2)}) copy-start(f32[2,64]{1,0:T(2,128)} %param.18) | copy-start | bytes 1540
  33.5 1.4 %collective-permute-start.11 = (bf16[64,768]{1,0:T(8,128)(2,1)S(1)}, bf16[64,768]{1,0:T(8,128)(2,1)S(1)}, u32[]{:S(2)}, u32[]{:S(2)}) collective-permute-start(bf16[64,768]{1,0:T(8,128)(2,1)S(1)} %broadcast_select_fusion.2), channel_id=1, source_target_pairs={{0,1},{1,0},{2,3},{3,2},{4,5},{5,4},{6,7},{7,6},{8,9},{9,8},{10,11... | collective-permute-start | bytes 294920 | tf_op jit(solution)/shard_map/ppermute | solution.py:41
  34.9 4.9 %collective-permute-start.12 = (bf16[64,768]{1,0:T(8,128)(2,1)S(1)}, bf16[64,768]{1,0:T(8,128)(2,1)S(1)}, u32[]{:S(2)}, u32[]{:S(2)}) collective-permute-start(bf16[64,768]{1,0:T(8,128)(2,1)S(1)} %add_convert_fusion), channel_id=1, source_target_pairs={{0,2},{1,3},{2,0},{3,1},{4,6},{5,7},{6,4},{7,5},{8,10},{9,11},{10,... | collective-permute-start | bytes 294920 | tf_op jit(solution)/shard_map/ppermute | solution.py:41
  39.9 1.5 %collective-permute-start.13 = (f32[64,768]{1,0:T(8,128)S(1)}, f32[64,768]{1,0:T(8,128)S(1)}, u32[]{:S(2)}, u32[]{:S(2)}) collective-permute-start(f32[64,768]{1,0:T(8,128)S(1)} %convert_add_fusion), channel_id=1, source_target_pairs={{0,1},{1,0},{2,3},{3,2},{4,5},{5,4},{6,7},{7,6},{8,9},{9,8},{10,11... | collective-permute-start | bytes 589832 | tf_op jit(solution)/shard_map/ppermute | solution.py:41
  40.1 1.6 %copy-start.10 = (bf16[768,768]{1,0:T(8,128)(2,1)S(1)}, bf16[768,768]{1,0:T(8,128)(2,1)}, u32[]{:S(2)}) copy-start(bf16[768,768]{1,0:T(8,128)(2,1)} %param.28) | copy-start | bytes 3538948
  40.2 1.6 %copy-start.11 = (f32[768]{0:T(1024)S(1)}, f32[768]{0:T(1024)}, u32[]{:S(2)}) copy-start(f32[768]{0:T(1024)} %param.22) | copy-start | bytes 9220
  43.6 2.9 %collective-permute-start.14 = (bf16[128,192]{1,0:T(8,128)(2,1)S(1)}, bf16[128,192]{1,0:T(8,128)(2,1)S(1)}, u32[]{:S(2)}, u32[]{:S(2)}) collective-permute-start(bf16[128,192]{1,0:T(8,128)(2,1)S(1)} %select_bitcast_fusion.2), channel_id=1, source_target_pairs={{0,1},{1,0},{2,3},{3,2},{4,5},{5,4},{6,7},{7,6},{8,9},{9,8},{10,11... | collective-permute-start | bytes 147464 | tf_op jit(solution)/shard_map/ppermute | solution.py:41
  43.9 5.0 %collective-permute-start.15 = (bf16[128,192]{1,0:T(8,128)(2,1)S(1)}, bf16[128,192]{1,0:T(8,128)(2,1)S(1)}, u32[]{:S(2)}, u32[]{:S(2)}) collective-permute-start(bf16[128,192]{1,0:T(8,128)(2,1)S(1)} %select_bitcast_fusion.1), channel_id=1, source_target_pairs={{0,2},{1,3},{2,0},{3,1},{4,6},{5,7},{6,4},{7,5},{8,10},{9,11},{10,... | collective-permute-start | bytes 147464 | tf_op jit(solution)/shard_map/ppermute | solution.py:41
  44.7 4.5 %collective-permute-start.16 = (bf16[128,192]{1,0:T(8,128)(2,1)S(1)}, bf16[128,192]{1,0:T(8,128)(2,1)S(1)}, u32[]{:S(2)}, u32[]{:S(2)}) collective-permute-start(bf16[128,192]{1,0:T(8,128)(2,1)S(1)} %select_bitcast_fusion), channel_id=1, source_target_pairs={{0,3},{1,2},{2,1},{3,0},{4,7},{5,6},{6,5},{7,4},{8,11},{9,10},{10,... | collective-permute-start | bytes 147464 | tf_op jit(solution)/shard_map/ppermute | solution.py:41
  50.1 5.6 %collective-permute-start.17 = (bf16[6272]{0:T(1024)(128)(2,1)S(1)}, bf16[6272]{0:T(1024)(128)(2,1)S(1)}, u32[]{:S(2)}, u32[]{:S(2)}) collective-permute-start(bf16[6272]{0:T(1024)(128)(2,1)S(1)} %get-tuple-element.17), channel_id=1, source_target_pairs={{0,4},{4,8},{8,12},{12,0},{1,5},{5,9},{9,13},{13,1},{2,6},{6,10},{... | collective-permute-start | bytes 37640 | tf_op jit(solution)/shard_map/ppermute | solution.py:37
  50.1 5.5 %collective-permute-start.18 = (bf16[6272]{0:T(1024)(128)(2,1)S(1)}, bf16[6272]{0:T(1024)(128)(2,1)S(1)}, u32[]{:S(2)}, u32[]{:S(2)}) collective-permute-start(bf16[6272]{0:T(1024)(128)(2,1)S(1)} %get-tuple-element.19), channel_id=1, source_target_pairs={{0,8},{4,12},{8,0},{12,4},{1,9},{5,13},{9,1},{13,5},{2,10},{6,14},... | collective-permute-start | bytes 37640 | tf_op jit(solution)/shard_map/ppermute | solution.py:37
  53.0 3.7 %collective-permute-start.19 = (bf16[6272]{0:T(1024)(128)(2,1)S(1)}, bf16[6272]{0:T(1024)(128)(2,1)S(1)}, u32[]{:S(2)}, u32[]{:S(2)}) collective-permute-start(bf16[6272]{0:T(1024)(128)(2,1)S(1)} %get-tuple-element.18), channel_id=1, source_target_pairs={{0,12},{4,0},{8,4},{12,8},{1,13},{5,1},{9,5},{13,9},{2,14},{6,2},{... | collective-permute-start | bytes 37640 | tf_op jit(solution)/shard_map/ppermute | solution.py:37

commit v4 on v2

--- a/solution.py
+++ b/solution.py
@@ -70,18 +70,12 @@
         quarter = term.shape[1] // lax.axis_size("mp")
         return lax.dynamic_slice_in_dim(full, lax.axis_index("mp") * quarter, quarter, 1)
     index = lax.axis_index("mp")
-    core = index % 2
-    chip = index // 2
     rows_n, width = term.shape
-    parts = term.reshape(rows_n, 2, 2, width // 4)
-    keep = jnp.where(core == 0, parts[:, :, 0], parts[:, :, 1])
-    send = jnp.where(core == 0, parts[:, :, 1], parts[:, :, 0])
-    got = swap(send, mp_pairs(1))
-    both = keep.astype(jnp.float32) + got.astype(jnp.float32)
-    mine = jnp.where(chip == 0, both[:, 0], both[:, 1])
-    theirs = jnp.where(chip == 0, both[:, 1], both[:, 0])
-    other = swap(theirs, mp_pairs(2))
-    return mine + other
+    parts = term.reshape(rows_n, 4, width // 4)
+    total = jnp.take(parts, index, axis=1).astype(jnp.float32)
+    for bit in (1, 2, 3):
+        total = total + swap(jnp.take(parts, index ^ bit, axis=1), mp_pairs(bit)).astype(jnp.float32)
+    return total
 
 
 def mp_gather_cols(part):
@@ -134,8 +128,13 @@
         every = lax.all_gather(tokens, "pairs", axis=0, tiled=True)
         at = ids
         targets = jnp.arange(owners_n)
-    every = every.reshape(owners_n * img_dev, TOKS, quarter)
-    slices = jnp.take(every, at, axis=0)
+    every = every.reshape(owners_n * img_dev, TOKS * quarter)
+    pick = (at[:, None] == jnp.arange(owners_n * img_dev)[None, :]).astype(jnp.bfloat16)
+    slices = (
+        jnp.dot(pick, every, preferred_element_type=jnp.float32)
+        .astype(jnp.bfloat16)
+        .reshape(views_n, TOKS, quarter)
+    )
     start = mp_gather_cols(slices)
     width = start.shape[2]
     rows_n = views_n * TOKS

time: 59.6 us -> 57.1 us (0.958)
  other arithmetic: 4.62 us -> 3.57 us
  local copies, waits for them, and re-layouts: 6.39 us -> 5.61 us
  waiting for transfers between devices: 25.9 us -> 25.3 us
    ppermute x10 -> x11, waiting for transfers between devices: 19.6 us -> 17.7 us  [swap(): return lax.ppermute(values, 'mp', pairs)]
    ppermute x6, waiting for transfers between devices: 6.27 us -> 7.65 us  [pairs_shift(): lax.ppermute(values, 'pairs', [(i, (i + step) % owners_n) for i in range(...]
    reshape x2 -> x1, local copies, waits for them, and re-layouts: 1.52 us -> 0.76 us  [per_device(): ids = pair_list.reshape(views_n)]
    and x2 -> x0, other arithmetic: 0.73 us -> none  [per_device(): slices = jnp.take(every, at, axis=0)]
    dot_general x1, matrix products: 2.14 us -> 1.44 us  [per_device(): jnp.dot(hidden.astype(jnp.bfloat16), mlp_down, preferred_element_type=jnp...]
    ppermute x10 -> x11, starting transfers between devices: 6.86 us -> 7.21 us  [swap(): return lax.ppermute(values, 'mp', pairs)]
  transfers between devices with their start and end apart: 16 -> 17, of which waited for: 15 -> 16; matrix products, arithmetic and copies ran while one was open for 7% -> 5% of each run, Pallas kernels for 0% -> 0%
where the time goes in v4:
time: 57.1 us; the launch traced here: 56.9 us
  waiting for transfers between devices  25.3 us (44%)
  starting transfers between devices  16.5 us (29%)
  local copies, waits for them, and re-layouts  5.61 us (10%)
  matrix products  5.23 us (9%)
  other arithmetic  3.57 us (6%)
  between operations  0.64 us (1%)
    ppermute x11, waiting for transfers between devices, swap(): return lax.ppermute(values, 'mp', pairs)  17.7 us
    ppermute x6, starting transfers between devices, pairs_shift(): lax.ppermute(values, 'pairs', [(i, (i + step) % owners_n) for i in range(...  9.27 us
    ppermute x6, waiting for transfers between devices, pairs_shift(): lax.ppermute(values, 'pairs', [(i, (i + step) % owners_n) for i in range(...  7.65 us
    ppermute x11, starting transfers between devices, swap(): return lax.ppermute(values, 'mp', pairs)  7.21 us
    dot_general x1, matrix products, per_device(): jnp.dot(hidden.astype(jnp.bfloat16), mlp_down, preferred_element_type=jnp...  1.44 us
  transfers between devices with their start and end apart: 17, of which 16 were waited for; matrix products, arithmetic and copies ran while one was open for 5% of the time, Pallas kernels for 0%

profile of v4, /device:TPU:0, one launch (start us, length us, event | category | flops | bytes accessed | tf_op | source)
XLA Modules:
  0.0 56.9 jit_solution(667854033660821224)
XLA Ops:
  0.0 5.0 %collective-permute-start.2 = (bf16[64,192]{1,0:T(8,128)(2,1)}, bf16[64,192]{1,0:T(8,128)(2,1)S(1)}, u32[]{:S(2)}, u32[]{:S(2)}) collective-permute-start(bf16[64,192]{1,0:T(8,128)(2,1)} %param.16), channel_id=1, source_target_pairs={{0,12},{4,0},{8,4},{12,8},{1,13},{5,1},{9,5},{13,9},{2,14},{6,2},{... | collective-permute-start | bytes 73736 | tf_op jit(solution)/shard_map/ppermute | solution.py:37
  5.1 1.0 %collective-permute-start = (bf16[64,192]{1,0:T(8,128)(2,1)}, bf16[64,192]{1,0:T(8,128)(2,1)S(1)}, u32[]{:S(2)}, u32[]{:S(2)}) collective-permute-start(bf16[64,192]{1,0:T(8,128)(2,1)} %param.16), channel_id=1, source_target_pairs={{0,4},{4,8},{8,12},{12,0},{1,5},{5,9},{9,13},{13,1},{2,6},{6,10},{... | collective-permute-start | bytes 73736 | tf_op jit(solution)/shard_map/ppermute | solution.py:37
  6.1 0.8 %reshape.259 = s32[4]{0:T(128)S(1)} reshape(s32[2,2]{1,0:T(2,128)} %param.17) | data formatting | bytes 32 | tf_op jit(solution)/shard_map/reshape | solution.py:119
  7.0 3.1 %collective-permute-done.1 = bf16[64,192]{1,0:T(8,128)(2,1)S(1)} collective-permute-done((bf16[64,192]{1,0:T(8,128)(2,1)}, bf16[64,192]{1,0:T(8,128)(2,1)S(1)}, u32[]{:S(2)}, u32[]{:S(2)}) %collective-permute-start.1) | collective-permute-done | bytes 24608 | tf_op jit(solution)/shard_map/ppermute | solution.py:37
  10.1 0.9 %collective-permute-done = bf16[64,192]{1,0:T(8,128)(2,1)S(1)} collective-permute-done((bf16[64,192]{1,0:T(8,128)(2,1)}, bf16[64,192]{1,0:T(8,128)(2,1)S(1)}, u32[]{:S(2)}, u32[]{:S(2)}) %collective-permute-start) | collective-permute-done | bytes 24608 | tf_op jit(solution)/shard_map/ppermute | solution.py:37
  11.0 0.8 %pad_maximum_fusion = bf16[256,192]{1,0:T(8,128)(2,1)S(1)} fusion(bf16[64,192]{1,0:T(8,128)(2,1)S(1)} %collective-permute-done.2, bf16[64,192]{1,0:T(8,128)(2,1)S(1)} %collective-permute-done.1, bf16[64,192]{1,0:T(8,128)(2,1)S(1)} %collective-permute-done, bf16[64,192]{1,0:T(8,128)(2,1)} %param.16), kind=kLoop, calls=%fused_computation.119 | loop fusion | flops 393216 | bytes 196608 | tf_op jit(solution)/shard_map/concatenate | solution.py:122
  11.8 0.2 reshape.260
  11.9 0.2 convolution_convert_fusion.1
  12.6 1.0 %collective-permute-done.3 = bf16[4,32,192]{2,1,0:T(8,128)(2,1)S(1)} collective-permute-done((bf16[4,32,192]{2,1,0:T(8,128)(2,1)S(1)}, bf16[4,32,192]{2,1,0:T(8,128)(2,1)S(1)}, u32[]{:S(2)}, u32[]{:S(2)}) %collective-permute-start.3) | collective-permute-done | bytes 49184 | tf_op jit(solution)/shard_map/ppermute | solution.py:41
  13.7 1.6 %collective-permute-start.4 = (bf16[4,32,384]{2,1,0:T(8,128)(2,1)S(1)}, bf16[4,32,384]{2,1,0:T(8,128)(2,1)S(1)}, u32[]{:S(2)}, u32[]{:S(2)}) collective-permute-start(bf16[4,32,384]{2,1,0:T(8,128)(2,1)S(1)} %maximum_select_fusion.3), channel_id=1, source_target_pairs={{0,2},{1,3},{2,0},{3,1},{4,6},{5,7},{6,4},{7,5},{8,10},{9,11},{10,... | collective-permute-start | bytes 294920 | tf_op jit(solution)/shard_map/ppermute | solution.py:41
  15.5 3.1 %collective-permute-done.4 = bf16[4,32,384]{2,1,0:T(8,128)(2,1)S(1)} collective-permute-done((bf16[4,32,384]{2,1,0:T(8,128)(2,1)S(1)}, bf16[4,32,384]{2,1,0:T(8,128)(2,1)S(1)}, u32[]{:S(2)}, u32[]{:S(2)}) %collective-permute-start.4) | collective-permute-done | bytes 98336 | tf_op jit(solution)/shard_map/ppermute | solution.py:41
  18.9 0.2 multiply_reduce_fusion.2
  19.4 0.2 fusion.13
  19.6 0.5 fusion.31
  20.1 0.1 reshape.373
  20.3 0.1 reshape.375
  20.4 0.1 reshape.374
  20.6 0.2 convolution_multiply_fusion.1
  20.9 0.3 fusion.6
  21.3 0.1 reshape.262
  21.5 0.2 convolution_convert_fusion.4
  22.0 0.3 copy-done.1
  22.3 0.3 fusion.154
  22.6 0.5 collective-permute-done.5
  23.2 1.6 %collective-permute-start.6 = (bf16[64,768]{1,0:T(8,128)(2,1)S(1)}, bf16[64,768]{1,0:T(8,128)(2,1)S(1)}, u32[]{:S(2)}, u32[]{:S(2)}) collective-permute-start(bf16[64,768]{1,0:T(8,128)(2,1)S(1)} %add_convert_fusion.1), channel_id=1, source_target_pairs={{0,2},{1,3},{2,0},{3,1},{4,6},{5,7},{6,4},{7,5},{8,10},{9,11},{10,... | collective-permute-start | bytes 294920 | tf_op jit(solution)/shard_map/ppermute | solution.py:41
  24.7 3.3 %collective-permute-done.6 = bf16[64,768]{1,0:T(8,128)(2,1)S(1)} collective-permute-done((bf16[64,768]{1,0:T(8,128)(2,1)S(1)}, bf16[64,768]{1,0:T(8,128)(2,1)S(1)}, u32[]{:S(2)}, u32[]{:S(2)}) %collective-permute-start.6) | collective-permute-done | bytes 98336 | tf_op jit(solution)/shard_map/ppermute | solution.py:41
  28.2 0.1 reshape.376
  28.5 1.1 %collective-permute-done.7 = f32[64,768]{1,0:T(8,128)S(1)} collective-permute-done((f32[64,768]{1,0:T(8,128)S(1)}, f32[64,768]{1,0:T(8,128)S(1)}, u32[]{:S(2)}, u32[]{:S(2)}) %collective-permute-start.7) | collective-permute-done | bytes 196640 | tf_op jit(solution)/shard_map/ppermute | solution.py:41
  29.6 0.1 fusion.146
  29.8 0.2 multiply_reduce_fusion.1
  30.0 0.3 convolution_convert_fusion.7
  30.3 0.1 reshape.377
  30.5 0.2 convolution_multiply_fusion
  30.8 0.3 fusion.7
  31.2 0.1 reshape.264
  31.4 0.2 convolution_convert_fusion.3
  31.7 0.2 collective-permute-start.8
  32.0 1.1 %collective-permute-done.8 = bf16[64,768]{1,0:T(8,128)(2,1)S(1)} collective-permute-done((bf16[64,768]{1,0:T(8,128)(2,1)S(1)}, bf16[64,768]{1,0:T(8,128)(2,1)S(1)}, u32[]{:S(2)}, u32[]{:S(2)}) %collective-permute-start.8) | collective-permute-done | bytes 98336 | tf_op jit(solution)/shard_map/ppermute | solution.py:41
  33.1 1.6 %collective-permute-start.9 = (bf16[64,768]{1,0:T(8,128)(2,1)S(1)}, bf16[64,768]{1,0:T(8,128)(2,1)S(1)}, u32[]{:S(2)}, u32[]{:S(2)}) collective-permute-start(bf16[64,768]{1,0:T(8,128)(2,1)S(1)} %add_convert_fusion), channel_id=1, source_target_pairs={{0,2},{1,3},{2,0},{3,1},{4,6},{5,7},{6,4},{7,5},{8,10},{9,11},{10,... | collective-permute-start | bytes 294920 | tf_op jit(solution)/shard_map/ppermute | solution.py:41
  34.6 3.3 %collective-permute-done.9 = bf16[64,768]{1,0:T(8,128)(2,1)S(1)} collective-permute-done((bf16[64,768]{1,0:T(8,128)(2,1)S(1)}, bf16[64,768]{1,0:T(8,128)(2,1)S(1)}, u32[]{:S(2)}, u32[]{:S(2)}) %collective-permute-start.9) | collective-permute-done | bytes 98336 | tf_op jit(solution)/shard_map/ppermute | solution.py:41
  38.1 0.2 convolution_convert_fusion.8
  38.3 1.2 %collective-permute-done.10 = f32[64,768]{1,0:T(8,128)S(1)} collective-permute-done((f32[64,768]{1,0:T(8,128)S(1)}, f32[64,768]{1,0:T(8,128)S(1)}, u32[]{:S(2)}, u32[]{:S(2)}) %collective-permute-start.10) | collective-permute-done | bytes 196640 | tf_op jit(solution)/shard_map/ppermute | solution.py:41
  39.6 0.1 fusion.147
  39.7 0.2 multiply_reduce_fusion
  40.0 1.4 %convolution_convert_fusion.2 = bf16[128,768]{1,0:T(8,128)(2,1)S(1)} fusion(bf16[768,768]{1,0:T(8,128)(2,1)S(1)} %copy-done, bf16[768,768]{1,0:T(8,128)(2,1)S(1)} %copy-done.6, f32[128,768]{1,0:T(8,128)S(1)} %get-tuple-element.21, f32[768]{0:T(1024)S(1)} %copy-done.11, f32[128]{0:T(128)S(1)} %add_rsqrt_fusion.1, f32[128]{0:T(128)S(1)} %broadcast_multiply_fusion.1), kind=kOutput, calls=%fused_computation.6 | convolution fusion | flops 308871168 | bytes 2953216 | tf_op jit(solution)/shard_map/dot_general | solution.py:166
  41.4 0.2 copy.42
  41.7 1.3 %collective-permute-start.13 = (bf16[128,192]{1,0:T(8,128)(2,1)S(1)}, bf16[128,192]{1,0:T(8,128)(2,1)S(1)}, u32[]{:S(2)}, u32[]{:S(2)}) collective-permute-start(bf16[128,192]{1,0:T(8,128)(2,1)S(1)} %select_bitcast_fusion), channel_id=1, source_target_pairs={{0,3},{1,2},{2,1},{3,0},{4,7},{5,6},{6,5},{7,4},{8,11},{9,10},{10,... | collective-permute-start | bytes 147464 | tf_op jit(solution)/shard_map/ppermute | solution.py:41
  43.2 0.6 %collective-permute-start.12 = (bf16[128,192]{1,0:T(8,128)(2,1)S(1)}, bf16[128,192]{1,0:T(8,128)(2,1)S(1)}, u32[]{:S(2)}, u32[]{:S(2)}) collective-permute-start(bf16[128,192]{1,0:T(8,128)(2,1)S(1)} %select_bitcast_fusion.1), channel_id=1, source_target_pairs={{0,2},{1,3},{2,0},{3,1},{4,6},{5,7},{6,4},{7,5},{8,10},{9,11},{10,... | collective-permute-start | bytes 147464 | tf_op jit(solution)/shard_map/ppermute | solution.py:41
  43.9 0.1 collective-permute-start.11
  44.1 0.2 fusion.10
  44.7 1.2 %collective-permute-done.13 = bf16[128,192]{1,0:T(8,128)(2,1)S(1)} collective-permute-done((bf16[128,192]{1,0:T(8,128)(2,1)S(1)}, bf16[128,192]{1,0:T(8,128)(2,1)S(1)}, u32[]{:S(2)}, u32[]{:S(2)}) %collective-permute-start.13) | collective-permute-done | bytes 49184 | tf_op jit(solution)/shard_map/ppermute | solution.py:41
  45.9 1.7 %collective-permute-done.12 = bf16[128,192]{1,0:T(8,128)(2,1)S(1)} collective-permute-done((bf16[128,192]{1,0:T(8,128)(2,1)S(1)}, bf16[128,192]{1,0:T(8,128)(2,1)S(1)}, u32[]{:S(2)}, u32[]{:S(2)}) %collective-permute-start.12) | collective-permute-done | bytes 49184 | tf_op jit(solution)/shard_map/ppermute | solution.py:41
  47.8 0.3 convolution_convert_fusion
  48.2 0.2 slice_reduce_fusion.2
  48.5 0.6 %collective-permute-start.16 = (bf16[6272]{0:T(1024)(128)(2,1)S(1)}, bf16[6272]{0:T(1024)(128)(2,1)S(1)}, u32[]{:S(2)}, u32[]{:S(2)}) collective-permute-start(bf16[6272]{0:T(1024)(128)(2,1)S(1)} %get-tuple-element.18), channel_id=1, source_target_pairs={{0,12},{4,0},{8,4},{12,8},{1,13},{5,1},{9,5},{13,9},{2,14},{6,2},{... | collective-permute-start | bytes 37640 | tf_op jit(solution)/shard_map/ppermute | solution.py:37
  49.1 0.6 %collective-permute-start.15 = (bf16[6272]{0:T(1024)(128)(2,1)S(1)}, bf16[6272]{0:T(1024)(128)(2,1)S(1)}, u32[]{:S(2)}, u32[]{:S(2)}) collective-permute-start(bf16[6272]{0:T(1024)(128)(2,1)S(1)} %get-tuple-element.19), channel_id=1, source_target_pairs={{0,8},{4,12},{8,0},{12,4},{1,9},{5,13},{9,1},{13,5},{2,10},{6,14},... | collective-permute-start | bytes 37640 | tf_op jit(solution)/shard_map/ppermute | solution.py:37
  49.7 1.9 %collective-permute-start.14 = (bf16[6272]{0:T(1024)(128)(2,1)S(1)}, bf16[6272]{0:T(1024)(128)(2,1)S(1)}, u32[]{:S(2)}, u32[]{:S(2)}) collective-permute-start(bf16[6272]{0:T(1024)(128)(2,1)S(1)} %get-tuple-element.17), channel_id=1, source_target_pairs={{0,4},{4,8},{8,12},{12,0},{1,5},{5,9},{9,13},{13,1},{2,6},{6,10},{... | collective-permute-start | bytes 37640 | tf_op jit(solution)/shard_map/ppermute | solution.py:37
  51.7 0.6 collective-permute-done.16
  52.3 1.5 %collective-permute-done.15 = bf16[6272]{0:T(1024)(128)(2,1)S(1)} collective-permute-done((bf16[6272]{0:T(1024)(128)(2,1)S(1)}, bf16[6272]{0:T(1024)(128)(2,1)S(1)}, u32[]{:S(2)}, u32[]{:S(2)}) %collective-permute-start.15) | collective-permute-done | bytes 12576 | tf_op jit(solution)/shard_map/ppermute | solution.py:37
  53.8 1.5 %collective-permute-done.14 = bf16[6272]{0:T(1024)(128)(2,1)S(1)} collective-permute-done((bf16[6272]{0:T(1024)(128)(2,1)S(1)}, bf16[6272]{0:T(1024)(128)(2,1)S(1)}, u32[]{:S(2)}, u32[]{:S(2)}) %collective-permute-start.14) | collective-permute-done | bytes 12576 | tf_op jit(solution)/shard_map/ppermute | solution.py:37
  55.4 0.2 convert_reduce_fusion.1
  55.7 0.2 convolution_maximum_fusion
  56.0 0.2 fusion.8
  56.3 0.6 %copy.50 = bf16[2,32,192]{2,1,0:T(8,128)(2,1)} copy(bf16[2,32,192]{2,0,1:T(2,128)(2,1)S(1)} %fusion.8) | data formatting | bytes 49152 | tf_op jit(solution)/shard_map/convert_element_type | solution.py:199
  (95 shorter events, 4.4 us)
Async XLA Ops:
  0.0 39.9 %copy-start = (bf16[768,768]{1,0:T(8,128)(2,1)S(1)}, bf16[768,768]{1,0:T(8,128)(2,1)}, u32[]{:S(2)}) copy-start(bf16[768,768]{1,0:T(8,128)(2,1)} %param.29) | copy-start | bytes 3538948
  0.0 7.0 %collective-permute-start.2 = (bf16[64,192]{1,0:T(8,128)(2,1)}, bf16[64,192]{1,0:T(8,128)(2,1)S(1)}, u32[]{:S(2)}, u32[]{:S(2)}) collective-permute-start(bf16[64,192]{1,0:T(8,128)(2,1)} %param.16), channel_id=1, source_target_pairs={{0,12},{4,0},{8,4},{12,8},{1,13},{5,1},{9,5},{13,9},{2,14},{6,2},{... | collective-permute-start | bytes 73736 | tf_op jit(solution)/shard_map/ppermute | solution.py:37
  5.1 5.0 %collective-permute-start.1 = (bf16[64,192]{1,0:T(8,128)(2,1)}, bf16[64,192]{1,0:T(8,128)(2,1)S(1)}, u32[]{:S(2)}, u32[]{:S(2)}) collective-permute-start(bf16[64,192]{1,0:T(8,128)(2,1)} %param.16), channel_id=1, source_target_pairs={{0,8},{4,12},{8,0},{12,4},{1,9},{5,13},{9,1},{13,5},{2,10},{6,14},... | collective-permute-start | bytes 73736 | tf_op jit(solution)/shard_map/ppermute | solution.py:37
  5.1 5.9 %collective-permute-start = (bf16[64,192]{1,0:T(8,128)(2,1)}, bf16[64,192]{1,0:T(8,128)(2,1)S(1)}, u32[]{:S(2)}, u32[]{:S(2)}) collective-permute-start(bf16[64,192]{1,0:T(8,128)(2,1)} %param.16), channel_id=1, source_target_pairs={{0,4},{4,8},{8,12},{12,0},{1,5},{5,9},{9,13},{13,1},{2,6},{6,10},{... | collective-permute-start | bytes 73736 | tf_op jit(solution)/shard_map/ppermute | solution.py:37
  12.3 1.3 %collective-permute-start.3 = (bf16[4,32,192]{2,1,0:T(8,128)(2,1)S(1)}, bf16[4,32,192]{2,1,0:T(8,128)(2,1)S(1)}, u32[]{:S(2)}, u32[]{:S(2)}) collective-permute-start(bf16[4,32,192]{2,1,0:T(8,128)(2,1)S(1)} %reshape.261), channel_id=1, source_target_pairs={{0,1},{1,0},{2,3},{3,2},{4,5},{5,4},{6,7},{7,6},{8,9},{9,8},{10,11... | collective-permute-start | bytes 147464 | tf_op jit(solution)/shard_map/ppermute | solution.py:41
  13.7 4.9 %collective-permute-start.4 = (bf16[4,32,384]{2,1,0:T(8,128)(2,1)S(1)}, bf16[4,32,384]{2,1,0:T(8,128)(2,1)S(1)}, u32[]{:S(2)}, u32[]{:S(2)}) collective-permute-start(bf16[4,32,384]{2,1,0:T(8,128)(2,1)S(1)} %maximum_select_fusion.3), channel_id=1, source_target_pairs={{0,2},{1,3},{2,0},{3,1},{4,6},{5,7},{6,4},{7,5},{8,10},{9,11},{10,... | collective-permute-start | bytes 294920 | tf_op jit(solution)/shard_map/ppermute | solution.py:41
  15.4 4.2 %copy-start.7 = (bf16[3,768,192]{1,2,0:T(8,128)(2,1)S(1)}, bf16[3,768,192]{1,2,0:T(8,128)(2,1)}, u32[]{:S(2)}) copy-start(bf16[3,768,192]{1,2,0:T(8,128)(2,1)} %param.23) | copy-start | bytes 2654212
  15.4 4.2 %copy-start.9 = (f32[768]{0:T(1024)S(1)}, f32[768]{0:T(1024)}, u32[]{:S(2)}) copy-start(f32[768]{0:T(1024)} %param.19) | copy-start | bytes 9220
  20.5 1.0 %copy-start.2 = (bf16[192,768]{1,0:T(8,128)(2,1)S(1)}, bf16[192,768]{1,0:T(8,128)(2,1)}, u32[]{:S(2)}) copy-start(bf16[192,768]{1,0:T(8,128)(2,1)} %param.24) | copy-start | bytes 884740
  20.9 1.0 %copy-start.4 = (f32[768]{0:T(1024)S(1)}, f32[768]{0:T(1024)}, u32[]{:S(2)}) copy-start(f32[768]{0:T(1024)} %param.21) | copy-start | bytes 9220
  21.2 1.1 %copy-start.1 = (bf16[2,768,192]{1,2,0:T(8,128)(2,1)S(1)}, bf16[2,768,192]{1,2,0:T(8,128)(2,1)}, u32[]{:S(2)}) copy-start(bf16[2,768,192]{1,2,0:T(8,128)(2,1)} %param.26) | copy-start | bytes 1769476
  21.7 1.4 %collective-permute-start.5 = (bf16[64,768]{1,0:T(8,128)(2,1)S(1)}, bf16[64,768]{1,0:T(8,128)(2,1)S(1)}, u32[]{:S(2)}, u32[]{:S(2)}) collective-permute-start(bf16[64,768]{1,0:T(8,128)(2,1)S(1)} %broadcast_select_fusion.5), channel_id=1, source_target_pairs={{0,1},{1,0},{2,3},{3,2},{4,5},{5,4},{6,7},{7,6},{8,9},{9,8},{10,11... | collective-permute-start | bytes 294920 | tf_op jit(solution)/shard_map/ppermute | solution.py:41
  23.2 4.9 %collective-permute-start.6 = (bf16[64,768]{1,0:T(8,128)(2,1)S(1)}, bf16[64,768]{1,0:T(8,128)(2,1)S(1)}, u32[]{:S(2)}, u32[]{:S(2)}) collective-permute-start(bf16[64,768]{1,0:T(8,128)(2,1)S(1)} %add_convert_fusion.1), channel_id=1, source_target_pairs={{0,2},{1,3},{2,0},{3,1},{4,6},{5,7},{6,4},{7,5},{8,10},{9,11},{10,... | collective-permute-start | bytes 294920 | tf_op jit(solution)/shard_map/ppermute | solution.py:41
  28.1 1.5 %collective-permute-start.7 = (f32[64,768]{1,0:T(8,128)S(1)}, f32[64,768]{1,0:T(8,128)S(1)}, u32[]{:S(2)}, u32[]{:S(2)}) collective-permute-start(f32[64,768]{1,0:T(8,128)S(1)} %convert_add_fusion.2), channel_id=1, source_target_pairs={{0,1},{1,0},{2,3},{3,2},{4,5},{5,4},{6,7},{7,6},{8,9},{9,8},{10,11... | collective-permute-start | bytes 589832 | tf_op jit(solution)/shard_map/ppermute | solution.py:41
  28.2 1.8 %copy-start.8 = (bf16[768,192]{0,1:T(8,128)(2,1)S(1)}, bf16[768,192]{0,1:T(8,128)(2,1)}, u32[]{:S(2)}) copy-start(bf16[768,192]{0,1:T(8,128)(2,1)} %param.25) | copy-start | bytes 884740
  28.2 1.8 %copy-start.10 = (f32[768]{0:T(1024)S(1)}, f32[768]{0:T(1024)}, u32[]{:S(2)}) copy-start(f32[768]{0:T(1024)} %param.20) | copy-start | bytes 9220
  30.5 1.0 %copy-start.3 = (bf16[192,768]{1,0:T(8,128)(2,1)S(1)}, bf16[192,768]{1,0:T(8,128)(2,1)}, u32[]{:S(2)}) copy-start(bf16[192,768]{1,0:T(8,128)(2,1)} %param.27) | copy-start | bytes 884740
  30.8 1.1 %copy-start.5 = (f32[2,64]{1,0:T(2,128)S(1)}, f32[2,64]{1,0:T(2,128)}, u32[]{:S(2)}) copy-start(f32[2,64]{1,0:T(2,128)} %param.18) | copy-start | bytes 1540
  31.7 1.4 %collective-permute-start.8 = (bf16[64,768]{1,0:T(8,128)(2,1)S(1)}, bf16[64,768]{1,0:T(8,128)(2,1)S(1)}, u32[]{:S(2)}, u32[]{:S(2)}) collective-permute-start(bf16[64,768]{1,0:T(8,128)(2,1)S(1)} %broadcast_select_fusion.2), channel_id=1, source_target_pairs={{0,1},{1,0},{2,3},{3,2},{4,5},{5,4},{6,7},{7,6},{8,9},{9,8},{10,11... | collective-permute-start | bytes 294920 | tf_op jit(solution)/shard_map/ppermute | solution.py:41
  33.1 4.9 %collective-permute-start.9 = (bf16[64,768]{1,0:T(8,128)(2,1)S(1)}, bf16[64,768]{1,0:T(8,128)(2,1)S(1)}, u32[]{:S(2)}, u32[]{:S(2)}) collective-permute-start(bf16[64,768]{1,0:T(8,128)(2,1)S(1)} %add_convert_fusion), channel_id=1, source_target_pairs={{0,2},{1,3},{2,0},{3,1},{4,6},{5,7},{6,4},{7,5},{8,10},{9,11},{10,... | collective-permute-start | bytes 294920 | tf_op jit(solution)/shard_map/ppermute | solution.py:41
  38.0 1.5 %collective-permute-start.10 = (f32[64,768]{1,0:T(8,128)S(1)}, f32[64,768]{1,0:T(8,128)S(1)}, u32[]{:S(2)}, u32[]{:S(2)}) collective-permute-start(f32[64,768]{1,0:T(8,128)S(1)} %convert_add_fusion.1), channel_id=1, source_target_pairs={{0,1},{1,0},{2,3},{3,2},{4,5},{5,4},{6,7},{7,6},{8,9},{9,8},{10,11... | collective-permute-start | bytes 589832 | tf_op jit(solution)/shard_map/ppermute | solution.py:41
  38.3 1.7 %copy-start.6 = (bf16[768,768]{1,0:T(8,128)(2,1)S(1)}, bf16[768,768]{1,0:T(8,128)(2,1)}, u32[]{:S(2)}) copy-start(bf16[768,768]{1,0:T(8,128)(2,1)} %param.28) | copy-start | bytes 3538948
  38.3 1.7 %copy-start.11 = (f32[768]{0:T(1024)S(1)}, f32[768]{0:T(1024)}, u32[]{:S(2)}) copy-start(f32[768]{0:T(1024)} %param.22) | copy-start | bytes 9220
  41.7 4.1 %collective-permute-start.13 = (bf16[128,192]{1,0:T(8,128)(2,1)S(1)}, bf16[128,192]{1,0:T(8,128)(2,1)S(1)}, u32[]{:S(2)}, u32[]{:S(2)}) collective-permute-start(bf16[128,192]{1,0:T(8,128)(2,1)S(1)} %select_bitcast_fusion), channel_id=1, source_target_pairs={{0,3},{1,2},{2,1},{3,0},{4,7},{5,6},{6,5},{7,4},{8,11},{9,10},{10,... | collective-permute-start | bytes 147464 | tf_op jit(solution)/shard_map/ppermute | solution.py:41
  43.2 4.4 %collective-permute-start.12 = (bf16[128,192]{1,0:T(8,128)(2,1)S(1)}, bf16[128,192]{1,0:T(8,128)(2,1)S(1)}, u32[]{:S(2)}, u32[]{:S(2)}) collective-permute-start(bf16[128,192]{1,0:T(8,128)(2,1)S(1)} %select_bitcast_fusion.1), channel_id=1, source_target_pairs={{0,2},{1,3},{2,0},{3,1},{4,6},{5,7},{6,4},{7,5},{8,10},{9,11},{10,... | collective-permute-start | bytes 147464 | tf_op jit(solution)/shard_map/ppermute | solution.py:41
  43.9 3.7 %collective-permute-start.11 = (bf16[128,192]{1,0:T(8,128)(2,1)S(1)}, bf16[128,192]{1,0:T(8,128)(2,1)S(1)}, u32[]{:S(2)}, u32[]{:S(2)}) collective-permute-start(bf16[128,192]{1,0:T(8,128)(2,1)S(1)} %select_bitcast_fusion.2), channel_id=1, source_target_pairs={{0,1},{1,0},{2,3},{3,2},{4,5},{5,4},{6,7},{7,6},{8,9},{9,8},{10,11... | collective-permute-start | bytes 147464 | tf_op jit(solution)/shard_map/ppermute | solution.py:41
  48.5 3.8 %collective-permute-start.16 = (bf16[6272]{0:T(1024)(128)(2,1)S(1)}, bf16[6272]{0:T(1024)(128)(2,1)S(1)}, u32[]{:S(2)}, u32[]{:S(2)}) collective-permute-start(bf16[6272]{0:T(1024)(128)(2,1)S(1)} %get-tuple-element.18), channel_id=1, source_target_pairs={{0,12},{4,0},{8,4},{12,8},{1,13},{5,1},{9,5},{13,9},{2,14},{6,2},{... | collective-permute-start | bytes 37640 | tf_op jit(solution)/shard_map/ppermute | solution.py:37
  49.1 4.6 %collective-permute-start.15 = (bf16[6272]{0:T(1024)(128)(2,1)S(1)}, bf16[6272]{0:T(1024)(128)(2,1)S(1)}, u32[]{:S(2)}, u32[]{:S(2)}) collective-permute-start(bf16[6272]{0:T(1024)(128)(2,1)S(1)} %get-tuple-element.19), channel_id=1, source_target_pairs={{0,8},{4,12},{8,0},{12,4},{1,9},{5,13},{9,1},{13,5},{2,10},{6,14},... | collective-permute-start | bytes 37640 | tf_op jit(solution)/shard_map/ppermute | solution.py:37
  49.7 5.5 %collective-permute-start.14 = (bf16[6272]{0:T(1024)(128)(2,1)S(1)}, bf16[6272]{0:T(1024)(128)(2,1)S(1)}, u32[]{:S(2)}, u32[]{:S(2)}) collective-permute-start(bf16[6272]{0:T(1024)(128)(2,1)S(1)} %get-tuple-element.17), channel_id=1, source_target_pairs={{0,4},{4,8},{8,12},{12,0},{1,5},{5,9},{9,13},{13,1},{2,6},{6,10},{... | collective-permute-start | bytes 37640 | tf_op jit(solution)/shard_map/ppermute | solution.py:37

commit v5 on v4

--- a/solution.py
+++ b/solution.py
@@ -92,6 +92,23 @@
     return jnp.where(
         chip == 0, jnp.concatenate([pair, other], axis=2), jnp.concatenate([other, pair], axis=2)
     )
+
+
+def pairs_gather(payload, owners_n):
+    if owners_n <= SHIFTS_MAX:
+        return jnp.stack(
+            [payload] + [pairs_shift(payload, step, owners_n) for step in range(1, owners_n)]
+        )
+    own = lax.axis_index("pairs")
+    every = lax.all_gather(payload, "pairs", axis=0)
+    return jnp.roll(every[::-1], own + 1, axis=0)
+
+
+def pick_rows(onehot, values):
+    shape = values.shape
+    flat = values.reshape(shape[0], -1)
+    picked = jnp.dot(onehot.astype(values.dtype), flat, preferred_element_type=jnp.float32)
+    return picked.astype(values.dtype).reshape((onehot.shape[0],) + shape[1:])
 
 
 def per_device(
@@ -116,45 +133,63 @@
     views_n = 2 * pair_dev
     owners_n = lax.axis_size("pairs")
     own = lax.axis_index("pairs")
-    ids = pair_list.reshape(views_n)
-    source = ids // img_dev
-    if owners_n <= SHIFTS_MAX:
-        every = jnp.concatenate(
-            [tokens] + [pairs_shift(tokens, step, owners_n) for step in range(1, owners_n)], axis=0
-        )
-        at = ((own - source) % owners_n) * img_dev + ids % img_dev
-        targets = (own + jnp.arange(owners_n)) % owners_n
-    else:
-        every = lax.all_gather(tokens, "pairs", axis=0, tiled=True)
-        at = ids
-        targets = jnp.arange(owners_n)
-    every = every.reshape(owners_n * img_dev, TOKS * quarter)
-    pick = (at[:, None] == jnp.arange(owners_n * img_dev)[None, :]).astype(jnp.bfloat16)
-    slices = (
-        jnp.dot(pick, every, preferred_element_type=jnp.float32)
-        .astype(jnp.bfloat16)
-        .reshape(views_n, TOKS, quarter)
-    )
-    start = mp_gather_cols(slices)
-    width = start.shape[2]
-    rows_n = views_n * TOKS
-    flipped = start.reshape(pair_dev, 2, TOKS, width)
-    flipped = jnp.concatenate([flipped[:, 1:], flipped[:, :1]], axis=1)
-    begin = start.astype(jnp.float32).reshape(rows_n, width)
-    context = layer_norm(flipped.astype(jnp.float32), gain_context).reshape(rows_n, width)
+
+    payload = jnp.concatenate(
+        [
+            tokens.astype(jnp.float32).reshape(-1),
+            pair_list.astype(jnp.float32).reshape(-1),
+            confidence.reshape(-1),
+        ]
+    )
+    table = pairs_gather(payload, owners_n)
+    cut_tok = img_dev * TOKS * quarter
+    cut_ids = cut_tok + views_n
+    all_tok = table[:, :cut_tok].astype(jnp.bfloat16).reshape(owners_n * img_dev, TOKS * quarter)
+    all_ids = table[:, cut_tok:cut_ids].astype(jnp.int32)
+    all_conf = table[:, cut_ids:].reshape(owners_n * views_n, TOKS)
+    partner_ids = all_ids.reshape(owners_n, pair_dev, 2)[:, :, ::-1].reshape(-1)
+    all_ids = all_ids.reshape(-1)
+
+    mine = (all_ids // img_dev == own).astype(jnp.int32)
+    rank = jnp.cumsum(mine) - 1
+    choose = (mine[None, :] == 1) & (rank[None, :] == jnp.arange(views_n)[:, None])
+    image = jnp.sum(jnp.where(choose, all_ids[None, :], 0), axis=1)
+    other = jnp.sum(jnp.where(choose, partner_ids[None, :], 0), axis=1)
+    conf = jnp.dot(choose.astype(jnp.float32), all_conf, precision=lax.Precision.HIGHEST)
+    local = image % img_dev
+    at = ((own - other // img_dev) % owners_n) * img_dev + other % img_dev
+    far = (at[:, None] == jnp.arange(owners_n * img_dev)[None, :]).astype(jnp.bfloat16)
+    context_q = pick_rows(far, all_tok).reshape(views_n, TOKS, quarter)
+
+    own_tok = mp_gather_cols(tokens.reshape(img_dev, TOKS, quarter))
+    width = own_tok.shape[2]
+    img_rows = img_dev * TOKS
+    begin = own_tok.astype(jnp.float32).reshape(img_rows, width)
     normed = layer_norm(begin, gain_self)
     qkv = jnp.einsum("rd,kdc->krc", normed, self_qkv, preferred_element_type=jnp.float32).astype(
         jnp.bfloat16
     )
     term = jnp.dot(
-        attend(qkv[0], qkv[1], qkv[2], views_n), self_out, preferred_element_type=jnp.float32
-    )
-    resid = begin + mp_allreduce(term.astype(jnp.bfloat16))
-    normed = layer_norm(resid, gain_query)
-    query = jnp.dot(normed, cross_query, preferred_element_type=jnp.float32).astype(jnp.bfloat16)
+        attend(qkv[0], qkv[1], qkv[2], img_dev), self_out, preferred_element_type=jnp.float32
+    )
+    resid_img = begin + mp_allreduce(term.astype(jnp.bfloat16))
+    normed = layer_norm(resid_img, gain_query)
+    query_img = jnp.dot(normed, cross_query, preferred_element_type=jnp.float32).astype(
+        jnp.bfloat16
+    )
+
+    rows_n = views_n * TOKS
+    context = layer_norm(mp_gather_cols(context_q).astype(jnp.float32), gain_context).reshape(
+        rows_n, width
+    )
     keyval = jnp.einsum(
         "rd,kdc->krc", context, cross_kv, preferred_element_type=jnp.float32
     ).astype(jnp.bfloat16)
+    near = (local[:, None] == jnp.arange(img_dev)[None, :]).astype(jnp.bfloat16)
+    query = pick_rows(near, query_img.reshape(img_dev, TOKS, -1)).reshape(rows_n, -1)
+    resid = jnp.take(resid_img.reshape(img_dev, TOKS, width), local, axis=0).reshape(
+        rows_n, width
+    )
     term = jnp.dot(
         attend(query, keyval[0], keyval[1], views_n), cross_out, preferred_element_type=jnp.float32
     )
@@ -168,33 +203,13 @@
     final = lax.dynamic_slice_in_dim(resid, offset, quarter, 1) + mp_reduce_cols(
         term.astype(jnp.bfloat16)
     )
-    conf = confidence.reshape(views_n, TOKS)
-    weighted = (final.reshape(views_n, TOKS, quarter) * conf[:, :, None]).reshape(
-        views_n, TOKS * quarter
-    )
-    slot = (ids % img_dev + 1).astype(jnp.float32)
-    route = (source[None, :] == targets[:, None]).astype(jnp.float32)
-    back = jnp.dot(route, weighted, precision=lax.Precision.HIGHEST)
-    back_weight = jnp.dot(route, conf, precision=lax.Precision.HIGHEST)
-    back_slot = jnp.dot(route, slot[:, None], precision=lax.Precision.HIGHEST)
-    pad = jnp.zeros((owners_n, 128 - TOKS - 1), jnp.float32)
-    payload = jnp.concatenate([back, back_weight, back_slot, pad], axis=1).astype(jnp.bfloat16)
-    if owners_n <= SHIFTS_MAX:
-        got = jnp.stack(
-            [payload[0]]
-            + [pairs_shift(payload[step], step, owners_n) for step in range(1, owners_n)]
-        )
-    else:
-        got = lax.all_to_all(payload, "pairs", split_axis=0, concat_axis=0, tiled=True)
-    got = got.astype(jnp.float32)
-    feat = got[:, : TOKS * quarter].reshape(owners_n, TOKS, quarter)
-    got_weight = got[:, TOKS * quarter : TOKS * quarter + TOKS]
-    got_slot = got[:, TOKS * quarter + TOKS]
-    owner_match = (got_slot[None, :] == (jnp.arange(img_dev) + 1)[:, None].astype(jnp.float32)).astype(
-        jnp.float32
-    )
-    numer = jnp.einsum("ij,jtc->itc", owner_match, feat, precision=lax.Precision.HIGHEST)
-    denom = jnp.dot(owner_match, got_weight, precision=lax.Precision.HIGHEST)
+    part = (final.reshape(views_n, TOKS, quarter) * conf[:, :, None]).astype(jnp.bfloat16)
+    weight = conf.astype(jnp.bfloat16)
+    owner_match = near.astype(jnp.float32).T
+    numer = jnp.einsum(
+        "iv,vtc->itc", owner_match, part.astype(jnp.float32), precision=lax.Precision.HIGHEST
+    )
+    denom = jnp.dot(owner_match, weight.astype(jnp.float32), precision=lax.Precision.HIGHEST)
     result = numer / jnp.maximum(denom, 1.0)[:, :, None]
     return result.astype(jnp.bfloat16).reshape(img_dev * TOKS, quarter)
 

time: 57.1 us -> 47.7 us (0.84)
  waiting for transfers between devices: 25.3 us -> 13.5 us
  other arithmetic: 3.57 us -> 5.23 us
  starting transfers between devices: 16.5 us -> 15.3 us
  local copies, waits for them, and re-layouts: 5.61 us -> 6.65 us
  matrix products: 5.23 us -> 6.14 us
    ppermute x6 -> x3, waiting for transfers between devices: 7.65 us -> 1.6 us  [pairs_shift(): lax.ppermute(values, 'pairs', [(i, (i + step) % owners_n) for i in range(...]
    ppermute x11 -> x13, waiting for transfers between devices: 17.7 us -> 11.9 us  [swap(): return lax.ppermute(values, 'mp', pairs)]
    ppermute x6 -> x3, starting transfers between devices: 9.27 us -> 5.71 us  [pairs_shift(): lax.ppermute(values, 'pairs', [(i, (i + step) % owners_n) for i in range(...]
    ppermute x11 -> x13, starting transfers between devices: 7.21 us -> 9.55 us  [swap(): return lax.ppermute(values, 'mp', pairs)]
    select_n x3 -> x4, other arithmetic: 0.34 us -> 2.08 us  [mp_gather_cols(): jnp.where(core == 0, jnp.concatenate([part, got], axis=2), jnp.concatenat...]
    dot_general x1, matrix products: 1.44 us -> 2.72 us  [per_device(): jnp.dot(hidden.astype(jnp.bfloat16), mlp_down, preferred_element_type=jnp...]
    reshape x6 -> x8, local copies, waits for them, and re-layouts: 1.39 us -> 2.07 us  [the longest x1 0.85 us: per_device(): tokens.astype(jnp.float32).reshape(-1)]
    concatenate x1, other arithmetic: 0.78 us -> 0.13 us  [mp_allreduce(): return jnp.concatenate([first, second], axis=0)]
  transfers between devices with their start and end apart: 17 -> 16, of which waited for: 16 -> 7; matrix products, arithmetic and copies ran while one was open for 5% -> 23% of each run, Pallas kernels for 0% -> 0%
where the time goes in v5:
time: 47.7 us; the launch traced here: 47.4 us
  starting transfers between devices  15.3 us (32%)
  waiting for transfers between devices  13.5 us (28%)
  local copies, waits for them, and re-layouts  6.65 us (14%)
  matrix products  6.14 us (13%)
  other arithmetic  5.23 us (11%)
  between operations  0.63 us (1%)
    ppermute x13, waiting for transfers between devices, swap(): return lax.ppermute(values, 'mp', pairs)  11.9 us
    ppermute x13, starting transfers between devices, swap(): return lax.ppermute(values, 'mp', pairs)  9.55 us
    ppermute x3, starting transfers between devices, pairs_shift(): lax.ppermute(values, 'pairs', [(i, (i + step) % owners_n) for i in range(...  5.71 us
    dot_general x1, matrix products, per_device(): jnp.dot(hidden.astype(jnp.bfloat16), mlp_down, preferred_element_type=jnp...  2.72 us
    select_n x4, other arithmetic, mp_gather_cols(): jnp.where(core == 0, jnp.concatenate([part, got], axis=2), jnp.concatenat...  2.08 us
    ppermute x3, waiting for transfers between devices, pairs_shift(): lax.ppermute(values, 'pairs', [(i, (i + step) % owners_n) for i in range(...  1.6 us
  transfers between devices with their start and end apart: 16, of which 7 were waited for; matrix products, arithmetic and copies ran while one was open for 23% of the time, Pallas kernels for 0%

profile of v5, /device:TPU:0, one launch (start us, length us, event | category | flops | bytes accessed | tf_op | source)
XLA Modules:
  0.0 47.4 jit_solution(8744999755315677154)
XLA Ops:
  0.0 0.5 collective-permute-start.3
  0.5 0.8 %reshape.542 = f32[12288]{0:T(1024)S(1)} reshape(bf16[64,192]{1,0:T(8,128)(2,1)} %param.16) | data formatting | bytes 73728 | tf_op jit(solution)/shard_map/reshape | solution.py:139
  1.3 0.8 %reshape.465 = f32[128]{0:T(128)S(1)} reshape(f32[2,64]{1,0:T(2,128)} %param.18) | data formatting | bytes 1024 | tf_op jit(solution)/shard_map/reshape | solution.py:141
  2.1 0.7 %convert_element_type.160 = f32[2,2]{1,0:T(2,128)S(1)} convert(s32[2,2]{1,0:T(2,128)} %param.17) | non-fusion elementwise | flops 4 | bytes 32 | tf_op jit(solution)/shard_map/convert_element_type | solution.py:140
  2.9 4.7 %collective-permute-start.2 = (f32[12420]{0:T(1024)S(1)}, f32[12420]{0:T(1024)S(1)}, u32[]{:S(2)}, u32[]{:S(2)}) collective-permute-start(f32[12420]{0:T(1024)S(1)} %concatenate.71), channel_id=1, source_target_pairs={{0,12},{4,0},{8,4},{12,8},{1,13},{5,1},{9,5},{13,9},{2,14},{6,2},{... | collective-permute-start | bytes 149048 | tf_op jit(solution)/shard_map/ppermute | solution.py:37
  7.6 1.0 %collective-permute-start = (f32[12420]{0:T(1024)S(1)}, f32[12420]{0:T(1024)S(1)}, u32[]{:S(2)}, u32[]{:S(2)}) collective-permute-start(f32[12420]{0:T(1024)S(1)} %concatenate.71), channel_id=1, source_target_pairs={{0,4},{4,8},{8,12},{12,0},{1,5},{5,9},{9,13},{13,1},{2,6},{6,10},{... | collective-permute-start | bytes 149048 | tf_op jit(solution)/shard_map/ppermute | solution.py:37
  8.7 0.9 %maximum_select_fusion.8 = bf16[64,384]{1,0:T(8,128)(2,1)S(1)} fusion(bf16[64,192]{1,0:T(8,128)(2,1)S(1)} %bitcast.77, bf16[64,192]{1,0:T(8,128)(2,1)} %param.16, pred[]{:T(512)S(6)} %eq.107), kind=kLoop, calls=%fused_computation.146 | loop fusion | flops 221184 | bytes 98305 | tf_op jit(solution)/shard_map/jit(_where)/select_n | solution.py:88
  9.7 0.9 %maximum_select_fusion.7 = bf16[2,32,384]{2,1,0:T(8,128)(2,1)S(1)} fusion(bf16[2,32,192]{2,1,0:T(8,128)(2,1)S(1)} %collective-permute-done.3, bf16[2,32,192]{2,1,0:T(8,128)(2,1)} %bitcast.74, pred[]{:T(512)S(6)} %eq.107), kind=kLoop, calls=%fused_computation.145 | loop fusion | flops 221184 | bytes 98305 | tf_op jit(solution)/shard_map/jit(_where)/select_n | solution.py:88
  10.6 1.6 %collective-permute-start.4 = (bf16[2,32,384]{2,1,0:T(8,128)(2,1)S(1)}, bf16[2,32,384]{2,1,0:T(8,128)(2,1)S(1)}, u32[]{:S(2)}, u32[]{:S(2)}) collective-permute-start(bf16[2,32,384]{2,1,0:T(8,128)(2,1)S(1)} %maximum_select_fusion.7), channel_id=1, source_target_pairs={{0,2},{1,3},{2,0},{3,1},{4,6},{5,7},{6,4},{7,5},{8,10},{9,11},{10,... | collective-permute-start | bytes 147464 | tf_op jit(solution)/shard_map/ppermute | solution.py:41
  12.2 1.6 %collective-permute-done.1 = f32[12420]{0:T(1024)S(1)} collective-permute-done((f32[12420]{0:T(1024)S(1)}, f32[12420]{0:T(1024)S(1)}, u32[]{:S(2)}, u32[]{:S(2)}) %collective-permute-start.1) | collective-permute-done | bytes 49712 | tf_op jit(solution)/shard_map/ppermute | solution.py:37
  14.0 0.2 pad_maximum_fusion
  14.8 0.1 add_reduce_fusion
  14.9 0.2 select_reduce_fusion.1
  15.2 0.1 fusion.151
  15.3 0.2 convolution_convert_fusion.1
  15.5 0.1 reshape.472
  15.7 0.1 concatenate.84
  15.9 0.1 convert_reduce_fusion.1
  16.0 0.2 fusion.25
  16.2 0.4 fusion.6
  16.9 0.2 fusion.156
  17.0 0.1 convolution_multiply_fusion.1
  17.3 0.2 fusion.9
  17.7 0.2 convolution_convert_fusion.6
  17.9 0.6 %collective-permute-start.5 = (bf16[32,768]{1,0:T(8,128)(2,1)S(1)}, bf16[32,768]{1,0:T(8,128)(2,1)S(1)}, u32[]{:S(2)}, u32[]{:S(2)}) collective-permute-start(bf16[32,768]{1,0:T(8,128)(2,1)S(1)} %broadcast_select_fusion.5), channel_id=1, source_target_pairs={{0,1},{1,0},{2,3},{3,2},{4,5},{5,4},{6,7},{7,6},{8,9},{9,8},{10,11... | collective-permute-start | bytes 147464 | tf_op jit(solution)/shard_map/ppermute | solution.py:41
  18.4 0.1 maximum_select_fusion.6
  18.6 1.6 %collective-permute-start.9 = (bf16[4,32,384]{2,1,0:T(8,128)(2,1)S(1)}, bf16[4,32,384]{2,1,0:T(8,128)(2,1)S(1)}, u32[]{:S(2)}, u32[]{:S(2)}) collective-permute-start(bf16[4,32,384]{2,1,0:T(8,128)(2,1)S(1)} %maximum_select_fusion.6), channel_id=1, source_target_pairs={{0,2},{1,3},{2,0},{3,1},{4,6},{5,7},{6,4},{7,5},{8,10},{9,11},{10,... | collective-permute-start | bytes 294920 | tf_op jit(solution)/shard_map/ppermute | solution.py:41
  20.2 0.8 %collective-permute-start.6 = (bf16[32,768]{1,0:T(8,128)(2,1)S(1)}, bf16[32,768]{1,0:T(8,128)(2,1)S(1)}, u32[]{:S(2)}, u32[]{:S(2)}) collective-permute-start(bf16[32,768]{1,0:T(8,128)(2,1)S(1)} %add_convert_fusion.1), channel_id=1, source_target_pairs={{0,2},{1,3},{2,0},{3,1},{4,6},{5,7},{6,4},{7,5},{8,10},{9,11},{10,... | collective-permute-start | bytes 147464 | tf_op jit(solution)/shard_map/ppermute | solution.py:41
  20.9 0.1 maximum_select_fusion.5
  21.0 3.4 %collective-permute-done.6 = bf16[32,768]{1,0:T(8,128)(2,1)S(1)} collective-permute-done((bf16[32,768]{1,0:T(8,128)(2,1)S(1)}, bf16[32,768]{1,0:T(8,128)(2,1)S(1)}, u32[]{:S(2)}, u32[]{:S(2)}) %collective-permute-start.6) | collective-permute-done | bytes 49184 | tf_op jit(solution)/shard_map/ppermute | solution.py:41
  24.5 0.1 convert_reduce_fusion
  24.7 0.2 fusion.11
  25.0 0.4 fusion.28
  25.5 0.1 reshape.588
  25.6 0.1 reshape.587
  25.8 0.1 pad_maximum_fusion.1
  25.9 0.2 multiply_reduce_fusion.1
  26.2 0.2 copy-done.5
  26.4 0.2 convolution_convert_fusion.8
  26.8 0.2 convolution_convert_fusion
  27.0 0.1 reshape_reshape_reshape.3
  27.2 0.2 convolution_multiply_fusion
  27.5 0.3 fusion.5
  27.8 0.1 reshape.473
  28.0 0.1 copy-done.1
  28.1 0.2 convolution_convert_fusion.3
  28.3 0.6 %collective-permute-start.10 = (bf16[64,768]{1,0:T(8,128)(2,1)S(1)}, bf16[64,768]{1,0:T(8,128)(2,1)S(1)}, u32[]{:S(2)}, u32[]{:S(2)}) collective-permute-start(bf16[64,768]{1,0:T(8,128)(2,1)S(1)} %broadcast_select_fusion.2), channel_id=1, source_target_pairs={{0,1},{1,0},{2,3},{3,2},{4,5},{5,4},{6,7},{7,6},{8,9},{9,8},{10,11... | collective-permute-start | bytes 294920 | tf_op jit(solution)/shard_map/ppermute | solution.py:41
  29.1 0.8 %collective-permute-done.10 = bf16[64,768]{1,0:T(8,128)(2,1)S(1)} collective-permute-done((bf16[64,768]{1,0:T(8,128)(2,1)S(1)}, bf16[64,768]{1,0:T(8,128)(2,1)S(1)}, u32[]{:S(2)}, u32[]{:S(2)}) %collective-permute-start.10) | collective-permute-done | bytes 98336 | tf_op jit(solution)/shard_map/ppermute | solution.py:41
  29.9 1.6 %collective-permute-start.11 = (bf16[64,768]{1,0:T(8,128)(2,1)S(1)}, bf16[64,768]{1,0:T(8,128)(2,1)S(1)}, u32[]{:S(2)}, u32[]{:S(2)}) collective-permute-start(bf16[64,768]{1,0:T(8,128)(2,1)S(1)} %add_convert_fusion), channel_id=1, source_target_pairs={{0,2},{1,3},{2,0},{3,1},{4,6},{5,7},{6,4},{7,5},{8,10},{9,11},{10,... | collective-permute-start | bytes 294920 | tf_op jit(solution)/shard_map/ppermute | solution.py:41
  31.5 3.5 %collective-permute-done.11 = bf16[64,768]{1,0:T(8,128)(2,1)S(1)} collective-permute-done((bf16[64,768]{1,0:T(8,128)(2,1)S(1)}, bf16[64,768]{1,0:T(8,128)(2,1)S(1)}, u32[]{:S(2)}, u32[]{:S(2)}) %collective-permute-start.11) | collective-permute-done | bytes 98336 | tf_op jit(solution)/shard_map/ppermute | solution.py:41
  35.2 0.6 %gather_fusion = f32[4,32,768]{2,1,0:T(8,128)S(1)} fusion(f32[2,32,768]{2,1,0:T(8,128)S(1)} %convert_add_fusion.2, s32[1024]{0:T(1024)S(1)} %pad_clamp_fusion), kind=kCustom, calls=%fused_computation | custom fusion | bytes 786448 | tf_op jit(solution)/shard_map/jit(_take)/gather | solution.py:190
  35.7 0.8 %collective-permute-done.12 = f32[64,768]{1,0:T(8,128)S(1)} collective-permute-done((f32[64,768]{1,0:T(8,128)S(1)}, f32[64,768]{1,0:T(8,128)S(1)}, u32[]{:S(2)}, u32[]{:S(2)}) %collective-permute-start.12) | collective-permute-done | bytes 196640 | tf_op jit(solution)/shard_map/ppermute | solution.py:41
  36.6 0.2 fusion.153
  36.8 0.2 multiply_reduce_fusion
  37.0 2.7 %convolution_convert_fusion.2 = bf16[128,768]{1,0:T(8,128)(2,1)S(1)} fusion(bf16[768,768]{1,0:T(8,128)(2,1)S(1)} %copy-done, bf16[768,768]{1,0:T(8,128)(2,1)} %param.28, f32[128,768]{1,0:T(8,128)S(1)} %get-tuple-element.20, f32[768]{0:T(1024)S(1)} %copy-done.9, f32[128]{0:T(128)S(1)} %add_rsqrt_fusion.1, f32[128]{0:T(128)S(1)} %broadcast_multiply_fusion.1), kind=kOutput, calls=%fused_computation.6 | convolution fusion | flops 308871168 | bytes 2953216 | tf_op jit(solution)/shard_map/dot_general | solution.py:201
  39.7 0.2 copy.78
  40.3 1.3 %collective-permute-start.15 = (bf16[128,192]{1,0:T(8,128)(2,1)S(1)}, bf16[128,192]{1,0:T(8,128)(2,1)S(1)}, u32[]{:S(2)}, u32[]{:S(2)}) collective-permute-start(bf16[128,192]{1,0:T(8,128)(2,1)S(1)} %select_bitcast_fusion), channel_id=1, source_target_pairs={{0,3},{1,2},{2,1},{3,0},{4,7},{5,6},{6,5},{7,4},{8,11},{9,10},{10,... | collective-permute-start | bytes 147464 | tf_op jit(solution)/shard_map/ppermute | solution.py:41
  41.6 0.4 collective-permute-start.13
  42.1 0.6 %collective-permute-start.14 = (bf16[128,192]{1,0:T(8,128)(2,1)S(1)}, bf16[128,192]{1,0:T(8,128)(2,1)S(1)}, u32[]{:S(2)}, u32[]{:S(2)}) collective-permute-start(bf16[128,192]{1,0:T(8,128)(2,1)S(1)} %select_bitcast_fusion.1), channel_id=1, source_target_pairs={{0,2},{1,3},{2,0},{3,1},{4,6},{5,7},{6,4},{7,5},{8,10},{9,11},{10,... | collective-permute-start | bytes 147464 | tf_op jit(solution)/shard_map/ppermute | solution.py:41
  42.7 0.1 convolution_maximum_fusion
  43.1 1.4 %collective-permute-done.15 = bf16[128,192]{1,0:T(8,128)(2,1)S(1)} collective-permute-done((bf16[128,192]{1,0:T(8,128)(2,1)S(1)}, bf16[128,192]{1,0:T(8,128)(2,1)S(1)}, u32[]{:S(2)}, u32[]{:S(2)}) %collective-permute-start.15) | collective-permute-done | bytes 49184 | tf_op jit(solution)/shard_map/ppermute | solution.py:41
  44.4 1.9 %collective-permute-done.14 = bf16[128,192]{1,0:T(8,128)(2,1)S(1)} collective-permute-done((bf16[128,192]{1,0:T(8,128)(2,1)S(1)}, bf16[128,192]{1,0:T(8,128)(2,1)S(1)}, u32[]{:S(2)}, u32[]{:S(2)}) %collective-permute-start.14) | collective-permute-done | bytes 49184 | tf_op jit(solution)/shard_map/ppermute | solution.py:41
  46.5 0.2 fusion.8
  46.8 0.6 %copy.86 = bf16[2,32,192]{2,1,0:T(8,128)(2,1)} copy(bf16[2,32,192]{2,0,1:T(2,128)(2,1)S(1)} %fusion.8) | data formatting | bytes 49152 | tf_op jit(solution)/shard_map/convert_element_type | solution.py:214
  (98 shorter events, 3.5 us)
Async XLA Ops:
  0.0 37.0 %copy-start = (bf16[768,768]{1,0:T(8,128)(2,1)S(1)}, bf16[768,768]{1,0:T(8,128)(2,1)}, u32[]{:S(2)}) copy-start(bf16[768,768]{1,0:T(8,128)(2,1)} %param.29) | copy-start | bytes 3538948
  0.0 8.7 %collective-permute-start.3 = (bf16[2,32,192]{2,1,0:T(8,128)(2,1)}, bf16[2,32,192]{2,1,0:T(8,128)(2,1)S(1)}, u32[]{:S(2)}, u32[]{:S(2)}) collective-permute-start(bf16[2,32,192]{2,1,0:T(8,128)(2,1)} %bitcast.73), channel_id=1, source_target_pairs={{0,1},{1,0},{2,3},{3,2},{4,5},{5,4},{6,7},{7,6},{8,9},{9,8},{10,11... | collective-permute-start | bytes 73736 | tf_op jit(solution)/shard_map/ppermute | solution.py:41
  2.9 9.2 %collective-permute-start.2 = (f32[12420]{0:T(1024)S(1)}, f32[12420]{0:T(1024)S(1)}, u32[]{:S(2)}, u32[]{:S(2)}) collective-permute-start(f32[12420]{0:T(1024)S(1)} %concatenate.71), channel_id=1, source_target_pairs={{0,12},{4,0},{8,4},{12,8},{1,13},{5,1},{9,5},{13,9},{2,14},{6,2},{... | collective-permute-start | bytes 149048 | tf_op jit(solution)/shard_map/ppermute | solution.py:37
  7.6 6.2 %collective-permute-start.1 = (f32[12420]{0:T(1024)S(1)}, f32[12420]{0:T(1024)S(1)}, u32[]{:S(2)}, u32[]{:S(2)}) collective-permute-start(f32[12420]{0:T(1024)S(1)} %concatenate.71), channel_id=1, source_target_pairs={{0,8},{4,12},{8,0},{12,4},{1,9},{5,13},{9,1},{13,5},{2,10},{6,14},... | collective-permute-start | bytes 149048 | tf_op jit(solution)/shard_map/ppermute | solution.py:37
  7.6 6.2 %collective-permute-start = (f32[12420]{0:T(1024)S(1)}, f32[12420]{0:T(1024)S(1)}, u32[]{:S(2)}, u32[]{:S(2)}) collective-permute-start(f32[12420]{0:T(1024)S(1)} %concatenate.71), channel_id=1, source_target_pairs={{0,4},{4,8},{8,12},{12,0},{1,5},{5,9},{9,13},{13,1},{2,6},{6,10},{... | collective-permute-start | bytes 149048 | tf_op jit(solution)/shard_map/ppermute | solution.py:37
  8.6 7.6 %copy-start.3 = (bf16[3,768,192]{1,2,0:T(8,128)(2,1)S(1)}, bf16[3,768,192]{1,2,0:T(8,128)(2,1)}, u32[]{:S(2)}) copy-start(bf16[3,768,192]{1,2,0:T(8,128)(2,1)} %param.23) | copy-start | bytes 2654212
  8.6 7.6 %copy-start.6 = (f32[768]{0:T(1024)S(1)}, f32[768]{0:T(1024)}, u32[]{:S(2)}) copy-start(f32[768]{0:T(1024)} %param.19) | copy-start | bytes 9220
  10.6 5.3 %collective-permute-start.4 = (bf16[2,32,384]{2,1,0:T(8,128)(2,1)S(1)}, bf16[2,32,384]{2,1,0:T(8,128)(2,1)S(1)}, u32[]{:S(2)}, u32[]{:S(2)}) collective-permute-start(bf16[2,32,384]{2,1,0:T(8,128)(2,1)S(1)} %maximum_select_fusion.7), channel_id=1, source_target_pairs={{0,2},{1,3},{2,0},{3,1},{4,6},{5,7},{6,4},{7,5},{8,10},{9,11},{10,... | collective-permute-start | bytes 147464 | tf_op jit(solution)/shard_map/ppermute | solution.py:41
  15.8 2.7 %collective-permute-start.8 = (bf16[4,32,192]{2,1,0:T(8,128)(2,1)S(1)}, bf16[4,32,192]{2,1,0:T(8,128)(2,1)S(1)}, u32[]{:S(2)}, u32[]{:S(2)}) collective-permute-start(bf16[4,32,192]{2,1,0:T(8,128)(2,1)S(1)} %reshape.472), channel_id=1, source_target_pairs={{0,1},{1,0},{2,3},{3,2},{4,5},{5,4},{6,7},{7,6},{8,9},{9,8},{10,11... | collective-permute-start | bytes 147464 | tf_op jit(solution)/shard_map/ppermute | solution.py:41
  16.2 1.5 %copy-start.2 = (bf16[192,768]{1,0:T(8,128)(2,1)S(1)}, bf16[192,768]{1,0:T(8,128)(2,1)}, u32[]{:S(2)}) copy-start(bf16[192,768]{1,0:T(8,128)(2,1)} %param.24) | copy-start | bytes 884740
  17.3 7.7 %copy-start.4 = (bf16[2,768,192]{1,2,0:T(8,128)(2,1)S(1)}, bf16[2,768,192]{1,2,0:T(8,128)(2,1)}, u32[]{:S(2)}) copy-start(bf16[2,768,192]{1,2,0:T(8,128)(2,1)} %param.26) | copy-start | bytes 1769476
  17.3 7.7 %copy-start.7 = (f32[768]{0:T(1024)S(1)}, f32[768]{0:T(1024)}, u32[]{:S(2)}) copy-start(f32[768]{0:T(1024)} %param.21) | copy-start | bytes 9220
  17.9 2.2 %collective-permute-start.5 = (bf16[32,768]{1,0:T(8,128)(2,1)S(1)}, bf16[32,768]{1,0:T(8,128)(2,1)S(1)}, u32[]{:S(2)}, u32[]{:S(2)}) collective-permute-start(bf16[32,768]{1,0:T(8,128)(2,1)S(1)} %broadcast_select_fusion.5), channel_id=1, source_target_pairs={{0,1},{1,0},{2,3},{3,2},{4,5},{5,4},{6,7},{7,6},{8,9},{9,8},{10,11... | collective-permute-start | bytes 147464 | tf_op jit(solution)/shard_map/ppermute | solution.py:41
  18.6 5.9 %collective-permute-start.9 = (bf16[4,32,384]{2,1,0:T(8,128)(2,1)S(1)}, bf16[4,32,384]{2,1,0:T(8,128)(2,1)S(1)}, u32[]{:S(2)}, u32[]{:S(2)}) collective-permute-start(bf16[4,32,384]{2,1,0:T(8,128)(2,1)S(1)} %maximum_select_fusion.6), channel_id=1, source_target_pairs={{0,2},{1,3},{2,0},{3,1},{4,6},{5,7},{6,4},{7,5},{8,10},{9,11},{10,... | collective-permute-start | bytes 294920 | tf_op jit(solution)/shard_map/ppermute | solution.py:41
  20.2 4.3 %collective-permute-start.6 = (bf16[32,768]{1,0:T(8,128)(2,1)S(1)}, bf16[32,768]{1,0:T(8,128)(2,1)S(1)}, u32[]{:S(2)}, u32[]{:S(2)}) collective-permute-start(bf16[32,768]{1,0:T(8,128)(2,1)S(1)} %add_convert_fusion.1), channel_id=1, source_target_pairs={{0,2},{1,3},{2,0},{3,1},{4,6},{5,7},{6,4},{7,5},{8,10},{9,11},{10,... | collective-permute-start | bytes 147464 | tf_op jit(solution)/shard_map/ppermute | solution.py:41
  24.4 1.4 %collective-permute-start.7 = (f32[32,768]{1,0:T(8,128)S(1)}, f32[32,768]{1,0:T(8,128)S(1)}, u32[]{:S(2)}, u32[]{:S(2)}) collective-permute-start(f32[32,768]{1,0:T(8,128)S(1)} %convert_add_fusion.3), channel_id=1, source_target_pairs={{0,1},{1,0},{2,3},{3,2},{4,5},{5,4},{6,7},{7,6},{8,9},{9,8},{10,11... | collective-permute-start | bytes 294920 | tf_op jit(solution)/shard_map/ppermute | solution.py:41
  25.4 1.0 %copy-start.5 = (bf16[768,192]{0,1:T(8,128)(2,1)S(1)}, bf16[768,192]{0,1:T(8,128)(2,1)}, u32[]{:S(2)}) copy-start(bf16[768,192]{0,1:T(8,128)(2,1)} %param.25) | copy-start | bytes 884740
  25.4 1.0 %copy-start.8 = (f32[768]{0:T(1024)S(1)}, f32[768]{0:T(1024)}, u32[]{:S(2)}) copy-start(f32[768]{0:T(1024)} %param.20) | copy-start | bytes 9220
  27.1 1.0 %copy-start.1 = (bf16[192,768]{1,0:T(8,128)(2,1)S(1)}, bf16[192,768]{1,0:T(8,128)(2,1)}, u32[]{:S(2)}) copy-start(bf16[192,768]{1,0:T(8,128)(2,1)} %param.27) | copy-start | bytes 884740
  28.3 1.5 %collective-permute-start.10 = (bf16[64,768]{1,0:T(8,128)(2,1)S(1)}, bf16[64,768]{1,0:T(8,128)(2,1)S(1)}, u32[]{:S(2)}, u32[]{:S(2)}) collective-permute-start(bf16[64,768]{1,0:T(8,128)(2,1)S(1)} %broadcast_select_fusion.2), channel_id=1, source_target_pairs={{0,1},{1,0},{2,3},{3,2},{4,5},{5,4},{6,7},{7,6},{8,9},{9,8},{10,11... | collective-permute-start | bytes 294920 | tf_op jit(solution)/shard_map/ppermute | solution.py:41
  29.9 5.1 %collective-permute-start.11 = (bf16[64,768]{1,0:T(8,128)(2,1)S(1)}, bf16[64,768]{1,0:T(8,128)(2,1)S(1)}, u32[]{:S(2)}, u32[]{:S(2)}) collective-permute-start(bf16[64,768]{1,0:T(8,128)(2,1)S(1)} %add_convert_fusion), channel_id=1, source_target_pairs={{0,2},{1,3},{2,0},{3,1},{4,6},{5,7},{6,4},{7,5},{8,10},{9,11},{10,... | collective-permute-start | bytes 294920 | tf_op jit(solution)/shard_map/ppermute | solution.py:41
  35.0 1.5 %collective-permute-start.12 = (f32[64,768]{1,0:T(8,128)S(1)}, f32[64,768]{1,0:T(8,128)S(1)}, u32[]{:S(2)}, u32[]{:S(2)}) collective-permute-start(f32[64,768]{1,0:T(8,128)S(1)} %convert_add_fusion.1), channel_id=1, source_target_pairs={{0,1},{1,0},{2,3},{3,2},{4,5},{5,4},{6,7},{7,6},{8,9},{9,8},{10,11... | collective-permute-start | bytes 589832 | tf_op jit(solution)/shard_map/ppermute | solution.py:41
  35.7 1.3 %copy-start.9 = (f32[768]{0:T(1024)S(1)}, f32[768]{0:T(1024)}, u32[]{:S(2)}) copy-start(f32[768]{0:T(1024)} %param.22) | copy-start | bytes 9220
  40.3 4.1 %collective-permute-start.15 = (bf16[128,192]{1,0:T(8,128)(2,1)S(1)}, bf16[128,192]{1,0:T(8,128)(2,1)S(1)}, u32[]{:S(2)}, u32[]{:S(2)}) collective-permute-start(bf16[128,192]{1,0:T(8,128)(2,1)S(1)} %select_bitcast_fusion), channel_id=1, source_target_pairs={{0,3},{1,2},{2,1},{3,0},{4,7},{5,6},{6,5},{7,4},{8,11},{9,10},{10,... | collective-permute-start | bytes 147464 | tf_op jit(solution)/shard_map/ppermute | solution.py:41
  41.6 2.8 %collective-permute-start.13 = (bf16[128,192]{1,0:T(8,128)(2,1)S(1)}, bf16[128,192]{1,0:T(8,128)(2,1)S(1)}, u32[]{:S(2)}, u32[]{:S(2)}) collective-permute-start(bf16[128,192]{1,0:T(8,128)(2,1)S(1)} %select_bitcast_fusion.2), channel_id=1, source_target_pairs={{0,1},{1,0},{2,3},{3,2},{4,5},{5,4},{6,7},{7,6},{8,9},{9,8},{10,11... | collective-permute-start | bytes 147464 | tf_op jit(solution)/shard_map/ppermute | solution.py:41
  42.1 4.3 %collective-permute-start.14 = (bf16[128,192]{1,0:T(8,128)(2,1)S(1)}, bf16[128,192]{1,0:T(8,128)(2,1)S(1)}, u32[]{:S(2)}, u32[]{:S(2)}) collective-permute-start(bf16[128,192]{1,0:T(8,128)(2,1)S(1)} %select_bitcast_fusion.1), channel_id=1, source_target_pairs={{0,2},{1,3},{2,0},{3,1},{4,6},{5,7},{6,4},{7,5},{8,10},{9,11},{10,... | collective-permute-start | bytes 147464 | tf_op jit(solution)/shard_map/ppermute | solution.py:41

commit v6 on v5

--- a/solution.py
+++ b/solution.py
@@ -85,12 +85,12 @@
     core = index % 2
     chip = index // 2
     got = swap(part, mp_pairs(1))
-    pair = jnp.where(
-        core == 0, jnp.concatenate([part, got], axis=2), jnp.concatenate([got, part], axis=2)
+    pair = jnp.concatenate(
+        [jnp.where(core == 0, part, got), jnp.where(core == 0, got, part)], axis=2
     )
     other = swap(pair, mp_pairs(2))
-    return jnp.where(
-        chip == 0, jnp.concatenate([pair, other], axis=2), jnp.concatenate([other, pair], axis=2)
+    return jnp.concatenate(
+        [jnp.where(chip == 0, pair, other), jnp.where(chip == 0, other, pair)], axis=2
     )
 
 
@@ -134,19 +134,20 @@
     owners_n = lax.axis_size("pairs")
     own = lax.axis_index("pairs")
 
-    payload = jnp.concatenate(
+    extra_n = -(-(pair_dev + 1) // 8) * 8
+    extra = jnp.concatenate(
         [
-            tokens.astype(jnp.float32).reshape(-1),
-            pair_list.astype(jnp.float32).reshape(-1),
-            confidence.reshape(-1),
+            jnp.pad(confidence, ((0, 0), (0, quarter - confidence.shape[1]))),
+            jnp.pad(pair_list.reshape(1, views_n).astype(jnp.float32), ((0, 0), (0, quarter - views_n))),
+            jnp.zeros((extra_n - pair_dev - 1, quarter), jnp.float32),
         ]
     )
+    payload = jnp.concatenate([tokens.astype(jnp.float32), extra])
     table = pairs_gather(payload, owners_n)
-    cut_tok = img_dev * TOKS * quarter
-    cut_ids = cut_tok + views_n
-    all_tok = table[:, :cut_tok].astype(jnp.bfloat16).reshape(owners_n * img_dev, TOKS * quarter)
-    all_ids = table[:, cut_tok:cut_ids].astype(jnp.int32)
-    all_conf = table[:, cut_ids:].reshape(owners_n * views_n, TOKS)
+    tok_rows = img_dev * TOKS
+    all_tok = table[:, :tok_rows].astype(jnp.bfloat16).reshape(owners_n * img_dev, TOKS * quarter)
+    all_conf = table[:, tok_rows : tok_rows + pair_dev, : 2 * TOKS].reshape(owners_n * views_n, TOKS)
+    all_ids = table[:, tok_rows + pair_dev, :views_n].astype(jnp.int32)
     partner_ids = all_ids.reshape(owners_n, pair_dev, 2)[:, :, ::-1].reshape(-1)
     all_ids = all_ids.reshape(-1)
 

time: 47.7 us -> 49.3 us (1.034)
  waiting for transfers between devices: 13.5 us -> 15.4 us
  local copies, waits for them, and re-layouts: 6.65 us -> 4.93 us
  other arithmetic: 5.23 us -> 6.45 us
    ppermute x13, waiting for transfers between devices: 11.9 us -> 15.4 us  [swap(): return lax.ppermute(values, 'mp', pairs)]
    ppermute x3, starting transfers between devices: 5.71 us -> 7.89 us  [pairs_shift(): lax.ppermute(values, 'pairs', [(i, (i + step) % owners_n) for i in range(...]
    ppermute x13, starting transfers between devices: 9.55 us -> 7.61 us  [swap(): return lax.ppermute(values, 'mp', pairs)]
    reshape x7 -> x2, local copies, waits for them, and re-layouts: 1.96 us -> 0.24 us  [the longest x1 0.16 us: per_device(): table[:, :tok_rows].astype(jnp.bfloat16)]
    ppermute x3, waiting for transfers between devices: 1.6 us -> 0.01 us  [pairs_shift(): lax.ppermute(values, 'pairs', [(i, (i + step) % owners_n) for i in range(...]
    select_n x4, other arithmetic: 2.08 us -> 0.98 us  [the longest x2 0.78 us: mp_gather_cols(): jnp.where(core == 0, part, got)]
    concatenate x0 -> x3, other arithmetic: none -> 0.93 us  [the longest x1 0.76 us: per_device(): payload = jnp.concatenate([tokens.astype(jnp.float32), extra])]
    convert_element_type x2 -> x4, other arithmetic: 0.69 us -> 1.57 us  [the longest x1 0.78 us: per_device(): pair_list.reshape(1, views_n).astype(jnp.float32)]
  transfers between devices with their start and end apart: 16 -> 16, of which waited for: 7 -> 10; matrix products, arithmetic and copies ran while one was open for 23% -> 16% of each run, Pallas kernels for 0% -> 0%
where the time goes in v6:
time: 49.3 us; the launch traced here: 49 us
  starting transfers between devices  15.5 us (31%)
  waiting for transfers between devices  15.4 us (31%)
  other arithmetic  6.45 us (13%)
  matrix products  6.15 us (12%)
  local copies, waits for them, and re-layouts  4.93 us (10%)
  between operations  0.6 us (1%)
    ppermute x13, waiting for transfers between devices, swap(): return lax.ppermute(values, 'mp', pairs)  15.4 us
    ppermute x3, starting transfers between devices, pairs_shift(): lax.ppermute(values, 'pairs', [(i, (i + step) % owners_n) for i in range(...  7.89 us
    ppermute x13, starting transfers between devices, swap(): return lax.ppermute(values, 'mp', pairs)  7.61 us
    dot_general x1, matrix products, per_device(): jnp.dot(hidden.astype(jnp.bfloat16), mlp_down, preferred_element_type=jnp...  2.72 us
  transfers between devices with their start and end apart: 16, of which 10 were waited for; matrix products, arithmetic and copies ran while one was open for 16% of the time, Pallas kernels for 0%

profile of v6, /device:TPU:0, one launch (start us, length us, event | category | flops | bytes accessed | tf_op | source)
XLA Modules:
  0.0 49.0 jit_solution(12244030096309216685)
XLA Ops:
  0.0 0.8 %convert_element_type.205 = f32[2,2]{1,0:T(2,128)S(1)} convert(s32[2,2]{1,0:T(2,128)} %param.17) | non-fusion elementwise | flops 4 | bytes 32 | tf_op jit(solution)/shard_map/convert_element_type | solution.py:141
  0.9 0.8 %convert_element_type.204 = f32[64,192]{1,0:T(8,128)S(1)} convert(bf16[64,192]{1,0:T(8,128)(2,1)} %param.16) | non-fusion elementwise | flops 12288 | bytes 73728 | tf_op jit(solution)/shard_map/convert_element_type | solution.py:145
  1.7 0.8 %fusion.86 = f32[72,192]{1,0:T(8,128)S(1)} fusion(f32[1,4]{1,0:T(1,128)S(1)} %convert_element_type.206, f32[2,64]{1,0:T(2,128)} %param.18, f32[64,192]{1,0:T(8,128)S(1)} %convert_element_type.204, f32[72]{0:T(128)S(1)} %pad.35.clone), kind=kLoop, calls=%fused_computation.142 | loop fusion | flops 152064 | bytes 105264 | tf_op jit(solution)/shard_map/concatenate | solution.py:145
  2.5 4.1 %collective-permute-start.1 = (f32[72,192]{1,0:T(8,128)S(1)}, f32[72,192]{1,0:T(8,128)S(1)}, u32[]{:S(2)}, u32[]{:S(2)}) collective-permute-start(f32[72,192]{1,0:T(8,128)S(1)} %fusion.86), channel_id=1, source_target_pairs={{0,8},{4,12},{8,0},{12,4},{1,9},{5,13},{9,1},{13,5},{2,10},{6,14},... | collective-permute-start | bytes 165896 | tf_op jit(solution)/shard_map/ppermute | solution.py:37
  6.5 1.6 %collective-permute-start = (f32[72,192]{1,0:T(8,128)S(1)}, f32[72,192]{1,0:T(8,128)S(1)}, u32[]{:S(2)}, u32[]{:S(2)}) collective-permute-start(f32[72,192]{1,0:T(8,128)S(1)} %fusion.86), channel_id=1, source_target_pairs={{0,4},{4,8},{8,12},{12,0},{1,5},{5,9},{9,13},{13,1},{2,6},{6,10},{... | collective-permute-start | bytes 165896 | tf_op jit(solution)/shard_map/ppermute | solution.py:37
  8.1 2.2 %collective-permute-start.2 = (f32[72,192]{1,0:T(8,128)S(1)}, f32[72,192]{1,0:T(8,128)S(1)}, u32[]{:S(2)}, u32[]{:S(2)}) collective-permute-start(f32[72,192]{1,0:T(8,128)S(1)} %fusion.86), channel_id=1, source_target_pairs={{0,12},{4,0},{8,4},{12,8},{1,13},{5,1},{9,5},{13,9},{2,14},{6,2},{... | collective-permute-start | bytes 165896 | tf_op jit(solution)/shard_map/ppermute | solution.py:37
  10.4 0.8 %fusion.178 = f32[1,72,192]{2,1,0:T(8,128)S(1)} fusion(f32[72]{0:T(128)S(1)} %pad.35.clone, f32[1,4]{1,0:T(1,128)S(1)} %convert_element_type.206, f32[2,64]{1,0:T(2,128)} %param.18, f32[64,192]{1,0:T(8,128)S(1)} %convert_element_type.204), kind=kLoop, calls=%fused_computation.271 | loop fusion | flops 152064 | bytes 105264 | tf_op jit(solution)/shard_map/stack | solution.py:99
  11.1 0.6 %collective-permute-done.3 = bf16[2,32,192]{2,1,0:T(8,128)(2,1)S(1)} collective-permute-done((bf16[2,32,192]{2,1,0:T(8,128)(2,1)}, bf16[2,32,192]{2,1,0:T(8,128)(2,1)S(1)}, u32[]{:S(2)}, u32[]{:S(2)}) %collective-permute-start.3) | collective-permute-done | bytes 24608 | tf_op jit(solution)/shard_map/ppermute | solution.py:41
  11.8 0.8 %broadcast_select_fusion.13 = (bf16[2,32,192]{2,1,0:T(8,128)(2,1)S(1)}, bf16[2,32,192]{2,1,0:T(8,128)(2,1)S(1)}) fusion(bf16[2,32,192]{2,1,0:T(8,128)(2,1)} %bitcast.94, bf16[2,32,192]{2,1,0:T(8,128)(2,1)S(1)} %collective-permute-done.3, pred[]{:T(512)S(6)} %eq.111), kind=kLoop, calls=%fused_computation.163 | loop fusion | flops 24576 | bytes 98305 | tf_op jit(solution)/shard_map/jit(_where)/select_n | solution.py:89
  12.6 1.6 %collective-permute-start.4 = (bf16[2,32,384]{2,1,0:T(8,128)(2,1)S(1)}, bf16[2,32,384]{2,1,0:T(8,128)(2,1)S(1)}, u32[]{:S(2)}, u32[]{:S(2)}) collective-permute-start(bf16[2,32,384]{2,1,0:T(8,128)(2,1)S(1)} %pad_maximum_fusion.5), channel_id=1, source_target_pairs={{0,2},{1,3},{2,0},{3,1},{4,6},{5,7},{6,4},{7,5},{8,10},{9,11},{10,... | collective-permute-start | bytes 147464 | tf_op jit(solution)/shard_map/ppermute | solution.py:41
  14.6 0.2 reshape.418
  15.1 0.1 add_reduce_fusion
  15.2 0.1 fusion.152
  15.3 0.2 select_reduce_fusion.1
  15.5 0.2 convolution_convert_fusion.1
  15.8 0.1 reshape.419
  16.0 0.8 %collective-permute-done.4 = bf16[2,32,384]{2,1,0:T(8,128)(2,1)S(1)} collective-permute-done((bf16[2,32,384]{2,1,0:T(8,128)(2,1)S(1)}, bf16[2,32,384]{2,1,0:T(8,128)(2,1)S(1)}, u32[]{:S(2)}, u32[]{:S(2)}) %collective-permute-start.4) | collective-permute-done | bytes 49184 | tf_op jit(solution)/shard_map/ppermute | solution.py:41
  16.9 0.1 convert_reduce_fusion.1
  17.0 0.2 fusion.25
  17.3 0.4 fusion.6
  17.9 0.2 fusion.157
  18.1 0.1 convolution_multiply_fusion.1
  18.3 0.2 fusion.9
  18.7 0.2 convolution_convert_fusion.6
  19.0 1.2 %collective-permute-done.5 = bf16[32,768]{1,0:T(8,128)(2,1)S(1)} collective-permute-done((bf16[32,768]{1,0:T(8,128)(2,1)S(1)}, bf16[32,768]{1,0:T(8,128)(2,1)S(1)}, u32[]{:S(2)}, u32[]{:S(2)}) %collective-permute-start.5) | collective-permute-done | bytes 49184 | tf_op jit(solution)/shard_map/ppermute | solution.py:41
  20.2 1.6 %collective-permute-start.6 = (bf16[32,768]{1,0:T(8,128)(2,1)S(1)}, bf16[32,768]{1,0:T(8,128)(2,1)S(1)}, u32[]{:S(2)}, u32[]{:S(2)}) collective-permute-start(bf16[32,768]{1,0:T(8,128)(2,1)S(1)} %add_convert_fusion.1), channel_id=1, source_target_pairs={{0,2},{1,3},{2,0},{3,1},{4,6},{5,7},{6,4},{7,5},{8,10},{9,11},{10,... | collective-permute-start | bytes 147464 | tf_op jit(solution)/shard_map/ppermute | solution.py:41
  21.9 0.6 %collective-permute-start.9 = (bf16[4,32,384]{2,1,0:T(8,128)(2,1)S(1)}, bf16[4,32,384]{2,1,0:T(8,128)(2,1)S(1)}, u32[]{:S(2)}, u32[]{:S(2)}) collective-permute-start(bf16[4,32,384]{2,1,0:T(8,128)(2,1)S(1)} %pad_maximum_fusion.4), channel_id=1, source_target_pairs={{0,2},{1,3},{2,0},{3,1},{4,6},{5,7},{6,4},{7,5},{8,10},{9,11},{10,... | collective-permute-start | bytes 294920 | tf_op jit(solution)/shard_map/ppermute | solution.py:41
  22.5 1.9 %collective-permute-done.6 = bf16[32,768]{1,0:T(8,128)(2,1)S(1)} collective-permute-done((bf16[32,768]{1,0:T(8,128)(2,1)S(1)}, bf16[32,768]{1,0:T(8,128)(2,1)S(1)}, u32[]{:S(2)}, u32[]{:S(2)}) %collective-permute-start.6) | collective-permute-done | bytes 49184 | tf_op jit(solution)/shard_map/ppermute | solution.py:41
  24.5 2.1 %collective-permute-done.9 = bf16[4,32,384]{2,1,0:T(8,128)(2,1)S(1)} collective-permute-done((bf16[4,32,384]{2,1,0:T(8,128)(2,1)S(1)}, bf16[4,32,384]{2,1,0:T(8,128)(2,1)S(1)}, u32[]{:S(2)}, u32[]{:S(2)}) %collective-permute-start.9) | collective-permute-done | bytes 98336 | tf_op jit(solution)/shard_map/ppermute | solution.py:41
  26.7 0.1 convert_reduce_fusion
  26.9 0.2 fusion.11
  27.2 0.4 fusion.28
  27.7 0.1 reshape.533
  27.8 0.1 reshape.532
  28.0 0.1 pad_maximum_fusion.1
  28.1 0.2 multiply_reduce_fusion.1
  28.3 0.3 copy-done.6
  28.6 0.2 convolution_convert_fusion.8
  28.8 0.1 reshape_reshape.3
  29.0 0.2 convolution_convert_fusion
  29.2 0.1 reshape_reshape_reshape.3
  29.3 0.2 convolution_multiply_fusion
  29.7 0.3 fusion.5
  30.0 0.1 reshape.420
  30.2 0.1 copy-done.2
  30.3 0.2 convolution_convert_fusion.3
  30.8 1.1 %collective-permute-done.10 = bf16[64,768]{1,0:T(8,128)(2,1)S(1)} collective-permute-done((bf16[64,768]{1,0:T(8,128)(2,1)S(1)}, bf16[64,768]{1,0:T(8,128)(2,1)S(1)}, u32[]{:S(2)}, u32[]{:S(2)}) %collective-permute-start.10) | collective-permute-done | bytes 98336 | tf_op jit(solution)/shard_map/ppermute | solution.py:41
  31.9 1.2 %collective-permute-start.11 = (bf16[64,768]{1,0:T(8,128)(2,1)S(1)}, bf16[64,768]{1,0:T(8,128)(2,1)S(1)}, u32[]{:S(2)}, u32[]{:S(2)}) collective-permute-start(bf16[64,768]{1,0:T(8,128)(2,1)S(1)} %add_convert_fusion), channel_id=1, source_target_pairs={{0,2},{1,3},{2,0},{3,1},{4,6},{5,7},{6,4},{7,5},{8,10},{9,11},{10,... | collective-permute-start | bytes 294920 | tf_op jit(solution)/shard_map/ppermute | solution.py:41
  33.2 3.7 %collective-permute-done.11 = bf16[64,768]{1,0:T(8,128)(2,1)S(1)} collective-permute-done((bf16[64,768]{1,0:T(8,128)(2,1)S(1)}, bf16[64,768]{1,0:T(8,128)(2,1)S(1)}, u32[]{:S(2)}, u32[]{:S(2)}) %collective-permute-start.11) | collective-permute-done | bytes 98336 | tf_op jit(solution)/shard_map/ppermute | solution.py:41
  37.0 0.6 %gather_fusion = f32[4,32,768]{2,1,0:T(8,128)S(1)} fusion(f32[2,32,768]{2,1,0:T(8,128)S(1)} %convert_add_fusion.2, s32[1024]{0:T(1024)S(1)} %pad_clamp_fusion), kind=kCustom, calls=%fused_computation | custom fusion | bytes 786448 | tf_op jit(solution)/shard_map/jit(_take)/gather | solution.py:191
  37.6 0.8 %collective-permute-done.12 = f32[64,768]{1,0:T(8,128)S(1)} collective-permute-done((f32[64,768]{1,0:T(8,128)S(1)}, f32[64,768]{1,0:T(8,128)S(1)}, u32[]{:S(2)}, u32[]{:S(2)}) %collective-permute-start.12) | collective-permute-done | bytes 196640 | tf_op jit(solution)/shard_map/ppermute | solution.py:41
  38.4 0.2 fusion.154
  38.6 0.2 multiply_reduce_fusion
  38.9 2.7 %convolution_convert_fusion.2 = bf16[128,768]{1,0:T(8,128)(2,1)S(1)} fusion(bf16[768,768]{1,0:T(8,128)(2,1)S(1)} %copy-done, bf16[768,768]{1,0:T(8,128)(2,1)} %param.28, f32[128,768]{1,0:T(8,128)S(1)} %get-tuple-element.20, f32[768]{0:T(1024)S(1)} %copy-done.9, f32[128]{0:T(128)S(1)} %add_rsqrt_fusion.1, f32[128]{0:T(128)S(1)} %broadcast_multiply_fusion.1), kind=kOutput, calls=%fused_computation.6 | convolution fusion | flops 308871168 | bytes 2953216 | tf_op jit(solution)/shard_map/dot_general | solution.py:202
  41.6 0.2 copy.77
  42.2 0.9 %collective-permute-start.15 = (bf16[128,192]{1,0:T(8,128)(2,1)S(1)}, bf16[128,192]{1,0:T(8,128)(2,1)S(1)}, u32[]{:S(2)}, u32[]{:S(2)}) collective-permute-start(bf16[128,192]{1,0:T(8,128)(2,1)S(1)} %select_bitcast_fusion), channel_id=1, source_target_pairs={{0,3},{1,2},{2,1},{3,0},{4,7},{5,6},{6,5},{7,4},{8,11},{9,10},{10,... | collective-permute-start | bytes 147464 | tf_op jit(solution)/shard_map/ppermute | solution.py:41
  43.1 0.4 collective-permute-start.13
  43.6 1.0 %collective-permute-start.14 = (bf16[128,192]{1,0:T(8,128)(2,1)S(1)}, bf16[128,192]{1,0:T(8,128)(2,1)S(1)}, u32[]{:S(2)}, u32[]{:S(2)}) collective-permute-start(bf16[128,192]{1,0:T(8,128)(2,1)S(1)} %select_bitcast_fusion.1), channel_id=1, source_target_pairs={{0,2},{1,3},{2,0},{3,1},{4,6},{5,7},{6,4},{7,5},{8,10},{9,11},{10,... | collective-permute-start | bytes 147464 | tf_op jit(solution)/shard_map/ppermute | solution.py:41
  44.5 0.1 convolution_maximum_fusion
  44.9 1.4 %collective-permute-done.15 = bf16[128,192]{1,0:T(8,128)(2,1)S(1)} collective-permute-done((bf16[128,192]{1,0:T(8,128)(2,1)S(1)}, bf16[128,192]{1,0:T(8,128)(2,1)S(1)}, u32[]{:S(2)}, u32[]{:S(2)}) %collective-permute-start.15) | collective-permute-done | bytes 49184 | tf_op jit(solution)/shard_map/ppermute | solution.py:41
  46.3 1.7 %collective-permute-done.14 = bf16[128,192]{1,0:T(8,128)(2,1)S(1)} collective-permute-done((bf16[128,192]{1,0:T(8,128)(2,1)S(1)}, bf16[128,192]{1,0:T(8,128)(2,1)S(1)}, u32[]{:S(2)}, u32[]{:S(2)}) %collective-permute-start.14) | collective-permute-done | bytes 49184 | tf_op jit(solution)/shard_map/ppermute | solution.py:41
  48.0 0.1 add_add_fusion
  48.1 0.2 fusion.8
  48.4 0.6 %copy.85 = bf16[2,32,192]{2,1,0:T(8,128)(2,1)} copy(bf16[2,32,192]{2,0,1:T(2,128)(2,1)S(1)} %fusion.8) | data formatting | bytes 49152 | tf_op jit(solution)/shard_map/convert_element_type | solution.py:215
  (98 shorter events, 3.6 us)
Async XLA Ops:
  0.0 38.8 %copy-start = (bf16[768,768]{1,0:T(8,128)(2,1)S(1)}, bf16[768,768]{1,0:T(8,128)(2,1)}, u32[]{:S(2)}) copy-start(bf16[768,768]{1,0:T(8,128)(2,1)} %param.29) | copy-start | bytes 3538948
  2.5 11.7 %collective-permute-start.1 = (f32[72,192]{1,0:T(8,128)S(1)}, f32[72,192]{1,0:T(8,128)S(1)}, u32[]{:S(2)}, u32[]{:S(2)}) collective-permute-start(f32[72,192]{1,0:T(8,128)S(1)} %fusion.86), channel_id=1, source_target_pairs={{0,8},{4,12},{8,0},{12,4},{1,9},{5,13},{9,1},{13,5},{2,10},{6,14},... | collective-permute-start | bytes 165896 | tf_op jit(solution)/shard_map/ppermute | solution.py:37
  6.5 7.7 %collective-permute-start = (f32[72,192]{1,0:T(8,128)S(1)}, f32[72,192]{1,0:T(8,128)S(1)}, u32[]{:S(2)}, u32[]{:S(2)}) collective-permute-start(f32[72,192]{1,0:T(8,128)S(1)} %fusion.86), channel_id=1, source_target_pairs={{0,4},{4,8},{8,12},{12,0},{1,5},{5,9},{9,13},{13,1},{2,6},{6,10},{... | collective-permute-start | bytes 165896 | tf_op jit(solution)/shard_map/ppermute | solution.py:37
  8.1 6.1 %collective-permute-start.2 = (f32[72,192]{1,0:T(8,128)S(1)}, f32[72,192]{1,0:T(8,128)S(1)}, u32[]{:S(2)}, u32[]{:S(2)}) collective-permute-start(f32[72,192]{1,0:T(8,128)S(1)} %fusion.86), channel_id=1, source_target_pairs={{0,12},{4,0},{8,4},{12,8},{1,13},{5,1},{9,5},{13,9},{2,14},{6,2},{... | collective-permute-start | bytes 165896 | tf_op jit(solution)/shard_map/ppermute | solution.py:37
  10.4 1.4 %collective-permute-start.3 = (bf16[2,32,192]{2,1,0:T(8,128)(2,1)}, bf16[2,32,192]{2,1,0:T(8,128)(2,1)S(1)}, u32[]{:S(2)}, u32[]{:S(2)}) collective-permute-start(bf16[2,32,192]{2,1,0:T(8,128)(2,1)} %bitcast.93), channel_id=1, source_target_pairs={{0,1},{1,0},{2,3},{3,2},{4,5},{5,4},{6,7},{7,6},{8,9},{9,8},{10,11... | collective-permute-start | bytes 73736 | tf_op jit(solution)/shard_map/ppermute | solution.py:41
  12.5 4.7 %copy-start.1 = (bf16[3,768,192]{1,2,0:T(8,128)(2,1)S(1)}, bf16[3,768,192]{1,2,0:T(8,128)(2,1)}, u32[]{:S(2)}) copy-start(bf16[3,768,192]{1,2,0:T(8,128)(2,1)} %param.23) | copy-start | bytes 2654212
  12.5 4.7 %copy-start.4 = (f32[768]{0:T(1024)S(1)}, f32[768]{0:T(1024)}, u32[]{:S(2)}) copy-start(f32[768]{0:T(1024)} %param.19) | copy-start | bytes 9220
  12.6 4.2 %collective-permute-start.4 = (bf16[2,32,384]{2,1,0:T(8,128)(2,1)S(1)}, bf16[2,32,384]{2,1,0:T(8,128)(2,1)S(1)}, u32[]{:S(2)}, u32[]{:S(2)}) collective-permute-start(bf16[2,32,384]{2,1,0:T(8,128)(2,1)S(1)} %pad_maximum_fusion.5), channel_id=1, source_target_pairs={{0,2},{1,3},{2,0},{3,1},{4,6},{5,7},{6,4},{7,5},{8,10},{9,11},{10,... | collective-permute-start | bytes 147464 | tf_op jit(solution)/shard_map/ppermute | solution.py:41
  15.9 3.1 %collective-permute-start.8 = (bf16[4,32,192]{2,1,0:T(8,128)(2,1)S(1)}, bf16[4,32,192]{2,1,0:T(8,128)(2,1)S(1)}, u32[]{:S(2)}, u32[]{:S(2)}) collective-permute-start(bf16[4,32,192]{2,1,0:T(8,128)(2,1)S(1)} %reshape.419), channel_id=1, source_target_pairs={{0,1},{1,0},{2,3},{3,2},{4,5},{5,4},{6,7},{7,6},{8,9},{9,8},{10,11... | collective-permute-start | bytes 147464 | tf_op jit(solution)/shard_map/ppermute | solution.py:41
  17.2 1.5 %copy-start.3 = (bf16[192,768]{1,0:T(8,128)(2,1)S(1)}, bf16[192,768]{1,0:T(8,128)(2,1)}, u32[]{:S(2)}) copy-start(bf16[192,768]{1,0:T(8,128)(2,1)} %param.24) | copy-start | bytes 884740
  18.7 8.5 %copy-start.5 = (bf16[2,768,192]{1,2,0:T(8,128)(2,1)S(1)}, bf16[2,768,192]{1,2,0:T(8,128)(2,1)}, u32[]{:S(2)}) copy-start(bf16[2,768,192]{1,2,0:T(8,128)(2,1)} %param.26) | copy-start | bytes 1769476
  18.7 8.5 %copy-start.7 = (f32[768]{0:T(1024)S(1)}, f32[768]{0:T(1024)}, u32[]{:S(2)}) copy-start(f32[768]{0:T(1024)} %param.21) | copy-start | bytes 9220
  18.9 1.3 %collective-permute-start.5 = (bf16[32,768]{1,0:T(8,128)(2,1)S(1)}, bf16[32,768]{1,0:T(8,128)(2,1)S(1)}, u32[]{:S(2)}, u32[]{:S(2)}) collective-permute-start(bf16[32,768]{1,0:T(8,128)(2,1)S(1)} %broadcast_select_fusion.9), channel_id=1, source_target_pairs={{0,1},{1,0},{2,3},{3,2},{4,5},{5,4},{6,7},{7,6},{8,9},{9,8},{10,11... | collective-permute-start | bytes 147464 | tf_op jit(solution)/shard_map/ppermute | solution.py:41
  20.2 4.2 %collective-permute-start.6 = (bf16[32,768]{1,0:T(8,128)(2,1)S(1)}, bf16[32,768]{1,0:T(8,128)(2,1)S(1)}, u32[]{:S(2)}, u32[]{:S(2)}) collective-permute-start(bf16[32,768]{1,0:T(8,128)(2,1)S(1)} %add_convert_fusion.1), channel_id=1, source_target_pairs={{0,2},{1,3},{2,0},{3,1},{4,6},{5,7},{6,4},{7,5},{8,10},{9,11},{10,... | collective-permute-start | bytes 147464 | tf_op jit(solution)/shard_map/ppermute | solution.py:41
  21.9 4.7 %collective-permute-start.9 = (bf16[4,32,384]{2,1,0:T(8,128)(2,1)S(1)}, bf16[4,32,384]{2,1,0:T(8,128)(2,1)S(1)}, u32[]{:S(2)}, u32[]{:S(2)}) collective-permute-start(bf16[4,32,384]{2,1,0:T(8,128)(2,1)S(1)} %pad_maximum_fusion.4), channel_id=1, source_target_pairs={{0,2},{1,3},{2,0},{3,1},{4,6},{5,7},{6,4},{7,5},{8,10},{9,11},{10,... | collective-permute-start | bytes 294920 | tf_op jit(solution)/shard_map/ppermute | solution.py:41
  24.4 3.5 %collective-permute-start.7 = (f32[32,768]{1,0:T(8,128)S(1)}, f32[32,768]{1,0:T(8,128)S(1)}, u32[]{:S(2)}, u32[]{:S(2)}) collective-permute-start(f32[32,768]{1,0:T(8,128)S(1)} %convert_add_fusion.3), channel_id=1, source_target_pairs={{0,1},{1,0},{2,3},{3,2},{4,5},{5,4},{6,7},{7,6},{8,9},{9,8},{10,11... | collective-permute-start | bytes 294920 | tf_op jit(solution)/shard_map/ppermute | solution.py:41
  27.6 1.0 %copy-start.6 = (bf16[768,192]{0,1:T(8,128)(2,1)S(1)}, bf16[768,192]{0,1:T(8,128)(2,1)}, u32[]{:S(2)}) copy-start(bf16[768,192]{0,1:T(8,128)(2,1)} %param.25) | copy-start | bytes 884740
  27.6 1.0 %copy-start.8 = (f32[768]{0:T(1024)S(1)}, f32[768]{0:T(1024)}, u32[]{:S(2)}) copy-start(f32[768]{0:T(1024)} %param.20) | copy-start | bytes 9220
  29.3 1.0 %copy-start.2 = (bf16[192,768]{1,0:T(8,128)(2,1)S(1)}, bf16[192,768]{1,0:T(8,128)(2,1)}, u32[]{:S(2)}) copy-start(bf16[192,768]{1,0:T(8,128)(2,1)} %param.27) | copy-start | bytes 884740
  30.5 1.4 %collective-permute-start.10 = (bf16[64,768]{1,0:T(8,128)(2,1)S(1)}, bf16[64,768]{1,0:T(8,128)(2,1)S(1)}, u32[]{:S(2)}, u32[]{:S(2)}) collective-permute-start(bf16[64,768]{1,0:T(8,128)(2,1)S(1)} %broadcast_select_fusion.4), channel_id=1, source_target_pairs={{0,1},{1,0},{2,3},{3,2},{4,5},{5,4},{6,7},{7,6},{8,9},{9,8},{10,11... | collective-permute-start | bytes 294920 | tf_op jit(solution)/shard_map/ppermute | solution.py:41
  31.9 4.9 %collective-permute-start.11 = (bf16[64,768]{1,0:T(8,128)(2,1)S(1)}, bf16[64,768]{1,0:T(8,128)(2,1)S(1)}, u32[]{:S(2)}, u32[]{:S(2)}) collective-permute-start(bf16[64,768]{1,0:T(8,128)(2,1)S(1)} %add_convert_fusion), channel_id=1, source_target_pairs={{0,2},{1,3},{2,0},{3,1},{4,6},{5,7},{6,4},{7,5},{8,10},{9,11},{10,... | collective-permute-start | bytes 294920 | tf_op jit(solution)/shard_map/ppermute | solution.py:41
  36.9 1.5 %collective-permute-start.12 = (f32[64,768]{1,0:T(8,128)S(1)}, f32[64,768]{1,0:T(8,128)S(1)}, u32[]{:S(2)}, u32[]{:S(2)}) collective-permute-start(f32[64,768]{1,0:T(8,128)S(1)} %convert_add_fusion.1), channel_id=1, source_target_pairs={{0,1},{1,0},{2,3},{3,2},{4,5},{5,4},{6,7},{7,6},{8,9},{9,8},{10,11... | collective-permute-start | bytes 589832 | tf_op jit(solution)/shard_map/ppermute | solution.py:41
  37.6 1.3 %copy-start.9 = (f32[768]{0:T(1024)S(1)}, f32[768]{0:T(1024)}, u32[]{:S(2)}) copy-start(f32[768]{0:T(1024)} %param.22) | copy-start | bytes 9220
  42.2 4.1 %collective-permute-start.15 = (bf16[128,192]{1,0:T(8,128)(2,1)S(1)}, bf16[128,192]{1,0:T(8,128)(2,1)S(1)}, u32[]{:S(2)}, u32[]{:S(2)}) collective-permute-start(bf16[128,192]{1,0:T(8,128)(2,1)S(1)} %select_bitcast_fusion), channel_id=1, source_target_pairs={{0,3},{1,2},{2,1},{3,0},{4,7},{5,6},{6,5},{7,4},{8,11},{9,10},{10,... | collective-permute-start | bytes 147464 | tf_op jit(solution)/shard_map/ppermute | solution.py:41
  43.1 3.2 %collective-permute-start.13 = (bf16[128,192]{1,0:T(8,128)(2,1)S(1)}, bf16[128,192]{1,0:T(8,128)(2,1)S(1)}, u32[]{:S(2)}, u32[]{:S(2)}) collective-permute-start(bf16[128,192]{1,0:T(8,128)(2,1)S(1)} %select_bitcast_fusion.2), channel_id=1, source_target_pairs={{0,1},{1,0},{2,3},{3,2},{4,5},{5,4},{6,7},{7,6},{8,9},{9,8},{10,11... | collective-permute-start | bytes 147464 | tf_op jit(solution)/shard_map/ppermute | solution.py:41
  43.6 4.5 %collective-permute-start.14 = (bf16[128,192]{1,0:T(8,128)(2,1)S(1)}, bf16[128,192]{1,0:T(8,128)(2,1)S(1)}, u32[]{:S(2)}, u32[]{:S(2)}) collective-permute-start(bf16[128,192]{1,0:T(8,128)(2,1)S(1)} %select_bitcast_fusion.1), channel_id=1, source_target_pairs={{0,2},{1,3},{2,0},{3,1},{4,6},{5,7},{6,4},{7,5},{8,10},{9,11},{10,... | collective-permute-start | bytes 147464 | tf_op jit(solution)/shard_map/ppermute | solution.py:41

commit v7 on v5

--- a/solution.py
+++ b/solution.py
@@ -134,19 +134,33 @@
     owners_n = lax.axis_size("pairs")
     own = lax.axis_index("pairs")
 
-    payload = jnp.concatenate(
+    own_tok = mp_gather_cols(tokens.reshape(img_dev, TOKS, quarter))
+    width = own_tok.shape[2]
+    img_rows = img_dev * TOKS
+
+    high = confidence.astype(jnp.bfloat16)
+    rest = confidence - high.astype(jnp.float32)
+    mid = rest.astype(jnp.bfloat16)
+    low = (rest - mid.astype(jnp.float32)).astype(jnp.bfloat16)
+    extra_n = -(-(3 * pair_dev + 1) // 8) * 8
+    conf_w = confidence.shape[1]
+    extra = jnp.concatenate(
         [
-            tokens.astype(jnp.float32).reshape(-1),
-            pair_list.astype(jnp.float32).reshape(-1),
-            confidence.reshape(-1),
+            jnp.concatenate([high, mid, low], axis=0),
+            pair_list.reshape(1, views_n).astype(jnp.bfloat16)
+            if views_n == conf_w
+            else jnp.pad(pair_list.reshape(1, views_n).astype(jnp.bfloat16), ((0, 0), (0, conf_w - views_n))),
+            jnp.zeros((extra_n - 3 * pair_dev - 1, conf_w), jnp.bfloat16),
         ]
     )
+    extra = jnp.pad(extra, ((0, 0), (0, width - conf_w)))
+    payload = jnp.concatenate([own_tok.reshape(img_rows, width), extra])
     table = pairs_gather(payload, owners_n)
-    cut_tok = img_dev * TOKS * quarter
-    cut_ids = cut_tok + views_n
-    all_tok = table[:, :cut_tok].astype(jnp.bfloat16).reshape(owners_n * img_dev, TOKS * quarter)
-    all_ids = table[:, cut_tok:cut_ids].astype(jnp.int32)
-    all_conf = table[:, cut_ids:].reshape(owners_n * views_n, TOKS)
+    all_tok = table[:, :img_rows].reshape(owners_n * img_dev, TOKS * width)
+    pieces = table[:, img_rows : img_rows + 3 * pair_dev, :conf_w].astype(jnp.float32)
+    pieces = pieces.reshape(owners_n, 3, pair_dev, conf_w)
+    all_conf = (pieces[:, 0] + pieces[:, 1] + pieces[:, 2]).reshape(owners_n * views_n, TOKS)
+    all_ids = table[:, img_rows + 3 * pair_dev, :views_n].astype(jnp.int32)
     partner_ids = all_ids.reshape(owners_n, pair_dev, 2)[:, :, ::-1].reshape(-1)
     all_ids = all_ids.reshape(-1)
 
@@ -159,11 +173,8 @@
     local = image % img_dev
     at = ((own - other // img_dev) % owners_n) * img_dev + other % img_dev
     far = (at[:, None] == jnp.arange(owners_n * img_dev)[None, :]).astype(jnp.bfloat16)
-    context_q = pick_rows(far, all_tok).reshape(views_n, TOKS, quarter)
-
-    own_tok = mp_gather_cols(tokens.reshape(img_dev, TOKS, quarter))
-    width = own_tok.shape[2]
-    img_rows = img_dev * TOKS
+    context_tok = pick_rows(far, all_tok).reshape(views_n, TOKS, width)
+
     begin = own_tok.astype(jnp.float32).reshape(img_rows, width)
     normed = layer_norm(begin, gain_self)
     qkv = jnp.einsum("rd,kdc->krc", normed, self_qkv, preferred_element_type=jnp.float32).astype(
@@ -179,9 +190,7 @@
     )
 
     rows_n = views_n * TOKS
-    context = layer_norm(mp_gather_cols(context_q).astype(jnp.float32), gain_context).reshape(
-        rows_n, width
-    )
+    context = layer_norm(context_tok.astype(jnp.float32), gain_context).reshape(rows_n, width)
     keyval = jnp.einsum(
         "rd,kdc->krc", context, cross_kv, preferred_element_type=jnp.float32
     ).astype(jnp.bfloat16)

time: 47.7 us -> 52.2 us (1.094)
  waiting for transfers between devices: 13.5 us -> 18.1 us
  matrix products: 6.14 us -> 7.47 us
  local copies, waits for them, and re-layouts: 6.65 us -> 5.57 us
    ppermute x3, waiting for transfers between devices: 1.6 us -> 5.56 us  [pairs_shift(): lax.ppermute(values, 'pairs', [(i, (i + step) % owners_n) for i in range(...]
    reshape x8 -> x2, local copies, waits for them, and re-layouts: 2.07 us -> 0.19 us  [the longest x1 0.18 us: per_device(): all_tok = table[:, :img_rows].reshape(owners_n * img_dev, TOKS * width)]
    dot_general x1, matrix products: 0.43 us -> 1.67 us  [per_device(): jnp.einsum('rd,kdc->krc', normed, self_qkv, preferred_element_type=jnp.fl...]
    convert_element_type x1 -> x6, local copies, waits for them, and re-layouts: 0.09 us -> 1.12 us  [the longest x4 0.77 us: per_device(): all_ids = table[:, img_rows + 3 * pair_dev, :views_n].astype(jnp.int32)]
    ppermute x13 -> x11, starting transfers between devices: 9.55 us -> 8.61 us  [swap(): return lax.ppermute(values, 'mp', pairs)]
    ppermute x3, starting transfers between devices: 5.71 us -> 6.48 us  [pairs_shift(): lax.ppermute(values, 'pairs', [(i, (i + step) % owners_n) for i in range(...]
    ppermute x13 -> x11, waiting for transfers between devices: 11.9 us -> 12.6 us  [swap(): return lax.ppermute(values, 'mp', pairs)]
    select_n x4 -> x2, other arithmetic: 2.08 us -> 1.85 us  [mp_gather_cols(): jnp.where(core == 0, jnp.concatenate([part, got], axis=2), jnp.concatenat...]
  transfers between devices with their start and end apart: 16 -> 14, of which waited for: 7 -> 10; matrix products, arithmetic and copies ran while one was open for 23% -> 13% of each run, Pallas kernels for 0% -> 0%
where the time goes in v7:
time: 52.2 us; the launch traced here: 51.8 us
  waiting for transfers between devices  18.1 us (35%)
  starting transfers between devices  15.1 us (29%)
  matrix products  7.47 us (14%)
  local copies, waits for them, and re-layouts  5.57 us (11%)
  other arithmetic  4.87 us (9%)
  between operations  0.65 us (1%)
    ppermute x11, waiting for transfers between devices, swap(): return lax.ppermute(values, 'mp', pairs)  12.6 us
    ppermute x11, starting transfers between devices, swap(): return lax.ppermute(values, 'mp', pairs)  8.61 us
    ppermute x3, starting transfers between devices, pairs_shift(): lax.ppermute(values, 'pairs', [(i, (i + step) % owners_n) for i in range(...  6.48 us
    ppermute x3, waiting for transfers between devices, pairs_shift(): lax.ppermute(values, 'pairs', [(i, (i + step) % owners_n) for i in range(...  5.56 us
    dot_general x1, matrix products, per_device(): jnp.dot(hidden.astype(jnp.bfloat16), mlp_down, preferred_element_type=jnp...  2.72 us
    select_n x2, other arithmetic, mp_gather_cols(): jnp.where(core == 0, jnp.concatenate([part, got], axis=2), jnp.concatenat...  1.85 us
    dot_general x1, matrix products, per_device(): jnp.einsum('rd,kdc->krc', normed, self_qkv, preferred_element_type=jnp.fl...  1.67 us
  transfers between devices with their start and end apart: 14, of which 10 were waited for; matrix products, arithmetic and copies ran while one was open for 13% of the time, Pallas kernels for 0%

profile of v7, /device:TPU:0, one launch (start us, length us, event | category | flops | bytes accessed | tf_op | source)
XLA Modules:
  0.0 51.8 jit_solution(6000377165944629901)
XLA Ops:
  0.0 0.5 collective-permute-start
  0.5 1.1 %collective-permute-done = bf16[2,32,192]{2,1,0:T(8,128)(2,1)S(1)} collective-permute-done((bf16[2,32,192]{2,1,0:T(8,128)(2,1)}, bf16[2,32,192]{2,1,0:T(8,128)(2,1)S(1)}, u32[]{:S(2)}, u32[]{:S(2)}) %collective-permute-start) | collective-permute-done | bytes 24608 | tf_op jit(solution)/shard_map/ppermute | solution.py:41
  1.5 0.9 %maximum_select_fusion.3 = bf16[2,32,384]{2,1,0:T(8,128)(2,1)S(1)} fusion(bf16[2,32,192]{2,1,0:T(8,128)(2,1)S(1)} %collective-permute-done, bf16[2,32,192]{2,1,0:T(8,128)(2,1)} %bitcast.96, pred[]{:T(512)S(6)} %eq.93), kind=kLoop, calls=%fused_computation.139 | loop fusion | flops 221184 | bytes 98305 | tf_op jit(solution)/shard_map/jit(_where)/select_n | solution.py:88
  2.5 2.9 %collective-permute-start.1 = (bf16[2,32,384]{2,1,0:T(8,128)(2,1)S(1)}, bf16[2,32,384]{2,1,0:T(8,128)(2,1)S(1)}, u32[]{:S(2)}, u32[]{:S(2)}) collective-permute-start(bf16[2,32,384]{2,1,0:T(8,128)(2,1)S(1)} %maximum_select_fusion.3), channel_id=1, source_target_pairs={{0,2},{1,3},{2,0},{3,1},{4,6},{5,7},{6,4},{7,5},{8,10},{9,11},{10,... | collective-permute-start | bytes 147464 | tf_op jit(solution)/shard_map/ppermute | solution.py:41
  5.4 0.9 %maximum_select_fusion.2 = bf16[64,384]{1,0:T(8,128)(2,1)S(1)} fusion(bf16[64,192]{1,0:T(8,128)(2,1)S(1)} %bitcast.97, bf16[64,192]{1,0:T(8,128)(2,1)} %param.16, pred[]{:T(512)S(6)} %eq.93), kind=kLoop, calls=%fused_computation.138 | loop fusion | flops 221184 | bytes 98305 | tf_op jit(solution)/shard_map/jit(_where)/select_n | solution.py:88
  6.3 1.1 %collective-permute-done.1 = bf16[2,32,384]{2,1,0:T(8,128)(2,1)S(1)} collective-permute-done((bf16[2,32,384]{2,1,0:T(8,128)(2,1)S(1)}, bf16[2,32,384]{2,1,0:T(8,128)(2,1)S(1)}, u32[]{:S(2)}, u32[]{:S(2)}) %collective-permute-start.1) | collective-permute-done | bytes 49184 | tf_op jit(solution)/shard_map/ppermute | solution.py:41
  7.4 0.1 convert_reduce_fusion
  7.6 0.2 fusion.27
  7.8 1.7 %fusion.7 = bf16[3,64,192]{2,1,0:T(8,128)(2,1)S(1)} fusion(bf16[3,768,192]{1,2,0:T(8,128)(2,1)} %param.23, bf16[64,768]{1,0:T(8,128)(2,1)S(1)} %get-tuple-element.24, f32[768]{0:T(1024)} %param.19, f32[64]{0:T(128)S(1)} %add_rsqrt_fusion.3, f32[64]{0:T(128)S(1)} %broadcast_multiply_fusion.3), kind=kOutput, calls=%fused_computation.16 | convolution fusion | flops 56905728 | bytes 1060352 | tf_op jit(solution)/shard_map/rd,kdc->krc/dot_general | solution.py:180
  9.7 0.2 fusion.155
  9.9 0.1 convolution_multiply_fusion.1
  10.1 0.2 fusion.10
  10.4 0.1 reshape.447
  10.5 0.2 convolution_convert_fusion.6
  11.0 1.0 %collective-permute-done.5 = bf16[32,768]{1,0:T(8,128)(2,1)S(1)} collective-permute-done((bf16[32,768]{1,0:T(8,128)(2,1)S(1)}, bf16[32,768]{1,0:T(8,128)(2,1)S(1)}, u32[]{:S(2)}, u32[]{:S(2)}) %collective-permute-start.5) | collective-permute-done | bytes 49184 | tf_op jit(solution)/shard_map/ppermute | solution.py:41
  12.0 2.1 %collective-permute-start.6 = (bf16[32,768]{1,0:T(8,128)(2,1)S(1)}, bf16[32,768]{1,0:T(8,128)(2,1)S(1)}, u32[]{:S(2)}, u32[]{:S(2)}) collective-permute-start(bf16[32,768]{1,0:T(8,128)(2,1)S(1)} %add_convert_fusion.1), channel_id=1, source_target_pairs={{0,2},{1,3},{2,0},{3,1},{4,6},{5,7},{6,4},{7,5},{8,10},{9,11},{10,... | collective-permute-start | bytes 147464 | tf_op jit(solution)/shard_map/ppermute | solution.py:41
  14.1 2.7 %collective-permute-start.3 = (bf16[72,768]{1,0:T(8,128)(2,1)S(1)}, bf16[72,768]{1,0:T(8,128)(2,1)S(1)}, u32[]{:S(2)}, u32[]{:S(2)}) collective-permute-start(bf16[72,768]{1,0:T(8,128)(2,1)S(1)} %get-tuple-element.38), channel_id=1, source_target_pairs={{0,8},{4,12},{8,0},{12,4},{1,9},{5,13},{9,1},{13,5},{2,10},{6,14},... | collective-permute-start | bytes 331784 | tf_op jit(solution)/shard_map/ppermute | solution.py:37
  16.8 1.6 %collective-permute-start.2 = (bf16[72,768]{1,0:T(8,128)(2,1)S(1)}, bf16[72,768]{1,0:T(8,128)(2,1)S(1)}, u32[]{:S(2)}, u32[]{:S(2)}) collective-permute-start(bf16[72,768]{1,0:T(8,128)(2,1)S(1)} %get-tuple-element.38), channel_id=1, source_target_pairs={{0,4},{4,8},{8,12},{12,0},{1,5},{5,9},{9,13},{13,1},{2,6},{6,10},{... | collective-permute-start | bytes 331784 | tf_op jit(solution)/shard_map/ppermute | solution.py:37
  18.3 2.2 %collective-permute-start.4 = (bf16[72,768]{1,0:T(8,128)(2,1)S(1)}, bf16[72,768]{1,0:T(8,128)(2,1)S(1)}, u32[]{:S(2)}, u32[]{:S(2)}) collective-permute-start(bf16[72,768]{1,0:T(8,128)(2,1)S(1)} %get-tuple-element.38), channel_id=1, source_target_pairs={{0,12},{4,0},{8,4},{12,8},{1,13},{5,1},{9,5},{13,9},{2,14},{6,2},{... | collective-permute-start | bytes 331784 | tf_op jit(solution)/shard_map/ppermute | solution.py:37
  20.7 5.1 %collective-permute-done.3 = bf16[72,768]{1,0:T(8,128)(2,1)S(1)} collective-permute-done((bf16[72,768]{1,0:T(8,128)(2,1)S(1)}, bf16[72,768]{1,0:T(8,128)(2,1)S(1)}, u32[]{:S(2)}, u32[]{:S(2)}) %collective-permute-start.3) | collective-permute-done | bytes 110624 | tf_op jit(solution)/shard_map/ppermute | solution.py:37
  25.8 0.5 collective-permute-done.4
  26.3 0.5 broadcast.587
  26.8 0.7 %fusion.152 = (s32[4,4]{1,0:T(4,128)S(1)}, s32[4,1,4]{2,1,0:T(1,128)S(1)}) fusion(s32[]{:T(128)} %broadcast.587, bf16[1,72,768]{2,1,0:T(8,128)(2,1)S(1)} %bitcast.89, bf16[1,72,768]{2,1,0:T(8,128)(2,1)S(1)} %bitcast.83, bf16[1,72,768]{2,1,0:T(8,128)(2,1)S(1)} %bitcast.86, bf16[1,72,768]{2,1,0:T(8,128)(2,1)S(1)} %get-tuple-element.37), kind=kLoop, calls=%fused_computation.254 | loop fusion | flops 128 | bytes 442500 | tf_op jit(solution)/shard_map/convert_element_type | solution.py:163
  28.0 0.1 add_reduce_fusion
  28.2 0.2 select_reduce_fusion.1
  28.4 0.2 reshape.448
  28.6 0.3 fusion.2
  28.9 0.1 bitcast_reduce_fusion
  29.1 0.2 fusion.15
  29.4 0.3 reshape.521
  29.9 0.1 fusion.148
  30.0 0.4 fusion.30
  30.5 0.1 reshape.570
  30.6 0.1 reshape.569
  30.8 0.1 pad_maximum_fusion.1
  30.9 0.2 multiply_reduce_fusion.1
  31.1 0.2 copy-done.6
  31.4 0.2 convolution_convert_fusion.8
  31.6 0.1 reshape_reshape.3
  31.7 0.2 convolution_convert_fusion.1
  32.0 0.1 reshape_reshape_reshape.3
  32.1 0.2 convolution_multiply_fusion
  32.5 0.3 fusion.6
  32.8 0.1 reshape.449
  33.0 0.1 copy-done.2
  33.1 0.2 convolution_convert_fusion.3
  33.6 1.1 %collective-permute-done.8 = bf16[64,768]{1,0:T(8,128)(2,1)S(1)} collective-permute-done((bf16[64,768]{1,0:T(8,128)(2,1)S(1)}, bf16[64,768]{1,0:T(8,128)(2,1)S(1)}, u32[]{:S(2)}, u32[]{:S(2)}) %collective-permute-start.8) | collective-permute-done | bytes 98336 | tf_op jit(solution)/shard_map/ppermute | solution.py:41
  34.7 0.6 %collective-permute-start.9 = (bf16[64,768]{1,0:T(8,128)(2,1)S(1)}, bf16[64,768]{1,0:T(8,128)(2,1)S(1)}, u32[]{:S(2)}, u32[]{:S(2)}) collective-permute-start(bf16[64,768]{1,0:T(8,128)(2,1)S(1)} %add_convert_fusion), channel_id=1, source_target_pairs={{0,2},{1,3},{2,0},{3,1},{4,6},{5,7},{6,4},{7,5},{8,10},{9,11},{10,... | collective-permute-start | bytes 294920 | tf_op jit(solution)/shard_map/ppermute | solution.py:41
  35.3 4.4 %collective-permute-done.9 = bf16[64,768]{1,0:T(8,128)(2,1)S(1)} collective-permute-done((bf16[64,768]{1,0:T(8,128)(2,1)S(1)}, bf16[64,768]{1,0:T(8,128)(2,1)S(1)}, u32[]{:S(2)}, u32[]{:S(2)}) %collective-permute-start.9) | collective-permute-done | bytes 98336 | tf_op jit(solution)/shard_map/ppermute | solution.py:41
  39.8 0.6 %gather_fusion = f32[4,32,768]{2,1,0:T(8,128)S(1)} fusion(f32[2,32,768]{2,1,0:T(8,128)S(1)} %convert_add_fusion.2, s32[1024]{0:T(1024)S(1)} %pad_clamp_fusion), kind=kCustom, calls=%fused_computation | custom fusion | bytes 786448 | tf_op jit(solution)/shard_map/jit(_take)/gather | solution.py:199
  40.4 0.8 %collective-permute-done.10 = f32[64,768]{1,0:T(8,128)S(1)} collective-permute-done((f32[64,768]{1,0:T(8,128)S(1)}, f32[64,768]{1,0:T(8,128)S(1)}, u32[]{:S(2)}, u32[]{:S(2)}) %collective-permute-start.10) | collective-permute-done | bytes 196640 | tf_op jit(solution)/shard_map/ppermute | solution.py:41
  41.2 0.2 fusion.151
  41.4 0.2 multiply_reduce_fusion
  41.7 2.7 %convolution_convert_fusion.2 = bf16[128,768]{1,0:T(8,128)(2,1)S(1)} fusion(bf16[768,768]{1,0:T(8,128)(2,1)S(1)} %copy-done, bf16[768,768]{1,0:T(8,128)(2,1)} %param.28, f32[128,768]{1,0:T(8,128)S(1)} %get-tuple-element.20, f32[768]{0:T(1024)S(1)} %copy-done.8, f32[128]{0:T(128)S(1)} %add_rsqrt_fusion.1, f32[128]{0:T(128)S(1)} %broadcast_multiply_fusion.1), kind=kOutput, calls=%fused_computation.7 | convolution fusion | flops 308871168 | bytes 2953216 | tf_op jit(solution)/shard_map/dot_general | solution.py:210
  44.4 0.2 copy.107
  44.9 0.3 collective-permute-start.13
  45.3 0.4 collective-permute-start.11
  45.7 1.6 %collective-permute-start.12 = (bf16[128,192]{1,0:T(8,128)(2,1)S(1)}, bf16[128,192]{1,0:T(8,128)(2,1)S(1)}, u32[]{:S(2)}, u32[]{:S(2)}) collective-permute-start(bf16[128,192]{1,0:T(8,128)(2,1)S(1)} %select_bitcast_fusion.1), channel_id=1, source_target_pairs={{0,2},{1,3},{2,0},{3,1},{4,6},{5,7},{6,4},{7,5},{8,10},{9,11},{10,... | collective-permute-start | bytes 147464 | tf_op jit(solution)/shard_map/ppermute | solution.py:41
  47.3 0.1 convolution_maximum_fusion
  47.7 1.4 %collective-permute-done.13 = bf16[128,192]{1,0:T(8,128)(2,1)S(1)} collective-permute-done((bf16[128,192]{1,0:T(8,128)(2,1)S(1)}, bf16[128,192]{1,0:T(8,128)(2,1)S(1)}, u32[]{:S(2)}, u32[]{:S(2)}) %collective-permute-start.13) | collective-permute-done | bytes 49184 | tf_op jit(solution)/shard_map/ppermute | solution.py:41
  49.1 1.7 %collective-permute-done.12 = bf16[128,192]{1,0:T(8,128)(2,1)S(1)} collective-permute-done((bf16[128,192]{1,0:T(8,128)(2,1)S(1)}, bf16[128,192]{1,0:T(8,128)(2,1)S(1)}, u32[]{:S(2)}, u32[]{:S(2)}) %collective-permute-start.12) | collective-permute-done | bytes 49184 | tf_op jit(solution)/shard_map/ppermute | solution.py:41
  50.8 0.1 add_add_fusion
  50.9 0.2 fusion.9
  51.2 0.6 %copy.117 = bf16[2,32,192]{2,1,0:T(8,128)(2,1)} copy(bf16[2,32,192]{2,0,1:T(2,128)(2,1)S(1)} %fusion.9) | data formatting | bytes 49152 | tf_op jit(solution)/shard_map/convert_element_type | solution.py:223
  (93 shorter events, 3.0 us)
Async XLA Ops:
  0.0 41.6 %copy-start = (bf16[768,768]{1,0:T(8,128)(2,1)S(1)}, bf16[768,768]{1,0:T(8,128)(2,1)}, u32[]{:S(2)}) copy-start(bf16[768,768]{1,0:T(8,128)(2,1)} %param.29) | copy-start | bytes 3538948
  0.0 1.5 %collective-permute-start = (bf16[2,32,192]{2,1,0:T(8,128)(2,1)}, bf16[2,32,192]{2,1,0:T(8,128)(2,1)S(1)}, u32[]{:S(2)}, u32[]{:S(2)}) collective-permute-start(bf16[2,32,192]{2,1,0:T(8,128)(2,1)} %bitcast.95), channel_id=1, source_target_pairs={{0,1},{1,0},{2,3},{3,2},{4,5},{5,4},{6,7},{7,6},{8,9},{9,8},{10,11... | collective-permute-start | bytes 73736 | tf_op jit(solution)/shard_map/ppermute | solution.py:41
  2.5 5.0 %collective-permute-start.1 = (bf16[2,32,384]{2,1,0:T(8,128)(2,1)S(1)}, bf16[2,32,384]{2,1,0:T(8,128)(2,1)S(1)}, u32[]{:S(2)}, u32[]{:S(2)}) collective-permute-start(bf16[2,32,384]{2,1,0:T(8,128)(2,1)S(1)} %maximum_select_fusion.3), channel_id=1, source_target_pairs={{0,2},{1,3},{2,0},{3,1},{4,6},{5,7},{6,4},{7,5},{8,10},{9,11},{10,... | collective-permute-start | bytes 147464 | tf_op jit(solution)/shard_map/ppermute | solution.py:41
  7.8 2.7 %copy-start.3 = (bf16[192,768]{1,0:T(8,128)(2,1)S(1)}, bf16[192,768]{1,0:T(8,128)(2,1)}, u32[]{:S(2)}) copy-start(bf16[192,768]{1,0:T(8,128)(2,1)} %param.24) | copy-start | bytes 884740
  9.4 1.3 %copy-start.5 = (f32[2,64]{1,0:T(2,128)S(1)}, f32[2,64]{1,0:T(2,128)}, u32[]{:S(2)}) copy-start(f32[2,64]{1,0:T(2,128)} %param.18) | copy-start | bytes 1540
  9.5 1.4 %copy-start.9 = (s32[2,2]{1,0:T(2,128)S(1)}, s32[2,2]{1,0:T(2,128)}, u32[]{:S(2)}) copy-start(s32[2,2]{1,0:T(2,128)} %param.17) | copy-start | bytes 52
  10.7 1.3 %collective-permute-start.5 = (bf16[32,768]{1,0:T(8,128)(2,1)S(1)}, bf16[32,768]{1,0:T(8,128)(2,1)S(1)}, u32[]{:S(2)}, u32[]{:S(2)}) collective-permute-start(bf16[32,768]{1,0:T(8,128)(2,1)S(1)} %broadcast_select_fusion.5), channel_id=1, source_target_pairs={{0,1},{1,0},{2,3},{3,2},{4,5},{5,4},{6,7},{7,6},{8,9},{9,8},{10,11... | collective-permute-start | bytes 147464 | tf_op jit(solution)/shard_map/ppermute | solution.py:41
  12.0 8.6 %collective-permute-start.6 = (bf16[32,768]{1,0:T(8,128)(2,1)S(1)}, bf16[32,768]{1,0:T(8,128)(2,1)S(1)}, u32[]{:S(2)}, u32[]{:S(2)}) collective-permute-start(bf16[32,768]{1,0:T(8,128)(2,1)S(1)} %add_convert_fusion.1), channel_id=1, source_target_pairs={{0,2},{1,3},{2,0},{3,1},{4,6},{5,7},{6,4},{7,5},{8,10},{9,11},{10,... | collective-permute-start | bytes 147464 | tf_op jit(solution)/shard_map/ppermute | solution.py:41
  14.1 11.7 %collective-permute-start.3 = (bf16[72,768]{1,0:T(8,128)(2,1)S(1)}, bf16[72,768]{1,0:T(8,128)(2,1)S(1)}, u32[]{:S(2)}, u32[]{:S(2)}) collective-permute-start(bf16[72,768]{1,0:T(8,128)(2,1)S(1)} %get-tuple-element.38), channel_id=1, source_target_pairs={{0,8},{4,12},{8,0},{12,4},{1,9},{5,13},{9,1},{13,5},{2,10},{6,14},... | collective-permute-start | bytes 331784 | tf_op jit(solution)/shard_map/ppermute | solution.py:37
  16.8 9.0 %collective-permute-start.2 = (bf16[72,768]{1,0:T(8,128)(2,1)S(1)}, bf16[72,768]{1,0:T(8,128)(2,1)S(1)}, u32[]{:S(2)}, u32[]{:S(2)}) collective-permute-start(bf16[72,768]{1,0:T(8,128)(2,1)S(1)} %get-tuple-element.38), channel_id=1, source_target_pairs={{0,4},{4,8},{8,12},{12,0},{1,5},{5,9},{9,13},{13,1},{2,6},{6,10},{... | collective-permute-start | bytes 331784 | tf_op jit(solution)/shard_map/ppermute | solution.py:37
  18.3 7.9 %collective-permute-start.4 = (bf16[72,768]{1,0:T(8,128)(2,1)S(1)}, bf16[72,768]{1,0:T(8,128)(2,1)S(1)}, u32[]{:S(2)}, u32[]{:S(2)}) collective-permute-start(bf16[72,768]{1,0:T(8,128)(2,1)S(1)} %get-tuple-element.38), channel_id=1, source_target_pairs={{0,12},{4,0},{8,4},{12,8},{1,13},{5,1},{9,5},{13,9},{2,14},{6,2},{... | collective-permute-start | bytes 331784 | tf_op jit(solution)/shard_map/ppermute | solution.py:37
  20.6 10.2 %collective-permute-start.7 = (f32[32,768]{1,0:T(8,128)S(1)}, f32[32,768]{1,0:T(8,128)S(1)}, u32[]{:S(2)}, u32[]{:S(2)}) collective-permute-start(f32[32,768]{1,0:T(8,128)S(1)} %convert_add_fusion.3), channel_id=1, source_target_pairs={{0,1},{1,0},{2,3},{3,2},{4,5},{5,4},{6,7},{7,6},{8,9},{9,8},{10,11... | collective-permute-start | bytes 294920 | tf_op jit(solution)/shard_map/ppermute | solution.py:41
  28.6 1.4 %copy-start.1 = (bf16[2,768,192]{1,2,0:T(8,128)(2,1)S(1)}, bf16[2,768,192]{1,2,0:T(8,128)(2,1)}, u32[]{:S(2)}) copy-start(bf16[2,768,192]{1,2,0:T(8,128)(2,1)} %param.26) | copy-start | bytes 1769476
  28.6 1.4 %copy-start.4 = (f32[768]{0:T(1024)S(1)}, f32[768]{0:T(1024)}, u32[]{:S(2)}) copy-start(f32[768]{0:T(1024)} %param.21) | copy-start | bytes 9220
  30.4 1.0 %copy-start.6 = (bf16[768,192]{0,1:T(8,128)(2,1)S(1)}, bf16[768,192]{0,1:T(8,128)(2,1)}, u32[]{:S(2)}) copy-start(bf16[768,192]{0,1:T(8,128)(2,1)} %param.25) | copy-start | bytes 884740
  30.4 1.0 %copy-start.7 = (f32[768]{0:T(1024)S(1)}, f32[768]{0:T(1024)}, u32[]{:S(2)}) copy-start(f32[768]{0:T(1024)} %param.20) | copy-start | bytes 9220
  32.1 1.0 %copy-start.2 = (bf16[192,768]{1,0:T(8,128)(2,1)S(1)}, bf16[192,768]{1,0:T(8,128)(2,1)}, u32[]{:S(2)}) copy-start(bf16[192,768]{1,0:T(8,128)(2,1)} %param.27) | copy-start | bytes 884740
  33.3 1.4 %collective-permute-start.8 = (bf16[64,768]{1,0:T(8,128)(2,1)S(1)}, bf16[64,768]{1,0:T(8,128)(2,1)S(1)}, u32[]{:S(2)}, u32[]{:S(2)}) collective-permute-start(bf16[64,768]{1,0:T(8,128)(2,1)S(1)} %broadcast_select_fusion.2), channel_id=1, source_target_pairs={{0,1},{1,0},{2,3},{3,2},{4,5},{5,4},{6,7},{7,6},{8,9},{9,8},{10,11... | collective-permute-start | bytes 294920 | tf_op jit(solution)/shard_map/ppermute | solution.py:41
  34.7 4.9 %collective-permute-start.9 = (bf16[64,768]{1,0:T(8,128)(2,1)S(1)}, bf16[64,768]{1,0:T(8,128)(2,1)S(1)}, u32[]{:S(2)}, u32[]{:S(2)}) collective-permute-start(bf16[64,768]{1,0:T(8,128)(2,1)S(1)} %add_convert_fusion), channel_id=1, source_target_pairs={{0,2},{1,3},{2,0},{3,1},{4,6},{5,7},{6,4},{7,5},{8,10},{9,11},{10,... | collective-permute-start | bytes 294920 | tf_op jit(solution)/shard_map/ppermute | solution.py:41
  39.7 1.5 %collective-permute-start.10 = (f32[64,768]{1,0:T(8,128)S(1)}, f32[64,768]{1,0:T(8,128)S(1)}, u32[]{:S(2)}, u32[]{:S(2)}) collective-permute-start(f32[64,768]{1,0:T(8,128)S(1)} %convert_add_fusion.1), channel_id=1, source_target_pairs={{0,1},{1,0},{2,3},{3,2},{4,5},{5,4},{6,7},{7,6},{8,9},{9,8},{10,11... | collective-permute-start | bytes 589832 | tf_op jit(solution)/shard_map/ppermute | solution.py:41
  40.4 1.3 %copy-start.8 = (f32[768]{0:T(1024)S(1)}, f32[768]{0:T(1024)}, u32[]{:S(2)}) copy-start(f32[768]{0:T(1024)} %param.22) | copy-start | bytes 9220
  44.9 4.1 %collective-permute-start.13 = (bf16[128,192]{1,0:T(8,128)(2,1)S(1)}, bf16[128,192]{1,0:T(8,128)(2,1)S(1)}, u32[]{:S(2)}, u32[]{:S(2)}) collective-permute-start(bf16[128,192]{1,0:T(8,128)(2,1)S(1)} %select_bitcast_fusion), channel_id=1, source_target_pairs={{0,3},{1,2},{2,1},{3,0},{4,7},{5,6},{6,5},{7,4},{8,11},{9,10},{10,... | collective-permute-start | bytes 147464 | tf_op jit(solution)/shard_map/ppermute | solution.py:41
  45.3 3.8 %collective-permute-start.11 = (bf16[128,192]{1,0:T(8,128)(2,1)S(1)}, bf16[128,192]{1,0:T(8,128)(2,1)S(1)}, u32[]{:S(2)}, u32[]{:S(2)}) collective-permute-start(bf16[128,192]{1,0:T(8,128)(2,1)S(1)} %select_bitcast_fusion.2), channel_id=1, source_target_pairs={{0,1},{1,0},{2,3},{3,2},{4,5},{5,4},{6,7},{7,6},{8,9},{9,8},{10,11... | collective-permute-start | bytes 147464 | tf_op jit(solution)/shard_map/ppermute | solution.py:41
  45.7 5.1 %collective-permute-start.12 = (bf16[128,192]{1,0:T(8,128)(2,1)S(1)}, bf16[128,192]{1,0:T(8,128)(2,1)S(1)}, u32[]{:S(2)}, u32[]{:S(2)}) collective-permute-start(bf16[128,192]{1,0:T(8,128)(2,1)S(1)} %select_bitcast_fusion.1), channel_id=1, source_target_pairs={{0,2},{1,3},{2,0},{3,1},{4,6},{5,7},{6,4},{7,5},{8,10},{9,11},{10,... | collective-permute-start | bytes 147464 | tf_op jit(solution)/shard_map/ppermute | solution.py:41

commit v8 on v5

--- a/solution.py
+++ b/solution.py
@@ -35,6 +35,25 @@
 
 def pairs_shift(values, step, owners_n):
     return lax.ppermute(values, "pairs", [(i, (i + step) % owners_n) for i in range(owners_n)])
+
+
+def layer_norm_quarters(values, gain):
+    center = values - jnp.mean(values, axis=(0, 2), keepdims=True)
+    spread = jnp.mean(center * center, axis=(0, 2), keepdims=True)
+    gain = gain.reshape(values.shape[0], 1, values.shape[2])
+    return (center * lax.rsqrt(spread + EPSILON) * gain).astype(jnp.bfloat16)
+
+
+def mp_gather_major(part):
+    if lax.axis_size("mp") != 4:
+        return lax.all_gather(part, "mp", axis=0)
+    index = lax.axis_index("mp")
+    core = index % 2
+    chip = index // 2
+    got = swap(part, mp_pairs(1))
+    pair = jnp.stack([jnp.where(core == 0, part, got), jnp.where(core == 0, got, part)])
+    other = swap(pair, mp_pairs(2))
+    return jnp.concatenate([jnp.where(chip == 0, pair, other), jnp.where(chip == 0, other, pair)])
 
 
 def swap(values, pairs):
@@ -134,6 +153,11 @@
     owners_n = lax.axis_size("pairs")
     own = lax.axis_index("pairs")
 
+    img_rows = img_dev * TOKS
+    own_tok = mp_gather_major(tokens)
+    parts_n = own_tok.shape[0]
+    width = parts_n * quarter
+
     payload = jnp.concatenate(
         [
             tokens.astype(jnp.float32).reshape(-1),
@@ -141,6 +165,7 @@
             confidence.reshape(-1),
         ]
     )
+    payload, own_tok = lax.optimization_barrier((payload, own_tok))
     table = pairs_gather(payload, owners_n)
     cut_tok = img_dev * TOKS * quarter
     cut_ids = cut_tok + views_n
@@ -159,16 +184,16 @@
     local = image % img_dev
     at = ((own - other // img_dev) % owners_n) * img_dev + other % img_dev
     far = (at[:, None] == jnp.arange(owners_n * img_dev)[None, :]).astype(jnp.bfloat16)
-    context_q = pick_rows(far, all_tok).reshape(views_n, TOKS, quarter)
-
-    own_tok = mp_gather_cols(tokens.reshape(img_dev, TOKS, quarter))
-    width = own_tok.shape[2]
-    img_rows = img_dev * TOKS
-    begin = own_tok.astype(jnp.float32).reshape(img_rows, width)
-    normed = layer_norm(begin, gain_self)
-    qkv = jnp.einsum("rd,kdc->krc", normed, self_qkv, preferred_element_type=jnp.float32).astype(
-        jnp.bfloat16
-    )
+    context_q = pick_rows(far, all_tok).reshape(views_n * TOKS, quarter)
+
+    begin = jnp.transpose(own_tok, (1, 0, 2)).reshape(img_rows, width).astype(jnp.float32)
+    normed = layer_norm_quarters(own_tok.astype(jnp.float32), gain_self)
+    qkv = jnp.einsum(
+        "qrd,kqdc->krc",
+        normed,
+        self_qkv.reshape(3, parts_n, quarter, -1),
+        preferred_element_type=jnp.float32,
+    ).astype(jnp.bfloat16)
     term = jnp.dot(
         attend(qkv[0], qkv[1], qkv[2], img_dev), self_out, preferred_element_type=jnp.float32
     )
@@ -179,11 +204,12 @@
     )
 
     rows_n = views_n * TOKS
-    context = layer_norm(mp_gather_cols(context_q).astype(jnp.float32), gain_context).reshape(
-        rows_n, width
-    )
+    context = layer_norm_quarters(mp_gather_major(context_q).astype(jnp.float32), gain_context)
     keyval = jnp.einsum(
-        "rd,kdc->krc", context, cross_kv, preferred_element_type=jnp.float32
+        "qrd,kqdc->krc",
+        context,
+        cross_kv.reshape(2, parts_n, quarter, -1),
+        preferred_element_type=jnp.float32,
     ).astype(jnp.bfloat16)
     near = (local[:, None] == jnp.arange(img_dev)[None, :]).astype(jnp.bfloat16)
     query = pick_rows(near, query_img.reshape(img_dev, TOKS, -1)).reshape(rows_n, -1)

time: 47.7 us -> 54 us (1.13)
  local copies, waits for them, and re-layouts: 6.65 us -> 11.9 us
  starting transfers between devices: 15.3 us -> 13.6 us
  matrix products: 6.14 us -> 7.56 us
  waiting for transfers between devices: 13.5 us -> 14.3 us
    reshape x1 -> x3, local copies, waits for them, and re-layouts: 0.11 us -> 3.88 us  [the longest x1 2.26 us: per_device(): cross_kv.reshape(2, parts_n, quarter, -1)]
    select_n x4 -> x2, other arithmetic: 2.08 us -> 0.05 us  [mp_gather_major(): jnp.where(chip == 0, pair, other)]
    ppermute x13, starting transfers between devices: 9.55 us -> 8 us  [swap(): return lax.ppermute(values, 'mp', pairs)]
    another operation x1 -> x5, other arithmetic: 0.03 us -> 1.49 us  [the longest x4 1.46 us: mp_gather_major(): jnp.stack([jnp.where(core == 0, part, got), jnp.where(core == 0, got, par...]
    mul x0 -> x2, local copies, waits for them, and re-layouts: none -> 0.74 us  [layer_norm_quarters(): return (center * lax.rsqrt(spread + EPSILON) * gain).astype(jnp.bfloat16)]
    dot_general x1, matrix products: 0.24 us -> 0.94 us  [per_device(): jnp.dot(normed, cross_query, preferred_element_type=jnp.float32)]
    reduce_sum x0 -> x4, other arithmetic: none -> 0.68 us  [the longest x2 0.42 us: layer_norm_quarters(): spread = jnp.mean(center * center, axis=(0, 2), keepdims=True)]
    dot_general x2, matrix products: 0.45 us -> 1.09 us  [pick_rows(): jnp.dot(onehot.astype(values.dtype), flat, preferred_element_type=jnp.flo...]
  transfers between devices with their start and end apart: 16 -> 16, of which waited for: 7 -> 9; matrix products, arithmetic and copies ran while one was open for 23% -> 29% of each run, Pallas kernels for 0% -> 0%
where the time goes in v8:
time: 54 us; the launch traced here: 53.6 us
  waiting for transfers between devices  14.3 us (26%)
  starting transfers between devices  13.6 us (25%)
  local copies, waits for them, and re-layouts  11.9 us (22%)
  matrix products  7.56 us (14%)
  other arithmetic  5.38 us (10%)
  between operations  0.8 us (1%)
    ppermute x13, waiting for transfers between devices, swap(): return lax.ppermute(values, 'mp', pairs)  12.4 us
    ppermute x13, starting transfers between devices, swap(): return lax.ppermute(values, 'mp', pairs)  8 us
    ppermute x3, starting transfers between devices, pairs_shift(): lax.ppermute(values, 'pairs', [(i, (i + step) % owners_n) for i in range(...  5.57 us
    dot_general x1, matrix products, per_device(): jnp.dot(hidden.astype(jnp.bfloat16), mlp_down, preferred_element_type=jnp...  2.72 us
    reshape x1, local copies, waits for them, and re-layouts, per_device(): cross_kv.reshape(2, parts_n, quarter, -1)  2.26 us
    ppermute x3, waiting for transfers between devices, pairs_shift(): lax.ppermute(values, 'pairs', [(i, (i + step) % owners_n) for i in range(...  1.96 us
    reshape x1, local copies, waits for them, and re-layouts, per_device(): self_qkv.reshape(3, parts_n, quarter, -1)  1.51 us
    another operation x4, other arithmetic, mp_gather_major(): jnp.stack([jnp.where(core == 0, part, got), jnp.where(core == 0, got, par...  1.46 us
  transfers between devices with their start and end apart: 16, of which 9 were waited for; matrix products, arithmetic and copies ran while one was open for 29% of the time, Pallas kernels for 0%

profile of v8, /device:TPU:0, one launch (start us, length us, event | category | flops | bytes accessed | tf_op | source)
XLA Modules:
  0.0 53.6 jit_solution(9877673846950776031)
XLA Ops:
  0.0 0.5 collective-permute-start
  0.5 1.1 %collective-permute-done = bf16[64,192]{1,0:T(8,128)(2,1)S(1)} collective-permute-done((bf16[64,192]{1,0:T(8,128)(2,1)}, bf16[64,192]{1,0:T(8,128)(2,1)S(1)}, u32[]{:S(2)}, u32[]{:S(2)}) %collective-permute-start) | collective-permute-done | bytes 24608 | tf_op jit(solution)/shard_map/ppermute | solution.py:60
  1.5 0.8 %select_bitcast_fusion.6 = (bf16[1,64,192]{2,1,0:T(8,128)(2,1)S(1)}, bf16[1,64,192]{2,1,0:T(8,128)(2,1)S(1)}) fusion(bf16[64,192]{1,0:T(8,128)(2,1)} %param.16, bf16[64,192]{1,0:T(8,128)(2,1)S(1)} %collective-permute-done, pred[]{:T(512)S(6)} %eq.100), kind=kLoop, calls=%fused_computation.157 | loop fusion | flops 24576 | bytes 98305 | tf_op jit(solution)/shard_map/stack | solution.py:54
  2.3 2.9 %collective-permute-start.1 = (bf16[2,64,192]{2,1,0:T(8,128)(2,1)S(1)}, bf16[2,64,192]{2,1,0:T(8,128)(2,1)S(1)}, u32[]{:S(2)}, u32[]{:S(2)}) collective-permute-start(bf16[2,64,192]{2,1,0:T(8,128)(2,1)S(1)} %pad_maximum_fusion.6), channel_id=1, source_target_pairs={{0,2},{1,3},{2,0},{3,1},{4,6},{5,7},{6,4},{7,5},{8,10},{9,11},{10,... | collective-permute-start | bytes 147464 | tf_op jit(solution)/shard_map/ppermute | solution.py:60
  5.2 0.8 %reshape.520 = f32[12288]{0:T(1024)S(1)} reshape(bf16[64,192]{1,0:T(8,128)(2,1)} %param.16) | data formatting | bytes 73728 | tf_op jit(solution)/shard_map/reshape | solution.py:163
  6.1 0.7 %convert_element_type.173 = f32[2,2]{1,0:T(2,128)S(1)} convert(s32[2,2]{1,0:T(2,128)} %param.17) | non-fusion elementwise | flops 4 | bytes 32 | tf_op jit(solution)/shard_map/convert_element_type | solution.py:164
  6.9 0.8 %reshape.442 = f32[128]{0:T(128)S(1)} reshape(f32[2,64]{1,0:T(2,128)} %param.18) | data formatting | bytes 1024 | tf_op jit(solution)/shard_map/reshape | solution.py:165
  7.7 1.5 %copy.114 = bf16[3,768,192]{2,1,0:T(8,128)(2,1)S(1)} copy(bf16[3,768,192]{1,2,0:T(8,128)(2,1)} %param.23) | data formatting | bytes 1769472 | tf_op jit(solution)/shard_map/reshape | solution.py:194
  9.3 2.3 %reshape.450 = bf16[2,4,192,192]{2,1,3,0:T(4,128)(2,1)S(1)} reshape(bf16[2,768,192]{1,2,0:T(8,128)(2,1)} %param.26) | data formatting | bytes 1179648 | tf_op jit(solution)/shard_map/reshape | solution.py:211
  11.6 0.7 %mul.142 = f32[4,192]{1,0:T(4,128)} reshape(f32[768]{0:T(1024)S(1)} %copy-done.8) | data formatting | bytes 6144 | tf_op jit(solution)/shard_map/mul | solution.py:44
  12.5 0.2 fusion.31
  12.7 0.5 fusion.10
  13.4 0.1 convolution_multiply_fusion.1
  13.5 0.2 fusion.158
  13.8 0.2 fusion.12
  14.2 0.2 convolution_convert_fusion.5
  14.5 1.6 %collective-permute-start.2 = (f32[12420]{0:T(1024)S(1)}, f32[12420]{0:T(1024)S(1)}, u32[]{:S(2)}, u32[]{:S(2)}) collective-permute-start(f32[12420]{0:T(1024)S(1)} %concatenate.25), channel_id=1, source_target_pairs={{0,4},{4,8},{8,12},{12,0},{1,5},{5,9},{9,13},{13,1},{2,6},{6,10},{... | collective-permute-start | bytes 149048 | tf_op jit(solution)/shard_map/ppermute | solution.py:37
  16.1 2.6 %collective-permute-start.3 = (f32[12420]{0:T(1024)S(1)}, f32[12420]{0:T(1024)S(1)}, u32[]{:S(2)}, u32[]{:S(2)}) collective-permute-start(f32[12420]{0:T(1024)S(1)} %concatenate.25), channel_id=1, source_target_pairs={{0,8},{4,12},{8,0},{12,4},{1,9},{5,13},{9,1},{13,5},{2,10},{6,14},... | collective-permute-start | bytes 149048 | tf_op jit(solution)/shard_map/ppermute | solution.py:37
  18.7 1.3 %collective-permute-start.4 = (f32[12420]{0:T(1024)S(1)}, f32[12420]{0:T(1024)S(1)}, u32[]{:S(2)}, u32[]{:S(2)}) collective-permute-start(f32[12420]{0:T(1024)S(1)} %concatenate.25), channel_id=1, source_target_pairs={{0,12},{4,0},{8,4},{12,8},{1,13},{5,1},{9,5},{13,9},{2,14},{6,2},{... | collective-permute-start | bytes 149048 | tf_op jit(solution)/shard_map/ppermute | solution.py:37
  20.1 0.2 copy.79
  20.3 0.2 reshape.521
  20.4 0.2 reshape.522
  20.7 0.6 %collective-permute-start.6 = (bf16[32,768]{1,0:T(8,128)(2,1)S(1)}, bf16[32,768]{1,0:T(8,128)(2,1)S(1)}, u32[]{:S(2)}, u32[]{:S(2)}) collective-permute-start(bf16[32,768]{1,0:T(8,128)(2,1)S(1)} %add_convert_fusion.1), channel_id=1, source_target_pairs={{0,2},{1,3},{2,0},{3,1},{4,6},{5,7},{6,4},{7,5},{8,10},{9,11},{10,... | collective-permute-start | bytes 147464 | tf_op jit(solution)/shard_map/ppermute | solution.py:60
  21.3 1.7 %collective-permute-done.3 = f32[12420]{0:T(1024)S(1)} collective-permute-done((f32[12420]{0:T(1024)S(1)}, f32[12420]{0:T(1024)S(1)}, u32[]{:S(2)}, u32[]{:S(2)}) %collective-permute-start.3) | collective-permute-done | bytes 49712 | tf_op jit(solution)/shard_map/ppermute | solution.py:37
  23.0 0.3 collective-permute-done.4
  23.3 0.2 pad_maximum_fusion.1
  24.3 0.1 select_reduce_fusion.1
  24.4 0.6 %compare_and_fusion = (pred[4]{0:T(512)(128)(4,1)}, s32[4]{0:T(128)}) fusion(s32[4]{0:T(128)S(1)} %get-tuple-element.21), kind=kLoop, calls=%fused_computation.189 | loop fusion | flops 68 | bytes 36 | tf_op jit(solution)/shard_map/jit(_take)/and | solution.py:216
  25.1 0.2 convolution_convert_fusion.1
  25.6 0.7 %reshape.454 = f32[16,32]{1,0:T(8,128)} reshape(f32[4,128]{1,0:T(4,128)S(1)} %pad_maximum_fusion.7) | data formatting | bytes 4096 | tf_op jit(solution)/shard_map/reshape | solution.py:174
  26.3 0.6 %collective-permute-start.7 = (f32[32,768]{1,0:T(8,128)S(1)}, f32[32,768]{1,0:T(8,128)S(1)}, u32[]{:S(2)}, u32[]{:S(2)}) collective-permute-start(f32[32,768]{1,0:T(8,128)S(1)} %convert_add_fusion.1), channel_id=1, source_target_pairs={{0,1},{1,0},{2,3},{3,2},{4,5},{5,4},{6,7},{7,6},{8,9},{9,8},{10,11... | collective-permute-start | bytes 294920 | tf_op jit(solution)/shard_map/ppermute | solution.py:60
  26.9 0.7 %pad_maximum_fusion.4 = bf16[2,128,192]{2,1,0:T(8,128)(2,1)} fusion(bf16[1,128,192]{2,1,0:T(8,128)(2,1)S(1)} %get-tuple-element.38, bf16[1,128,192]{2,1,0:T(8,128)(2,1)S(1)} %get-tuple-element.37), kind=kLoop, calls=%fused_computation.119 | loop fusion | flops 49152 | bytes 196608 | tf_op jit(solution)/shard_map/stack | solution.py:54
  27.5 0.5 collective-permute-start.9
  28.1 0.1 concatenate.30
  28.3 0.1 concatenate.31
  28.4 0.1 fusion.90
  28.6 0.2 multiply_reduce_fusion.1
  28.8 0.9 %convolution_convert_fusion.7 = bf16[64,192]{1,0:T(8,128)(2,1)S(1)} fusion(bf16[768,192]{0,1:T(8,128)(2,1)S(1)} %copy-done.1, f32[64,768]{1,0:T(8,128)S(1)} %reshape.522, f32[768]{0:T(1024)} %param.20, f32[64]{0:T(128)S(1)} %add_rsqrt_fusion.1, f32[64]{0:T(128)S(1)} %broadcast_multiply_fusion.2, f32[32,768]{1,0:T(8,128)S(1)} %get-tuple-element.36, ...), kind=kOutput, calls=%fused_computation.26 | convolution fusion | flops 19181568 | bytes 716288 | tf_op jit(solution)/shard_map/dot_general | solution.py:202
  29.9 0.9 %convolution_convert_fusion = bf16[4,6144]{1,0:T(4,128)(2,1)S(1)} fusion(bf16[2,6144]{1,0:T(2,128)(2,1)S(1)} %reshape_reshape.3, s32[4]{0:T(128)} %get-tuple-element.26), kind=kOutput, calls=%fused_computation.3 | convolution fusion | flops 122888 | bytes 73744 | tf_op jit(solution)/shard_map/dot_general | solution.py:129
  30.7 0.1 reshape_reshape_reshape.3
  30.9 2.4 %collective-permute-done.9 = bf16[2,128,192]{2,1,0:T(8,128)(2,1)S(1)} collective-permute-done((bf16[2,128,192]{2,1,0:T(8,128)(2,1)}, bf16[2,128,192]{2,1,0:T(8,128)(2,1)S(1)}, u32[]{:S(2)}, u32[]{:S(2)}) %collective-permute-start.9) | collective-permute-done | bytes 98336 | tf_op jit(solution)/shard_map/ppermute | solution.py:60
  33.3 0.1 convert_reduce_fusion
  33.5 0.2 fusion.16
  33.7 0.5 fusion.9
  34.3 0.2 convolution_multiply_fusion
  34.8 0.3 fusion.7
  35.2 0.1 reshape.451
  35.3 0.2 convolution_convert_fusion.3
  35.8 1.1 %collective-permute-done.10 = bf16[64,768]{1,0:T(8,128)(2,1)S(1)} collective-permute-done((bf16[64,768]{1,0:T(8,128)(2,1)S(1)}, bf16[64,768]{1,0:T(8,128)(2,1)S(1)}, u32[]{:S(2)}, u32[]{:S(2)}) %collective-permute-start.10) | collective-permute-done | bytes 98336 | tf_op jit(solution)/shard_map/ppermute | solution.py:60
  37.0 0.6 %collective-permute-start.11 = (bf16[64,768]{1,0:T(8,128)(2,1)S(1)}, bf16[64,768]{1,0:T(8,128)(2,1)S(1)}, u32[]{:S(2)}, u32[]{:S(2)}) collective-permute-start(bf16[64,768]{1,0:T(8,128)(2,1)S(1)} %add_convert_fusion), channel_id=1, source_target_pairs={{0,2},{1,3},{2,0},{3,1},{4,6},{5,7},{6,4},{7,5},{8,10},{9,11},{10,... | collective-permute-start | bytes 294920 | tf_op jit(solution)/shard_map/ppermute | solution.py:60
  37.8 4.1 %collective-permute-done.11 = bf16[64,768]{1,0:T(8,128)(2,1)S(1)} collective-permute-done((bf16[64,768]{1,0:T(8,128)(2,1)S(1)}, bf16[64,768]{1,0:T(8,128)(2,1)S(1)}, u32[]{:S(2)}, u32[]{:S(2)}) %collective-permute-start.11) | collective-permute-done | bytes 98336 | tf_op jit(solution)/shard_map/ppermute | solution.py:60
  42.1 0.6 %gather_fusion = f32[4,32,768]{2,1,0:T(8,128)S(1)} fusion(f32[2,32,768]{2,1,0:T(8,128)S(1)} %add.189, s32[1024]{0:T(1024)S(1)} %pad_clamp_fusion), kind=kCustom, calls=%fused_computation | custom fusion | bytes 786448 | tf_op jit(solution)/shard_map/jit(_take)/gather | solution.py:216
  42.7 0.8 %collective-permute-done.12 = f32[64,768]{1,0:T(8,128)S(1)} collective-permute-done((f32[64,768]{1,0:T(8,128)S(1)}, f32[64,768]{1,0:T(8,128)S(1)}, u32[]{:S(2)}, u32[]{:S(2)}) %collective-permute-start.12) | collective-permute-done | bytes 196640 | tf_op jit(solution)/shard_map/ppermute | solution.py:60
  43.5 0.2 fusion.155
  43.7 0.2 multiply_reduce_fusion
  43.9 2.7 %convolution_convert_fusion.2 = bf16[128,768]{1,0:T(8,128)(2,1)S(1)} fusion(bf16[768,768]{1,0:T(8,128)(2,1)S(1)} %copy-done, bf16[768,768]{1,0:T(8,128)(2,1)} %param.28, f32[128,768]{1,0:T(8,128)S(1)} %get-tuple-element.24, f32[768]{0:T(1024)S(1)} %copy-done.14, f32[128]{0:T(128)S(1)} %add_rsqrt_fusion, f32[128]{0:T(128)S(1)} %broadcast_multiply_fusion), kind=kOutput, calls=%fused_computation.6 | convolution fusion | flops 308871168 | bytes 2953216 | tf_op jit(solution)/shard_map/dot_general | solution.py:227
  46.6 0.2 copy.100
  47.0 0.2 collective-permute-start.13
  47.3 0.6 %collective-permute-start.14 = (bf16[128,192]{1,0:T(8,128)(2,1)S(1)}, bf16[128,192]{1,0:T(8,128)(2,1)S(1)}, u32[]{:S(2)}, u32[]{:S(2)}) collective-permute-start(bf16[128,192]{1,0:T(8,128)(2,1)S(1)} %select_bitcast_fusion.1), channel_id=1, source_target_pairs={{0,2},{1,3},{2,0},{3,1},{4,6},{5,7},{6,4},{7,5},{8,10},{9,11},{10,... | collective-permute-start | bytes 147464 | tf_op jit(solution)/shard_map/ppermute | solution.py:60
  48.1 1.2 %collective-permute-start.15 = (bf16[128,192]{1,0:T(8,128)(2,1)S(1)}, bf16[128,192]{1,0:T(8,128)(2,1)S(1)}, u32[]{:S(2)}, u32[]{:S(2)}) collective-permute-start(bf16[128,192]{1,0:T(8,128)(2,1)S(1)} %select_bitcast_fusion), channel_id=1, source_target_pairs={{0,3},{1,2},{2,1},{3,0},{4,7},{5,6},{6,5},{7,4},{8,11},{9,10},{10,... | collective-permute-start | bytes 147464 | tf_op jit(solution)/shard_map/ppermute | solution.py:60
  49.7 2.6 %collective-permute-done.14 = bf16[128,192]{1,0:T(8,128)(2,1)S(1)} collective-permute-done((bf16[128,192]{1,0:T(8,128)(2,1)S(1)}, bf16[128,192]{1,0:T(8,128)(2,1)S(1)}, u32[]{:S(2)}, u32[]{:S(2)}) %collective-permute-start.14) | collective-permute-done | bytes 49184 | tf_op jit(solution)/shard_map/ppermute | solution.py:60
  52.3 0.3 collective-permute-done.15
  52.7 0.2 fusion.11
  52.9 0.6 %copy.108 = bf16[2,32,192]{2,1,0:T(8,128)(2,1)} copy(bf16[2,32,192]{2,0,1:T(2,128)(2,1)S(1)} %fusion.11) | data formatting | bytes 49152 | tf_op jit(solution)/shard_map/convert_element_type | solution.py:240
  (124 shorter events, 4.4 us)
Async XLA Ops:
  0.0 43.9 %copy-start = (bf16[768,768]{1,0:T(8,128)(2,1)S(1)}, bf16[768,768]{1,0:T(8,128)(2,1)}, u32[]{:S(2)}) copy-start(bf16[768,768]{1,0:T(8,128)(2,1)} %param.29) | copy-start | bytes 3538948
  0.0 1.5 %collective-permute-start = (bf16[64,192]{1,0:T(8,128)(2,1)}, bf16[64,192]{1,0:T(8,128)(2,1)S(1)}, u32[]{:S(2)}, u32[]{:S(2)}) collective-permute-start(bf16[64,192]{1,0:T(8,128)(2,1)} %param.16), channel_id=1, source_target_pairs={{0,1},{1,0},{2,3},{3,2},{4,5},{5,4},{6,7},{7,6},{8,9},{9,8},{10,11... | collective-permute-start | bytes 73736 | tf_op jit(solution)/shard_map/ppermute | solution.py:60
  2.3 6.9 %copy-start.7 = (f32[768]{0:T(1024)S(1)}, f32[768]{0:T(1024)}, u32[]{:S(2)}) copy-start(f32[768]{0:T(1024)} %param.19) | copy-start | bytes 9220
  2.3 10.0 %collective-permute-start.1 = (bf16[2,64,192]{2,1,0:T(8,128)(2,1)S(1)}, bf16[2,64,192]{2,1,0:T(8,128)(2,1)S(1)}, u32[]{:S(2)}, u32[]{:S(2)}) collective-permute-start(bf16[2,64,192]{2,1,0:T(8,128)(2,1)S(1)} %pad_maximum_fusion.6), channel_id=1, source_target_pairs={{0,2},{1,3},{2,0},{3,1},{4,6},{5,7},{6,4},{7,5},{8,10},{9,11},{10,... | collective-permute-start | bytes 147464 | tf_op jit(solution)/shard_map/ppermute | solution.py:60
  9.2 2.4 %copy-start.8 = (f32[768]{0:T(1024)S(1)}, f32[768]{0:T(1024)}, u32[]{:S(2)}) copy-start(f32[768]{0:T(1024)} %param.21) | copy-start | bytes 9220
  13.2 1.0 %copy-start.3 = (bf16[192,768]{1,0:T(8,128)(2,1)S(1)}, bf16[192,768]{1,0:T(8,128)(2,1)}, u32[]{:S(2)}) copy-start(bf16[192,768]{1,0:T(8,128)(2,1)} %param.24) | copy-start | bytes 884740
  14.4 6.2 %collective-permute-start.5 = (bf16[32,768]{1,0:T(8,128)(2,1)S(1)}, bf16[32,768]{1,0:T(8,128)(2,1)S(1)}, u32[]{:S(2)}, u32[]{:S(2)}) collective-permute-start(bf16[32,768]{1,0:T(8,128)(2,1)S(1)} %broadcast_select_fusion.9), channel_id=1, source_target_pairs={{0,1},{1,0},{2,3},{3,2},{4,5},{5,4},{6,7},{7,6},{8,9},{9,8},{10,11... | collective-permute-start | bytes 147464 | tf_op jit(solution)/shard_map/ppermute | solution.py:60
  14.5 6.8 %collective-permute-start.2 = (f32[12420]{0:T(1024)S(1)}, f32[12420]{0:T(1024)S(1)}, u32[]{:S(2)}, u32[]{:S(2)}) collective-permute-start(f32[12420]{0:T(1024)S(1)} %concatenate.25), channel_id=1, source_target_pairs={{0,4},{4,8},{8,12},{12,0},{1,5},{5,9},{9,13},{13,1},{2,6},{6,10},{... | collective-permute-start | bytes 149048 | tf_op jit(solution)/shard_map/ppermute | solution.py:37
  16.1 6.9 %collective-permute-start.3 = (f32[12420]{0:T(1024)S(1)}, f32[12420]{0:T(1024)S(1)}, u32[]{:S(2)}, u32[]{:S(2)}) collective-permute-start(f32[12420]{0:T(1024)S(1)} %concatenate.25), channel_id=1, source_target_pairs={{0,8},{4,12},{8,0},{12,4},{1,9},{5,13},{9,1},{13,5},{2,10},{6,14},... | collective-permute-start | bytes 149048 | tf_op jit(solution)/shard_map/ppermute | solution.py:37
  18.7 4.6 %collective-permute-start.4 = (f32[12420]{0:T(1024)S(1)}, f32[12420]{0:T(1024)S(1)}, u32[]{:S(2)}, u32[]{:S(2)}) collective-permute-start(f32[12420]{0:T(1024)S(1)} %concatenate.25), channel_id=1, source_target_pairs={{0,12},{4,0},{8,4},{12,8},{1,13},{5,1},{9,5},{13,9},{2,14},{6,2},{... | collective-permute-start | bytes 149048 | tf_op jit(solution)/shard_map/ppermute | solution.py:37
  20.7 5.6 %collective-permute-start.6 = (bf16[32,768]{1,0:T(8,128)(2,1)S(1)}, bf16[32,768]{1,0:T(8,128)(2,1)S(1)}, u32[]{:S(2)}, u32[]{:S(2)}) collective-permute-start(bf16[32,768]{1,0:T(8,128)(2,1)S(1)} %add_convert_fusion.1), channel_id=1, source_target_pairs={{0,2},{1,3},{2,0},{3,1},{4,6},{5,7},{6,4},{7,5},{8,10},{9,11},{10,... | collective-permute-start | bytes 147464 | tf_op jit(solution)/shard_map/ppermute | solution.py:60
  24.0 4.1 %copy-start.5 = (s32[16]{0:T(128)}, s32[16]{0:T(128)S(1)}, u32[]{:S(2)}) copy-start(s32[16]{0:T(128)S(1)} %add_reduce_fusion) | copy-start | bytes 196
  24.3 0.8 %copy-start.10 = (pred[16]{0:T(512)(128)(4,1)}, pred[16]{0:T(512)(128)(4,1)S(1)}, u32[]{:S(2)}) copy-start(pred[16]{0:T(512)(128)(4,1)S(1)} %fusion.106) | copy-start | bytes 52
  24.4 3.7 %copy-start.12 = (s32[4]{0:T(128)}, s32[4]{0:T(128)S(1)}, u32[]{:S(2)}) copy-start(s32[4]{0:T(128)S(1)} %get-tuple-element.21) | copy-start | bytes 52
  25.5 1.3 %collective-permute-start.8 = (bf16[128,192]{1,0:T(8,128)(2,1)S(1)}, bf16[128,192]{1,0:T(8,128)(2,1)S(1)}, u32[]{:S(2)}, u32[]{:S(2)}) collective-permute-start(bf16[128,192]{1,0:T(8,128)(2,1)S(1)} %reshape.449), channel_id=1, source_target_pairs={{0,1},{1,0},{2,3},{3,2},{4,5},{5,4},{6,7},{7,6},{8,9},{9,8},{10,11... | collective-permute-start | bytes 147464 | tf_op jit(solution)/shard_map/ppermute | solution.py:60
  26.3 1.8 %collective-permute-start.7 = (f32[32,768]{1,0:T(8,128)S(1)}, f32[32,768]{1,0:T(8,128)S(1)}, u32[]{:S(2)}, u32[]{:S(2)}) collective-permute-start(f32[32,768]{1,0:T(8,128)S(1)} %convert_add_fusion.1), channel_id=1, source_target_pairs={{0,1},{1,0},{2,3},{3,2},{4,5},{5,4},{6,7},{7,6},{8,9},{9,8},{10,11... | collective-permute-start | bytes 294920 | tf_op jit(solution)/shard_map/ppermute | solution.py:60
  26.8 2.0 %copy-start.1 = (bf16[768,192]{0,1:T(8,128)(2,1)S(1)}, bf16[768,192]{0,1:T(8,128)(2,1)}, u32[]{:S(2)}) copy-start(bf16[768,192]{0,1:T(8,128)(2,1)} %param.25) | copy-start | bytes 884740
  27.5 5.8 %collective-permute-start.9 = (bf16[2,128,192]{2,1,0:T(8,128)(2,1)}, bf16[2,128,192]{2,1,0:T(8,128)(2,1)S(1)}, u32[]{:S(2)}, u32[]{:S(2)}) collective-permute-start(bf16[2,128,192]{2,1,0:T(8,128)(2,1)} %pad_maximum_fusion.4), channel_id=1, source_target_pairs={{0,2},{1,3},{2,0},{3,1},{4,6},{5,7},{6,4},{7,5},{8,10},{9,11},{10,... | collective-permute-start | bytes 294920 | tf_op jit(solution)/shard_map/ppermute | solution.py:60
  28.6 5.1 %copy-start.9 = (f32[4,192]{1,0:T(4,128)S(1)}, f32[4,192]{1,0:T(4,128)}, u32[]{:S(2)}) copy-start(f32[4,192]{1,0:T(4,128)} %mul.142) | copy-start | bytes 9220
  34.3 1.0 %copy-start.2 = (bf16[192,768]{1,0:T(8,128)(2,1)S(1)}, bf16[192,768]{1,0:T(8,128)(2,1)}, u32[]{:S(2)}) copy-start(bf16[192,768]{1,0:T(8,128)(2,1)} %param.27) | copy-start | bytes 884740
  34.8 0.9 %copy-start.4 = (f32[16,32]{1,0:T(8,128)S(1)}, f32[16,32]{1,0:T(8,128)}, u32[]{:S(2)}) copy-start(f32[16,32]{1,0:T(8,128)} %reshape.454) | copy-start | bytes 6148
  34.8 0.9 %copy-start.6 = (s32[16]{0:T(128)S(1)}, s32[16]{0:T(128)}, u32[]{:S(2)}) copy-start(s32[16]{0:T(128)} %copy-done.5) | copy-start | bytes 196
  34.8 0.9 %copy-start.11 = (pred[16]{0:T(512)(128)(4,1)S(1)}, pred[16]{0:T(512)(128)(4,1)}, u32[]{:S(2)}) copy-start(pred[16]{0:T(512)(128)(4,1)} %copy-done.10) | copy-start | bytes 52
  34.8 2.8 %copy-start.13 = (s32[4]{0:T(128)S(1)}, s32[4]{0:T(128)}, u32[]{:S(2)}) copy-start(s32[4]{0:T(128)} %copy-done.12) | copy-start | bytes 52
  34.8 2.8 %copy-start.16 = (pred[4]{0:T(512)(128)(4,1)S(1)}, pred[4]{0:T(512)(128)(4,1)}, u32[]{:S(2)}) copy-start(pred[4]{0:T(512)(128)(4,1)} %get-tuple-element.25) | copy-start | bytes 16
  35.6 1.4 %collective-permute-start.10 = (bf16[64,768]{1,0:T(8,128)(2,1)S(1)}, bf16[64,768]{1,0:T(8,128)(2,1)S(1)}, u32[]{:S(2)}, u32[]{:S(2)}) collective-permute-start(bf16[64,768]{1,0:T(8,128)(2,1)S(1)} %broadcast_select_fusion.4), channel_id=1, source_target_pairs={{0,1},{1,0},{2,3},{3,2},{4,5},{5,4},{6,7},{7,6},{8,9},{9,8},{10,11... | collective-permute-start | bytes 294920 | tf_op jit(solution)/shard_map/ppermute | solution.py:60
  37.0 4.9 %collective-permute-start.11 = (bf16[64,768]{1,0:T(8,128)(2,1)S(1)}, bf16[64,768]{1,0:T(8,128)(2,1)S(1)}, u32[]{:S(2)}, u32[]{:S(2)}) collective-permute-start(bf16[64,768]{1,0:T(8,128)(2,1)S(1)} %add_convert_fusion), channel_id=1, source_target_pairs={{0,2},{1,3},{2,0},{3,1},{4,6},{5,7},{6,4},{7,5},{8,10},{9,11},{10,... | collective-permute-start | bytes 294920 | tf_op jit(solution)/shard_map/ppermute | solution.py:60
  41.9 1.5 %collective-permute-start.12 = (f32[64,768]{1,0:T(8,128)S(1)}, f32[64,768]{1,0:T(8,128)S(1)}, u32[]{:S(2)}, u32[]{:S(2)}) collective-permute-start(f32[64,768]{1,0:T(8,128)S(1)} %convert_add_fusion), channel_id=1, source_target_pairs={{0,1},{1,0},{2,3},{3,2},{4,5},{5,4},{6,7},{7,6},{8,9},{9,8},{10,11... | collective-permute-start | bytes 589832 | tf_op jit(solution)/shard_map/ppermute | solution.py:60
  42.6 1.2 %copy-start.14 = (f32[768]{0:T(1024)S(1)}, f32[768]{0:T(1024)}, u32[]{:S(2)}) copy-start(f32[768]{0:T(1024)} %param.22) | copy-start | bytes 9220
  46.6 2.7 %copy-start.15 = (s32[4]{0:T(128)S(1)}, s32[4]{0:T(128)}, u32[]{:S(2)}) copy-start(s32[4]{0:T(128)} %get-tuple-element.26) | copy-start | bytes 52
  47.0 2.7 %collective-permute-start.13 = (bf16[128,192]{1,0:T(8,128)(2,1)S(1)}, bf16[128,192]{1,0:T(8,128)(2,1)S(1)}, u32[]{:S(2)}, u32[]{:S(2)}) collective-permute-start(bf16[128,192]{1,0:T(8,128)(2,1)S(1)} %select_bitcast_fusion.2), channel_id=1, source_target_pairs={{0,1},{1,0},{2,3},{3,2},{4,5},{5,4},{6,7},{7,6},{8,9},{9,8},{10,11... | collective-permute-start | bytes 147464 | tf_op jit(solution)/shard_map/ppermute | solution.py:60
  47.3 5.0 %collective-permute-start.14 = (bf16[128,192]{1,0:T(8,128)(2,1)S(1)}, bf16[128,192]{1,0:T(8,128)(2,1)S(1)}, u32[]{:S(2)}, u32[]{:S(2)}) collective-permute-start(bf16[128,192]{1,0:T(8,128)(2,1)S(1)} %select_bitcast_fusion.1), channel_id=1, source_target_pairs={{0,2},{1,3},{2,0},{3,1},{4,6},{5,7},{6,4},{7,5},{8,10},{9,11},{10,... | collective-permute-start | bytes 147464 | tf_op jit(solution)/shard_map/ppermute | solution.py:60
  48.1 4.5 %collective-permute-start.15 = (bf16[128,192]{1,0:T(8,128)(2,1)S(1)}, bf16[128,192]{1,0:T(8,128)(2,1)S(1)}, u32[]{:S(2)}, u32[]{:S(2)}) collective-permute-start(bf16[128,192]{1,0:T(8,128)(2,1)S(1)} %select_bitcast_fusion), channel_id=1, source_target_pairs={{0,3},{1,2},{2,1},{3,0},{4,7},{5,6},{6,5},{7,4},{8,11},{9,10},{10,... | collective-permute-start | bytes 147464 | tf_op jit(solution)/shard_map/ppermute | solution.py:60

commit v9 on v5

--- a/solution.py
+++ b/solution.py
@@ -141,6 +141,8 @@
             confidence.reshape(-1),
         ]
     )
+    own_tok = mp_gather_cols(tokens.reshape(img_dev, TOKS, quarter))
+    payload, own_tok = lax.optimization_barrier((payload, own_tok))
     table = pairs_gather(payload, owners_n)
     cut_tok = img_dev * TOKS * quarter
     cut_ids = cut_tok + views_n
@@ -161,7 +163,6 @@
     far = (at[:, None] == jnp.arange(owners_n * img_dev)[None, :]).astype(jnp.bfloat16)
     context_q = pick_rows(far, all_tok).reshape(views_n, TOKS, quarter)
 
-    own_tok = mp_gather_cols(tokens.reshape(img_dev, TOKS, quarter))
     width = own_tok.shape[2]
     img_rows = img_dev * TOKS
     begin = own_tok.astype(jnp.float32).reshape(img_rows, width)

time: 47.7 us -> 51.8 us (1.086)
  waiting for transfers between devices: 13.5 us -> 15.6 us
  matrix products: 6.14 us -> 7.29 us
  starting transfers between devices: 15.3 us -> 15.9 us
    ppermute x3, waiting for transfers between devices: 1.6 us -> 3.54 us  [pairs_shift(): lax.ppermute(values, 'pairs', [(i, (i + step) % owners_n) for i in range(...]
    ppermute x13, starting transfers between devices: 9.55 us -> 11.1 us  [swap(): return lax.ppermute(values, 'mp', pairs)]
    dot_general x1, matrix products: 0.43 us -> 1.62 us  [per_device(): jnp.einsum('rd,kdc->krc', normed, self_qkv, preferred_element_type=jnp.fl...]
    select_n x4 -> x3, other arithmetic: 2.08 us -> 1.15 us  [mp_gather_cols(): jnp.where(core == 0, jnp.concatenate([part, got], axis=2), jnp.concatenat...]
    ppermute x3, starting transfers between devices: 5.71 us -> 4.79 us  [pairs_shift(): lax.ppermute(values, 'pairs', [(i, (i + step) % owners_n) for i in range(...]
    convert_element_type x0 -> x2, other arithmetic: none -> 0.89 us  [layer_norm(): return (center * lax.rsqrt(spread + EPSILON) * gain).astype(jnp.bfloat16)]
  transfers between devices with their start and end apart: 16 -> 16, of which waited for: 7 -> 9; matrix products, arithmetic and copies ran while one was open for 23% -> 14% of each run, Pallas kernels for 0% -> 0%
where the time goes in v9:
time: 51.8 us; the launch traced here: 51.4 us
  starting transfers between devices  15.9 us (31%)
  waiting for transfers between devices  15.6 us (30%)
  matrix products  7.29 us (14%)
  local copies, waits for them, and re-layouts  6.74 us (13%)
  other arithmetic  5.13 us (10%)
  between operations  0.67 us (1%)
    ppermute x13, waiting for transfers between devices, swap(): return lax.ppermute(values, 'mp', pairs)  12.1 us
    ppermute x13, starting transfers between devices, swap(): return lax.ppermute(values, 'mp', pairs)  11.1 us
    ppermute x3, starting transfers between devices, pairs_shift(): lax.ppermute(values, 'pairs', [(i, (i + step) % owners_n) for i in range(...  4.79 us
    ppermute x3, waiting for transfers between devices, pairs_shift(): lax.ppermute(values, 'pairs', [(i, (i + step) % owners_n) for i in range(...  3.54 us
    dot_general x1, matrix products, per_device(): jnp.dot(hidden.astype(jnp.bfloat16), mlp_down, preferred_element_type=jnp...  2.72 us
    dot_general x1, matrix products, per_device(): jnp.einsum('rd,kdc->krc', normed, self_qkv, preferred_element_type=jnp.fl...  1.62 us
    select_n x3, other arithmetic, mp_gather_cols(): jnp.where(core == 0, jnp.concatenate([part, got], axis=2), jnp.concatenat...  1.15 us
  transfers between devices with their start and end apart: 16, of which 9 were waited for; matrix products, arithmetic and copies ran while one was open for 14% of the time, Pallas kernels for 0%

profile of v9, /device:TPU:0, one launch (start us, length us, event | category | flops | bytes accessed | tf_op | source)
XLA Modules:
  0.0 51.4 jit_solution(250167517903881135)
XLA Ops:
  0.0 0.5 collective-permute-start
  0.5 1.1 %collective-permute-done = bf16[2,32,192]{2,1,0:T(8,128)(2,1)S(1)} collective-permute-done((bf16[2,32,192]{2,1,0:T(8,128)(2,1)}, bf16[2,32,192]{2,1,0:T(8,128)(2,1)S(1)}, u32[]{:S(2)}, u32[]{:S(2)}) %collective-permute-start) | collective-permute-done | bytes 24608 | tf_op jit(solution)/shard_map/ppermute | solution.py:41
  1.5 0.9 %maximum_select_fusion.6 = bf16[2,32,384]{2,1,0:T(8,128)(2,1)S(1)} fusion(bf16[2,32,192]{2,1,0:T(8,128)(2,1)S(1)} %collective-permute-done, bf16[2,32,192]{2,1,0:T(8,128)(2,1)} %bitcast.86, pred[]{:T(512)S(6)} %eq.96), kind=kLoop, calls=%fused_computation.141 | loop fusion | flops 221184 | bytes 98305 | tf_op jit(solution)/shard_map/jit(_where)/select_n | solution.py:88
  2.5 2.9 %collective-permute-start.1 = (bf16[2,32,384]{2,1,0:T(8,128)(2,1)S(1)}, bf16[2,32,384]{2,1,0:T(8,128)(2,1)S(1)}, u32[]{:S(2)}, u32[]{:S(2)}) collective-permute-start(bf16[2,32,384]{2,1,0:T(8,128)(2,1)S(1)} %maximum_select_fusion.6), channel_id=1, source_target_pairs={{0,2},{1,3},{2,0},{3,1},{4,6},{5,7},{6,4},{7,5},{8,10},{9,11},{10,... | collective-permute-start | bytes 147464 | tf_op jit(solution)/shard_map/ppermute | solution.py:41
  5.4 0.8 %reshape.569 = f32[12288]{0:T(1024)S(1)} reshape(bf16[64,192]{1,0:T(8,128)(2,1)} %param.16) | data formatting | bytes 73728 | tf_op jit(solution)/shard_map/reshape | solution.py:139
  6.2 0.8 %reshape.491 = f32[128]{0:T(128)S(1)} reshape(f32[2,64]{1,0:T(2,128)} %param.18) | data formatting | bytes 1024 | tf_op jit(solution)/shard_map/reshape | solution.py:141
  7.0 0.7 %convert_element_type.156 = f32[2,2]{1,0:T(2,128)S(1)} convert(s32[2,2]{1,0:T(2,128)} %param.17) | non-fusion elementwise | flops 4 | bytes 32 | tf_op jit(solution)/shard_map/convert_element_type | solution.py:140
  8.0 0.2 fusion.33
  8.3 0.8 %fusion.36 = bf16[64,768]{1,0:T(8,128)(2,1)S(1)} fusion(bf16[2,32,768]{2,1,0:T(8,128)(2,1)S(1)} %maximum_select_fusion.3, f32[768]{0:T(1024)} %param.19, f32[64]{0:T(128)S(1)} %rsqrt.42, f32[64]{0:T(128)S(1)} %div.99), kind=kLoop, calls=%fused_computation.75 | loop fusion | flops 245760 | bytes 200192 | tf_op jit(solution)/shard_map/convert_element_type | solution.py:16
  9.1 1.6 %fusion.6 = bf16[3,64,192]{2,1,0:T(8,128)(2,1)S(1)} fusion(bf16[3,768,192]{1,2,0:T(8,128)(2,1)} %param.23, bf16[64,768]{1,0:T(8,128)(2,1)S(1)} %fusion.36), kind=kOutput, calls=%fused_computation.15 | convolution fusion | flops 56659968 | bytes 1056768 | tf_op jit(solution)/shard_map/rd,kdc->krc/dot_general | solution.py:170
  10.9 0.2 fusion.153
  11.1 0.1 convolution_multiply_fusion.1
  11.4 0.2 fusion.9
  11.8 0.2 convolution_convert_fusion.6
  12.1 3.8 %collective-permute-start.4 = (f32[12420]{0:T(1024)S(1)}, f32[12420]{0:T(1024)S(1)}, u32[]{:S(2)}, u32[]{:S(2)}) collective-permute-start(f32[12420]{0:T(1024)S(1)} %concatenate.53), channel_id=1, source_target_pairs={{0,12},{4,0},{8,4},{12,8},{1,13},{5,1},{9,5},{13,9},{2,14},{6,2},{... | collective-permute-start | bytes 149048 | tf_op jit(solution)/shard_map/ppermute | solution.py:37
  15.9 1.0 %collective-permute-start.2 = (f32[12420]{0:T(1024)S(1)}, f32[12420]{0:T(1024)S(1)}, u32[]{:S(2)}, u32[]{:S(2)}) collective-permute-start(f32[12420]{0:T(1024)S(1)} %concatenate.53), channel_id=1, source_target_pairs={{0,4},{4,8},{8,12},{12,0},{1,5},{5,9},{9,13},{13,1},{2,6},{6,10},{... | collective-permute-start | bytes 149048 | tf_op jit(solution)/shard_map/ppermute | solution.py:37
  16.9 1.6 %collective-permute-start.6 = (bf16[32,768]{1,0:T(8,128)(2,1)S(1)}, bf16[32,768]{1,0:T(8,128)(2,1)S(1)}, u32[]{:S(2)}, u32[]{:S(2)}) collective-permute-start(bf16[32,768]{1,0:T(8,128)(2,1)S(1)} %add_convert_fusion.1), channel_id=1, source_target_pairs={{0,2},{1,3},{2,0},{3,1},{4,6},{5,7},{6,4},{7,5},{8,10},{9,11},{10,... | collective-permute-start | bytes 147464 | tf_op jit(solution)/shard_map/ppermute | solution.py:41
  18.5 3.5 %collective-permute-done.3 = f32[12420]{0:T(1024)S(1)} collective-permute-done((f32[12420]{0:T(1024)S(1)}, f32[12420]{0:T(1024)S(1)}, u32[]{:S(2)}, u32[]{:S(2)}) %collective-permute-start.3) | collective-permute-done | bytes 49712 | tf_op jit(solution)/shard_map/ppermute | solution.py:37
  22.2 0.2 pad_maximum_fusion
  23.0 0.1 add_reduce_fusion
  23.1 0.2 select_reduce_fusion.1
  23.3 0.2 convolution_convert_fusion.1
  23.6 0.1 reshape.499
  23.7 0.1 concatenate.60
  24.0 0.6 %collective-permute-start.7 = (f32[32,768]{1,0:T(8,128)S(1)}, f32[32,768]{1,0:T(8,128)S(1)}, u32[]{:S(2)}, u32[]{:S(2)}) collective-permute-start(f32[32,768]{1,0:T(8,128)S(1)} %convert_add_fusion.2), channel_id=1, source_target_pairs={{0,1},{1,0},{2,3},{3,2},{4,5},{5,4},{6,7},{7,6},{8,9},{9,8},{10,11... | collective-permute-start | bytes 294920 | tf_op jit(solution)/shard_map/ppermute | solution.py:41
  24.6 0.6 %collective-permute-done.8 = bf16[4,32,192]{2,1,0:T(8,128)(2,1)S(1)} collective-permute-done((bf16[4,32,192]{2,1,0:T(8,128)(2,1)S(1)}, bf16[4,32,192]{2,1,0:T(8,128)(2,1)S(1)}, u32[]{:S(2)}, u32[]{:S(2)}) %collective-permute-start.8) | collective-permute-done | bytes 49184 | tf_op jit(solution)/shard_map/ppermute | solution.py:41
  25.2 0.1 maximum_select_fusion.5
  25.3 1.6 %collective-permute-start.9 = (bf16[4,32,384]{2,1,0:T(8,128)(2,1)S(1)}, bf16[4,32,384]{2,1,0:T(8,128)(2,1)S(1)}, u32[]{:S(2)}, u32[]{:S(2)}) collective-permute-start(bf16[4,32,384]{2,1,0:T(8,128)(2,1)S(1)} %maximum_select_fusion.5), channel_id=1, source_target_pairs={{0,2},{1,3},{2,0},{3,1},{4,6},{5,7},{6,4},{7,5},{8,10},{9,11},{10,... | collective-permute-start | bytes 294920 | tf_op jit(solution)/shard_map/ppermute | solution.py:41
  26.9 0.1 maximum_select_fusion.4
  27.3 0.2 multiply_reduce_fusion.1
  27.7 0.2 convolution_convert_fusion.8
  27.9 0.1 reshape_reshape.3
  28.0 0.2 convolution_convert_fusion
  28.2 0.1 reshape_reshape_reshape.3
  28.4 1.8 %collective-permute-done.9 = bf16[4,32,384]{2,1,0:T(8,128)(2,1)S(1)} collective-permute-done((bf16[4,32,384]{2,1,0:T(8,128)(2,1)S(1)}, bf16[4,32,384]{2,1,0:T(8,128)(2,1)S(1)}, u32[]{:S(2)}, u32[]{:S(2)}) %collective-permute-start.9) | collective-permute-done | bytes 98336 | tf_op jit(solution)/shard_map/ppermute | solution.py:41
  30.2 0.1 convert_reduce_fusion
  30.5 0.2 fusion.11
  30.8 0.4 fusion.23
  31.2 0.1 reshape.615
  31.3 0.1 reshape.614
  31.5 0.2 convolution_multiply_fusion
  31.8 0.3 fusion.5
  32.2 0.1 reshape.500
  32.3 0.1 copy-done.1
  32.4 0.2 convolution_convert_fusion.3
  32.9 1.1 %collective-permute-done.10 = bf16[64,768]{1,0:T(8,128)(2,1)S(1)} collective-permute-done((bf16[64,768]{1,0:T(8,128)(2,1)S(1)}, bf16[64,768]{1,0:T(8,128)(2,1)S(1)}, u32[]{:S(2)}, u32[]{:S(2)}) %collective-permute-start.10) | collective-permute-done | bytes 98336 | tf_op jit(solution)/shard_map/ppermute | solution.py:41
  34.1 1.6 %collective-permute-start.11 = (bf16[64,768]{1,0:T(8,128)(2,1)S(1)}, bf16[64,768]{1,0:T(8,128)(2,1)S(1)}, u32[]{:S(2)}, u32[]{:S(2)}) collective-permute-start(bf16[64,768]{1,0:T(8,128)(2,1)S(1)} %add_convert_fusion), channel_id=1, source_target_pairs={{0,2},{1,3},{2,0},{3,1},{4,6},{5,7},{6,4},{7,5},{8,10},{9,11},{10,... | collective-permute-start | bytes 294920 | tf_op jit(solution)/shard_map/ppermute | solution.py:41
  35.6 3.4 %collective-permute-done.11 = bf16[64,768]{1,0:T(8,128)(2,1)S(1)} collective-permute-done((bf16[64,768]{1,0:T(8,128)(2,1)S(1)}, bf16[64,768]{1,0:T(8,128)(2,1)S(1)}, u32[]{:S(2)}, u32[]{:S(2)}) %collective-permute-start.11) | collective-permute-done | bytes 98336 | tf_op jit(solution)/shard_map/ppermute | solution.py:41
  39.1 0.1 fusion.147
  39.2 0.6 %gather_fusion = f32[4,32,768]{2,1,0:T(8,128)S(1)} fusion(f32[2,32,768]{2,1,0:T(8,128)S(1)} %get-tuple-element.28, s32[1024]{0:T(1024)S(1)} %pad_clamp_fusion), kind=kCustom, calls=%fused_computation | custom fusion | bytes 786448 | tf_op jit(solution)/shard_map/jit(_take)/gather | solution.py:191
  39.8 0.7 %collective-permute-done.12 = f32[64,768]{1,0:T(8,128)S(1)} collective-permute-done((f32[64,768]{1,0:T(8,128)S(1)}, f32[64,768]{1,0:T(8,128)S(1)}, u32[]{:S(2)}, u32[]{:S(2)}) %collective-permute-start.12) | collective-permute-done | bytes 196640 | tf_op jit(solution)/shard_map/ppermute | solution.py:41
  40.6 0.2 fusion.149
  40.8 0.2 multiply_reduce_fusion
  41.0 2.7 %convolution_convert_fusion.2 = bf16[128,768]{1,0:T(8,128)(2,1)S(1)} fusion(bf16[768,768]{1,0:T(8,128)(2,1)S(1)} %copy-done, bf16[768,768]{1,0:T(8,128)(2,1)} %param.28, f32[128,768]{1,0:T(8,128)S(1)} %get-tuple-element.24, f32[768]{0:T(1024)S(1)} %copy-done.7, f32[128]{0:T(128)S(1)} %add_rsqrt_fusion.3, f32[128]{0:T(128)S(1)} %broadcast_multiply_fusion.3), kind=kOutput, calls=%fused_computation.6 | convolution fusion | flops 308871168 | bytes 2953216 | tf_op jit(solution)/shard_map/dot_general | solution.py:202
  43.7 0.2 copy.78
  44.3 1.3 %collective-permute-start.15 = (bf16[128,192]{1,0:T(8,128)(2,1)S(1)}, bf16[128,192]{1,0:T(8,128)(2,1)S(1)}, u32[]{:S(2)}, u32[]{:S(2)}) collective-permute-start(bf16[128,192]{1,0:T(8,128)(2,1)S(1)} %select_bitcast_fusion), channel_id=1, source_target_pairs={{0,3},{1,2},{2,1},{3,0},{4,7},{5,6},{6,5},{7,4},{8,11},{9,10},{10,... | collective-permute-start | bytes 147464 | tf_op jit(solution)/shard_map/ppermute | solution.py:41
  45.6 0.4 collective-permute-start.13
  46.1 0.6 %collective-permute-start.14 = (bf16[128,192]{1,0:T(8,128)(2,1)S(1)}, bf16[128,192]{1,0:T(8,128)(2,1)S(1)}, u32[]{:S(2)}, u32[]{:S(2)}) collective-permute-start(bf16[128,192]{1,0:T(8,128)(2,1)S(1)} %select_bitcast_fusion.1), channel_id=1, source_target_pairs={{0,2},{1,3},{2,0},{3,1},{4,6},{5,7},{6,4},{7,5},{8,10},{9,11},{10,... | collective-permute-start | bytes 147464 | tf_op jit(solution)/shard_map/ppermute | solution.py:41
  46.7 0.1 convolution_maximum_fusion
  47.1 1.4 %collective-permute-done.15 = bf16[128,192]{1,0:T(8,128)(2,1)S(1)} collective-permute-done((bf16[128,192]{1,0:T(8,128)(2,1)S(1)}, bf16[128,192]{1,0:T(8,128)(2,1)S(1)}, u32[]{:S(2)}, u32[]{:S(2)}) %collective-permute-start.15) | collective-permute-done | bytes 49184 | tf_op jit(solution)/shard_map/ppermute | solution.py:41
  48.4 1.9 %collective-permute-done.14 = bf16[128,192]{1,0:T(8,128)(2,1)S(1)} collective-permute-done((bf16[128,192]{1,0:T(8,128)(2,1)S(1)}, bf16[128,192]{1,0:T(8,128)(2,1)S(1)}, u32[]{:S(2)}, u32[]{:S(2)}) %collective-permute-start.14) | collective-permute-done | bytes 49184 | tf_op jit(solution)/shard_map/ppermute | solution.py:41
  50.4 0.1 add_add_fusion
  50.5 0.2 fusion.8
  50.7 0.6 %copy.86 = bf16[2,32,192]{2,1,0:T(8,128)(2,1)} copy(bf16[2,32,192]{2,0,1:T(2,128)(2,1)S(1)} %fusion.8) | data formatting | bytes 49152 | tf_op jit(solution)/shard_map/convert_element_type | solution.py:215
  (100 shorter events, 3.9 us)
Async XLA Ops:
  0.0 41.0 %copy-start = (bf16[768,768]{1,0:T(8,128)(2,1)S(1)}, bf16[768,768]{1,0:T(8,128)(2,1)}, u32[]{:S(2)}) copy-start(bf16[768,768]{1,0:T(8,128)(2,1)} %param.29) | copy-start | bytes 3538948
  0.0 1.5 %collective-permute-start = (bf16[2,32,192]{2,1,0:T(8,128)(2,1)}, bf16[2,32,192]{2,1,0:T(8,128)(2,1)S(1)}, u32[]{:S(2)}, u32[]{:S(2)}) collective-permute-start(bf16[2,32,192]{2,1,0:T(8,128)(2,1)} %bitcast.85), channel_id=1, source_target_pairs={{0,1},{1,0},{2,3},{3,2},{4,5},{5,4},{6,7},{7,6},{8,9},{9,8},{10,11... | collective-permute-start | bytes 73736 | tf_op jit(solution)/shard_map/ppermute | solution.py:41
  2.5 5.4 %collective-permute-start.1 = (bf16[2,32,384]{2,1,0:T(8,128)(2,1)S(1)}, bf16[2,32,384]{2,1,0:T(8,128)(2,1)S(1)}, u32[]{:S(2)}, u32[]{:S(2)}) collective-permute-start(bf16[2,32,384]{2,1,0:T(8,128)(2,1)S(1)} %maximum_select_fusion.6), channel_id=1, source_target_pairs={{0,2},{1,3},{2,0},{3,1},{4,6},{5,7},{6,4},{7,5},{8,10},{9,11},{10,... | collective-permute-start | bytes 147464 | tf_op jit(solution)/shard_map/ppermute | solution.py:41
  9.1 2.6 %copy-start.2 = (bf16[192,768]{1,0:T(8,128)(2,1)S(1)}, bf16[192,768]{1,0:T(8,128)(2,1)}, u32[]{:S(2)}) copy-start(bf16[192,768]{1,0:T(8,128)(2,1)} %param.24) | copy-start | bytes 884740
  12.0 5.0 %collective-permute-start.5 = (bf16[32,768]{1,0:T(8,128)(2,1)S(1)}, bf16[32,768]{1,0:T(8,128)(2,1)S(1)}, u32[]{:S(2)}, u32[]{:S(2)}) collective-permute-start(bf16[32,768]{1,0:T(8,128)(2,1)S(1)} %broadcast_select_fusion.5), channel_id=1, source_target_pairs={{0,1},{1,0},{2,3},{3,2},{4,5},{5,4},{6,7},{7,6},{8,9},{9,8},{10,11... | collective-permute-start | bytes 147464 | tf_op jit(solution)/shard_map/ppermute | solution.py:41
  12.1 6.4 %collective-permute-start.4 = (f32[12420]{0:T(1024)S(1)}, f32[12420]{0:T(1024)S(1)}, u32[]{:S(2)}, u32[]{:S(2)}) collective-permute-start(f32[12420]{0:T(1024)S(1)} %concatenate.53), channel_id=1, source_target_pairs={{0,12},{4,0},{8,4},{12,8},{1,13},{5,1},{9,5},{13,9},{2,14},{6,2},{... | collective-permute-start | bytes 149048 | tf_op jit(solution)/shard_map/ppermute | solution.py:37
  15.9 6.2 %collective-permute-start.3 = (f32[12420]{0:T(1024)S(1)}, f32[12420]{0:T(1024)S(1)}, u32[]{:S(2)}, u32[]{:S(2)}) collective-permute-start(f32[12420]{0:T(1024)S(1)} %concatenate.53), channel_id=1, source_target_pairs={{0,8},{4,12},{8,0},{12,4},{1,9},{5,13},{9,1},{13,5},{2,10},{6,14},... | collective-permute-start | bytes 149048 | tf_op jit(solution)/shard_map/ppermute | solution.py:37
  15.9 6.2 %collective-permute-start.2 = (f32[12420]{0:T(1024)S(1)}, f32[12420]{0:T(1024)S(1)}, u32[]{:S(2)}, u32[]{:S(2)}) collective-permute-start(f32[12420]{0:T(1024)S(1)} %concatenate.53), channel_id=1, source_target_pairs={{0,4},{4,8},{8,12},{12,0},{1,5},{5,9},{9,13},{13,1},{2,6},{6,10},{... | collective-permute-start | bytes 149048 | tf_op jit(solution)/shard_map/ppermute | solution.py:37
  16.9 7.0 %collective-permute-start.6 = (bf16[32,768]{1,0:T(8,128)(2,1)S(1)}, bf16[32,768]{1,0:T(8,128)(2,1)S(1)}, u32[]{:S(2)}, u32[]{:S(2)}) collective-permute-start(bf16[32,768]{1,0:T(8,128)(2,1)S(1)} %add_convert_fusion.1), channel_id=1, source_target_pairs={{0,2},{1,3},{2,0},{3,1},{4,6},{5,7},{6,4},{7,5},{8,10},{9,11},{10,... | collective-permute-start | bytes 147464 | tf_op jit(solution)/shard_map/ppermute | solution.py:41
  23.6 4.0 %copy-start.4 = (f32[768]{0:T(1024)S(1)}, f32[768]{0:T(1024)}, u32[]{:S(2)}) copy-start(f32[768]{0:T(1024)} %param.20) | copy-start | bytes 9220
  23.9 1.3 %collective-permute-start.8 = (bf16[4,32,192]{2,1,0:T(8,128)(2,1)S(1)}, bf16[4,32,192]{2,1,0:T(8,128)(2,1)S(1)}, u32[]{:S(2)}, u32[]{:S(2)}) collective-permute-start(bf16[4,32,192]{2,1,0:T(8,128)(2,1)S(1)} %reshape.499), channel_id=1, source_target_pairs={{0,1},{1,0},{2,3},{3,2},{4,5},{5,4},{6,7},{7,6},{8,9},{9,8},{10,11... | collective-permute-start | bytes 147464 | tf_op jit(solution)/shard_map/ppermute | solution.py:41
  24.0 3.7 %copy-start.3 = (bf16[768,192]{0,1:T(8,128)(2,1)S(1)}, bf16[768,192]{0,1:T(8,128)(2,1)}, u32[]{:S(2)}) copy-start(bf16[768,192]{0,1:T(8,128)(2,1)} %param.25) | copy-start | bytes 884740
  24.0 3.0 %collective-permute-start.7 = (f32[32,768]{1,0:T(8,128)S(1)}, f32[32,768]{1,0:T(8,128)S(1)}, u32[]{:S(2)}, u32[]{:S(2)}) collective-permute-start(f32[32,768]{1,0:T(8,128)S(1)} %convert_add_fusion.2), channel_id=1, source_target_pairs={{0,1},{1,0},{2,3},{3,2},{4,5},{5,4},{6,7},{7,6},{8,9},{9,8},{10,11... | collective-permute-start | bytes 294920 | tf_op jit(solution)/shard_map/ppermute | solution.py:41
  25.3 4.9 %collective-permute-start.9 = (bf16[4,32,384]{2,1,0:T(8,128)(2,1)S(1)}, bf16[4,32,384]{2,1,0:T(8,128)(2,1)S(1)}, u32[]{:S(2)}, u32[]{:S(2)}) collective-permute-start(bf16[4,32,384]{2,1,0:T(8,128)(2,1)S(1)} %maximum_select_fusion.5), channel_id=1, source_target_pairs={{0,2},{1,3},{2,0},{3,1},{4,6},{5,7},{6,4},{7,5},{8,10},{9,11},{10,... | collective-permute-start | bytes 294920 | tf_op jit(solution)/shard_map/ppermute | solution.py:41
  27.1 3.7 %copy-start.5 = (bf16[2,768,192]{1,2,0:T(8,128)(2,1)S(1)}, bf16[2,768,192]{1,2,0:T(8,128)(2,1)}, u32[]{:S(2)}) copy-start(bf16[2,768,192]{1,2,0:T(8,128)(2,1)} %param.26) | copy-start | bytes 1769476
  27.1 3.7 %copy-start.6 = (f32[768]{0:T(1024)S(1)}, f32[768]{0:T(1024)}, u32[]{:S(2)}) copy-start(f32[768]{0:T(1024)} %param.21) | copy-start | bytes 9220
  31.5 1.0 %copy-start.1 = (bf16[192,768]{1,0:T(8,128)(2,1)S(1)}, bf16[192,768]{1,0:T(8,128)(2,1)}, u32[]{:S(2)}) copy-start(bf16[192,768]{1,0:T(8,128)(2,1)} %param.27) | copy-start | bytes 884740
  32.7 1.4 %collective-permute-start.10 = (bf16[64,768]{1,0:T(8,128)(2,1)S(1)}, bf16[64,768]{1,0:T(8,128)(2,1)S(1)}, u32[]{:S(2)}, u32[]{:S(2)}) collective-permute-start(bf16[64,768]{1,0:T(8,128)(2,1)S(1)} %broadcast_select_fusion.2), channel_id=1, source_target_pairs={{0,1},{1,0},{2,3},{3,2},{4,5},{5,4},{6,7},{7,6},{8,9},{9,8},{10,11... | collective-permute-start | bytes 294920 | tf_op jit(solution)/shard_map/ppermute | solution.py:41
  34.1 4.9 %collective-permute-start.11 = (bf16[64,768]{1,0:T(8,128)(2,1)S(1)}, bf16[64,768]{1,0:T(8,128)(2,1)S(1)}, u32[]{:S(2)}, u32[]{:S(2)}) collective-permute-start(bf16[64,768]{1,0:T(8,128)(2,1)S(1)} %add_convert_fusion), channel_id=1, source_target_pairs={{0,2},{1,3},{2,0},{3,1},{4,6},{5,7},{6,4},{7,5},{8,10},{9,11},{10,... | collective-permute-start | bytes 294920 | tf_op jit(solution)/shard_map/ppermute | solution.py:41
  39.0 1.5 %collective-permute-start.12 = (f32[64,768]{1,0:T(8,128)S(1)}, f32[64,768]{1,0:T(8,128)S(1)}, u32[]{:S(2)}, u32[]{:S(2)}) collective-permute-start(f32[64,768]{1,0:T(8,128)S(1)} %convert_add_fusion.1), channel_id=1, source_target_pairs={{0,1},{1,0},{2,3},{3,2},{4,5},{5,4},{6,7},{7,6},{8,9},{9,8},{10,11... | collective-permute-start | bytes 589832 | tf_op jit(solution)/shard_map/ppermute | solution.py:41
  39.8 1.2 %copy-start.7 = (f32[768]{0:T(1024)S(1)}, f32[768]{0:T(1024)}, u32[]{:S(2)}) copy-start(f32[768]{0:T(1024)} %param.22) | copy-start | bytes 9220
  44.3 4.1 %collective-permute-start.15 = (bf16[128,192]{1,0:T(8,128)(2,1)S(1)}, bf16[128,192]{1,0:T(8,128)(2,1)S(1)}, u32[]{:S(2)}, u32[]{:S(2)}) collective-permute-start(bf16[128,192]{1,0:T(8,128)(2,1)S(1)} %select_bitcast_fusion), channel_id=1, source_target_pairs={{0,3},{1,2},{2,1},{3,0},{4,7},{5,6},{6,5},{7,4},{8,11},{9,10},{10,... | collective-permute-start | bytes 147464 | tf_op jit(solution)/shard_map/ppermute | solution.py:41
  45.6 2.8 %collective-permute-start.13 = (bf16[128,192]{1,0:T(8,128)(2,1)S(1)}, bf16[128,192]{1,0:T(8,128)(2,1)S(1)}, u32[]{:S(2)}, u32[]{:S(2)}) collective-permute-start(bf16[128,192]{1,0:T(8,128)(2,1)S(1)} %select_bitcast_fusion.2), channel_id=1, source_target_pairs={{0,1},{1,0},{2,3},{3,2},{4,5},{5,4},{6,7},{7,6},{8,9},{9,8},{10,11... | collective-permute-start | bytes 147464 | tf_op jit(solution)/shard_map/ppermute | solution.py:41
  46.1 4.3 %collective-permute-start.14 = (bf16[128,192]{1,0:T(8,128)(2,1)S(1)}, bf16[128,192]{1,0:T(8,128)(2,1)S(1)}, u32[]{:S(2)}, u32[]{:S(2)}) collective-permute-start(bf16[128,192]{1,0:T(8,128)(2,1)S(1)} %select_bitcast_fusion.1), channel_id=1, source_target_pairs={{0,2},{1,3},{2,0},{3,1},{4,6},{5,7},{6,4},{7,5},{8,10},{9,11},{10,... | collective-permute-start | bytes 147464 | tf_op jit(solution)/shard_map/ppermute | solution.py:41

commit v10 on v5

--- a/solution.py
+++ b/solution.py
@@ -82,16 +82,14 @@
     if lax.axis_size("mp") != 4:
         return lax.all_gather(part, "mp", axis=2, tiled=True)
     index = lax.axis_index("mp")
-    core = index % 2
-    chip = index // 2
-    got = swap(part, mp_pairs(1))
-    pair = jnp.where(
-        core == 0, jnp.concatenate([part, got], axis=2), jnp.concatenate([got, part], axis=2)
-    )
-    other = swap(pair, mp_pairs(2))
-    return jnp.where(
-        chip == 0, jnp.concatenate([pair, other], axis=2), jnp.concatenate([other, pair], axis=2)
-    )
+    moved = [part] + [swap(part, mp_pairs(bit)) for bit in (1, 2, 3)]
+    placed = []
+    for q in range(4):
+        rel = index ^ q
+        piece = jnp.where(rel == 0, moved[0], moved[1])
+        piece = jnp.where(rel == 2, moved[2], piece)
+        placed.append(jnp.where(rel == 3, moved[3], piece))
+    return jnp.concatenate(placed, axis=2)
 
 
 def pairs_gather(payload, owners_n):

time: 47.7 us -> 47.3 us (level)
  waiting for transfers between devices: 13.5 us -> 12.2 us
  matrix products: 6.14 us -> 7.41 us
  other arithmetic: 5.23 us -> 4.25 us
  starting transfers between devices: 15.3 us -> 16.2 us
    ppermute x13 -> x15, starting transfers between devices: 9.55 us -> 11.3 us  [swap(): return lax.ppermute(values, 'mp', pairs)]
    select_n x4 -> x2, other arithmetic: 2.08 us -> 0.82 us  [mp_gather_cols(): placed.append(jnp.where(rel == 3, moved[3], piece))]
    dot_general x1, matrix products: 0.43 us -> 1.67 us  [per_device(): jnp.einsum('rd,kdc->krc', normed, self_qkv, preferred_element_type=jnp.fl...]
    ppermute x3, starting transfers between devices: 5.71 us -> 4.89 us  [pairs_shift(): lax.ppermute(values, 'pairs', [(i, (i + step) % owners_n) for i in range(...]
    ppermute x3, waiting for transfers between devices: 1.6 us -> 0.8 us  [pairs_shift(): lax.ppermute(values, 'pairs', [(i, (i + step) % owners_n) for i in range(...]
    ppermute x13 -> x15, waiting for transfers between devices: 11.9 us -> 11.4 us  [swap(): return lax.ppermute(values, 'mp', pairs)]
  transfers between devices with their start and end apart: 16 -> 18, of which waited for: 7 -> 10; matrix products, arithmetic and copies ran while one was open for 23% -> 23% of each run, Pallas kernels for 0% -> 0%
where the time goes in v10:
time: 47.3 us; the launch traced here: 46.9 us
  starting transfers between devices  16.2 us (34%)
  waiting for transfers between devices  12.2 us (26%)
  matrix products  7.41 us (16%)
  local copies, waits for them, and re-layouts  6.31 us (13%)
  other arithmetic  4.25 us (9%)
  between operations  0.61 us (1%)
    ppermute x15, waiting for transfers between devices, swap(): return lax.ppermute(values, 'mp', pairs)  11.4 us
    ppermute x15, starting transfers between devices, swap(): return lax.ppermute(values, 'mp', pairs)  11.3 us
    ppermute x3, starting transfers between devices, pairs_shift(): lax.ppermute(values, 'pairs', [(i, (i + step) % owners_n) for i in range(...  4.89 us
    dot_general x1, matrix products, per_device(): jnp.dot(hidden.astype(jnp.bfloat16), mlp_down, preferred_element_type=jnp...  2.72 us
    dot_general x1, matrix products, per_device(): jnp.einsum('rd,kdc->krc', normed, self_qkv, preferred_element_type=jnp.fl...  1.67 us
  transfers between devices with their start and end apart: 18, of which 10 were waited for; matrix products, arithmetic and copies ran while one was open for 23% of the time, Pallas kernels for 0%

profile of v10, /device:TPU:0, one launch (start us, length us, event | category | flops | bytes accessed | tf_op | source)
XLA Modules:
  0.0 46.9 jit_solution(13414782140100155288)
XLA Ops:
  0.0 0.5 collective-permute-start.5
  0.5 2.6 %collective-permute-start.4 = (bf16[2,32,192]{2,1,0:T(8,128)(2,1)}, bf16[2,32,192]{2,1,0:T(8,128)(2,1)S(1)}, u32[]{:S(2)}, u32[]{:S(2)}) collective-permute-start(bf16[2,32,192]{2,1,0:T(8,128)(2,1)} %bitcast.81), channel_id=1, source_target_pairs={{0,2},{1,3},{2,0},{3,1},{4,6},{5,7},{6,4},{7,5},{8,10},{9,11},{10,... | collective-permute-start | bytes 73736 | tf_op jit(solution)/shard_map/ppermute | solution.py:41
  3.1 0.9 %reshape.530 = f32[12288]{0:T(1024)S(1)} reshape(bf16[64,192]{1,0:T(8,128)(2,1)} %param.16) | data formatting | bytes 73728 | tf_op jit(solution)/shard_map/reshape | solution.py:137
  4.0 0.8 %reshape.453 = f32[128]{0:T(128)S(1)} reshape(f32[2,64]{1,0:T(2,128)} %param.18) | data formatting | bytes 1024 | tf_op jit(solution)/shard_map/reshape | solution.py:139
  4.7 0.7 %convert_element_type.160 = f32[2,2]{1,0:T(2,128)S(1)} convert(s32[2,2]{1,0:T(2,128)} %param.17) | non-fusion elementwise | flops 4 | bytes 32 | tf_op jit(solution)/shard_map/convert_element_type | solution.py:138
  5.6 3.8 %collective-permute-start.2 = (f32[12420]{0:T(1024)S(1)}, f32[12420]{0:T(1024)S(1)}, u32[]{:S(2)}, u32[]{:S(2)}) collective-permute-start(f32[12420]{0:T(1024)S(1)} %concatenate.40), channel_id=1, source_target_pairs={{0,12},{4,0},{8,4},{12,8},{1,13},{5,1},{9,5},{13,9},{2,14},{6,2},{... | collective-permute-start | bytes 149048 | tf_op jit(solution)/shard_map/ppermute | solution.py:37
  9.5 1.1 %collective-permute-start = (f32[12420]{0:T(1024)S(1)}, f32[12420]{0:T(1024)S(1)}, u32[]{:S(2)}, u32[]{:S(2)}) collective-permute-start(f32[12420]{0:T(1024)S(1)} %concatenate.40), channel_id=1, source_target_pairs={{0,4},{4,8},{8,12},{12,0},{1,5},{5,9},{9,13},{13,1},{2,6},{6,10},{... | collective-permute-start | bytes 149048 | tf_op jit(solution)/shard_map/ppermute | solution.py:37
  10.6 0.8 %select_select_fusion.7 = (bf16[2,32,192]{2,1,0:T(8,128)(2,1)S(1)}, bf16[2,32,192]{2,1,0:T(8,128)(2,1)S(1)}, bf16[2,32,192]{2,1,0:T(8,128)(2,1)S(1)}, bf16[2,32,192]{2,1,0:T(8,128)(2,1)S(1)}) fusion(bf16[2,32,192]{2,1,0:T(8,128)(2,1)S(1)} %collective-permute-done.3, bf16[2,32,192]{2,1,0:T(8,128)(2,1)S(1)} %collective-permute-done.4, ...), kind=kLoop, calls=%fused_computation.156 | loop fusion | flops 147456 | bytes 196620 | tf_op jit(solution)/shard_map/jit(_where)/select_n | solution.py:91
  11.3 0.2 convert_reduce_fusion.1
  11.5 0.2 fusion.25
  11.8 1.7 %fusion.6 = bf16[3,64,192]{2,1,0:T(8,128)(2,1)S(1)} fusion(bf16[3,768,192]{1,2,0:T(8,128)(2,1)} %param.23, bf16[64,768]{1,0:T(8,128)(2,1)S(1)} %get-tuple-element.24, f32[768]{0:T(1024)} %param.19, f32[64]{0:T(128)S(1)} %add_rsqrt_fusion.3, f32[64]{0:T(128)S(1)} %broadcast_multiply_fusion.3), kind=kOutput, calls=%fused_computation.15 | convolution fusion | flops 56905728 | bytes 1060352 | tf_op jit(solution)/shard_map/rd,kdc->krc/dot_general | solution.py:167
  13.6 0.2 fusion.157
  13.8 0.1 convolution_multiply_fusion.1
  14.1 0.2 fusion.9
  14.4 0.2 convolution_convert_fusion.6
  14.8 0.8 %collective-permute-done.1 = f32[12420]{0:T(1024)S(1)} collective-permute-done((f32[12420]{0:T(1024)S(1)}, f32[12420]{0:T(1024)S(1)}, u32[]{:S(2)}, u32[]{:S(2)}) %collective-permute-start.1) | collective-permute-done | bytes 49712 | tf_op jit(solution)/shard_map/ppermute | solution.py:37
  15.8 0.2 pad_maximum_fusion
  16.6 0.1 add_reduce_fusion
  16.7 0.2 select_reduce_fusion.1
  16.9 0.2 convolution_convert_fusion.1
  17.1 0.1 reshape.460
  17.3 1.6 %collective-permute-start.10 = (bf16[4,32,192]{2,1,0:T(8,128)(2,1)S(1)}, bf16[4,32,192]{2,1,0:T(8,128)(2,1)S(1)}, u32[]{:S(2)}, u32[]{:S(2)}) collective-permute-start(bf16[4,32,192]{2,1,0:T(8,128)(2,1)S(1)} %reshape.460), channel_id=1, source_target_pairs={{0,2},{1,3},{2,0},{3,1},{4,6},{5,7},{6,4},{7,5},{8,10},{9,11},{10,... | collective-permute-start | bytes 147464 | tf_op jit(solution)/shard_map/ppermute | solution.py:41
  18.9 0.3 collective-permute-start.9
  19.2 0.1 fusion.152
  19.4 1.6 %collective-permute-start.7 = (bf16[32,768]{1,0:T(8,128)(2,1)S(1)}, bf16[32,768]{1,0:T(8,128)(2,1)S(1)}, u32[]{:S(2)}, u32[]{:S(2)}) collective-permute-start(bf16[32,768]{1,0:T(8,128)(2,1)S(1)} %add_convert_fusion.1), channel_id=1, source_target_pairs={{0,2},{1,3},{2,0},{3,1},{4,6},{5,7},{6,4},{7,5},{8,10},{9,11},{10,... | collective-permute-start | bytes 147464 | tf_op jit(solution)/shard_map/ppermute | solution.py:41
  21.0 0.8 %collective-permute-done.10 = bf16[4,32,192]{2,1,0:T(8,128)(2,1)S(1)} collective-permute-done((bf16[4,32,192]{2,1,0:T(8,128)(2,1)S(1)}, bf16[4,32,192]{2,1,0:T(8,128)(2,1)S(1)}, u32[]{:S(2)}, u32[]{:S(2)}) %collective-permute-start.10) | collective-permute-done | bytes 49184 | tf_op jit(solution)/shard_map/ppermute | solution.py:41
  21.8 1.1 %collective-permute-done.9 = bf16[4,32,192]{2,1,0:T(8,128)(2,1)S(1)} collective-permute-done((bf16[4,32,192]{2,1,0:T(8,128)(2,1)S(1)}, bf16[4,32,192]{2,1,0:T(8,128)(2,1)S(1)}, u32[]{:S(2)}, u32[]{:S(2)}) %collective-permute-start.9) | collective-permute-done | bytes 49184 | tf_op jit(solution)/shard_map/ppermute | solution.py:41
  23.0 0.2 convert_reduce_fusion
  23.3 0.2 fusion.11
  23.6 0.4 fusion.28
  24.1 0.2 collective-permute-done.7
  24.3 0.3 collective-permute-start.8
  24.7 0.1 reshape.576
  24.8 0.1 reshape.575
  25.0 0.7 %collective-permute-done.8 = f32[32,768]{1,0:T(8,128)S(1)} collective-permute-done((f32[32,768]{1,0:T(8,128)S(1)}, f32[32,768]{1,0:T(8,128)S(1)}, u32[]{:S(2)}, u32[]{:S(2)}) %collective-permute-start.8) | collective-permute-done | bytes 98336 | tf_op jit(solution)/shard_map/ppermute | solution.py:41
  25.7 0.1 pad_maximum_fusion.1
  25.9 0.2 multiply_reduce_fusion.1
  26.1 0.2 convolution_convert_fusion.8
  26.4 0.2 convolution_convert_fusion
  26.7 0.1 reshape_reshape_reshape.3
  26.8 0.2 convolution_multiply_fusion
  27.2 0.3 fusion.5
  27.5 0.1 reshape.461
  27.7 0.1 copy-done.1
  27.8 0.2 convolution_convert_fusion.3
  28.0 0.3 collective-permute-start.12
  28.6 0.8 %collective-permute-done.12 = bf16[64,768]{1,0:T(8,128)(2,1)S(1)} collective-permute-done((bf16[64,768]{1,0:T(8,128)(2,1)S(1)}, bf16[64,768]{1,0:T(8,128)(2,1)S(1)}, u32[]{:S(2)}, u32[]{:S(2)}) %collective-permute-start.12) | collective-permute-done | bytes 98336 | tf_op jit(solution)/shard_map/ppermute | solution.py:41
  29.4 1.6 %collective-permute-start.13 = (bf16[64,768]{1,0:T(8,128)(2,1)S(1)}, bf16[64,768]{1,0:T(8,128)(2,1)S(1)}, u32[]{:S(2)}, u32[]{:S(2)}) collective-permute-start(bf16[64,768]{1,0:T(8,128)(2,1)S(1)} %add_convert_fusion), channel_id=1, source_target_pairs={{0,2},{1,3},{2,0},{3,1},{4,6},{5,7},{6,4},{7,5},{8,10},{9,11},{10,... | collective-permute-start | bytes 294920 | tf_op jit(solution)/shard_map/ppermute | solution.py:41
  31.0 3.5 %collective-permute-done.13 = bf16[64,768]{1,0:T(8,128)(2,1)S(1)} collective-permute-done((bf16[64,768]{1,0:T(8,128)(2,1)S(1)}, bf16[64,768]{1,0:T(8,128)(2,1)S(1)}, u32[]{:S(2)}, u32[]{:S(2)}) %collective-permute-start.13) | collective-permute-done | bytes 98336 | tf_op jit(solution)/shard_map/ppermute | solution.py:41
  34.7 0.6 %gather_fusion = f32[4,32,768]{2,1,0:T(8,128)S(1)} fusion(f32[2,32,768]{2,1,0:T(8,128)S(1)} %convert_add_fusion.2, s32[1024]{0:T(1024)S(1)} %pad_clamp_fusion), kind=kCustom, calls=%fused_computation | custom fusion | bytes 786448 | tf_op jit(solution)/shard_map/jit(_take)/gather | solution.py:188
  35.3 0.7 %collective-permute-done.14 = f32[64,768]{1,0:T(8,128)S(1)} collective-permute-done((f32[64,768]{1,0:T(8,128)S(1)}, f32[64,768]{1,0:T(8,128)S(1)}, u32[]{:S(2)}, u32[]{:S(2)}) %collective-permute-start.14) | collective-permute-done | bytes 196640 | tf_op jit(solution)/shard_map/ppermute | solution.py:41
  36.1 0.2 fusion.154
  36.3 0.2 multiply_reduce_fusion
  36.5 2.7 %convolution_convert_fusion.2 = bf16[128,768]{1,0:T(8,128)(2,1)S(1)} fusion(bf16[768,768]{1,0:T(8,128)(2,1)S(1)} %copy-done, bf16[768,768]{1,0:T(8,128)(2,1)} %param.28, f32[128,768]{1,0:T(8,128)S(1)} %get-tuple-element.20, f32[768]{0:T(1024)S(1)} %copy-done.7, f32[128]{0:T(128)S(1)} %add_rsqrt_fusion.1, f32[128]{0:T(128)S(1)} %broadcast_multiply_fusion.1), kind=kOutput, calls=%fused_computation.6 | convolution fusion | flops 308871168 | bytes 2953216 | tf_op jit(solution)/shard_map/dot_general | solution.py:199
  39.2 0.2 copy.78
  39.8 1.4 %collective-permute-start.17 = (bf16[128,192]{1,0:T(8,128)(2,1)S(1)}, bf16[128,192]{1,0:T(8,128)(2,1)S(1)}, u32[]{:S(2)}, u32[]{:S(2)}) collective-permute-start(bf16[128,192]{1,0:T(8,128)(2,1)S(1)} %select_bitcast_fusion), channel_id=1, source_target_pairs={{0,3},{1,2},{2,1},{3,0},{4,7},{5,6},{6,5},{7,4},{8,11},{9,10},{10,... | collective-permute-start | bytes 147464 | tf_op jit(solution)/shard_map/ppermute | solution.py:41
  41.2 0.4 collective-permute-start.15
  41.6 0.5 %collective-permute-start.16 = (bf16[128,192]{1,0:T(8,128)(2,1)S(1)}, bf16[128,192]{1,0:T(8,128)(2,1)S(1)}, u32[]{:S(2)}, u32[]{:S(2)}) collective-permute-start(bf16[128,192]{1,0:T(8,128)(2,1)S(1)} %select_bitcast_fusion.1), channel_id=1, source_target_pairs={{0,2},{1,3},{2,0},{3,1},{4,6},{5,7},{6,4},{7,5},{8,10},{9,11},{10,... | collective-permute-start | bytes 147464 | tf_op jit(solution)/shard_map/ppermute | solution.py:41
  42.2 0.1 convolution_maximum_fusion
  42.6 1.4 %collective-permute-done.17 = bf16[128,192]{1,0:T(8,128)(2,1)S(1)} collective-permute-done((bf16[128,192]{1,0:T(8,128)(2,1)S(1)}, bf16[128,192]{1,0:T(8,128)(2,1)S(1)}, u32[]{:S(2)}, u32[]{:S(2)}) %collective-permute-start.17) | collective-permute-done | bytes 49184 | tf_op jit(solution)/shard_map/ppermute | solution.py:41
  43.9 2.0 %collective-permute-done.16 = bf16[128,192]{1,0:T(8,128)(2,1)S(1)} collective-permute-done((bf16[128,192]{1,0:T(8,128)(2,1)S(1)}, bf16[128,192]{1,0:T(8,128)(2,1)S(1)}, u32[]{:S(2)}, u32[]{:S(2)}) %collective-permute-start.16) | collective-permute-done | bytes 49184 | tf_op jit(solution)/shard_map/ppermute | solution.py:41
  46.0 0.1 add_add_fusion
  46.1 0.2 fusion.8
  46.3 0.6 %copy.86 = bf16[2,32,192]{2,1,0:T(8,128)(2,1)} copy(bf16[2,32,192]{2,0,1:T(2,128)(2,1)S(1)} %fusion.8) | data formatting | bytes 49152 | tf_op jit(solution)/shard_map/convert_element_type | solution.py:212
  (95 shorter events, 3.5 us)
Async XLA Ops:
  0.0 36.5 %copy-start = (bf16[768,768]{1,0:T(8,128)(2,1)S(1)}, bf16[768,768]{1,0:T(8,128)(2,1)}, u32[]{:S(2)}) copy-start(bf16[768,768]{1,0:T(8,128)(2,1)} %param.29) | copy-start | bytes 3538948
  0.0 9.5 %collective-permute-start.5 = (bf16[2,32,192]{2,1,0:T(8,128)(2,1)}, bf16[2,32,192]{2,1,0:T(8,128)(2,1)S(1)}, u32[]{:S(2)}, u32[]{:S(2)}) collective-permute-start(bf16[2,32,192]{2,1,0:T(8,128)(2,1)} %bitcast.80), channel_id=1, source_target_pairs={{0,1},{1,0},{2,3},{3,2},{4,5},{5,4},{6,7},{7,6},{8,9},{9,8},{10,11... | collective-permute-start | bytes 73736 | tf_op jit(solution)/shard_map/ppermute | solution.py:41
  0.5 10.1 %collective-permute-start.4 = (bf16[2,32,192]{2,1,0:T(8,128)(2,1)}, bf16[2,32,192]{2,1,0:T(8,128)(2,1)S(1)}, u32[]{:S(2)}, u32[]{:S(2)}) collective-permute-start(bf16[2,32,192]{2,1,0:T(8,128)(2,1)} %bitcast.81), channel_id=1, source_target_pairs={{0,2},{1,3},{2,0},{3,1},{4,6},{5,7},{6,4},{7,5},{8,10},{9,11},{10,... | collective-permute-start | bytes 73736 | tf_op jit(solution)/shard_map/ppermute | solution.py:41
  3.0 7.5 %collective-permute-start.3 = (bf16[2,32,192]{2,1,0:T(8,128)(2,1)}, bf16[2,32,192]{2,1,0:T(8,128)(2,1)S(1)}, u32[]{:S(2)}, u32[]{:S(2)}) collective-permute-start(bf16[2,32,192]{2,1,0:T(8,128)(2,1)} %bitcast.82), channel_id=1, source_target_pairs={{0,3},{1,2},{2,1},{3,0},{4,7},{5,6},{6,5},{7,4},{8,11},{9,10},{10,... | collective-permute-start | bytes 73736 | tf_op jit(solution)/shard_map/ppermute | solution.py:41
  5.6 9.1 %collective-permute-start.2 = (f32[12420]{0:T(1024)S(1)}, f32[12420]{0:T(1024)S(1)}, u32[]{:S(2)}, u32[]{:S(2)}) collective-permute-start(f32[12420]{0:T(1024)S(1)} %concatenate.40), channel_id=1, source_target_pairs={{0,12},{4,0},{8,4},{12,8},{1,13},{5,1},{9,5},{13,9},{2,14},{6,2},{... | collective-permute-start | bytes 149048 | tf_op jit(solution)/shard_map/ppermute | solution.py:37
  9.4 6.2 %collective-permute-start.1 = (f32[12420]{0:T(1024)S(1)}, f32[12420]{0:T(1024)S(1)}, u32[]{:S(2)}, u32[]{:S(2)}) collective-permute-start(f32[12420]{0:T(1024)S(1)} %concatenate.40), channel_id=1, source_target_pairs={{0,8},{4,12},{8,0},{12,4},{1,9},{5,13},{9,1},{13,5},{2,10},{6,14},... | collective-permute-start | bytes 149048 | tf_op jit(solution)/shard_map/ppermute | solution.py:37
  9.5 6.1 %collective-permute-start = (f32[12420]{0:T(1024)S(1)}, f32[12420]{0:T(1024)S(1)}, u32[]{:S(2)}, u32[]{:S(2)}) collective-permute-start(f32[12420]{0:T(1024)S(1)} %concatenate.40), channel_id=1, source_target_pairs={{0,4},{4,8},{8,12},{12,0},{1,5},{5,9},{9,13},{13,1},{2,6},{6,10},{... | collective-permute-start | bytes 149048 | tf_op jit(solution)/shard_map/ppermute | solution.py:37
  11.8 2.7 %copy-start.2 = (bf16[192,768]{1,0:T(8,128)(2,1)S(1)}, bf16[192,768]{1,0:T(8,128)(2,1)}, u32[]{:S(2)}) copy-start(bf16[192,768]{1,0:T(8,128)(2,1)} %param.24) | copy-start | bytes 884740
  14.7 4.7 %collective-permute-start.6 = (bf16[32,768]{1,0:T(8,128)(2,1)S(1)}, bf16[32,768]{1,0:T(8,128)(2,1)S(1)}, u32[]{:S(2)}, u32[]{:S(2)}) collective-permute-start(bf16[32,768]{1,0:T(8,128)(2,1)S(1)} %broadcast_select_fusion.5), channel_id=1, source_target_pairs={{0,1},{1,0},{2,3},{3,2},{4,5},{5,4},{6,7},{7,6},{8,9},{9,8},{10,11... | collective-permute-start | bytes 147464 | tf_op jit(solution)/shard_map/ppermute | solution.py:41
  15.8 7.8 %copy-start.3 = (bf16[2,768,192]{1,2,0:T(8,128)(2,1)S(1)}, bf16[2,768,192]{1,2,0:T(8,128)(2,1)}, u32[]{:S(2)}) copy-start(bf16[2,768,192]{1,2,0:T(8,128)(2,1)} %param.26) | copy-start | bytes 1769476
  15.8 7.8 %copy-start.5 = (f32[768]{0:T(1024)S(1)}, f32[768]{0:T(1024)}, u32[]{:S(2)}) copy-start(f32[768]{0:T(1024)} %param.21) | copy-start | bytes 9220
  17.2 3.8 %collective-permute-start.11 = (bf16[4,32,192]{2,1,0:T(8,128)(2,1)S(1)}, bf16[4,32,192]{2,1,0:T(8,128)(2,1)S(1)}, u32[]{:S(2)}, u32[]{:S(2)}) collective-permute-start(bf16[4,32,192]{2,1,0:T(8,128)(2,1)S(1)} %reshape.460), channel_id=1, source_target_pairs={{0,1},{1,0},{2,3},{3,2},{4,5},{5,4},{6,7},{7,6},{8,9},{9,8},{10,11... | collective-permute-start | bytes 147464 | tf_op jit(solution)/shard_map/ppermute | solution.py:41
  17.3 4.5 %collective-permute-start.10 = (bf16[4,32,192]{2,1,0:T(8,128)(2,1)S(1)}, bf16[4,32,192]{2,1,0:T(8,128)(2,1)S(1)}, u32[]{:S(2)}, u32[]{:S(2)}) collective-permute-start(bf16[4,32,192]{2,1,0:T(8,128)(2,1)S(1)} %reshape.460), channel_id=1, source_target_pairs={{0,2},{1,3},{2,0},{3,1},{4,6},{5,7},{6,4},{7,5},{8,10},{9,11},{10,... | collective-permute-start | bytes 147464 | tf_op jit(solution)/shard_map/ppermute | solution.py:41
  18.9 4.0 %collective-permute-start.9 = (bf16[4,32,192]{2,1,0:T(8,128)(2,1)S(1)}, bf16[4,32,192]{2,1,0:T(8,128)(2,1)S(1)}, u32[]{:S(2)}, u32[]{:S(2)}) collective-permute-start(bf16[4,32,192]{2,1,0:T(8,128)(2,1)S(1)} %reshape.460), channel_id=1, source_target_pairs={{0,3},{1,2},{2,1},{3,0},{4,7},{5,6},{6,5},{7,4},{8,11},{9,10},{10,... | collective-permute-start | bytes 147464 | tf_op jit(solution)/shard_map/ppermute | solution.py:41
  19.4 4.9 %collective-permute-start.7 = (bf16[32,768]{1,0:T(8,128)(2,1)S(1)}, bf16[32,768]{1,0:T(8,128)(2,1)S(1)}, u32[]{:S(2)}, u32[]{:S(2)}) collective-permute-start(bf16[32,768]{1,0:T(8,128)(2,1)S(1)} %add_convert_fusion.1), channel_id=1, source_target_pairs={{0,2},{1,3},{2,0},{3,1},{4,6},{5,7},{6,4},{7,5},{8,10},{9,11},{10,... | collective-permute-start | bytes 147464 | tf_op jit(solution)/shard_map/ppermute | solution.py:41
  24.0 2.0 %copy-start.4 = (bf16[768,192]{0,1:T(8,128)(2,1)S(1)}, bf16[768,192]{0,1:T(8,128)(2,1)}, u32[]{:S(2)}) copy-start(bf16[768,192]{0,1:T(8,128)(2,1)} %param.25) | copy-start | bytes 884740
  24.0 2.0 %copy-start.6 = (f32[768]{0:T(1024)S(1)}, f32[768]{0:T(1024)}, u32[]{:S(2)}) copy-start(f32[768]{0:T(1024)} %param.20) | copy-start | bytes 9220
  24.3 1.4 %collective-permute-start.8 = (f32[32,768]{1,0:T(8,128)S(1)}, f32[32,768]{1,0:T(8,128)S(1)}, u32[]{:S(2)}, u32[]{:S(2)}) collective-permute-start(f32[32,768]{1,0:T(8,128)S(1)} %convert_add_fusion.3), channel_id=1, source_target_pairs={{0,1},{1,0},{2,3},{3,2},{4,5},{5,4},{6,7},{7,6},{8,9},{9,8},{10,11... | collective-permute-start | bytes 294920 | tf_op jit(solution)/shard_map/ppermute | solution.py:41
  26.8 1.0 %copy-start.1 = (bf16[192,768]{1,0:T(8,128)(2,1)S(1)}, bf16[192,768]{1,0:T(8,128)(2,1)}, u32[]{:S(2)}) copy-start(bf16[192,768]{1,0:T(8,128)(2,1)} %param.27) | copy-start | bytes 884740
  28.0 1.4 %collective-permute-start.12 = (bf16[64,768]{1,0:T(8,128)(2,1)S(1)}, bf16[64,768]{1,0:T(8,128)(2,1)S(1)}, u32[]{:S(2)}, u32[]{:S(2)}) collective-permute-start(bf16[64,768]{1,0:T(8,128)(2,1)S(1)} %broadcast_select_fusion.2), channel_id=1, source_target_pairs={{0,1},{1,0},{2,3},{3,2},{4,5},{5,4},{6,7},{7,6},{8,9},{9,8},{10,11... | collective-permute-start | bytes 294920 | tf_op jit(solution)/shard_map/ppermute | solution.py:41
  29.4 5.0 %collective-permute-start.13 = (bf16[64,768]{1,0:T(8,128)(2,1)S(1)}, bf16[64,768]{1,0:T(8,128)(2,1)S(1)}, u32[]{:S(2)}, u32[]{:S(2)}) collective-permute-start(bf16[64,768]{1,0:T(8,128)(2,1)S(1)} %add_convert_fusion), channel_id=1, source_target_pairs={{0,2},{1,3},{2,0},{3,1},{4,6},{5,7},{6,4},{7,5},{8,10},{9,11},{10,... | collective-permute-start | bytes 294920 | tf_op jit(solution)/shard_map/ppermute | solution.py:41
  34.5 1.5 %collective-permute-start.14 = (f32[64,768]{1,0:T(8,128)S(1)}, f32[64,768]{1,0:T(8,128)S(1)}, u32[]{:S(2)}, u32[]{:S(2)}) collective-permute-start(f32[64,768]{1,0:T(8,128)S(1)} %convert_add_fusion.1), channel_id=1, source_target_pairs={{0,1},{1,0},{2,3},{3,2},{4,5},{5,4},{6,7},{7,6},{8,9},{9,8},{10,11... | collective-permute-start | bytes 589832 | tf_op jit(solution)/shard_map/ppermute | solution.py:41
  35.3 1.2 %copy-start.7 = (f32[768]{0:T(1024)S(1)}, f32[768]{0:T(1024)}, u32[]{:S(2)}) copy-start(f32[768]{0:T(1024)} %param.22) | copy-start | bytes 9220
  39.8 4.1 %collective-permute-start.17 = (bf16[128,192]{1,0:T(8,128)(2,1)S(1)}, bf16[128,192]{1,0:T(8,128)(2,1)S(1)}, u32[]{:S(2)}, u32[]{:S(2)}) collective-permute-start(bf16[128,192]{1,0:T(8,128)(2,1)S(1)} %select_bitcast_fusion), channel_id=1, source_target_pairs={{0,3},{1,2},{2,1},{3,0},{4,7},{5,6},{6,5},{7,4},{8,11},{9,10},{10,... | collective-permute-start | bytes 147464 | tf_op jit(solution)/shard_map/ppermute | solution.py:41
  41.2 2.8 %collective-permute-start.15 = (bf16[128,192]{1,0:T(8,128)(2,1)S(1)}, bf16[128,192]{1,0:T(8,128)(2,1)S(1)}, u32[]{:S(2)}, u32[]{:S(2)}) collective-permute-start(bf16[128,192]{1,0:T(8,128)(2,1)S(1)} %select_bitcast_fusion.2), channel_id=1, source_target_pairs={{0,1},{1,0},{2,3},{3,2},{4,5},{5,4},{6,7},{7,6},{8,9},{9,8},{10,11... | collective-permute-start | bytes 147464 | tf_op jit(solution)/shard_map/ppermute | solution.py:41
  41.6 4.3 %collective-permute-start.16 = (bf16[128,192]{1,0:T(8,128)(2,1)S(1)}, bf16[128,192]{1,0:T(8,128)(2,1)S(1)}, u32[]{:S(2)}, u32[]{:S(2)}) collective-permute-start(bf16[128,192]{1,0:T(8,128)(2,1)S(1)} %select_bitcast_fusion.1), channel_id=1, source_target_pairs={{0,2},{1,3},{2,0},{3,1},{4,6},{5,7},{6,4},{7,5},{8,10},{9,11},{10,... | collective-permute-start | bytes 147464 | tf_op jit(solution)/shard_map/ppermute | solution.py:41

commit v11 on v5

--- a/solution.py
+++ b/solution.py
@@ -79,6 +79,20 @@
 
 
 def mp_gather_cols(part):
+    if lax.axis_size("mp") != 4:
+        return lax.all_gather(part, "mp", axis=2, tiled=True)
+    index = lax.axis_index("mp")
+    moved = [part] + [swap(part, mp_pairs(bit)) for bit in (1, 2, 3)]
+    placed = []
+    for q in range(4):
+        rel = index ^ q
+        piece = jnp.where(rel == 0, moved[0], moved[1])
+        piece = jnp.where(rel == 2, moved[2], piece)
+        placed.append(jnp.where(rel == 3, moved[3], piece))
+    return jnp.concatenate(placed, axis=2)
+
+
+def mp_gather_steps(part):
     if lax.axis_size("mp") != 4:
         return lax.all_gather(part, "mp", axis=2, tiled=True)
     index = lax.axis_index("mp")
@@ -179,7 +193,7 @@
     )
 
     rows_n = views_n * TOKS
-    context = layer_norm(mp_gather_cols(context_q).astype(jnp.float32), gain_context).reshape(
+    context = layer_norm(mp_gather_steps(context_q).astype(jnp.float32), gain_context).reshape(
         rows_n, width
     )
     keyval = jnp.einsum(

time: 47.7 us -> 47 us (0.985)
  matrix products: 6.14 us -> 7.38 us
  other arithmetic: 5.23 us -> 4.32 us
  starting transfers between devices: 15.3 us -> 14.6 us
  waiting for transfers between devices: 13.5 us -> 13 us
    dot_general x1, matrix products: 0.43 us -> 1.67 us  [per_device(): jnp.einsum('rd,kdc->krc', normed, self_qkv, preferred_element_type=jnp.fl...]
    select_n x4 -> x3, other arithmetic: 2.08 us -> 1.01 us  [the longest x1 0.78 us: mp_gather_cols(): placed.append(jnp.where(rel == 3, moved[3], piece))]
    ppermute x3, starting transfers between devices: 5.71 us -> 4.89 us  [pairs_shift(): lax.ppermute(values, 'pairs', [(i, (i + step) % owners_n) for i in range(...]
    ppermute x3, waiting for transfers between devices: 1.6 us -> 0.79 us  [pairs_shift(): lax.ppermute(values, 'pairs', [(i, (i + step) % owners_n) for i in range(...]
    ppermute x13 -> x14, waiting for transfers between devices: 11.9 us -> 12.2 us  [swap(): return lax.ppermute(values, 'mp', pairs)]
    ppermute x13 -> x14, starting transfers between devices: 9.55 us -> 9.75 us  [swap(): return lax.ppermute(values, 'mp', pairs)]
  transfers between devices with their start and end apart: 16 -> 17, of which waited for: 7 -> 8; matrix products, arithmetic and copies ran while one was open for 23% -> 24% of each run, Pallas kernels for 0% -> 0%
where the time goes in v11:
time: 47 us; the launch traced here: 46.6 us
  starting transfers between devices  14.6 us (31%)
  waiting for transfers between devices  13 us (28%)
  matrix products  7.38 us (16%)
  local copies, waits for them, and re-layouts  6.66 us (14%)
  other arithmetic  4.32 us (9%)
  between operations  0.64 us (1%)
    ppermute x14, waiting for transfers between devices, swap(): return lax.ppermute(values, 'mp', pairs)  12.2 us
    ppermute x14, starting transfers between devices, swap(): return lax.ppermute(values, 'mp', pairs)  9.75 us
    ppermute x3, starting transfers between devices, pairs_shift(): lax.ppermute(values, 'pairs', [(i, (i + step) % owners_n) for i in range(...  4.89 us
    dot_general x1, matrix products, per_device(): jnp.dot(hidden.astype(jnp.bfloat16), mlp_down, preferred_element_type=jnp...  2.72 us
    dot_general x1, matrix products, per_device(): jnp.einsum('rd,kdc->krc', normed, self_qkv, preferred_element_type=jnp.fl...  1.67 us
  transfers between devices with their start and end apart: 17, of which 8 were waited for; matrix products, arithmetic and copies ran while one was open for 24% of the time, Pallas kernels for 0%

profile of v11, /device:TPU:0, one launch (start us, length us, event | category | flops | bytes accessed | tf_op | source)
XLA Modules:
  0.0 46.6 jit_solution(422897328465365328)
XLA Ops:
  0.0 0.5 collective-permute-start.5
  0.5 2.6 %collective-permute-start.4 = (bf16[2,32,192]{2,1,0:T(8,128)(2,1)}, bf16[2,32,192]{2,1,0:T(8,128)(2,1)S(1)}, u32[]{:S(2)}, u32[]{:S(2)}) collective-permute-start(bf16[2,32,192]{2,1,0:T(8,128)(2,1)} %bitcast.77), channel_id=1, source_target_pairs={{0,2},{1,3},{2,0},{3,1},{4,6},{5,7},{6,4},{7,5},{8,10},{9,11},{10,... | collective-permute-start | bytes 73736 | tf_op jit(solution)/shard_map/ppermute | solution.py:41
  3.1 0.9 %reshape.536 = f32[12288]{0:T(1024)S(1)} reshape(bf16[64,192]{1,0:T(8,128)(2,1)} %param.16) | data formatting | bytes 73728 | tf_op jit(solution)/shard_map/reshape | solution.py:153
  4.0 0.8 %reshape.459 = f32[128]{0:T(128)S(1)} reshape(f32[2,64]{1,0:T(2,128)} %param.18) | data formatting | bytes 1024 | tf_op jit(solution)/shard_map/reshape | solution.py:155
  4.7 0.7 %convert_element_type.160 = f32[2,2]{1,0:T(2,128)S(1)} convert(s32[2,2]{1,0:T(2,128)} %param.17) | non-fusion elementwise | flops 4 | bytes 32 | tf_op jit(solution)/shard_map/convert_element_type | solution.py:154
  5.6 3.8 %collective-permute-start.2 = (f32[12420]{0:T(1024)S(1)}, f32[12420]{0:T(1024)S(1)}, u32[]{:S(2)}, u32[]{:S(2)}) collective-permute-start(f32[12420]{0:T(1024)S(1)} %concatenate.56), channel_id=1, source_target_pairs={{0,12},{4,0},{8,4},{12,8},{1,13},{5,1},{9,5},{13,9},{2,14},{6,2},{... | collective-permute-start | bytes 149048 | tf_op jit(solution)/shard_map/ppermute | solution.py:37
  9.5 1.1 %collective-permute-start = (f32[12420]{0:T(1024)S(1)}, f32[12420]{0:T(1024)S(1)}, u32[]{:S(2)}, u32[]{:S(2)}) collective-permute-start(f32[12420]{0:T(1024)S(1)} %concatenate.56), channel_id=1, source_target_pairs={{0,4},{4,8},{8,12},{12,0},{1,5},{5,9},{9,13},{13,1},{2,6},{6,10},{... | collective-permute-start | bytes 149048 | tf_op jit(solution)/shard_map/ppermute | solution.py:37
  10.6 0.8 %select_select_fusion.3 = (bf16[2,32,192]{2,1,0:T(8,128)(2,1)S(1)}, bf16[2,32,192]{2,1,0:T(8,128)(2,1)S(1)}, bf16[2,32,192]{2,1,0:T(8,128)(2,1)S(1)}, bf16[2,32,192]{2,1,0:T(8,128)(2,1)S(1)}) fusion(bf16[2,32,192]{2,1,0:T(8,128)(2,1)S(1)} %collective-permute-done.3, bf16[2,32,192]{2,1,0:T(8,128)(2,1)S(1)} %collective-permute-done.4, ...), kind=kLoop, calls=%fused_computation.154 | loop fusion | flops 147456 | bytes 196620 | tf_op jit(solution)/shard_map/jit(_where)/select_n | solution.py:91
  11.4 0.2 convert_reduce_fusion.1
  11.6 0.2 fusion.25
  11.8 1.7 %fusion.6 = bf16[3,64,192]{2,1,0:T(8,128)(2,1)S(1)} fusion(bf16[3,768,192]{1,2,0:T(8,128)(2,1)} %param.23, bf16[64,768]{1,0:T(8,128)(2,1)S(1)} %get-tuple-element.24, f32[768]{0:T(1024)} %param.19, f32[64]{0:T(128)S(1)} %add_rsqrt_fusion.3, f32[64]{0:T(128)S(1)} %broadcast_multiply_fusion.3), kind=kOutput, calls=%fused_computation.15 | convolution fusion | flops 56905728 | bytes 1060352 | tf_op jit(solution)/shard_map/rd,kdc->krc/dot_general | solution.py:183
  13.7 0.2 fusion.156
  13.8 0.1 convolution_multiply_fusion.1
  14.1 0.2 fusion.9
  14.5 0.2 convolution_convert_fusion.6
  14.8 0.8 %collective-permute-done.1 = f32[12420]{0:T(1024)S(1)} collective-permute-done((f32[12420]{0:T(1024)S(1)}, f32[12420]{0:T(1024)S(1)}, u32[]{:S(2)}, u32[]{:S(2)}) %collective-permute-start.1) | collective-permute-done | bytes 49712 | tf_op jit(solution)/shard_map/ppermute | solution.py:37
  15.8 0.2 pad_maximum_fusion
  16.6 0.1 add_reduce_fusion
  16.7 0.2 select_reduce_fusion.1
  17.0 0.1 fusion.151
  17.1 0.2 convolution_convert_fusion.1
  17.3 0.1 reshape.466
  17.5 0.1 concatenate.65
  17.7 1.6 %collective-permute-start.7 = (bf16[32,768]{1,0:T(8,128)(2,1)S(1)}, bf16[32,768]{1,0:T(8,128)(2,1)S(1)}, u32[]{:S(2)}, u32[]{:S(2)}) collective-permute-start(bf16[32,768]{1,0:T(8,128)(2,1)S(1)} %add_convert_fusion.1), channel_id=1, source_target_pairs={{0,2},{1,3},{2,0},{3,1},{4,6},{5,7},{6,4},{7,5},{8,10},{9,11},{10,... | collective-permute-start | bytes 147464 | tf_op jit(solution)/shard_map/ppermute | solution.py:41
  19.2 0.1 maximum_select_fusion.4
  19.4 1.2 %collective-permute-start.10 = (bf16[4,32,384]{2,1,0:T(8,128)(2,1)S(1)}, bf16[4,32,384]{2,1,0:T(8,128)(2,1)S(1)}, u32[]{:S(2)}, u32[]{:S(2)}) collective-permute-start(bf16[4,32,384]{2,1,0:T(8,128)(2,1)S(1)} %maximum_select_fusion.4), channel_id=1, source_target_pairs={{0,2},{1,3},{2,0},{3,1},{4,6},{5,7},{6,4},{7,5},{8,10},{9,11},{10,... | collective-permute-start | bytes 294920 | tf_op jit(solution)/shard_map/ppermute | solution.py:41
  20.6 0.1 maximum_select_fusion.3
  20.7 1.2 %collective-permute-done.7 = bf16[32,768]{1,0:T(8,128)(2,1)S(1)} collective-permute-done((bf16[32,768]{1,0:T(8,128)(2,1)S(1)}, bf16[32,768]{1,0:T(8,128)(2,1)S(1)}, u32[]{:S(2)}, u32[]{:S(2)}) %collective-permute-start.7) | collective-permute-done | bytes 49184 | tf_op jit(solution)/shard_map/ppermute | solution.py:41
  22.0 2.4 %collective-permute-done.10 = bf16[4,32,384]{2,1,0:T(8,128)(2,1)S(1)} collective-permute-done((bf16[4,32,384]{2,1,0:T(8,128)(2,1)S(1)}, bf16[4,32,384]{2,1,0:T(8,128)(2,1)S(1)}, u32[]{:S(2)}, u32[]{:S(2)}) %collective-permute-start.10) | collective-permute-done | bytes 98336 | tf_op jit(solution)/shard_map/ppermute | solution.py:41
  24.3 0.1 convert_reduce_fusion
  24.5 0.2 fusion.11
  24.8 0.4 fusion.28
  25.3 0.1 reshape.582
  25.4 0.1 reshape.581
  25.6 0.1 pad_maximum_fusion.1
  25.8 0.2 multiply_reduce_fusion.1
  26.0 0.2 copy-done.4
  26.2 0.2 convolution_convert_fusion.8
  26.5 0.1 reshape_reshape.3
  26.6 0.2 convolution_convert_fusion
  26.8 0.1 reshape_reshape_reshape.3
  27.0 0.2 convolution_multiply_fusion
  27.3 0.3 fusion.5
  27.7 0.1 reshape.467
  27.8 0.1 copy-done.1
  27.9 0.2 convolution_convert_fusion.3
  28.4 1.1 %collective-permute-done.11 = bf16[64,768]{1,0:T(8,128)(2,1)S(1)} collective-permute-done((bf16[64,768]{1,0:T(8,128)(2,1)S(1)}, bf16[64,768]{1,0:T(8,128)(2,1)S(1)}, u32[]{:S(2)}, u32[]{:S(2)}) %collective-permute-start.11) | collective-permute-done | bytes 98336 | tf_op jit(solution)/shard_map/ppermute | solution.py:41
  29.6 1.2 %collective-permute-start.12 = (bf16[64,768]{1,0:T(8,128)(2,1)S(1)}, bf16[64,768]{1,0:T(8,128)(2,1)S(1)}, u32[]{:S(2)}, u32[]{:S(2)}) collective-permute-start(bf16[64,768]{1,0:T(8,128)(2,1)S(1)} %add_convert_fusion), channel_id=1, source_target_pairs={{0,2},{1,3},{2,0},{3,1},{4,6},{5,7},{6,4},{7,5},{8,10},{9,11},{10,... | collective-permute-start | bytes 294920 | tf_op jit(solution)/shard_map/ppermute | solution.py:41
  30.8 3.7 %collective-permute-done.12 = bf16[64,768]{1,0:T(8,128)(2,1)S(1)} collective-permute-done((bf16[64,768]{1,0:T(8,128)(2,1)S(1)}, bf16[64,768]{1,0:T(8,128)(2,1)S(1)}, u32[]{:S(2)}, u32[]{:S(2)}) %collective-permute-start.12) | collective-permute-done | bytes 98336 | tf_op jit(solution)/shard_map/ppermute | solution.py:41
  34.7 0.6 %gather_fusion = f32[4,32,768]{2,1,0:T(8,128)S(1)} fusion(f32[2,32,768]{2,1,0:T(8,128)S(1)} %convert_add_fusion.2, s32[1024]{0:T(1024)S(1)} %pad_clamp_fusion), kind=kCustom, calls=%fused_computation | custom fusion | bytes 786448 | tf_op jit(solution)/shard_map/jit(_take)/gather | solution.py:204
  35.3 0.7 %collective-permute-done.13 = f32[64,768]{1,0:T(8,128)S(1)} collective-permute-done((f32[64,768]{1,0:T(8,128)S(1)}, f32[64,768]{1,0:T(8,128)S(1)}, u32[]{:S(2)}, u32[]{:S(2)}) %collective-permute-start.13) | collective-permute-done | bytes 196640 | tf_op jit(solution)/shard_map/ppermute | solution.py:41
  36.1 0.2 fusion.153
  36.3 0.2 multiply_reduce_fusion
  36.5 2.7 %convolution_convert_fusion.2 = bf16[128,768]{1,0:T(8,128)(2,1)S(1)} fusion(bf16[768,768]{1,0:T(8,128)(2,1)S(1)} %copy-done, bf16[768,768]{1,0:T(8,128)(2,1)} %param.28, f32[128,768]{1,0:T(8,128)S(1)} %get-tuple-element.20, f32[768]{0:T(1024)S(1)} %copy-done.7, f32[128]{0:T(128)S(1)} %add_rsqrt_fusion.1, f32[128]{0:T(128)S(1)} %broadcast_multiply_fusion.1), kind=kOutput, calls=%fused_computation.6 | convolution fusion | flops 308871168 | bytes 2953216 | tf_op jit(solution)/shard_map/dot_general | solution.py:215
  39.2 0.2 copy.78
  39.8 1.0 %collective-permute-start.16 = (bf16[128,192]{1,0:T(8,128)(2,1)S(1)}, bf16[128,192]{1,0:T(8,128)(2,1)S(1)}, u32[]{:S(2)}, u32[]{:S(2)}) collective-permute-start(bf16[128,192]{1,0:T(8,128)(2,1)S(1)} %select_bitcast_fusion), channel_id=1, source_target_pairs={{0,3},{1,2},{2,1},{3,0},{4,7},{5,6},{6,5},{7,4},{8,11},{9,10},{10,... | collective-permute-start | bytes 147464 | tf_op jit(solution)/shard_map/ppermute | solution.py:41
  40.8 0.4 collective-permute-start.14
  41.2 0.9 %collective-permute-start.15 = (bf16[128,192]{1,0:T(8,128)(2,1)S(1)}, bf16[128,192]{1,0:T(8,128)(2,1)S(1)}, u32[]{:S(2)}, u32[]{:S(2)}) collective-permute-start(bf16[128,192]{1,0:T(8,128)(2,1)S(1)} %select_bitcast_fusion.1), channel_id=1, source_target_pairs={{0,2},{1,3},{2,0},{3,1},{4,6},{5,7},{6,4},{7,5},{8,10},{9,11},{10,... | collective-permute-start | bytes 147464 | tf_op jit(solution)/shard_map/ppermute | solution.py:41
  42.2 0.1 convolution_maximum_fusion
  42.6 1.4 %collective-permute-done.16 = bf16[128,192]{1,0:T(8,128)(2,1)S(1)} collective-permute-done((bf16[128,192]{1,0:T(8,128)(2,1)S(1)}, bf16[128,192]{1,0:T(8,128)(2,1)S(1)}, u32[]{:S(2)}, u32[]{:S(2)}) %collective-permute-start.16) | collective-permute-done | bytes 49184 | tf_op jit(solution)/shard_map/ppermute | solution.py:41
  43.9 1.7 %collective-permute-done.15 = bf16[128,192]{1,0:T(8,128)(2,1)S(1)} collective-permute-done((bf16[128,192]{1,0:T(8,128)(2,1)S(1)}, bf16[128,192]{1,0:T(8,128)(2,1)S(1)}, u32[]{:S(2)}, u32[]{:S(2)}) %collective-permute-start.15) | collective-permute-done | bytes 49184 | tf_op jit(solution)/shard_map/ppermute | solution.py:41
  45.7 0.1 add_add_fusion
  45.8 0.2 fusion.8
  46.0 0.6 %copy.86 = bf16[2,32,192]{2,1,0:T(8,128)(2,1)} copy(bf16[2,32,192]{2,0,1:T(2,128)(2,1)S(1)} %fusion.8) | data formatting | bytes 49152 | tf_op jit(solution)/shard_map/convert_element_type | solution.py:228
  (95 shorter events, 3.5 us)
Async XLA Ops:
  0.0 36.5 %copy-start = (bf16[768,768]{1,0:T(8,128)(2,1)S(1)}, bf16[768,768]{1,0:T(8,128)(2,1)}, u32[]{:S(2)}) copy-start(bf16[768,768]{1,0:T(8,128)(2,1)} %param.29) | copy-start | bytes 3538948
  0.0 9.5 %collective-permute-start.5 = (bf16[2,32,192]{2,1,0:T(8,128)(2,1)}, bf16[2,32,192]{2,1,0:T(8,128)(2,1)S(1)}, u32[]{:S(2)}, u32[]{:S(2)}) collective-permute-start(bf16[2,32,192]{2,1,0:T(8,128)(2,1)} %bitcast.76), channel_id=1, source_target_pairs={{0,1},{1,0},{2,3},{3,2},{4,5},{5,4},{6,7},{7,6},{8,9},{9,8},{10,11... | collective-permute-start | bytes 73736 | tf_op jit(solution)/shard_map/ppermute | solution.py:41
  0.5 10.1 %collective-permute-start.4 = (bf16[2,32,192]{2,1,0:T(8,128)(2,1)}, bf16[2,32,192]{2,1,0:T(8,128)(2,1)S(1)}, u32[]{:S(2)}, u32[]{:S(2)}) collective-permute-start(bf16[2,32,192]{2,1,0:T(8,128)(2,1)} %bitcast.77), channel_id=1, source_target_pairs={{0,2},{1,3},{2,0},{3,1},{4,6},{5,7},{6,4},{7,5},{8,10},{9,11},{10,... | collective-permute-start | bytes 73736 | tf_op jit(solution)/shard_map/ppermute | solution.py:41
  3.0 7.6 %collective-permute-start.3 = (bf16[2,32,192]{2,1,0:T(8,128)(2,1)}, bf16[2,32,192]{2,1,0:T(8,128)(2,1)S(1)}, u32[]{:S(2)}, u32[]{:S(2)}) collective-permute-start(bf16[2,32,192]{2,1,0:T(8,128)(2,1)} %bitcast.78), channel_id=1, source_target_pairs={{0,3},{1,2},{2,1},{3,0},{4,7},{5,6},{6,5},{7,4},{8,11},{9,10},{10,... | collective-permute-start | bytes 73736 | tf_op jit(solution)/shard_map/ppermute | solution.py:41
  5.6 9.2 %collective-permute-start.2 = (f32[12420]{0:T(1024)S(1)}, f32[12420]{0:T(1024)S(1)}, u32[]{:S(2)}, u32[]{:S(2)}) collective-permute-start(f32[12420]{0:T(1024)S(1)} %concatenate.56), channel_id=1, source_target_pairs={{0,12},{4,0},{8,4},{12,8},{1,13},{5,1},{9,5},{13,9},{2,14},{6,2},{... | collective-permute-start | bytes 149048 | tf_op jit(solution)/shard_map/ppermute | solution.py:37
  9.4 6.2 %collective-permute-start.1 = (f32[12420]{0:T(1024)S(1)}, f32[12420]{0:T(1024)S(1)}, u32[]{:S(2)}, u32[]{:S(2)}) collective-permute-start(f32[12420]{0:T(1024)S(1)} %concatenate.56), channel_id=1, source_target_pairs={{0,8},{4,12},{8,0},{12,4},{1,9},{5,13},{9,1},{13,5},{2,10},{6,14},... | collective-permute-start | bytes 149048 | tf_op jit(solution)/shard_map/ppermute | solution.py:37
  9.5 6.1 %collective-permute-start = (f32[12420]{0:T(1024)S(1)}, f32[12420]{0:T(1024)S(1)}, u32[]{:S(2)}, u32[]{:S(2)}) collective-permute-start(f32[12420]{0:T(1024)S(1)} %concatenate.56), channel_id=1, source_target_pairs={{0,4},{4,8},{8,12},{12,0},{1,5},{5,9},{9,13},{13,1},{2,6},{6,10},{... | collective-permute-start | bytes 149048 | tf_op jit(solution)/shard_map/ppermute | solution.py:37
  11.8 2.7 %copy-start.2 = (bf16[192,768]{1,0:T(8,128)(2,1)S(1)}, bf16[192,768]{1,0:T(8,128)(2,1)}, u32[]{:S(2)}) copy-start(bf16[192,768]{1,0:T(8,128)(2,1)} %param.24) | copy-start | bytes 884740
  14.7 3.0 %collective-permute-start.6 = (bf16[32,768]{1,0:T(8,128)(2,1)S(1)}, bf16[32,768]{1,0:T(8,128)(2,1)S(1)}, u32[]{:S(2)}, u32[]{:S(2)}) collective-permute-start(bf16[32,768]{1,0:T(8,128)(2,1)S(1)} %broadcast_select_fusion.5), channel_id=1, source_target_pairs={{0,1},{1,0},{2,3},{3,2},{4,5},{5,4},{6,7},{7,6},{8,9},{9,8},{10,11... | collective-permute-start | bytes 147464 | tf_op jit(solution)/shard_map/ppermute | solution.py:41
  15.8 9.1 %copy-start.3 = (bf16[2,768,192]{1,2,0:T(8,128)(2,1)S(1)}, bf16[2,768,192]{1,2,0:T(8,128)(2,1)}, u32[]{:S(2)}) copy-start(bf16[2,768,192]{1,2,0:T(8,128)(2,1)} %param.26) | copy-start | bytes 1769476
  15.8 9.1 %copy-start.5 = (f32[768]{0:T(1024)S(1)}, f32[768]{0:T(1024)}, u32[]{:S(2)}) copy-start(f32[768]{0:T(1024)} %param.21) | copy-start | bytes 9220
  17.6 1.7 %collective-permute-start.9 = (bf16[4,32,192]{2,1,0:T(8,128)(2,1)S(1)}, bf16[4,32,192]{2,1,0:T(8,128)(2,1)S(1)}, u32[]{:S(2)}, u32[]{:S(2)}) collective-permute-start(bf16[4,32,192]{2,1,0:T(8,128)(2,1)S(1)} %reshape.466), channel_id=1, source_target_pairs={{0,1},{1,0},{2,3},{3,2},{4,5},{5,4},{6,7},{7,6},{8,9},{9,8},{10,11... | collective-permute-start | bytes 147464 | tf_op jit(solution)/shard_map/ppermute | solution.py:41
  17.7 4.2 %collective-permute-start.7 = (bf16[32,768]{1,0:T(8,128)(2,1)S(1)}, bf16[32,768]{1,0:T(8,128)(2,1)S(1)}, u32[]{:S(2)}, u32[]{:S(2)}) collective-permute-start(bf16[32,768]{1,0:T(8,128)(2,1)S(1)} %add_convert_fusion.1), channel_id=1, source_target_pairs={{0,2},{1,3},{2,0},{3,1},{4,6},{5,7},{6,4},{7,5},{8,10},{9,11},{10,... | collective-permute-start | bytes 147464 | tf_op jit(solution)/shard_map/ppermute | solution.py:41
  19.4 5.0 %collective-permute-start.10 = (bf16[4,32,384]{2,1,0:T(8,128)(2,1)S(1)}, bf16[4,32,384]{2,1,0:T(8,128)(2,1)S(1)}, u32[]{:S(2)}, u32[]{:S(2)}) collective-permute-start(bf16[4,32,384]{2,1,0:T(8,128)(2,1)S(1)} %maximum_select_fusion.4), channel_id=1, source_target_pairs={{0,2},{1,3},{2,0},{3,1},{4,6},{5,7},{6,4},{7,5},{8,10},{9,11},{10,... | collective-permute-start | bytes 294920 | tf_op jit(solution)/shard_map/ppermute | solution.py:41
  21.9 3.7 %collective-permute-start.8 = (f32[32,768]{1,0:T(8,128)S(1)}, f32[32,768]{1,0:T(8,128)S(1)}, u32[]{:S(2)}, u32[]{:S(2)}) collective-permute-start(f32[32,768]{1,0:T(8,128)S(1)} %convert_add_fusion.3), channel_id=1, source_target_pairs={{0,1},{1,0},{2,3},{3,2},{4,5},{5,4},{6,7},{7,6},{8,9},{9,8},{10,11... | collective-permute-start | bytes 294920 | tf_op jit(solution)/shard_map/ppermute | solution.py:41
  25.2 1.0 %copy-start.4 = (bf16[768,192]{0,1:T(8,128)(2,1)S(1)}, bf16[768,192]{0,1:T(8,128)(2,1)}, u32[]{:S(2)}) copy-start(bf16[768,192]{0,1:T(8,128)(2,1)} %param.25) | copy-start | bytes 884740
  25.3 1.0 %copy-start.6 = (f32[768]{0:T(1024)S(1)}, f32[768]{0:T(1024)}, u32[]{:S(2)}) copy-start(f32[768]{0:T(1024)} %param.20) | copy-start | bytes 9220
  27.0 1.0 %copy-start.1 = (bf16[192,768]{1,0:T(8,128)(2,1)S(1)}, bf16[192,768]{1,0:T(8,128)(2,1)}, u32[]{:S(2)}) copy-start(bf16[192,768]{1,0:T(8,128)(2,1)} %param.27) | copy-start | bytes 884740
  28.2 1.4 %collective-permute-start.11 = (bf16[64,768]{1,0:T(8,128)(2,1)S(1)}, bf16[64,768]{1,0:T(8,128)(2,1)S(1)}, u32[]{:S(2)}, u32[]{:S(2)}) collective-permute-start(bf16[64,768]{1,0:T(8,128)(2,1)S(1)} %broadcast_select_fusion.2), channel_id=1, source_target_pairs={{0,1},{1,0},{2,3},{3,2},{4,5},{5,4},{6,7},{7,6},{8,9},{9,8},{10,11... | collective-permute-start | bytes 294920 | tf_op jit(solution)/shard_map/ppermute | solution.py:41
  29.6 4.9 %collective-permute-start.12 = (bf16[64,768]{1,0:T(8,128)(2,1)S(1)}, bf16[64,768]{1,0:T(8,128)(2,1)S(1)}, u32[]{:S(2)}, u32[]{:S(2)}) collective-permute-start(bf16[64,768]{1,0:T(8,128)(2,1)S(1)} %add_convert_fusion), channel_id=1, source_target_pairs={{0,2},{1,3},{2,0},{3,1},{4,6},{5,7},{6,4},{7,5},{8,10},{9,11},{10,... | collective-permute-start | bytes 294920 | tf_op jit(solution)/shard_map/ppermute | solution.py:41
  34.5 1.5 %collective-permute-start.13 = (f32[64,768]{1,0:T(8,128)S(1)}, f32[64,768]{1,0:T(8,128)S(1)}, u32[]{:S(2)}, u32[]{:S(2)}) collective-permute-start(f32[64,768]{1,0:T(8,128)S(1)} %convert_add_fusion.1), channel_id=1, source_target_pairs={{0,1},{1,0},{2,3},{3,2},{4,5},{5,4},{6,7},{7,6},{8,9},{9,8},{10,11... | collective-permute-start | bytes 589832 | tf_op jit(solution)/shard_map/ppermute | solution.py:41
  35.3 1.2 %copy-start.7 = (f32[768]{0:T(1024)S(1)}, f32[768]{0:T(1024)}, u32[]{:S(2)}) copy-start(f32[768]{0:T(1024)} %param.22) | copy-start | bytes 9220
  39.8 4.1 %collective-permute-start.16 = (bf16[128,192]{1,0:T(8,128)(2,1)S(1)}, bf16[128,192]{1,0:T(8,128)(2,1)S(1)}, u32[]{:S(2)}, u32[]{:S(2)}) collective-permute-start(bf16[128,192]{1,0:T(8,128)(2,1)S(1)} %select_bitcast_fusion), channel_id=1, source_target_pairs={{0,3},{1,2},{2,1},{3,0},{4,7},{5,6},{6,5},{7,4},{8,11},{9,10},{10,... | collective-permute-start | bytes 147464 | tf_op jit(solution)/shard_map/ppermute | solution.py:41
  40.8 3.2 %collective-permute-start.14 = (bf16[128,192]{1,0:T(8,128)(2,1)S(1)}, bf16[128,192]{1,0:T(8,128)(2,1)S(1)}, u32[]{:S(2)}, u32[]{:S(2)}) collective-permute-start(bf16[128,192]{1,0:T(8,128)(2,1)S(1)} %select_bitcast_fusion.2), channel_id=1, source_target_pairs={{0,1},{1,0},{2,3},{3,2},{4,5},{5,4},{6,7},{7,6},{8,9},{9,8},{10,11... | collective-permute-start | bytes 147464 | tf_op jit(solution)/shard_map/ppermute | solution.py:41
  41.2 4.4 %collective-permute-start.15 = (bf16[128,192]{1,0:T(8,128)(2,1)S(1)}, bf16[128,192]{1,0:T(8,128)(2,1)S(1)}, u32[]{:S(2)}, u32[]{:S(2)}) collective-permute-start(bf16[128,192]{1,0:T(8,128)(2,1)S(1)} %select_bitcast_fusion.1), channel_id=1, source_target_pairs={{0,2},{1,3},{2,0},{3,1},{4,6},{5,7},{6,4},{7,5},{8,10},{9,11},{10,... | collective-permute-start | bytes 147464 | tf_op jit(solution)/shard_map/ppermute | solution.py:41

commit v12 on v11

--- a/solution.py
+++ b/solution.py
@@ -148,19 +148,12 @@
     owners_n = lax.axis_size("pairs")
     own = lax.axis_index("pairs")
 
-    payload = jnp.concatenate(
-        [
-            tokens.astype(jnp.float32).reshape(-1),
-            pair_list.astype(jnp.float32).reshape(-1),
-            confidence.reshape(-1),
-        ]
-    )
-    table = pairs_gather(payload, owners_n)
-    cut_tok = img_dev * TOKS * quarter
-    cut_ids = cut_tok + views_n
-    all_tok = table[:, :cut_tok].astype(jnp.bfloat16).reshape(owners_n * img_dev, TOKS * quarter)
-    all_ids = table[:, cut_tok:cut_ids].astype(jnp.int32)
-    all_conf = table[:, cut_ids:].reshape(owners_n * views_n, TOKS)
+    small = jnp.concatenate(
+        [pair_list.astype(jnp.float32).reshape(-1), confidence.reshape(-1)]
+    )
+    table = pairs_gather(small, owners_n)
+    all_ids = table[:, :views_n].astype(jnp.int32)
+    all_conf = table[:, views_n:].reshape(owners_n * views_n, TOKS)
     partner_ids = all_ids.reshape(owners_n, pair_dev, 2)[:, :, ::-1].reshape(-1)
     all_ids = all_ids.reshape(-1)
 
@@ -173,11 +166,15 @@
     local = image % img_dev
     at = ((own - other // img_dev) % owners_n) * img_dev + other % img_dev
     far = (at[:, None] == jnp.arange(owners_n * img_dev)[None, :]).astype(jnp.bfloat16)
-    context_q = pick_rows(far, all_tok).reshape(views_n, TOKS, quarter)
 
     own_tok = mp_gather_cols(tokens.reshape(img_dev, TOKS, quarter))
     width = own_tok.shape[2]
     img_rows = img_dev * TOKS
+    all_tok = pairs_gather(own_tok.reshape(img_rows, width), owners_n).reshape(
+        owners_n * img_dev, TOKS * width
+    )
+    context_tok = pick_rows(far, all_tok).reshape(views_n * TOKS, width)
+
     begin = own_tok.astype(jnp.float32).reshape(img_rows, width)
     normed = layer_norm(begin, gain_self)
     qkv = jnp.einsum("rd,kdc->krc", normed, self_qkv, preferred_element_type=jnp.float32).astype(
@@ -193,9 +190,7 @@
     )
 
     rows_n = views_n * TOKS
-    context = layer_norm(mp_gather_steps(context_q).astype(jnp.float32), gain_context).reshape(
-        rows_n, width
-    )
+    context = layer_norm(context_tok.astype(jnp.float32), gain_context)
     keyval = jnp.einsum(
         "rd,kdc->krc", context, cross_kv, preferred_element_type=jnp.float32
     ).astype(jnp.bfloat16)

time: 47 us -> 57.5 us (1.22)
  waiting for transfers between devices: 13 us -> 22.1 us
  starting transfers between devices: 14.6 us -> 17.7 us
  local copies, waits for them, and re-layouts: 6.66 us -> 5.39 us
    ppermute x3 -> x6, waiting for transfers between devices: 0.79 us -> 8.58 us  [pairs_shift(): lax.ppermute(values, 'pairs', [(i, (i + step) % owners_n) for i in range(...]
    ppermute x3 -> x6, starting transfers between devices: 4.89 us -> 9.39 us  [pairs_shift(): lax.ppermute(values, 'pairs', [(i, (i + step) % owners_n) for i in range(...]
    ppermute x14 -> x12, starting transfers between devices: 9.75 us -> 8.27 us  [swap(): return lax.ppermute(values, 'mp', pairs)]
    ppermute x14 -> x12, waiting for transfers between devices: 12.2 us -> 13.5 us  [swap(): return lax.ppermute(values, 'mp', pairs)]
    reshape x4 -> x2, local copies, waits for them, and re-layouts: 1.1 us -> 0.26 us  [the longest x1 0.18 us: per_device(): pairs_gather(own_tok.reshape(img_rows, width), owners_n)]
  transfers between devices with their start and end apart: 17 -> 18, of which waited for: 8 -> 12; matrix products, arithmetic and copies ran while one was open for 24% -> 8% of each run, Pallas kernels for 0% -> 0%
where the time goes in v12:
time: 57.5 us; the launch traced here: 57.1 us
  waiting for transfers between devices  22.1 us (38%)
  starting transfers between devices  17.7 us (31%)
  matrix products  7.47 us (13%)
  local copies, waits for them, and re-layouts  5.39 us (9%)
  other arithmetic  3.95 us (7%)
    ppermute x12, waiting for transfers between devices, swap(): return lax.ppermute(values, 'mp', pairs)  13.5 us
    ppermute x6, starting transfers between devices, pairs_shift(): lax.ppermute(values, 'pairs', [(i, (i + step) % owners_n) for i in range(...  9.39 us
    ppermute x6, waiting for transfers between devices, pairs_shift(): lax.ppermute(values, 'pairs', [(i, (i + step) % owners_n) for i in range(...  8.58 us
    ppermute x12, starting transfers between devices, swap(): return lax.ppermute(values, 'mp', pairs)  8.27 us
    dot_general x1, matrix products, per_device(): jnp.dot(hidden.astype(jnp.bfloat16), mlp_down, preferred_element_type=jnp...  2.72 us
    dot_general x1, matrix products, per_device(): jnp.einsum('rd,kdc->krc', normed, self_qkv, preferred_element_type=jnp.fl...  1.67 us
  transfers between devices with their start and end apart: 18, of which 12 were waited for; matrix products, arithmetic and copies ran while one was open for 8% of the time, Pallas kernels for 0%

profile of v12, /device:TPU:0, one launch (start us, length us, event | category | flops | bytes accessed | tf_op | source)
XLA Modules:
  0.0 57.1 jit_solution(15577960683677148814)
XLA Ops:
  0.0 2.4 %collective-permute-start.3 = (bf16[2,32,192]{2,1,0:T(8,128)(2,1)}, bf16[2,32,192]{2,1,0:T(8,128)(2,1)S(1)}, u32[]{:S(2)}, u32[]{:S(2)}) collective-permute-start(bf16[2,32,192]{2,1,0:T(8,128)(2,1)} %bitcast.89), channel_id=1, source_target_pairs={{0,3},{1,2},{2,1},{3,0},{4,7},{5,6},{6,5},{7,4},{8,11},{9,10},{10,... | collective-permute-start | bytes 73736 | tf_op jit(solution)/shard_map/ppermute | solution.py:41
  2.4 0.6 %collective-permute-start.4 = (bf16[2,32,192]{2,1,0:T(8,128)(2,1)}, bf16[2,32,192]{2,1,0:T(8,128)(2,1)S(1)}, u32[]{:S(2)}, u32[]{:S(2)}) collective-permute-start(bf16[2,32,192]{2,1,0:T(8,128)(2,1)} %bitcast.90), channel_id=1, source_target_pairs={{0,2},{1,3},{2,0},{3,1},{4,6},{5,7},{6,4},{7,5},{8,10},{9,11},{10,... | collective-permute-start | bytes 73736 | tf_op jit(solution)/shard_map/ppermute | solution.py:41
  3.0 0.7 %convert_element_type.157 = f32[2,2]{1,0:T(2,128)S(1)} convert(s32[2,2]{1,0:T(2,128)} %param.17) | non-fusion elementwise | flops 4 | bytes 32 | tf_op jit(solution)/shard_map/convert_element_type | solution.py:152
  3.8 0.8 %reshape.430 = f32[128]{0:T(128)S(1)} reshape(f32[2,64]{1,0:T(2,128)} %param.18) | data formatting | bytes 1024 | tf_op jit(solution)/shard_map/reshape | solution.py:152
  4.6 1.6 %collective-permute-start = (f32[132]{0:T(256)S(1)}, f32[132]{0:T(256)S(1)}, u32[]{:S(2)}, u32[]{:S(2)}) collective-permute-start(f32[132]{0:T(256)S(1)} %pad_maximum_fusion.5), channel_id=1, source_target_pairs={{0,4},{4,8},{8,12},{12,0},{1,5},{5,9},{9,13},{13,1},{2,6},{6,10},{... | collective-permute-start | bytes 1592 | tf_op jit(solution)/shard_map/ppermute | solution.py:37
  6.2 2.6 %collective-permute-start.1 = (f32[132]{0:T(256)S(1)}, f32[132]{0:T(256)S(1)}, u32[]{:S(2)}, u32[]{:S(2)}) collective-permute-start(f32[132]{0:T(256)S(1)} %pad_maximum_fusion.5), channel_id=1, source_target_pairs={{0,8},{4,12},{8,0},{12,4},{1,9},{5,13},{9,1},{13,5},{2,10},{6,14},... | collective-permute-start | bytes 1592 | tf_op jit(solution)/shard_map/ppermute | solution.py:37
  8.8 1.3 %collective-permute-start.2 = (f32[132]{0:T(256)S(1)}, f32[132]{0:T(256)S(1)}, u32[]{:S(2)}, u32[]{:S(2)}) collective-permute-start(f32[132]{0:T(256)S(1)} %pad_maximum_fusion.5), channel_id=1, source_target_pairs={{0,12},{4,0},{8,4},{12,8},{1,13},{5,1},{9,5},{13,9},{2,14},{6,2},{... | collective-permute-start | bytes 1592 | tf_op jit(solution)/shard_map/ppermute | solution.py:37
  10.1 0.5 collective-permute-done.1
  10.7 1.7 %collective-permute-done.2 = f32[132]{0:T(256)S(1)} collective-permute-done((f32[132]{0:T(256)S(1)}, f32[132]{0:T(256)S(1)}, u32[]{:S(2)}, u32[]{:S(2)}) %collective-permute-start.2) | collective-permute-done | bytes 560 | tf_op jit(solution)/shard_map/ppermute | solution.py:37
  12.6 0.1 add_reduce_fusion
  13.1 0.8 %select_select_fusion.3 = (bf16[2,32,192]{2,1,0:T(8,128)(2,1)S(1)}, bf16[2,32,192]{2,1,0:T(8,128)(2,1)S(1)}, bf16[2,32,192]{2,1,0:T(8,128)(2,1)S(1)}, bf16[2,32,192]{2,1,0:T(8,128)(2,1)S(1)}) fusion(bf16[2,32,192]{2,1,0:T(8,128)(2,1)S(1)} %collective-permute-done.3, bf16[2,32,192]{2,1,0:T(8,128)(2,1)S(1)} %collective-permute-done.4, ...), kind=kLoop, calls=%fused_computation.142 | loop fusion | flops 147456 | bytes 196620 | tf_op jit(solution)/shard_map/jit(_where)/select_n | solution.py:91
  13.9 0.2 convert_reduce_fusion
  14.1 0.2 fusion.24
  14.3 1.7 %fusion.7 = bf16[3,64,192]{2,1,0:T(8,128)(2,1)S(1)} fusion(bf16[3,768,192]{1,2,0:T(8,128)(2,1)} %param.23, bf16[64,768]{1,0:T(8,128)(2,1)S(1)} %get-tuple-element.26, f32[768]{0:T(1024)} %param.19, f32[64]{0:T(128)S(1)} %add_rsqrt_fusion.3, f32[64]{0:T(128)S(1)} %broadcast_multiply_fusion.3), kind=kOutput, calls=%fused_computation.16 | convolution fusion | flops 56905728 | bytes 1060352 | tf_op jit(solution)/shard_map/rd,kdc->krc/dot_general | solution.py:180
  16.1 0.1 convolution_multiply_fusion.1
  16.3 0.2 fusion.148
  16.6 0.2 fusion.10
  17.0 0.2 convolution_convert_fusion.6
  17.3 0.1 select_reduce_fusion.1
  17.4 1.1 %collective-permute-done.6 = bf16[32,768]{1,0:T(8,128)(2,1)S(1)} collective-permute-done((bf16[32,768]{1,0:T(8,128)(2,1)S(1)}, bf16[32,768]{1,0:T(8,128)(2,1)S(1)}, u32[]{:S(2)}, u32[]{:S(2)}) %collective-permute-start.6) | collective-permute-done | bytes 49184 | tf_op jit(solution)/shard_map/ppermute | solution.py:41
  18.5 1.5 %collective-permute-start.7 = (bf16[32,768]{1,0:T(8,128)(2,1)S(1)}, bf16[32,768]{1,0:T(8,128)(2,1)S(1)}, u32[]{:S(2)}, u32[]{:S(2)}) collective-permute-start(bf16[32,768]{1,0:T(8,128)(2,1)S(1)} %add_convert_fusion.1), channel_id=1, source_target_pairs={{0,2},{1,3},{2,0},{3,1},{4,6},{5,7},{6,4},{7,5},{8,10},{9,11},{10,... | collective-permute-start | bytes 147464 | tf_op jit(solution)/shard_map/ppermute | solution.py:41
  20.0 2.7 %collective-permute-done.7 = bf16[32,768]{1,0:T(8,128)(2,1)S(1)} collective-permute-done((bf16[32,768]{1,0:T(8,128)(2,1)S(1)}, bf16[32,768]{1,0:T(8,128)(2,1)S(1)}, u32[]{:S(2)}, u32[]{:S(2)}) %collective-permute-start.7) | collective-permute-done | bytes 49184 | tf_op jit(solution)/shard_map/ppermute | solution.py:41
  22.8 1.3 %collective-permute-done.8 = f32[32,768]{1,0:T(8,128)S(1)} collective-permute-done((f32[32,768]{1,0:T(8,128)S(1)}, f32[32,768]{1,0:T(8,128)S(1)}, u32[]{:S(2)}, u32[]{:S(2)}) %collective-permute-start.8) | collective-permute-done | bytes 98336 | tf_op jit(solution)/shard_map/ppermute | solution.py:41
  24.1 0.1 fusion.81
  24.2 0.2 multiply_reduce_fusion.2
  24.5 0.3 collective-permute-start.9
  24.8 3.5 %collective-permute-start.10 = (bf16[64,768]{1,0:T(8,128)(2,1)S(1)}, bf16[64,768]{1,0:T(8,128)(2,1)S(1)}, u32[]{:S(2)}, u32[]{:S(2)}) collective-permute-start(bf16[64,768]{1,0:T(8,128)(2,1)S(1)} %bitcast.78), channel_id=1, source_target_pairs={{0,8},{4,12},{8,0},{12,4},{1,9},{5,13},{9,1},{13,5},{2,10},{6,14},... | collective-permute-start | bytes 294920 | tf_op jit(solution)/shard_map/ppermute | solution.py:37
  28.3 0.1 collective-permute-start.11
  28.4 0.2 convolution_convert_fusion.8
  28.8 0.2 convolution_convert_fusion.1
  29.0 0.1 reshape_reshape_reshape.3
  29.1 2.9 %collective-permute-done.9 = bf16[64,768]{1,0:T(8,128)(2,1)S(1)} collective-permute-done((bf16[64,768]{1,0:T(8,128)(2,1)S(1)}, bf16[64,768]{1,0:T(8,128)(2,1)S(1)}, u32[]{:S(2)}, u32[]{:S(2)}) %collective-permute-start.9) | collective-permute-done | bytes 98336 | tf_op jit(solution)/shard_map/ppermute | solution.py:37
  32.1 3.4 %collective-permute-done.10 = bf16[64,768]{1,0:T(8,128)(2,1)S(1)} collective-permute-done((bf16[64,768]{1,0:T(8,128)(2,1)S(1)}, bf16[64,768]{1,0:T(8,128)(2,1)S(1)}, u32[]{:S(2)}, u32[]{:S(2)}) %collective-permute-start.10) | collective-permute-done | bytes 98336 | tf_op jit(solution)/shard_map/ppermute | solution.py:37
  35.6 0.2 reshape.437
  35.8 0.3 fusion.2
  36.1 0.3 reshape.506
  36.5 0.2 multiply_reduce_fusion.1
  36.7 0.1 copy-done.1
  36.8 0.4 fusion.27
  37.3 0.1 reshape.552
  37.4 0.2 convolution_multiply_fusion
  37.7 0.1 reshape.551
  37.9 0.3 fusion.6
  38.2 0.1 reshape.438
  38.4 0.2 convolution_convert_fusion.3
  39.0 1.0 %collective-permute-done.12 = bf16[64,768]{1,0:T(8,128)(2,1)S(1)} collective-permute-done((bf16[64,768]{1,0:T(8,128)(2,1)S(1)}, bf16[64,768]{1,0:T(8,128)(2,1)S(1)}, u32[]{:S(2)}, u32[]{:S(2)}) %collective-permute-start.12) | collective-permute-done | bytes 98336 | tf_op jit(solution)/shard_map/ppermute | solution.py:41
  40.0 1.5 %collective-permute-start.13 = (bf16[64,768]{1,0:T(8,128)(2,1)S(1)}, bf16[64,768]{1,0:T(8,128)(2,1)S(1)}, u32[]{:S(2)}, u32[]{:S(2)}) collective-permute-start(bf16[64,768]{1,0:T(8,128)(2,1)S(1)} %add_convert_fusion), channel_id=1, source_target_pairs={{0,2},{1,3},{2,0},{3,1},{4,6},{5,7},{6,4},{7,5},{8,10},{9,11},{10,... | collective-permute-start | bytes 294920 | tf_op jit(solution)/shard_map/ppermute | solution.py:41
  41.5 3.5 %collective-permute-done.13 = bf16[64,768]{1,0:T(8,128)(2,1)S(1)} collective-permute-done((bf16[64,768]{1,0:T(8,128)(2,1)S(1)}, bf16[64,768]{1,0:T(8,128)(2,1)S(1)}, u32[]{:S(2)}, u32[]{:S(2)}) %collective-permute-start.13) | collective-permute-done | bytes 98336 | tf_op jit(solution)/shard_map/ppermute | solution.py:41
  45.1 0.1 fusion.143
  45.2 0.6 %gather_fusion = f32[4,32,768]{2,1,0:T(8,128)S(1)} fusion(f32[2,32,768]{2,1,0:T(8,128)S(1)} %get-tuple-element.23, s32[1024]{0:T(1024)S(1)} %pad_clamp_fusion), kind=kCustom, calls=%fused_computation | custom fusion | bytes 786448 | tf_op jit(solution)/shard_map/jit(_take)/gather | solution.py:199
  45.8 0.7 %collective-permute-done.14 = f32[64,768]{1,0:T(8,128)S(1)} collective-permute-done((f32[64,768]{1,0:T(8,128)S(1)}, f32[64,768]{1,0:T(8,128)S(1)}, u32[]{:S(2)}, u32[]{:S(2)}) %collective-permute-start.14) | collective-permute-done | bytes 196640 | tf_op jit(solution)/shard_map/ppermute | solution.py:41
  46.5 0.2 fusion.145
  46.7 0.2 multiply_reduce_fusion
  47.0 2.7 %convolution_convert_fusion.2 = bf16[128,768]{1,0:T(8,128)(2,1)S(1)} fusion(bf16[768,768]{1,0:T(8,128)(2,1)S(1)} %copy-done, bf16[768,768]{1,0:T(8,128)(2,1)} %param.28, f32[128,768]{1,0:T(8,128)S(1)} %get-tuple-element.20, f32[768]{0:T(1024)S(1)} %copy-done.7, f32[128]{0:T(128)S(1)} %add_rsqrt_fusion, f32[128]{0:T(128)S(1)} %broadcast_multiply_fusion), kind=kOutput, calls=%fused_computation.7 | convolution fusion | flops 308871168 | bytes 2953216 | tf_op jit(solution)/shard_map/dot_general | solution.py:210
  49.7 0.2 copy.78
  50.0 0.2 collective-permute-start.15
  50.4 1.5 %collective-permute-start.16 = (bf16[128,192]{1,0:T(8,128)(2,1)S(1)}, bf16[128,192]{1,0:T(8,128)(2,1)S(1)}, u32[]{:S(2)}, u32[]{:S(2)}) collective-permute-start(bf16[128,192]{1,0:T(8,128)(2,1)S(1)} %select_bitcast_fusion.1), channel_id=1, source_target_pairs={{0,2},{1,3},{2,0},{3,1},{4,6},{5,7},{6,4},{7,5},{8,10},{9,11},{10,... | collective-permute-start | bytes 147464 | tf_op jit(solution)/shard_map/ppermute | solution.py:41
  52.0 0.4 collective-permute-start.17
  52.3 0.1 convolution_maximum_fusion
  52.8 2.0 %collective-permute-done.16 = bf16[128,192]{1,0:T(8,128)(2,1)S(1)} collective-permute-done((bf16[128,192]{1,0:T(8,128)(2,1)S(1)}, bf16[128,192]{1,0:T(8,128)(2,1)S(1)}, u32[]{:S(2)}, u32[]{:S(2)}) %collective-permute-start.16) | collective-permute-done | bytes 49184 | tf_op jit(solution)/shard_map/ppermute | solution.py:41
  54.8 1.4 %collective-permute-done.17 = bf16[128,192]{1,0:T(8,128)(2,1)S(1)} collective-permute-done((bf16[128,192]{1,0:T(8,128)(2,1)S(1)}, bf16[128,192]{1,0:T(8,128)(2,1)S(1)}, u32[]{:S(2)}, u32[]{:S(2)}) %collective-permute-start.17) | collective-permute-done | bytes 49184 | tf_op jit(solution)/shard_map/ppermute | solution.py:41
  56.2 0.1 add_add_fusion
  56.3 0.2 fusion.9
  56.5 0.6 %copy.86 = bf16[2,32,192]{2,1,0:T(8,128)(2,1)} copy(bf16[2,32,192]{2,0,1:T(2,128)(2,1)S(1)} %fusion.9) | data formatting | bytes 49152 | tf_op jit(solution)/shard_map/convert_element_type | solution.py:223
  (87 shorter events, 3.3 us)
Async XLA Ops:
  0.0 46.9 %copy-start = (bf16[768,768]{1,0:T(8,128)(2,1)S(1)}, bf16[768,768]{1,0:T(8,128)(2,1)}, u32[]{:S(2)}) copy-start(bf16[768,768]{1,0:T(8,128)(2,1)} %param.29) | copy-start | bytes 3538948
  0.0 13.0 %collective-permute-start.3 = (bf16[2,32,192]{2,1,0:T(8,128)(2,1)}, bf16[2,32,192]{2,1,0:T(8,128)(2,1)S(1)}, u32[]{:S(2)}, u32[]{:S(2)}) collective-permute-start(bf16[2,32,192]{2,1,0:T(8,128)(2,1)} %bitcast.89), channel_id=1, source_target_pairs={{0,3},{1,2},{2,1},{3,0},{4,7},{5,6},{6,5},{7,4},{8,11},{9,10},{10,... | collective-permute-start | bytes 73736 | tf_op jit(solution)/shard_map/ppermute | solution.py:41
  2.4 10.7 %collective-permute-start.4 = (bf16[2,32,192]{2,1,0:T(8,128)(2,1)}, bf16[2,32,192]{2,1,0:T(8,128)(2,1)S(1)}, u32[]{:S(2)}, u32[]{:S(2)}) collective-permute-start(bf16[2,32,192]{2,1,0:T(8,128)(2,1)} %bitcast.90), channel_id=1, source_target_pairs={{0,2},{1,3},{2,0},{3,1},{4,6},{5,7},{6,4},{7,5},{8,10},{9,11},{10,... | collective-permute-start | bytes 73736 | tf_op jit(solution)/shard_map/ppermute | solution.py:41
  4.6 5.5 %collective-permute-start = (f32[132]{0:T(256)S(1)}, f32[132]{0:T(256)S(1)}, u32[]{:S(2)}, u32[]{:S(2)}) collective-permute-start(f32[132]{0:T(256)S(1)} %pad_maximum_fusion.5), channel_id=1, source_target_pairs={{0,4},{4,8},{8,12},{12,0},{1,5},{5,9},{9,13},{13,1},{2,6},{6,10},{... | collective-permute-start | bytes 1592 | tf_op jit(solution)/shard_map/ppermute | solution.py:37
  6.2 4.5 %collective-permute-start.1 = (f32[132]{0:T(256)S(1)}, f32[132]{0:T(256)S(1)}, u32[]{:S(2)}, u32[]{:S(2)}) collective-permute-start(f32[132]{0:T(256)S(1)} %pad_maximum_fusion.5), channel_id=1, source_target_pairs={{0,8},{4,12},{8,0},{12,4},{1,9},{5,13},{9,1},{13,5},{2,10},{6,14},... | collective-permute-start | bytes 1592 | tf_op jit(solution)/shard_map/ppermute | solution.py:37
  8.8 3.6 %collective-permute-start.2 = (f32[132]{0:T(256)S(1)}, f32[132]{0:T(256)S(1)}, u32[]{:S(2)}, u32[]{:S(2)}) collective-permute-start(f32[132]{0:T(256)S(1)} %pad_maximum_fusion.5), channel_id=1, source_target_pairs={{0,12},{4,0},{8,4},{12,8},{1,13},{5,1},{9,5},{13,9},{2,14},{6,2},{... | collective-permute-start | bytes 1592 | tf_op jit(solution)/shard_map/ppermute | solution.py:37
  10.1 2.9 %collective-permute-start.5 = (bf16[2,32,192]{2,1,0:T(8,128)(2,1)}, bf16[2,32,192]{2,1,0:T(8,128)(2,1)S(1)}, u32[]{:S(2)}, u32[]{:S(2)}) collective-permute-start(bf16[2,32,192]{2,1,0:T(8,128)(2,1)} %bitcast.91), channel_id=1, source_target_pairs={{0,1},{1,0},{2,3},{3,2},{4,5},{5,4},{6,7},{7,6},{8,9},{9,8},{10,11... | collective-permute-start | bytes 73736 | tf_op jit(solution)/shard_map/ppermute | solution.py:41
  14.3 2.7 %copy-start.3 = (bf16[192,768]{1,0:T(8,128)(2,1)S(1)}, bf16[192,768]{1,0:T(8,128)(2,1)}, u32[]{:S(2)}) copy-start(bf16[192,768]{1,0:T(8,128)(2,1)} %param.24) | copy-start | bytes 884740
  17.1 11.3 %copy-start.5 = (bf16[768,192]{0,1:T(8,128)(2,1)S(1)}, bf16[768,192]{0,1:T(8,128)(2,1)}, u32[]{:S(2)}) copy-start(bf16[768,192]{0,1:T(8,128)(2,1)} %param.25) | copy-start | bytes 884740
  17.1 11.2 %copy-start.6 = (f32[768]{0:T(1024)S(1)}, f32[768]{0:T(1024)}, u32[]{:S(2)}) copy-start(f32[768]{0:T(1024)} %param.20) | copy-start | bytes 9220
  17.2 1.3 %collective-permute-start.6 = (bf16[32,768]{1,0:T(8,128)(2,1)S(1)}, bf16[32,768]{1,0:T(8,128)(2,1)S(1)}, u32[]{:S(2)}, u32[]{:S(2)}) collective-permute-start(bf16[32,768]{1,0:T(8,128)(2,1)S(1)} %broadcast_select_fusion.5), channel_id=1, source_target_pairs={{0,1},{1,0},{2,3},{3,2},{4,5},{5,4},{6,7},{7,6},{8,9},{9,8},{10,11... | collective-permute-start | bytes 147464 | tf_op jit(solution)/shard_map/ppermute | solution.py:41
  18.5 4.2 %collective-permute-start.7 = (bf16[32,768]{1,0:T(8,128)(2,1)S(1)}, bf16[32,768]{1,0:T(8,128)(2,1)S(1)}, u32[]{:S(2)}, u32[]{:S(2)}) collective-permute-start(bf16[32,768]{1,0:T(8,128)(2,1)S(1)} %add_convert_fusion.1), channel_id=1, source_target_pairs={{0,2},{1,3},{2,0},{3,1},{4,6},{5,7},{6,4},{7,5},{8,10},{9,11},{10,... | collective-permute-start | bytes 147464 | tf_op jit(solution)/shard_map/ppermute | solution.py:41
  22.7 1.4 %collective-permute-start.8 = (f32[32,768]{1,0:T(8,128)S(1)}, f32[32,768]{1,0:T(8,128)S(1)}, u32[]{:S(2)}, u32[]{:S(2)}) collective-permute-start(f32[32,768]{1,0:T(8,128)S(1)} %convert_add_fusion.3), channel_id=1, source_target_pairs={{0,1},{1,0},{2,3},{3,2},{4,5},{5,4},{6,7},{7,6},{8,9},{9,8},{10,11... | collective-permute-start | bytes 294920 | tf_op jit(solution)/shard_map/ppermute | solution.py:41
  24.5 7.6 %collective-permute-start.9 = (bf16[64,768]{1,0:T(8,128)(2,1)S(1)}, bf16[64,768]{1,0:T(8,128)(2,1)S(1)}, u32[]{:S(2)}, u32[]{:S(2)}) collective-permute-start(bf16[64,768]{1,0:T(8,128)(2,1)S(1)} %bitcast.77), channel_id=1, source_target_pairs={{0,4},{4,8},{8,12},{12,0},{1,5},{5,9},{9,13},{13,1},{2,6},{6,10},{... | collective-permute-start | bytes 294920 | tf_op jit(solution)/shard_map/ppermute | solution.py:37
  24.8 10.7 %collective-permute-start.10 = (bf16[64,768]{1,0:T(8,128)(2,1)S(1)}, bf16[64,768]{1,0:T(8,128)(2,1)S(1)}, u32[]{:S(2)}, u32[]{:S(2)}) collective-permute-start(bf16[64,768]{1,0:T(8,128)(2,1)S(1)} %bitcast.78), channel_id=1, source_target_pairs={{0,8},{4,12},{8,0},{12,4},{1,9},{5,13},{9,1},{13,5},{2,10},{6,14},... | collective-permute-start | bytes 294920 | tf_op jit(solution)/shard_map/ppermute | solution.py:37
  28.3 7.3 %collective-permute-start.11 = (bf16[64,768]{1,0:T(8,128)(2,1)S(1)}, bf16[64,768]{1,0:T(8,128)(2,1)S(1)}, u32[]{:S(2)}, u32[]{:S(2)}) collective-permute-start(bf16[64,768]{1,0:T(8,128)(2,1)S(1)} %bitcast.79), channel_id=1, source_target_pairs={{0,12},{4,0},{8,4},{12,8},{1,13},{5,1},{9,5},{13,9},{2,14},{6,2},{... | collective-permute-start | bytes 294920 | tf_op jit(solution)/shard_map/ppermute | solution.py:37
  35.8 1.1 %copy-start.1 = (bf16[2,768,192]{1,2,0:T(8,128)(2,1)S(1)}, bf16[2,768,192]{1,2,0:T(8,128)(2,1)}, u32[]{:S(2)}) copy-start(bf16[2,768,192]{1,2,0:T(8,128)(2,1)} %param.26) | copy-start | bytes 1769476
  35.8 1.1 %copy-start.4 = (f32[768]{0:T(1024)S(1)}, f32[768]{0:T(1024)}, u32[]{:S(2)}) copy-start(f32[768]{0:T(1024)} %param.21) | copy-start | bytes 9220
  37.4 1.0 %copy-start.2 = (bf16[192,768]{1,0:T(8,128)(2,1)S(1)}, bf16[192,768]{1,0:T(8,128)(2,1)}, u32[]{:S(2)}) copy-start(bf16[192,768]{1,0:T(8,128)(2,1)} %param.27) | copy-start | bytes 884740
  38.6 1.4 %collective-permute-start.12 = (bf16[64,768]{1,0:T(8,128)(2,1)S(1)}, bf16[64,768]{1,0:T(8,128)(2,1)S(1)}, u32[]{:S(2)}, u32[]{:S(2)}) collective-permute-start(bf16[64,768]{1,0:T(8,128)(2,1)S(1)} %broadcast_select_fusion.2), channel_id=1, source_target_pairs={{0,1},{1,0},{2,3},{3,2},{4,5},{5,4},{6,7},{7,6},{8,9},{9,8},{10,11... | collective-permute-start | bytes 294920 | tf_op jit(solution)/shard_map/ppermute | solution.py:41
  40.0 4.9 %collective-permute-start.13 = (bf16[64,768]{1,0:T(8,128)(2,1)S(1)}, bf16[64,768]{1,0:T(8,128)(2,1)S(1)}, u32[]{:S(2)}, u32[]{:S(2)}) collective-permute-start(bf16[64,768]{1,0:T(8,128)(2,1)S(1)} %add_convert_fusion), channel_id=1, source_target_pairs={{0,2},{1,3},{2,0},{3,1},{4,6},{5,7},{6,4},{7,5},{8,10},{9,11},{10,... | collective-permute-start | bytes 294920 | tf_op jit(solution)/shard_map/ppermute | solution.py:41
  45.0 1.5 %collective-permute-start.14 = (f32[64,768]{1,0:T(8,128)S(1)}, f32[64,768]{1,0:T(8,128)S(1)}, u32[]{:S(2)}, u32[]{:S(2)}) collective-permute-start(f32[64,768]{1,0:T(8,128)S(1)} %convert_add_fusion.1), channel_id=1, source_target_pairs={{0,1},{1,0},{2,3},{3,2},{4,5},{5,4},{6,7},{7,6},{8,9},{9,8},{10,11... | collective-permute-start | bytes 589832 | tf_op jit(solution)/shard_map/ppermute | solution.py:41
  45.8 1.2 %copy-start.7 = (f32[768]{0:T(1024)S(1)}, f32[768]{0:T(1024)}, u32[]{:S(2)}) copy-start(f32[768]{0:T(1024)} %param.22) | copy-start | bytes 9220
  50.0 2.7 %collective-permute-start.15 = (bf16[128,192]{1,0:T(8,128)(2,1)S(1)}, bf16[128,192]{1,0:T(8,128)(2,1)S(1)}, u32[]{:S(2)}, u32[]{:S(2)}) collective-permute-start(bf16[128,192]{1,0:T(8,128)(2,1)S(1)} %select_bitcast_fusion.2), channel_id=1, source_target_pairs={{0,1},{1,0},{2,3},{3,2},{4,5},{5,4},{6,7},{7,6},{8,9},{9,8},{10,11... | collective-permute-start | bytes 147464 | tf_op jit(solution)/shard_map/ppermute | solution.py:41
  50.4 4.4 %collective-permute-start.16 = (bf16[128,192]{1,0:T(8,128)(2,1)S(1)}, bf16[128,192]{1,0:T(8,128)(2,1)S(1)}, u32[]{:S(2)}, u32[]{:S(2)}) collective-permute-start(bf16[128,192]{1,0:T(8,128)(2,1)S(1)} %select_bitcast_fusion.1), channel_id=1, source_target_pairs={{0,2},{1,3},{2,0},{3,1},{4,6},{5,7},{6,4},{7,5},{8,10},{9,11},{10,... | collective-permute-start | bytes 147464 | tf_op jit(solution)/shard_map/ppermute | solution.py:41
  52.0 4.2 %collective-permute-start.17 = (bf16[128,192]{1,0:T(8,128)(2,1)S(1)}, bf16[128,192]{1,0:T(8,128)(2,1)S(1)}, u32[]{:S(2)}, u32[]{:S(2)}) collective-permute-start(bf16[128,192]{1,0:T(8,128)(2,1)S(1)} %select_bitcast_fusion), channel_id=1, source_target_pairs={{0,3},{1,2},{2,1},{3,0},{4,7},{5,6},{6,5},{7,4},{8,11},{9,10},{10,... | collective-permute-start | bytes 147464 | tf_op jit(solution)/shard_map/ppermute | solution.py:41

commit v13 on v12

--- a/solution.py
+++ b/solution.py
@@ -148,12 +148,12 @@
     owners_n = lax.axis_size("pairs")
     own = lax.axis_index("pairs")
 
-    small = jnp.concatenate(
-        [pair_list.astype(jnp.float32).reshape(-1), confidence.reshape(-1)]
-    )
+    all_tok = pairs_gather(tokens, owners_n).reshape(owners_n * img_dev, TOKS * quarter)
+    small = jnp.concatenate([confidence, pair_list.astype(jnp.float32)], axis=1)
     table = pairs_gather(small, owners_n)
-    all_ids = table[:, :views_n].astype(jnp.int32)
-    all_conf = table[:, views_n:].reshape(owners_n * views_n, TOKS)
+    conf_w = confidence.shape[1]
+    all_conf = table[:, :, :conf_w].reshape(owners_n * views_n, TOKS)
+    all_ids = table[:, :, conf_w:].reshape(owners_n, views_n).astype(jnp.int32)
     partner_ids = all_ids.reshape(owners_n, pair_dev, 2)[:, :, ::-1].reshape(-1)
     all_ids = all_ids.reshape(-1)
 
@@ -166,15 +166,11 @@
     local = image % img_dev
     at = ((own - other // img_dev) % owners_n) * img_dev + other % img_dev
     far = (at[:, None] == jnp.arange(owners_n * img_dev)[None, :]).astype(jnp.bfloat16)
+    context_q = pick_rows(far, all_tok).reshape(views_n, TOKS, quarter)
 
     own_tok = mp_gather_cols(tokens.reshape(img_dev, TOKS, quarter))
     width = own_tok.shape[2]
     img_rows = img_dev * TOKS
-    all_tok = pairs_gather(own_tok.reshape(img_rows, width), owners_n).reshape(
-        owners_n * img_dev, TOKS * width
-    )
-    context_tok = pick_rows(far, all_tok).reshape(views_n * TOKS, width)
-
     begin = own_tok.astype(jnp.float32).reshape(img_rows, width)
     normed = layer_norm(begin, gain_self)
     qkv = jnp.einsum("rd,kdc->krc", normed, self_qkv, preferred_element_type=jnp.float32).astype(
@@ -190,7 +186,9 @@
     )
 
     rows_n = views_n * TOKS
-    context = layer_norm(context_tok.astype(jnp.float32), gain_context)
+    context = layer_norm(mp_gather_steps(context_q).astype(jnp.float32), gain_context).reshape(
+        rows_n, width
+    )
     keyval = jnp.einsum(
         "rd,kdc->krc", context, cross_kv, preferred_element_type=jnp.float32
     ).astype(jnp.bfloat16)

time: 57.5 us -> 51.5 us (0.90)
  waiting for transfers between devices: 22.1 us -> 13 us
  starting transfers between devices: 17.7 us -> 20.7 us
  other arithmetic: 3.95 us -> 4.94 us
  local copies, waits for them, and re-layouts: 5.39 us -> 4.69 us
    ppermute x6, waiting for transfers between devices: 8.58 us -> 0.65 us  [pairs_shift(): lax.ppermute(values, 'pairs', [(i, (i + step) % owners_n) for i in range(...]
    ppermute x6, starting transfers between devices: 9.39 us -> 11 us  [pairs_shift(): lax.ppermute(values, 'pairs', [(i, (i + step) % owners_n) for i in range(...]
    ppermute x12 -> x14, starting transfers between devices: 8.27 us -> 9.68 us  [swap(): return lax.ppermute(values, 'mp', pairs)]
    ppermute x12 -> x14, waiting for transfers between devices: 13.5 us -> 12.3 us  [swap(): return lax.ppermute(values, 'mp', pairs)]
    reshape x6 -> x3, local copies, waits for them, and re-layouts: 1.26 us -> 0.35 us  [the longest x1 0.16 us: per_device(): pairs_gather(tokens, owners_n).reshape(owners_n * img_dev, TOKS * quarter)]
    concatenate x1 -> x2, other arithmetic: 0.08 us -> 0.88 us  [the longest x1 0.75 us: per_device(): small = jnp.concatenate([confidence, pair_list.astype(jnp.float32)], axis=1)]
  transfers between devices with their start and end apart: 18 -> 20, of which waited for: 12 -> 9; matrix products, arithmetic and copies ran while one was open for 8% -> 20% of each run, Pallas kernels for 0% -> 0%
where the time goes in v13:
time: 51.5 us; the launch traced here: 51.2 us
  starting transfers between devices  20.7 us (40%)
  waiting for transfers between devices  13 us (25%)
  matrix products  7.38 us (14%)
  other arithmetic  4.94 us (10%)
  local copies, waits for them, and re-layouts  4.69 us (9%)
  between operations  0.59 us (1%)
    ppermute x14, waiting for transfers between devices, swap(): return lax.ppermute(values, 'mp', pairs)  12.3 us
    ppermute x6, starting transfers between devices, pairs_shift(): lax.ppermute(values, 'pairs', [(i, (i + step) % owners_n) for i in range(...  11 us
    ppermute x14, starting transfers between devices, swap(): return lax.ppermute(values, 'mp', pairs)  9.68 us
    dot_general x1, matrix products, per_device(): jnp.dot(hidden.astype(jnp.bfloat16), mlp_down, preferred_element_type=jnp...  2.71 us
    dot_general x1, matrix products, per_device(): jnp.einsum('rd,kdc->krc', normed, self_qkv, preferred_element_type=jnp.fl...  1.67 us
  transfers between devices with their start and end apart: 20, of which 9 were waited for; matrix products, arithmetic and copies ran while one was open for 20% of the time, Pallas kernels for 0%

profile of v13, /device:TPU:0, one launch (start us, length us, event | category | flops | bytes accessed | tf_op | source)
XLA Modules:
  0.0 51.2 jit_solution(12906830896736403305)
XLA Ops:
  0.0 2.4 %collective-permute-start.3 = (bf16[2,32,192]{2,1,0:T(8,128)(2,1)}, bf16[2,32,192]{2,1,0:T(8,128)(2,1)S(1)}, u32[]{:S(2)}, u32[]{:S(2)}) collective-permute-start(bf16[2,32,192]{2,1,0:T(8,128)(2,1)} %bitcast.84), channel_id=1, source_target_pairs={{0,3},{1,2},{2,1},{3,0},{4,7},{5,6},{6,5},{7,4},{8,11},{9,10},{10,... | collective-permute-start | bytes 73736 | tf_op jit(solution)/shard_map/ppermute | solution.py:41
  2.4 0.6 %collective-permute-start.4 = (bf16[2,32,192]{2,1,0:T(8,128)(2,1)}, bf16[2,32,192]{2,1,0:T(8,128)(2,1)S(1)}, u32[]{:S(2)}, u32[]{:S(2)}) collective-permute-start(bf16[2,32,192]{2,1,0:T(8,128)(2,1)} %bitcast.85), channel_id=1, source_target_pairs={{0,2},{1,3},{2,0},{3,1},{4,6},{5,7},{6,4},{7,5},{8,10},{9,11},{10,... | collective-permute-start | bytes 73736 | tf_op jit(solution)/shard_map/ppermute | solution.py:41
  3.0 0.7 %convert_element_type.182 = f32[2,2]{1,0:T(2,128)S(1)} convert(s32[2,2]{1,0:T(2,128)} %param.17) | non-fusion elementwise | flops 4 | bytes 32 | tf_op jit(solution)/shard_map/convert_element_type | solution.py:152
  3.7 0.8 %pad_maximum_fusion.4 = f32[2,66]{1,0:T(2,128)S(1)} fusion(f32[2,2]{1,0:T(2,128)S(1)} %convert_element_type.182, f32[2,64]{1,0:T(2,128)} %param.18), kind=kLoop, calls=%fused_computation.200 | loop fusion | flops 132 | bytes 1056 | tf_op jit(solution)/shard_map/concatenate | solution.py:152
  4.4 1.6 %collective-permute-start = (f32[2,66]{1,0:T(2,128)S(1)}, f32[2,66]{1,0:T(2,128)S(1)}, u32[]{:S(2)}, u32[]{:S(2)}) collective-permute-start(f32[2,66]{1,0:T(2,128)S(1)} %pad_maximum_fusion.4), channel_id=1, source_target_pairs={{0,4},{4,8},{8,12},{12,0},{1,5},{5,9},{9,13},{13,1},{2,6},{6,10},{... | collective-permute-start | bytes 1592 | tf_op jit(solution)/shard_map/ppermute | solution.py:37
  6.0 2.6 %collective-permute-start.1 = (f32[2,66]{1,0:T(2,128)S(1)}, f32[2,66]{1,0:T(2,128)S(1)}, u32[]{:S(2)}, u32[]{:S(2)}) collective-permute-start(f32[2,66]{1,0:T(2,128)S(1)} %pad_maximum_fusion.4), channel_id=1, source_target_pairs={{0,8},{4,12},{8,0},{12,4},{1,9},{5,13},{9,1},{13,5},{2,10},{6,14},... | collective-permute-start | bytes 1592 | tf_op jit(solution)/shard_map/ppermute | solution.py:37
  8.6 1.3 %collective-permute-start.2 = (f32[2,66]{1,0:T(2,128)S(1)}, f32[2,66]{1,0:T(2,128)S(1)}, u32[]{:S(2)}, u32[]{:S(2)}) collective-permute-start(f32[2,66]{1,0:T(2,128)S(1)} %pad_maximum_fusion.4), channel_id=1, source_target_pairs={{0,12},{4,0},{8,4},{12,8},{1,13},{5,1},{9,5},{13,9},{2,14},{6,2},{... | collective-permute-start | bytes 1592 | tf_op jit(solution)/shard_map/ppermute | solution.py:37
  10.0 0.5 %collective-permute-done.1 = f32[2,66]{1,0:T(2,128)S(1)} collective-permute-done((f32[2,66]{1,0:T(2,128)S(1)}, f32[2,66]{1,0:T(2,128)S(1)}, u32[]{:S(2)}, u32[]{:S(2)}) %collective-permute-start.1) | collective-permute-done | bytes 560 | tf_op jit(solution)/shard_map/ppermute | solution.py:37
  10.5 1.6 %collective-permute-start.9 = (bf16[64,192]{1,0:T(8,128)(2,1)}, bf16[64,192]{1,0:T(8,128)(2,1)S(1)}, u32[]{:S(2)}, u32[]{:S(2)}) collective-permute-start(bf16[64,192]{1,0:T(8,128)(2,1)} %param.16), channel_id=1, source_target_pairs={{0,4},{4,8},{8,12},{12,0},{1,5},{5,9},{9,13},{13,1},{2,6},{6,10},{... | collective-permute-start | bytes 73736 | tf_op jit(solution)/shard_map/ppermute | solution.py:37
  12.1 0.1 collective-permute-done.2
  12.2 1.1 %collective-permute-start.10 = (bf16[64,192]{1,0:T(8,128)(2,1)}, bf16[64,192]{1,0:T(8,128)(2,1)S(1)}, u32[]{:S(2)}, u32[]{:S(2)}) collective-permute-start(bf16[64,192]{1,0:T(8,128)(2,1)} %param.16), channel_id=1, source_target_pairs={{0,8},{4,12},{8,0},{12,4},{1,9},{5,13},{9,1},{13,5},{2,10},{6,14},... | collective-permute-start | bytes 73736 | tf_op jit(solution)/shard_map/ppermute | solution.py:37
  13.7 0.1 add_reduce_fusion
  13.9 0.2 select_reduce_fusion.1
  14.2 0.1 fusion.151
  14.3 2.8 %collective-permute-start.11 = (bf16[64,192]{1,0:T(8,128)(2,1)}, bf16[64,192]{1,0:T(8,128)(2,1)S(1)}, u32[]{:S(2)}, u32[]{:S(2)}) collective-permute-start(bf16[64,192]{1,0:T(8,128)(2,1)} %param.16), channel_id=1, source_target_pairs={{0,12},{4,0},{8,4},{12,8},{1,13},{5,1},{9,5},{13,9},{2,14},{6,2},{... | collective-permute-start | bytes 73736 | tf_op jit(solution)/shard_map/ppermute | solution.py:37
  17.1 0.8 %select_select_fusion.3 = (bf16[2,32,192]{2,1,0:T(8,128)(2,1)S(1)}, bf16[2,32,192]{2,1,0:T(8,128)(2,1)S(1)}, bf16[2,32,192]{2,1,0:T(8,128)(2,1)S(1)}, bf16[2,32,192]{2,1,0:T(8,128)(2,1)S(1)}) fusion(bf16[2,32,192]{2,1,0:T(8,128)(2,1)S(1)} %collective-permute-done.3, bf16[2,32,192]{2,1,0:T(8,128)(2,1)S(1)} %collective-permute-done.4, ...), kind=kLoop, calls=%fused_computation.153 | loop fusion | flops 147456 | bytes 196620 | tf_op jit(solution)/shard_map/jit(_where)/select_n | solution.py:91
  17.9 0.2 convert_reduce_fusion.1
  18.1 0.2 fusion.25
  18.3 1.7 %fusion.6 = bf16[3,64,192]{2,1,0:T(8,128)(2,1)S(1)} fusion(bf16[3,768,192]{1,2,0:T(8,128)(2,1)} %param.23, bf16[64,768]{1,0:T(8,128)(2,1)S(1)} %get-tuple-element.24, f32[768]{0:T(1024)} %param.19, f32[64]{0:T(128)S(1)} %add_rsqrt_fusion.3, f32[64]{0:T(128)S(1)} %broadcast_multiply_fusion.3), kind=kOutput, calls=%fused_computation.15 | convolution fusion | flops 56905728 | bytes 1060352 | tf_op jit(solution)/shard_map/rd,kdc->krc/dot_general | solution.py:176
  20.2 0.1 convolution_multiply_fusion.1
  20.4 0.2 fusion.156
  20.7 0.2 fusion.9
  21.0 0.2 convolution_convert_fusion.6
  21.4 0.2 reshape.417
  21.6 0.2 convolution_convert_fusion.1
  22.0 0.5 %collective-permute-start.12 = (bf16[4,32,192]{2,1,0:T(8,128)(2,1)S(1)}, bf16[4,32,192]{2,1,0:T(8,128)(2,1)S(1)}, u32[]{:S(2)}, u32[]{:S(2)}) collective-permute-start(bf16[4,32,192]{2,1,0:T(8,128)(2,1)S(1)} %reshape.418), channel_id=1, source_target_pairs={{0,1},{1,0},{2,3},{3,2},{4,5},{5,4},{6,7},{7,6},{8,9},{9,8},{10,11... | collective-permute-start | bytes 147464 | tf_op jit(solution)/shard_map/ppermute | solution.py:41
  22.6 1.5 %collective-permute-start.7 = (bf16[32,768]{1,0:T(8,128)(2,1)S(1)}, bf16[32,768]{1,0:T(8,128)(2,1)S(1)}, u32[]{:S(2)}, u32[]{:S(2)}) collective-permute-start(bf16[32,768]{1,0:T(8,128)(2,1)S(1)} %add_convert_fusion.1), channel_id=1, source_target_pairs={{0,2},{1,3},{2,0},{3,1},{4,6},{5,7},{6,4},{7,5},{8,10},{9,11},{10,... | collective-permute-start | bytes 147464 | tf_op jit(solution)/shard_map/ppermute | solution.py:41
  24.1 0.1 maximum_select_fusion.4
  24.2 0.9 %collective-permute-start.13 = (bf16[4,32,384]{2,1,0:T(8,128)(2,1)S(1)}, bf16[4,32,384]{2,1,0:T(8,128)(2,1)S(1)}, u32[]{:S(2)}, u32[]{:S(2)}) collective-permute-start(bf16[4,32,384]{2,1,0:T(8,128)(2,1)S(1)} %maximum_select_fusion.4), channel_id=1, source_target_pairs={{0,2},{1,3},{2,0},{3,1},{4,6},{5,7},{6,4},{7,5},{8,10},{9,11},{10,... | collective-permute-start | bytes 294920 | tf_op jit(solution)/shard_map/ppermute | solution.py:41
  25.2 1.7 %collective-permute-done.7 = bf16[32,768]{1,0:T(8,128)(2,1)S(1)} collective-permute-done((bf16[32,768]{1,0:T(8,128)(2,1)S(1)}, bf16[32,768]{1,0:T(8,128)(2,1)S(1)}, u32[]{:S(2)}, u32[]{:S(2)}) %collective-permute-start.7) | collective-permute-done | bytes 49184 | tf_op jit(solution)/shard_map/ppermute | solution.py:41
  27.0 1.9 %collective-permute-done.13 = bf16[4,32,384]{2,1,0:T(8,128)(2,1)S(1)} collective-permute-done((bf16[4,32,384]{2,1,0:T(8,128)(2,1)S(1)}, bf16[4,32,384]{2,1,0:T(8,128)(2,1)S(1)}, u32[]{:S(2)}, u32[]{:S(2)}) %collective-permute-start.13) | collective-permute-done | bytes 98336 | tf_op jit(solution)/shard_map/ppermute | solution.py:41
  28.9 0.1 convert_reduce_fusion
  29.1 0.2 fusion.11
  29.4 0.4 fusion.28
  29.8 0.1 reshape.532
  30.0 0.1 reshape.531
  30.2 0.1 pad_maximum_fusion
  30.3 0.2 multiply_reduce_fusion.1
  30.5 0.2 copy-done.5
  30.8 0.2 convolution_convert_fusion.8
  31.1 0.2 convolution_convert_fusion
  31.3 0.1 reshape_reshape_reshape.3
  31.5 0.2 convolution_multiply_fusion
  31.8 0.3 fusion.5
  32.2 0.1 reshape.419
  32.3 0.1 copy-done.1
  32.5 0.2 convolution_convert_fusion.3
  33.0 1.1 %collective-permute-done.14 = bf16[64,768]{1,0:T(8,128)(2,1)S(1)} collective-permute-done((bf16[64,768]{1,0:T(8,128)(2,1)S(1)}, bf16[64,768]{1,0:T(8,128)(2,1)S(1)}, u32[]{:S(2)}, u32[]{:S(2)}) %collective-permute-start.14) | collective-permute-done | bytes 98336 | tf_op jit(solution)/shard_map/ppermute | solution.py:41
  34.1 1.5 %collective-permute-start.15 = (bf16[64,768]{1,0:T(8,128)(2,1)S(1)}, bf16[64,768]{1,0:T(8,128)(2,1)S(1)}, u32[]{:S(2)}, u32[]{:S(2)}) collective-permute-start(bf16[64,768]{1,0:T(8,128)(2,1)S(1)} %add_convert_fusion), channel_id=1, source_target_pairs={{0,2},{1,3},{2,0},{3,1},{4,6},{5,7},{6,4},{7,5},{8,10},{9,11},{10,... | collective-permute-start | bytes 294920 | tf_op jit(solution)/shard_map/ppermute | solution.py:41
  35.6 3.5 %collective-permute-done.15 = bf16[64,768]{1,0:T(8,128)(2,1)S(1)} collective-permute-done((bf16[64,768]{1,0:T(8,128)(2,1)S(1)}, bf16[64,768]{1,0:T(8,128)(2,1)S(1)}, u32[]{:S(2)}, u32[]{:S(2)}) %collective-permute-start.15) | collective-permute-done | bytes 98336 | tf_op jit(solution)/shard_map/ppermute | solution.py:41
  39.2 0.6 %gather_fusion = f32[4,32,768]{2,1,0:T(8,128)S(1)} fusion(f32[2,32,768]{2,1,0:T(8,128)S(1)} %convert_add_fusion.2, s32[1024]{0:T(1024)S(1)} %pad_clamp_fusion), kind=kCustom, calls=%fused_computation | custom fusion | bytes 786448 | tf_op jit(solution)/shard_map/jit(_take)/gather | solution.py:197
  39.8 0.7 %collective-permute-done.16 = f32[64,768]{1,0:T(8,128)S(1)} collective-permute-done((f32[64,768]{1,0:T(8,128)S(1)}, f32[64,768]{1,0:T(8,128)S(1)}, u32[]{:S(2)}, u32[]{:S(2)}) %collective-permute-start.16) | collective-permute-done | bytes 196640 | tf_op jit(solution)/shard_map/ppermute | solution.py:41
  40.6 0.2 fusion.153
  40.8 0.2 multiply_reduce_fusion
  41.0 2.7 %convolution_convert_fusion.2 = bf16[128,768]{1,0:T(8,128)(2,1)S(1)} fusion(bf16[768,768]{1,0:T(8,128)(2,1)S(1)} %copy-done, bf16[768,768]{1,0:T(8,128)(2,1)} %param.28, f32[128,768]{1,0:T(8,128)S(1)} %get-tuple-element.20, f32[768]{0:T(1024)S(1)} %copy-done.8, f32[128]{0:T(128)S(1)} %add_rsqrt_fusion.1, f32[128]{0:T(128)S(1)} %broadcast_multiply_fusion.1), kind=kOutput, calls=%fused_computation.6 | convolution fusion | flops 308871168 | bytes 2953216 | tf_op jit(solution)/shard_map/dot_general | solution.py:208
  43.8 0.2 copy.71
  44.1 0.2 collective-permute-start.17
  44.4 1.5 %collective-permute-start.18 = (bf16[128,192]{1,0:T(8,128)(2,1)S(1)}, bf16[128,192]{1,0:T(8,128)(2,1)S(1)}, u32[]{:S(2)}, u32[]{:S(2)}) collective-permute-start(bf16[128,192]{1,0:T(8,128)(2,1)S(1)} %select_bitcast_fusion.1), channel_id=1, source_target_pairs={{0,2},{1,3},{2,0},{3,1},{4,6},{5,7},{6,4},{7,5},{8,10},{9,11},{10,... | collective-permute-start | bytes 147464 | tf_op jit(solution)/shard_map/ppermute | solution.py:41
  46.0 0.4 collective-permute-start.19
  46.4 0.1 convolution_maximum_fusion
  46.8 2.0 %collective-permute-done.18 = bf16[128,192]{1,0:T(8,128)(2,1)S(1)} collective-permute-done((bf16[128,192]{1,0:T(8,128)(2,1)S(1)}, bf16[128,192]{1,0:T(8,128)(2,1)S(1)}, u32[]{:S(2)}, u32[]{:S(2)}) %collective-permute-start.18) | collective-permute-done | bytes 49184 | tf_op jit(solution)/shard_map/ppermute | solution.py:41
  48.9 1.4 %collective-permute-done.19 = bf16[128,192]{1,0:T(8,128)(2,1)S(1)} collective-permute-done((bf16[128,192]{1,0:T(8,128)(2,1)S(1)}, bf16[128,192]{1,0:T(8,128)(2,1)S(1)}, u32[]{:S(2)}, u32[]{:S(2)}) %collective-permute-start.19) | collective-permute-done | bytes 49184 | tf_op jit(solution)/shard_map/ppermute | solution.py:41
  50.4 0.2 fusion.8
  50.6 0.6 %copy.79 = bf16[2,32,192]{2,1,0:T(8,128)(2,1)} copy(bf16[2,32,192]{2,0,1:T(2,128)(2,1)S(1)} %fusion.8) | data formatting | bytes 49152 | tf_op jit(solution)/shard_map/convert_element_type | solution.py:221
  (93 shorter events, 3.5 us)
Async XLA Ops:
  0.0 41.0 %copy-start = (bf16[768,768]{1,0:T(8,128)(2,1)S(1)}, bf16[768,768]{1,0:T(8,128)(2,1)}, u32[]{:S(2)}) copy-start(bf16[768,768]{1,0:T(8,128)(2,1)} %param.29) | copy-start | bytes 3538948
  0.0 14.3 %collective-permute-start.3 = (bf16[2,32,192]{2,1,0:T(8,128)(2,1)}, bf16[2,32,192]{2,1,0:T(8,128)(2,1)S(1)}, u32[]{:S(2)}, u32[]{:S(2)}) collective-permute-start(bf16[2,32,192]{2,1,0:T(8,128)(2,1)} %bitcast.84), channel_id=1, source_target_pairs={{0,3},{1,2},{2,1},{3,0},{4,7},{5,6},{6,5},{7,4},{8,11},{9,10},{10,... | collective-permute-start | bytes 73736 | tf_op jit(solution)/shard_map/ppermute | solution.py:41
  2.4 14.7 %collective-permute-start.4 = (bf16[2,32,192]{2,1,0:T(8,128)(2,1)}, bf16[2,32,192]{2,1,0:T(8,128)(2,1)S(1)}, u32[]{:S(2)}, u32[]{:S(2)}) collective-permute-start(bf16[2,32,192]{2,1,0:T(8,128)(2,1)} %bitcast.85), channel_id=1, source_target_pairs={{0,2},{1,3},{2,0},{3,1},{4,6},{5,7},{6,4},{7,5},{8,10},{9,11},{10,... | collective-permute-start | bytes 73736 | tf_op jit(solution)/shard_map/ppermute | solution.py:41
  4.4 5.5 %collective-permute-start = (f32[2,66]{1,0:T(2,128)S(1)}, f32[2,66]{1,0:T(2,128)S(1)}, u32[]{:S(2)}, u32[]{:S(2)}) collective-permute-start(f32[2,66]{1,0:T(2,128)S(1)} %pad_maximum_fusion.4), channel_id=1, source_target_pairs={{0,4},{4,8},{8,12},{12,0},{1,5},{5,9},{9,13},{13,1},{2,6},{6,10},{... | collective-permute-start | bytes 1592 | tf_op jit(solution)/shard_map/ppermute | solution.py:37
  6.0 4.5 %collective-permute-start.1 = (f32[2,66]{1,0:T(2,128)S(1)}, f32[2,66]{1,0:T(2,128)S(1)}, u32[]{:S(2)}, u32[]{:S(2)}) collective-permute-start(f32[2,66]{1,0:T(2,128)S(1)} %pad_maximum_fusion.4), channel_id=1, source_target_pairs={{0,8},{4,12},{8,0},{12,4},{1,9},{5,13},{9,1},{13,5},{2,10},{6,14},... | collective-permute-start | bytes 1592 | tf_op jit(solution)/shard_map/ppermute | solution.py:37
  8.6 3.6 %collective-permute-start.2 = (f32[2,66]{1,0:T(2,128)S(1)}, f32[2,66]{1,0:T(2,128)S(1)}, u32[]{:S(2)}, u32[]{:S(2)}) collective-permute-start(f32[2,66]{1,0:T(2,128)S(1)} %pad_maximum_fusion.4), channel_id=1, source_target_pairs={{0,12},{4,0},{8,4},{12,8},{1,13},{5,1},{9,5},{13,9},{2,14},{6,2},{... | collective-permute-start | bytes 1592 | tf_op jit(solution)/shard_map/ppermute | solution.py:37
  10.0 7.1 %collective-permute-start.5 = (bf16[2,32,192]{2,1,0:T(8,128)(2,1)}, bf16[2,32,192]{2,1,0:T(8,128)(2,1)S(1)}, u32[]{:S(2)}, u32[]{:S(2)}) collective-permute-start(bf16[2,32,192]{2,1,0:T(8,128)(2,1)} %bitcast.86), channel_id=1, source_target_pairs={{0,1},{1,0},{2,3},{3,2},{4,5},{5,4},{6,7},{7,6},{8,9},{9,8},{10,11... | collective-permute-start | bytes 73736 | tf_op jit(solution)/shard_map/ppermute | solution.py:41
  10.5 10.8 %collective-permute-start.9 = (bf16[64,192]{1,0:T(8,128)(2,1)}, bf16[64,192]{1,0:T(8,128)(2,1)S(1)}, u32[]{:S(2)}, u32[]{:S(2)}) collective-permute-start(bf16[64,192]{1,0:T(8,128)(2,1)} %param.16), channel_id=1, source_target_pairs={{0,4},{4,8},{8,12},{12,0},{1,5},{5,9},{9,13},{13,1},{2,6},{6,10},{... | collective-permute-start | bytes 73736 | tf_op jit(solution)/shard_map/ppermute | solution.py:37
  12.2 9.2 %collective-permute-start.10 = (bf16[64,192]{1,0:T(8,128)(2,1)}, bf16[64,192]{1,0:T(8,128)(2,1)S(1)}, u32[]{:S(2)}, u32[]{:S(2)}) collective-permute-start(bf16[64,192]{1,0:T(8,128)(2,1)} %param.16), channel_id=1, source_target_pairs={{0,8},{4,12},{8,0},{12,4},{1,9},{5,13},{9,1},{13,5},{2,10},{6,14},... | collective-permute-start | bytes 73736 | tf_op jit(solution)/shard_map/ppermute | solution.py:37
  14.3 7.0 %collective-permute-start.11 = (bf16[64,192]{1,0:T(8,128)(2,1)}, bf16[64,192]{1,0:T(8,128)(2,1)S(1)}, u32[]{:S(2)}, u32[]{:S(2)}) collective-permute-start(bf16[64,192]{1,0:T(8,128)(2,1)} %param.16), channel_id=1, source_target_pairs={{0,12},{4,0},{8,4},{12,8},{1,13},{5,1},{9,5},{13,9},{2,14},{6,2},{... | collective-permute-start | bytes 73736 | tf_op jit(solution)/shard_map/ppermute | solution.py:37
  18.3 2.7 %copy-start.2 = (bf16[192,768]{1,0:T(8,128)(2,1)S(1)}, bf16[192,768]{1,0:T(8,128)(2,1)}, u32[]{:S(2)}) copy-start(bf16[192,768]{1,0:T(8,128)(2,1)} %param.24) | copy-start | bytes 884740
  20.0 1.4 %copy-start.3 = (bf16[64,192]{1,0:T(8,128)(2,1)S(1)}, bf16[64,192]{1,0:T(8,128)(2,1)}, u32[]{:S(2)}) copy-start(bf16[64,192]{1,0:T(8,128)(2,1)} %param.16) | copy-start | bytes 73732
  21.2 8.2 %copy-start.4 = (bf16[2,768,192]{1,2,0:T(8,128)(2,1)S(1)}, bf16[2,768,192]{1,2,0:T(8,128)(2,1)}, u32[]{:S(2)}) copy-start(bf16[2,768,192]{1,2,0:T(8,128)(2,1)} %param.26) | copy-start | bytes 1769476
  21.2 8.2 %copy-start.6 = (f32[768]{0:T(1024)S(1)}, f32[768]{0:T(1024)}, u32[]{:S(2)}) copy-start(f32[768]{0:T(1024)} %param.21) | copy-start | bytes 9220
  21.3 1.3 %collective-permute-start.6 = (bf16[32,768]{1,0:T(8,128)(2,1)S(1)}, bf16[32,768]{1,0:T(8,128)(2,1)S(1)}, u32[]{:S(2)}, u32[]{:S(2)}) collective-permute-start(bf16[32,768]{1,0:T(8,128)(2,1)S(1)} %broadcast_select_fusion.5), channel_id=1, source_target_pairs={{0,1},{1,0},{2,3},{3,2},{4,5},{5,4},{6,7},{7,6},{8,9},{9,8},{10,11... | collective-permute-start | bytes 147464 | tf_op jit(solution)/shard_map/ppermute | solution.py:41
  22.0 2.0 %collective-permute-start.12 = (bf16[4,32,192]{2,1,0:T(8,128)(2,1)S(1)}, bf16[4,32,192]{2,1,0:T(8,128)(2,1)S(1)}, u32[]{:S(2)}, u32[]{:S(2)}) collective-permute-start(bf16[4,32,192]{2,1,0:T(8,128)(2,1)S(1)} %reshape.418), channel_id=1, source_target_pairs={{0,1},{1,0},{2,3},{3,2},{4,5},{5,4},{6,7},{7,6},{8,9},{9,8},{10,11... | collective-permute-start | bytes 147464 | tf_op jit(solution)/shard_map/ppermute | solution.py:41
  22.6 4.3 %collective-permute-start.7 = (bf16[32,768]{1,0:T(8,128)(2,1)S(1)}, bf16[32,768]{1,0:T(8,128)(2,1)S(1)}, u32[]{:S(2)}, u32[]{:S(2)}) collective-permute-start(bf16[32,768]{1,0:T(8,128)(2,1)S(1)} %add_convert_fusion.1), channel_id=1, source_target_pairs={{0,2},{1,3},{2,0},{3,1},{4,6},{5,7},{6,4},{7,5},{8,10},{9,11},{10,... | collective-permute-start | bytes 147464 | tf_op jit(solution)/shard_map/ppermute | solution.py:41
  24.2 4.7 %collective-permute-start.13 = (bf16[4,32,384]{2,1,0:T(8,128)(2,1)S(1)}, bf16[4,32,384]{2,1,0:T(8,128)(2,1)S(1)}, u32[]{:S(2)}, u32[]{:S(2)}) collective-permute-start(bf16[4,32,384]{2,1,0:T(8,128)(2,1)S(1)} %maximum_select_fusion.4), channel_id=1, source_target_pairs={{0,2},{1,3},{2,0},{3,1},{4,6},{5,7},{6,4},{7,5},{8,10},{9,11},{10,... | collective-permute-start | bytes 294920 | tf_op jit(solution)/shard_map/ppermute | solution.py:41
  26.9 3.2 %collective-permute-start.8 = (f32[32,768]{1,0:T(8,128)S(1)}, f32[32,768]{1,0:T(8,128)S(1)}, u32[]{:S(2)}, u32[]{:S(2)}) collective-permute-start(f32[32,768]{1,0:T(8,128)S(1)} %convert_add_fusion.3), channel_id=1, source_target_pairs={{0,1},{1,0},{2,3},{3,2},{4,5},{5,4},{6,7},{7,6},{8,9},{9,8},{10,11... | collective-permute-start | bytes 294920 | tf_op jit(solution)/shard_map/ppermute | solution.py:41
  29.8 1.0 %copy-start.5 = (bf16[768,192]{0,1:T(8,128)(2,1)S(1)}, bf16[768,192]{0,1:T(8,128)(2,1)}, u32[]{:S(2)}) copy-start(bf16[768,192]{0,1:T(8,128)(2,1)} %param.25) | copy-start | bytes 884740
  29.8 1.0 %copy-start.7 = (f32[768]{0:T(1024)S(1)}, f32[768]{0:T(1024)}, u32[]{:S(2)}) copy-start(f32[768]{0:T(1024)} %param.20) | copy-start | bytes 9220
  31.5 1.0 %copy-start.1 = (bf16[192,768]{1,0:T(8,128)(2,1)S(1)}, bf16[192,768]{1,0:T(8,128)(2,1)}, u32[]{:S(2)}) copy-start(bf16[192,768]{1,0:T(8,128)(2,1)} %param.27) | copy-start | bytes 884740
  32.7 1.4 %collective-permute-start.14 = (bf16[64,768]{1,0:T(8,128)(2,1)S(1)}, bf16[64,768]{1,0:T(8,128)(2,1)S(1)}, u32[]{:S(2)}, u32[]{:S(2)}) collective-permute-start(bf16[64,768]{1,0:T(8,128)(2,1)S(1)} %broadcast_select_fusion.2), channel_id=1, source_target_pairs={{0,1},{1,0},{2,3},{3,2},{4,5},{5,4},{6,7},{7,6},{8,9},{9,8},{10,11... | collective-permute-start | bytes 294920 | tf_op jit(solution)/shard_map/ppermute | solution.py:41
  34.1 4.9 %collective-permute-start.15 = (bf16[64,768]{1,0:T(8,128)(2,1)S(1)}, bf16[64,768]{1,0:T(8,128)(2,1)S(1)}, u32[]{:S(2)}, u32[]{:S(2)}) collective-permute-start(bf16[64,768]{1,0:T(8,128)(2,1)S(1)} %add_convert_fusion), channel_id=1, source_target_pairs={{0,2},{1,3},{2,0},{3,1},{4,6},{5,7},{6,4},{7,5},{8,10},{9,11},{10,... | collective-permute-start | bytes 294920 | tf_op jit(solution)/shard_map/ppermute | solution.py:41
  39.1 1.5 %collective-permute-start.16 = (f32[64,768]{1,0:T(8,128)S(1)}, f32[64,768]{1,0:T(8,128)S(1)}, u32[]{:S(2)}, u32[]{:S(2)}) collective-permute-start(f32[64,768]{1,0:T(8,128)S(1)} %convert_add_fusion.1), channel_id=1, source_target_pairs={{0,1},{1,0},{2,3},{3,2},{4,5},{5,4},{6,7},{7,6},{8,9},{9,8},{10,11... | collective-permute-start | bytes 589832 | tf_op jit(solution)/shard_map/ppermute | solution.py:41
  39.8 1.2 %copy-start.8 = (f32[768]{0:T(1024)S(1)}, f32[768]{0:T(1024)}, u32[]{:S(2)}) copy-start(f32[768]{0:T(1024)} %param.22) | copy-start | bytes 9220
  44.1 2.7 %collective-permute-start.17 = (bf16[128,192]{1,0:T(8,128)(2,1)S(1)}, bf16[128,192]{1,0:T(8,128)(2,1)S(1)}, u32[]{:S(2)}, u32[]{:S(2)}) collective-permute-start(bf16[128,192]{1,0:T(8,128)(2,1)S(1)} %select_bitcast_fusion.2), channel_id=1, source_target_pairs={{0,1},{1,0},{2,3},{3,2},{4,5},{5,4},{6,7},{7,6},{8,9},{9,8},{10,11... | collective-permute-start | bytes 147464 | tf_op jit(solution)/shard_map/ppermute | solution.py:41
  44.4 4.4 %collective-permute-start.18 = (bf16[128,192]{1,0:T(8,128)(2,1)S(1)}, bf16[128,192]{1,0:T(8,128)(2,1)S(1)}, u32[]{:S(2)}, u32[]{:S(2)}) collective-permute-start(bf16[128,192]{1,0:T(8,128)(2,1)S(1)} %select_bitcast_fusion.1), channel_id=1, source_target_pairs={{0,2},{1,3},{2,0},{3,1},{4,6},{5,7},{6,4},{7,5},{8,10},{9,11},{10,... | collective-permute-start | bytes 147464 | tf_op jit(solution)/shard_map/ppermute | solution.py:41
  46.0 4.2 %collective-permute-start.19 = (bf16[128,192]{1,0:T(8,128)(2,1)S(1)}, bf16[128,192]{1,0:T(8,128)(2,1)S(1)}, u32[]{:S(2)}, u32[]{:S(2)}) collective-permute-start(bf16[128,192]{1,0:T(8,128)(2,1)S(1)} %select_bitcast_fusion), channel_id=1, source_target_pairs={{0,3},{1,2},{2,1},{3,0},{4,7},{5,6},{6,5},{7,4},{8,11},{9,10},{10,... | collective-permute-start | bytes 147464 | tf_op jit(solution)/shard_map/ppermute | solution.py:41

commit v14 on v11

--- a/solution.py
+++ b/solution.py
@@ -212,7 +212,8 @@
     hidden = jax.nn.gelu(
         jnp.dot(normed, mlp_up, preferred_element_type=jnp.float32), approximate=False
     )
-    term = jnp.dot(hidden.astype(jnp.bfloat16), mlp_down, preferred_element_type=jnp.float32)
+    hidden = lax.optimization_barrier(hidden.astype(jnp.bfloat16))
+    term = jnp.dot(hidden, mlp_down, preferred_element_type=jnp.float32)
     offset = lax.axis_index("mp") * quarter
     final = lax.dynamic_slice_in_dim(resid, offset, quarter, 1) + mp_reduce_cols(
         term.astype(jnp.bfloat16)

time: 47 us -> 45.9 us (0.977)
  matrix products: 7.38 us -> 6.09 us
    dot_general x1 -> x2, matrix products: 2.72 us -> 1.42 us  [the longest x1 1.1 us: per_device(): jnp.dot(normed, mlp_up, preferred_element_type=jnp.float32)]
    unnamed x20 -> x22, local copies, waits for them, and re-layouts: 0.83 us -> 1 us
where the time goes in v14:
time: 45.9 us; the launch traced here: 45.5 us
  starting transfers between devices  14.6 us (32%)
  waiting for transfers between devices  13 us (28%)
  local copies, waits for them, and re-layouts  6.82 us (15%)
  matrix products  6.09 us (13%)
  other arithmetic  4.3 us (9%)
  between operations  0.66 us (1%)
    ppermute x14, waiting for transfers between devices, swap(): return lax.ppermute(values, 'mp', pairs)  12.2 us
    ppermute x14, starting transfers between devices, swap(): return lax.ppermute(values, 'mp', pairs)  9.74 us
    ppermute x3, starting transfers between devices, pairs_shift(): lax.ppermute(values, 'pairs', [(i, (i + step) % owners_n) for i in range(...  4.89 us
    dot_general x1, matrix products, per_device(): jnp.einsum('rd,kdc->krc', normed, self_qkv, preferred_element_type=jnp.fl...  1.67 us
    dot_general x1, matrix products, per_device(): jnp.dot(normed, mlp_up, preferred_element_type=jnp.float32)  1.1 us
    unnamed x22, local copies, waits for them, and re-layouts  1 us
  transfers between devices with their start and end apart: 17, of which 8 were waited for; matrix products, arithmetic and copies ran while one was open for 24% of the time, Pallas kernels for 0%

profile of v14, /device:TPU:0, one launch (start us, length us, event | category | flops | bytes accessed | tf_op | source)
XLA Modules:
  0.0 45.5 jit_solution(11678297419297980806)
XLA Ops:
  0.0 0.5 collective-permute-start.5
  0.5 2.6 %collective-permute-start.4 = (bf16[2,32,192]{2,1,0:T(8,128)(2,1)}, bf16[2,32,192]{2,1,0:T(8,128)(2,1)S(1)}, u32[]{:S(2)}, u32[]{:S(2)}) collective-permute-start(bf16[2,32,192]{2,1,0:T(8,128)(2,1)} %bitcast.78), channel_id=1, source_target_pairs={{0,2},{1,3},{2,0},{3,1},{4,6},{5,7},{6,4},{7,5},{8,10},{9,11},{10,... | collective-permute-start | bytes 73736 | tf_op jit(solution)/shard_map/ppermute | solution.py:41
  3.1 0.9 %reshape.536 = f32[12288]{0:T(1024)S(1)} reshape(bf16[64,192]{1,0:T(8,128)(2,1)} %param.16) | data formatting | bytes 73728 | tf_op jit(solution)/shard_map/reshape | solution.py:153
  4.0 0.8 %reshape.459 = f32[128]{0:T(128)S(1)} reshape(f32[2,64]{1,0:T(2,128)} %param.18) | data formatting | bytes 1024 | tf_op jit(solution)/shard_map/reshape | solution.py:155
  4.7 0.7 %convert_element_type.160 = f32[2,2]{1,0:T(2,128)S(1)} convert(s32[2,2]{1,0:T(2,128)} %param.17) | non-fusion elementwise | flops 4 | bytes 32 | tf_op jit(solution)/shard_map/convert_element_type | solution.py:154
  5.6 3.8 %collective-permute-start.2 = (f32[12420]{0:T(1024)S(1)}, f32[12420]{0:T(1024)S(1)}, u32[]{:S(2)}, u32[]{:S(2)}) collective-permute-start(f32[12420]{0:T(1024)S(1)} %concatenate.56), channel_id=1, source_target_pairs={{0,12},{4,0},{8,4},{12,8},{1,13},{5,1},{9,5},{13,9},{2,14},{6,2},{... | collective-permute-start | bytes 149048 | tf_op jit(solution)/shard_map/ppermute | solution.py:37
  9.5 1.1 %collective-permute-start = (f32[12420]{0:T(1024)S(1)}, f32[12420]{0:T(1024)S(1)}, u32[]{:S(2)}, u32[]{:S(2)}) collective-permute-start(f32[12420]{0:T(1024)S(1)} %concatenate.56), channel_id=1, source_target_pairs={{0,4},{4,8},{8,12},{12,0},{1,5},{5,9},{9,13},{13,1},{2,6},{6,10},{... | collective-permute-start | bytes 149048 | tf_op jit(solution)/shard_map/ppermute | solution.py:37
  10.6 0.8 %select_select_fusion.3 = (bf16[2,32,192]{2,1,0:T(8,128)(2,1)S(1)}, bf16[2,32,192]{2,1,0:T(8,128)(2,1)S(1)}, bf16[2,32,192]{2,1,0:T(8,128)(2,1)S(1)}, bf16[2,32,192]{2,1,0:T(8,128)(2,1)S(1)}) fusion(bf16[2,32,192]{2,1,0:T(8,128)(2,1)S(1)} %collective-permute-done.3, bf16[2,32,192]{2,1,0:T(8,128)(2,1)S(1)} %collective-permute-done.4, ...), kind=kLoop, calls=%fused_computation.124 | loop fusion | flops 147456 | bytes 196620 | tf_op jit(solution)/shard_map/jit(_where)/select_n | solution.py:91
  11.4 0.2 convert_reduce_fusion.1
  11.6 0.2 fusion.24
  11.8 1.7 %fusion.6 = bf16[3,64,192]{2,1,0:T(8,128)(2,1)S(1)} fusion(bf16[3,768,192]{1,2,0:T(8,128)(2,1)} %param.23, bf16[64,768]{1,0:T(8,128)(2,1)S(1)} %get-tuple-element.24, f32[768]{0:T(1024)} %param.19, f32[64]{0:T(128)S(1)} %add_rsqrt_fusion.3, f32[64]{0:T(128)S(1)} %broadcast_multiply_fusion.3), kind=kOutput, calls=%fused_computation.15 | convolution fusion | flops 56905728 | bytes 1060352 | tf_op jit(solution)/shard_map/rd,kdc->krc/dot_general | solution.py:183
  13.7 0.2 fusion.92
  13.8 0.1 convolution_multiply_fusion.1
  14.1 0.2 fusion.9
  14.5 0.2 convolution_convert_fusion.6
  14.8 0.8 %collective-permute-done.1 = f32[12420]{0:T(1024)S(1)} collective-permute-done((f32[12420]{0:T(1024)S(1)}, f32[12420]{0:T(1024)S(1)}, u32[]{:S(2)}, u32[]{:S(2)}) %collective-permute-start.1) | collective-permute-done | bytes 49712 | tf_op jit(solution)/shard_map/ppermute | solution.py:37
  15.8 0.2 pad_maximum_fusion
  16.6 0.1 add_reduce_fusion
  16.7 0.2 select_reduce_fusion.1
  17.0 0.1 fusion.87
  17.1 0.2 convolution_convert_fusion.1
  17.3 0.1 reshape.466
  17.5 0.1 concatenate.65
  17.7 1.6 %collective-permute-start.7 = (bf16[32,768]{1,0:T(8,128)(2,1)S(1)}, bf16[32,768]{1,0:T(8,128)(2,1)S(1)}, u32[]{:S(2)}, u32[]{:S(2)}) collective-permute-start(bf16[32,768]{1,0:T(8,128)(2,1)S(1)} %add_convert_fusion.1), channel_id=1, source_target_pairs={{0,2},{1,3},{2,0},{3,1},{4,6},{5,7},{6,4},{7,5},{8,10},{9,11},{10,... | collective-permute-start | bytes 147464 | tf_op jit(solution)/shard_map/ppermute | solution.py:41
  19.2 0.1 maximum_select_fusion.4
  19.4 1.2 %collective-permute-start.10 = (bf16[4,32,384]{2,1,0:T(8,128)(2,1)S(1)}, bf16[4,32,384]{2,1,0:T(8,128)(2,1)S(1)}, u32[]{:S(2)}, u32[]{:S(2)}) collective-permute-start(bf16[4,32,384]{2,1,0:T(8,128)(2,1)S(1)} %maximum_select_fusion.4), channel_id=1, source_target_pairs={{0,2},{1,3},{2,0},{3,1},{4,6},{5,7},{6,4},{7,5},{8,10},{9,11},{10,... | collective-permute-start | bytes 294920 | tf_op jit(solution)/shard_map/ppermute | solution.py:41
  20.6 0.1 maximum_select_fusion.3
  20.7 1.2 %collective-permute-done.7 = bf16[32,768]{1,0:T(8,128)(2,1)S(1)} collective-permute-done((bf16[32,768]{1,0:T(8,128)(2,1)S(1)}, bf16[32,768]{1,0:T(8,128)(2,1)S(1)}, u32[]{:S(2)}, u32[]{:S(2)}) %collective-permute-start.7) | collective-permute-done | bytes 49184 | tf_op jit(solution)/shard_map/ppermute | solution.py:41
  22.0 2.4 %collective-permute-done.10 = bf16[4,32,384]{2,1,0:T(8,128)(2,1)S(1)} collective-permute-done((bf16[4,32,384]{2,1,0:T(8,128)(2,1)S(1)}, bf16[4,32,384]{2,1,0:T(8,128)(2,1)S(1)}, u32[]{:S(2)}, u32[]{:S(2)}) %collective-permute-start.10) | collective-permute-done | bytes 98336 | tf_op jit(solution)/shard_map/ppermute | solution.py:41
  24.3 0.1 convert_reduce_fusion
  24.5 0.2 fusion.11
  24.8 0.4 fusion.27
  25.3 0.1 reshape.582
  25.4 0.1 reshape.581
  25.6 0.1 pad_maximum_fusion.1
  25.8 0.2 multiply_reduce_fusion.1
  26.0 0.2 copy-done.5
  26.2 0.2 convolution_convert_fusion.8
  26.6 0.2 convolution_convert_fusion
  26.8 0.1 reshape_reshape_reshape.3
  27.0 0.2 convolution_multiply_fusion
  27.3 0.3 fusion.5
  27.7 0.1 reshape.467
  27.8 0.1 copy-done.2
  27.9 0.2 convolution_convert_fusion.3
  28.4 1.1 %collective-permute-done.11 = bf16[64,768]{1,0:T(8,128)(2,1)S(1)} collective-permute-done((bf16[64,768]{1,0:T(8,128)(2,1)S(1)}, bf16[64,768]{1,0:T(8,128)(2,1)S(1)}, u32[]{:S(2)}, u32[]{:S(2)}) %collective-permute-start.11) | collective-permute-done | bytes 98336 | tf_op jit(solution)/shard_map/ppermute | solution.py:41
  29.6 1.2 %collective-permute-start.12 = (bf16[64,768]{1,0:T(8,128)(2,1)S(1)}, bf16[64,768]{1,0:T(8,128)(2,1)S(1)}, u32[]{:S(2)}, u32[]{:S(2)}) collective-permute-start(bf16[64,768]{1,0:T(8,128)(2,1)S(1)} %add_convert_fusion), channel_id=1, source_target_pairs={{0,2},{1,3},{2,0},{3,1},{4,6},{5,7},{6,4},{7,5},{8,10},{9,11},{10,... | collective-permute-start | bytes 294920 | tf_op jit(solution)/shard_map/ppermute | solution.py:41
  30.8 3.7 %collective-permute-done.12 = bf16[64,768]{1,0:T(8,128)(2,1)S(1)} collective-permute-done((bf16[64,768]{1,0:T(8,128)(2,1)S(1)}, bf16[64,768]{1,0:T(8,128)(2,1)S(1)}, u32[]{:S(2)}, u32[]{:S(2)}) %collective-permute-start.12) | collective-permute-done | bytes 98336 | tf_op jit(solution)/shard_map/ppermute | solution.py:41
  34.7 0.6 %gather_fusion = f32[4,32,768]{2,1,0:T(8,128)S(1)} fusion(f32[2,32,768]{2,1,0:T(8,128)S(1)} %convert_add_fusion.2, s32[1024]{0:T(1024)S(1)} %pad_clamp_fusion), kind=kCustom, calls=%fused_computation | custom fusion | bytes 786448 | tf_op jit(solution)/shard_map/jit(_take)/gather | solution.py:204
  35.3 0.7 %collective-permute-done.13 = f32[64,768]{1,0:T(8,128)S(1)} collective-permute-done((f32[64,768]{1,0:T(8,128)S(1)}, f32[64,768]{1,0:T(8,128)S(1)}, u32[]{:S(2)}, u32[]{:S(2)}) %collective-permute-start.13) | collective-permute-done | bytes 196640 | tf_op jit(solution)/shard_map/ppermute | solution.py:41
  36.1 0.2 fusion.89
  36.3 0.2 multiply_reduce_fusion
  36.5 1.1 %fusion.14 = bf16[128,768]{1,0:T(8,128)(2,1)S(1)} fusion(bf16[768,768]{1,0:T(8,128)(2,1)S(1)} %copy-done, f32[128,768]{1,0:T(8,128)S(1)} %get-tuple-element.20, f32[768]{0:T(1024)S(1)} %copy-done.8, f32[128]{0:T(128)S(1)} %add_rsqrt_fusion.1, f32[128]{0:T(128)S(1)} %broadcast_multiply_fusion.1), kind=kOutput, calls=%fused_computation.31 | convolution fusion | flops 157777920 | bytes 1773568 | tf_op jit(solution)/shard_map/dot_general | solution.py:213
  37.6 0.2 copy-done.1
  37.8 0.3 convolution_convert_fusion.2
  38.1 0.2 copy.78
  38.7 1.0 %collective-permute-start.16 = (bf16[128,192]{1,0:T(8,128)(2,1)S(1)}, bf16[128,192]{1,0:T(8,128)(2,1)S(1)}, u32[]{:S(2)}, u32[]{:S(2)}) collective-permute-start(bf16[128,192]{1,0:T(8,128)(2,1)S(1)} %select_bitcast_fusion), channel_id=1, source_target_pairs={{0,3},{1,2},{2,1},{3,0},{4,7},{5,6},{6,5},{7,4},{8,11},{9,10},{10,... | collective-permute-start | bytes 147464 | tf_op jit(solution)/shard_map/ppermute | solution.py:41
  39.6 0.4 collective-permute-start.14
  40.1 0.9 %collective-permute-start.15 = (bf16[128,192]{1,0:T(8,128)(2,1)S(1)}, bf16[128,192]{1,0:T(8,128)(2,1)S(1)}, u32[]{:S(2)}, u32[]{:S(2)}) collective-permute-start(bf16[128,192]{1,0:T(8,128)(2,1)S(1)} %select_bitcast_fusion.1), channel_id=1, source_target_pairs={{0,2},{1,3},{2,0},{3,1},{4,6},{5,7},{6,4},{7,5},{8,10},{9,11},{10,... | collective-permute-start | bytes 147464 | tf_op jit(solution)/shard_map/ppermute | solution.py:41
  41.0 0.1 convolution_maximum_fusion
  41.4 1.4 %collective-permute-done.16 = bf16[128,192]{1,0:T(8,128)(2,1)S(1)} collective-permute-done((bf16[128,192]{1,0:T(8,128)(2,1)S(1)}, bf16[128,192]{1,0:T(8,128)(2,1)S(1)}, u32[]{:S(2)}, u32[]{:S(2)}) %collective-permute-start.16) | collective-permute-done | bytes 49184 | tf_op jit(solution)/shard_map/ppermute | solution.py:41
  42.8 1.7 %collective-permute-done.15 = bf16[128,192]{1,0:T(8,128)(2,1)S(1)} collective-permute-done((bf16[128,192]{1,0:T(8,128)(2,1)S(1)}, bf16[128,192]{1,0:T(8,128)(2,1)S(1)}, u32[]{:S(2)}, u32[]{:S(2)}) %collective-permute-start.15) | collective-permute-done | bytes 49184 | tf_op jit(solution)/shard_map/ppermute | solution.py:41
  44.6 0.2 fusion.8
  44.9 0.6 %copy.86 = bf16[2,32,192]{2,1,0:T(8,128)(2,1)} copy(bf16[2,32,192]{2,0,1:T(2,128)(2,1)S(1)} %fusion.8) | data formatting | bytes 49152 | tf_op jit(solution)/shard_map/convert_element_type | solution.py:229
  (98 shorter events, 3.7 us)
Async XLA Ops:
  0.0 36.5 %copy-start = (bf16[768,768]{1,0:T(8,128)(2,1)S(1)}, bf16[768,768]{1,0:T(8,128)(2,1)}, u32[]{:S(2)}) copy-start(bf16[768,768]{1,0:T(8,128)(2,1)} %param.28) | copy-start | bytes 3538948
  0.0 9.5 %collective-permute-start.5 = (bf16[2,32,192]{2,1,0:T(8,128)(2,1)}, bf16[2,32,192]{2,1,0:T(8,128)(2,1)S(1)}, u32[]{:S(2)}, u32[]{:S(2)}) collective-permute-start(bf16[2,32,192]{2,1,0:T(8,128)(2,1)} %bitcast.77), channel_id=1, source_target_pairs={{0,1},{1,0},{2,3},{3,2},{4,5},{5,4},{6,7},{7,6},{8,9},{9,8},{10,11... | collective-permute-start | bytes 73736 | tf_op jit(solution)/shard_map/ppermute | solution.py:41
  0.5 10.1 %collective-permute-start.4 = (bf16[2,32,192]{2,1,0:T(8,128)(2,1)}, bf16[2,32,192]{2,1,0:T(8,128)(2,1)S(1)}, u32[]{:S(2)}, u32[]{:S(2)}) collective-permute-start(bf16[2,32,192]{2,1,0:T(8,128)(2,1)} %bitcast.78), channel_id=1, source_target_pairs={{0,2},{1,3},{2,0},{3,1},{4,6},{5,7},{6,4},{7,5},{8,10},{9,11},{10,... | collective-permute-start | bytes 73736 | tf_op jit(solution)/shard_map/ppermute | solution.py:41
  3.0 7.6 %collective-permute-start.3 = (bf16[2,32,192]{2,1,0:T(8,128)(2,1)}, bf16[2,32,192]{2,1,0:T(8,128)(2,1)S(1)}, u32[]{:S(2)}, u32[]{:S(2)}) collective-permute-start(bf16[2,32,192]{2,1,0:T(8,128)(2,1)} %bitcast.79), channel_id=1, source_target_pairs={{0,3},{1,2},{2,1},{3,0},{4,7},{5,6},{6,5},{7,4},{8,11},{9,10},{10,... | collective-permute-start | bytes 73736 | tf_op jit(solution)/shard_map/ppermute | solution.py:41
  5.6 9.2 %collective-permute-start.2 = (f32[12420]{0:T(1024)S(1)}, f32[12420]{0:T(1024)S(1)}, u32[]{:S(2)}, u32[]{:S(2)}) collective-permute-start(f32[12420]{0:T(1024)S(1)} %concatenate.56), channel_id=1, source_target_pairs={{0,12},{4,0},{8,4},{12,8},{1,13},{5,1},{9,5},{13,9},{2,14},{6,2},{... | collective-permute-start | bytes 149048 | tf_op jit(solution)/shard_map/ppermute | solution.py:37
  9.4 6.2 %collective-permute-start.1 = (f32[12420]{0:T(1024)S(1)}, f32[12420]{0:T(1024)S(1)}, u32[]{:S(2)}, u32[]{:S(2)}) collective-permute-start(f32[12420]{0:T(1024)S(1)} %concatenate.56), channel_id=1, source_target_pairs={{0,8},{4,12},{8,0},{12,4},{1,9},{5,13},{9,1},{13,5},{2,10},{6,14},... | collective-permute-start | bytes 149048 | tf_op jit(solution)/shard_map/ppermute | solution.py:37
  9.5 6.1 %collective-permute-start = (f32[12420]{0:T(1024)S(1)}, f32[12420]{0:T(1024)S(1)}, u32[]{:S(2)}, u32[]{:S(2)}) collective-permute-start(f32[12420]{0:T(1024)S(1)} %concatenate.56), channel_id=1, source_target_pairs={{0,4},{4,8},{8,12},{12,0},{1,5},{5,9},{9,13},{13,1},{2,6},{6,10},{... | collective-permute-start | bytes 149048 | tf_op jit(solution)/shard_map/ppermute | solution.py:37
  11.8 2.7 %copy-start.3 = (bf16[192,768]{1,0:T(8,128)(2,1)S(1)}, bf16[192,768]{1,0:T(8,128)(2,1)}, u32[]{:S(2)}) copy-start(bf16[192,768]{1,0:T(8,128)(2,1)} %param.24) | copy-start | bytes 884740
  14.7 3.0 %collective-permute-start.6 = (bf16[32,768]{1,0:T(8,128)(2,1)S(1)}, bf16[32,768]{1,0:T(8,128)(2,1)S(1)}, u32[]{:S(2)}, u32[]{:S(2)}) collective-permute-start(bf16[32,768]{1,0:T(8,128)(2,1)S(1)} %broadcast_select_fusion.5), channel_id=1, source_target_pairs={{0,1},{1,0},{2,3},{3,2},{4,5},{5,4},{6,7},{7,6},{8,9},{9,8},{10,11... | collective-permute-start | bytes 147464 | tf_op jit(solution)/shard_map/ppermute | solution.py:41
  15.8 9.1 %copy-start.4 = (bf16[2,768,192]{1,2,0:T(8,128)(2,1)S(1)}, bf16[2,768,192]{1,2,0:T(8,128)(2,1)}, u32[]{:S(2)}) copy-start(bf16[2,768,192]{1,2,0:T(8,128)(2,1)} %param.26) | copy-start | bytes 1769476
  15.8 9.1 %copy-start.6 = (f32[768]{0:T(1024)S(1)}, f32[768]{0:T(1024)}, u32[]{:S(2)}) copy-start(f32[768]{0:T(1024)} %param.21) | copy-start | bytes 9220
  17.6 1.7 %collective-permute-start.9 = (bf16[4,32,192]{2,1,0:T(8,128)(2,1)S(1)}, bf16[4,32,192]{2,1,0:T(8,128)(2,1)S(1)}, u32[]{:S(2)}, u32[]{:S(2)}) collective-permute-start(bf16[4,32,192]{2,1,0:T(8,128)(2,1)S(1)} %reshape.466), channel_id=1, source_target_pairs={{0,1},{1,0},{2,3},{3,2},{4,5},{5,4},{6,7},{7,6},{8,9},{9,8},{10,11... | collective-permute-start | bytes 147464 | tf_op jit(solution)/shard_map/ppermute | solution.py:41
  17.7 4.2 %collective-permute-start.7 = (bf16[32,768]{1,0:T(8,128)(2,1)S(1)}, bf16[32,768]{1,0:T(8,128)(2,1)S(1)}, u32[]{:S(2)}, u32[]{:S(2)}) collective-permute-start(bf16[32,768]{1,0:T(8,128)(2,1)S(1)} %add_convert_fusion.1), channel_id=1, source_target_pairs={{0,2},{1,3},{2,0},{3,1},{4,6},{5,7},{6,4},{7,5},{8,10},{9,11},{10,... | collective-permute-start | bytes 147464 | tf_op jit(solution)/shard_map/ppermute | solution.py:41
  19.4 5.0 %collective-permute-start.10 = (bf16[4,32,384]{2,1,0:T(8,128)(2,1)S(1)}, bf16[4,32,384]{2,1,0:T(8,128)(2,1)S(1)}, u32[]{:S(2)}, u32[]{:S(2)}) collective-permute-start(bf16[4,32,384]{2,1,0:T(8,128)(2,1)S(1)} %maximum_select_fusion.4), channel_id=1, source_target_pairs={{0,2},{1,3},{2,0},{3,1},{4,6},{5,7},{6,4},{7,5},{8,10},{9,11},{10,... | collective-permute-start | bytes 294920 | tf_op jit(solution)/shard_map/ppermute | solution.py:41
  21.9 3.7 %collective-permute-start.8 = (f32[32,768]{1,0:T(8,128)S(1)}, f32[32,768]{1,0:T(8,128)S(1)}, u32[]{:S(2)}, u32[]{:S(2)}) collective-permute-start(f32[32,768]{1,0:T(8,128)S(1)} %convert_add_fusion.3), channel_id=1, source_target_pairs={{0,1},{1,0},{2,3},{3,2},{4,5},{5,4},{6,7},{7,6},{8,9},{9,8},{10,11... | collective-permute-start | bytes 294920 | tf_op jit(solution)/shard_map/ppermute | solution.py:41
  25.2 1.0 %copy-start.5 = (bf16[768,192]{0,1:T(8,128)(2,1)S(1)}, bf16[768,192]{0,1:T(8,128)(2,1)}, u32[]{:S(2)}) copy-start(bf16[768,192]{0,1:T(8,128)(2,1)} %param.25) | copy-start | bytes 884740
  25.3 1.0 %copy-start.7 = (f32[768]{0:T(1024)S(1)}, f32[768]{0:T(1024)}, u32[]{:S(2)}) copy-start(f32[768]{0:T(1024)} %param.20) | copy-start | bytes 9220
  27.0 1.0 %copy-start.2 = (bf16[192,768]{1,0:T(8,128)(2,1)S(1)}, bf16[192,768]{1,0:T(8,128)(2,1)}, u32[]{:S(2)}) copy-start(bf16[192,768]{1,0:T(8,128)(2,1)} %param.27) | copy-start | bytes 884740
  28.2 1.4 %collective-permute-start.11 = (bf16[64,768]{1,0:T(8,128)(2,1)S(1)}, bf16[64,768]{1,0:T(8,128)(2,1)S(1)}, u32[]{:S(2)}, u32[]{:S(2)}) collective-permute-start(bf16[64,768]{1,0:T(8,128)(2,1)S(1)} %broadcast_select_fusion.2), channel_id=1, source_target_pairs={{0,1},{1,0},{2,3},{3,2},{4,5},{5,4},{6,7},{7,6},{8,9},{9,8},{10,11... | collective-permute-start | bytes 294920 | tf_op jit(solution)/shard_map/ppermute | solution.py:41
  29.6 4.9 %collective-permute-start.12 = (bf16[64,768]{1,0:T(8,128)(2,1)S(1)}, bf16[64,768]{1,0:T(8,128)(2,1)S(1)}, u32[]{:S(2)}, u32[]{:S(2)}) collective-permute-start(bf16[64,768]{1,0:T(8,128)(2,1)S(1)} %add_convert_fusion), channel_id=1, source_target_pairs={{0,2},{1,3},{2,0},{3,1},{4,6},{5,7},{6,4},{7,5},{8,10},{9,11},{10,... | collective-permute-start | bytes 294920 | tf_op jit(solution)/shard_map/ppermute | solution.py:41
  34.5 1.5 %collective-permute-start.13 = (f32[64,768]{1,0:T(8,128)S(1)}, f32[64,768]{1,0:T(8,128)S(1)}, u32[]{:S(2)}, u32[]{:S(2)}) collective-permute-start(f32[64,768]{1,0:T(8,128)S(1)} %convert_add_fusion.1), channel_id=1, source_target_pairs={{0,1},{1,0},{2,3},{3,2},{4,5},{5,4},{6,7},{7,6},{8,9},{9,8},{10,11... | collective-permute-start | bytes 589832 | tf_op jit(solution)/shard_map/ppermute | solution.py:41
  35.3 1.2 %copy-start.8 = (f32[768]{0:T(1024)S(1)}, f32[768]{0:T(1024)}, u32[]{:S(2)}) copy-start(f32[768]{0:T(1024)} %param.22) | copy-start | bytes 9220
  36.5 1.3 %copy-start.1 = (bf16[768,768]{1,0:T(8,128)(2,1)S(1)}, bf16[768,768]{1,0:T(8,128)(2,1)}, u32[]{:S(2)}) copy-start(bf16[768,768]{1,0:T(8,128)(2,1)} %param.29) | copy-start | bytes 3538948
  38.7 4.1 %collective-permute-start.16 = (bf16[128,192]{1,0:T(8,128)(2,1)S(1)}, bf16[128,192]{1,0:T(8,128)(2,1)S(1)}, u32[]{:S(2)}, u32[]{:S(2)}) collective-permute-start(bf16[128,192]{1,0:T(8,128)(2,1)S(1)} %select_bitcast_fusion), channel_id=1, source_target_pairs={{0,3},{1,2},{2,1},{3,0},{4,7},{5,6},{6,5},{7,4},{8,11},{9,10},{10,... | collective-permute-start | bytes 147464 | tf_op jit(solution)/shard_map/ppermute | solution.py:41
  39.6 3.2 %collective-permute-start.14 = (bf16[128,192]{1,0:T(8,128)(2,1)S(1)}, bf16[128,192]{1,0:T(8,128)(2,1)S(1)}, u32[]{:S(2)}, u32[]{:S(2)}) collective-permute-start(bf16[128,192]{1,0:T(8,128)(2,1)S(1)} %select_bitcast_fusion.2), channel_id=1, source_target_pairs={{0,1},{1,0},{2,3},{3,2},{4,5},{5,4},{6,7},{7,6},{8,9},{9,8},{10,11... | collective-permute-start | bytes 147464 | tf_op jit(solution)/shard_map/ppermute | solution.py:41
  40.1 4.4 %collective-permute-start.15 = (bf16[128,192]{1,0:T(8,128)(2,1)S(1)}, bf16[128,192]{1,0:T(8,128)(2,1)S(1)}, u32[]{:S(2)}, u32[]{:S(2)}) collective-permute-start(bf16[128,192]{1,0:T(8,128)(2,1)S(1)} %select_bitcast_fusion.1), channel_id=1, source_target_pairs={{0,2},{1,3},{2,0},{3,1},{4,6},{5,7},{6,4},{7,5},{8,10},{9,11},{10,... | collective-permute-start | bytes 147464 | tf_op jit(solution)/shard_map/ppermute | solution.py:41

commit v15 on v14

--- a/solution.py
+++ b/solution.py
@@ -179,7 +179,7 @@
     width = own_tok.shape[2]
     img_rows = img_dev * TOKS
     begin = own_tok.astype(jnp.float32).reshape(img_rows, width)
-    normed = layer_norm(begin, gain_self)
+    normed = lax.optimization_barrier(layer_norm(begin, gain_self))
     qkv = jnp.einsum("rd,kdc->krc", normed, self_qkv, preferred_element_type=jnp.float32).astype(
         jnp.bfloat16
     )
@@ -187,7 +187,7 @@
         attend(qkv[0], qkv[1], qkv[2], img_dev), self_out, preferred_element_type=jnp.float32
     )
     resid_img = begin + mp_allreduce(term.astype(jnp.bfloat16))
-    normed = layer_norm(resid_img, gain_query)
+    normed = lax.optimization_barrier(layer_norm(resid_img, gain_query))
     query_img = jnp.dot(normed, cross_query, preferred_element_type=jnp.float32).astype(
         jnp.bfloat16
     )
@@ -208,7 +208,7 @@
         attend(query, keyval[0], keyval[1], views_n), cross_out, preferred_element_type=jnp.float32
     )
     resid = resid + mp_allreduce(term.astype(jnp.bfloat16))
-    normed = layer_norm(resid, gain_mlp)
+    normed = lax.optimization_barrier(layer_norm(resid, gain_mlp))
     hidden = jax.nn.gelu(
         jnp.dot(normed, mlp_up, preferred_element_type=jnp.float32), approximate=False
     )
@@ -221,12 +221,14 @@
     part = (final.reshape(views_n, TOKS, quarter) * conf[:, :, None]).astype(jnp.bfloat16)
     weight = conf.astype(jnp.bfloat16)
     owner_match = near.astype(jnp.float32).T
-    numer = jnp.einsum(
-        "iv,vtc->itc", owner_match, part.astype(jnp.float32), precision=lax.Precision.HIGHEST
-    )
-    denom = jnp.dot(owner_match, weight.astype(jnp.float32), precision=lax.Precision.HIGHEST)
-    result = numer / jnp.maximum(denom, 1.0)[:, :, None]
-    return result.astype(jnp.bfloat16).reshape(img_dev * TOKS, quarter)
+    partf = part.astype(jnp.float32)
+    weightf = weight.astype(jnp.float32)
+    rows = []
+    for i in range(img_dev):
+        numer = jnp.sum(owner_match[i][:, None, None] * partf, axis=0)
+        denom = jnp.sum(owner_match[i][:, None] * weightf, axis=0)
+        rows.append(numer / jnp.maximum(denom, 1.0)[:, None])
+    return jnp.concatenate(rows, axis=0).astype(jnp.bfloat16)
 
 
 def solution(mesh):

time: 45.9 us -> 46.1 us (level)
  other arithmetic: 4.3 us -> 6.21 us
  matrix products: 6.09 us -> 4.39 us
  local copies, waits for them, and re-layouts: 6.82 us -> 6.01 us
  waiting for transfers between devices: 13 us -> 13.8 us
    dot_general x1, matrix products: 1.67 us -> 0.4 us  [per_device(): jnp.einsum('rd,kdc->krc', normed, self_qkv, preferred_element_type=jnp.fl...]
    convert_element_type x0 -> x4, other arithmetic: none -> 1.02 us  [the longest x3 1.02 us: layer_norm(): return (center * lax.rsqrt(spread + EPSILON) * gain).astype(jnp.bfloat16)]
    concatenate x0 -> x1, other arithmetic: none -> 0.63 us  [per_device(): return jnp.concatenate(rows, axis=0).astype(jnp.bfloat16)]
    convert_element_type x1 -> x0, local copies, waits for them, and re-layouts: 0.62 us -> none  [per_device(): return result.astype(jnp.bfloat16).reshape(img_dev * TOKS, quarter)]
    unnamed x22 -> x24, local copies, waits for them, and re-layouts: 1 us -> 0.95 us
  transfers between devices with their start and end apart: 17 -> 17, of which waited for: 8 -> 8; matrix products, arithmetic and copies ran while one was open for 24% -> 23% of each run, Pallas kernels for 0% -> 0%
where the time goes in v15:
time: 46.1 us; the launch traced here: 45.7 us
  starting transfers between devices  14.6 us (32%)
  waiting for transfers between devices  13.8 us (30%)
  other arithmetic  6.21 us (13%)
  local copies, waits for them, and re-layouts  6.01 us (13%)
  matrix products  4.39 us (10%)
  between operations  0.73 us (2%)
    ppermute x14, waiting for transfers between devices, swap(): return lax.ppermute(values, 'mp', pairs)  12.5 us
    ppermute x14, starting transfers between devices, swap(): return lax.ppermute(values, 'mp', pairs)  9.74 us
    ppermute x3, starting transfers between devices, pairs_shift(): lax.ppermute(values, 'pairs', [(i, (i + step) % owners_n) for i in range(...  4.9 us
    ppermute x3, waiting for transfers between devices, pairs_shift(): lax.ppermute(values, 'pairs', [(i, (i + step) % owners_n) for i in range(...  1.25 us
    dot_general x1, matrix products, per_device(): jnp.dot(normed, mlp_up, preferred_element_type=jnp.float32)  1.06 us
    convert_element_type x3, other arithmetic, layer_norm(): return (center * lax.rsqrt(spread + EPSILON) * gain).astype(jnp.bfloat16)  1.02 us
    unnamed x24, local copies, waits for them, and re-layouts  0.95 us
  transfers between devices with their start and end apart: 17, of which 8 were waited for; matrix products, arithmetic and copies ran while one was open for 23% of the time, Pallas kernels for 0%

profile of v15, /device:TPU:0, one launch (start us, length us, event | category | flops | bytes accessed | tf_op | source)
XLA Modules:
  0.0 45.7 jit_solution(7031623362544432827)
XLA Ops:
  0.0 0.5 collective-permute-start.5
  0.5 2.6 %collective-permute-start.4 = (bf16[2,32,192]{2,1,0:T(8,128)(2,1)}, bf16[2,32,192]{2,1,0:T(8,128)(2,1)S(1)}, u32[]{:S(2)}, u32[]{:S(2)}) collective-permute-start(bf16[2,32,192]{2,1,0:T(8,128)(2,1)} %bitcast.80), channel_id=1, source_target_pairs={{0,2},{1,3},{2,0},{3,1},{4,6},{5,7},{6,4},{7,5},{8,10},{9,11},{10,... | collective-permute-start | bytes 73736 | tf_op jit(solution)/shard_map/ppermute | solution.py:41
  3.1 0.9 %reshape.541 = f32[12288]{0:T(1024)S(1)} reshape(bf16[64,192]{1,0:T(8,128)(2,1)} %param.16) | data formatting | bytes 73728 | tf_op jit(solution)/shard_map/reshape | solution.py:153
  4.0 0.8 %reshape.465 = f32[128]{0:T(128)S(1)} reshape(f32[2,64]{1,0:T(2,128)} %param.18) | data formatting | bytes 1024 | tf_op jit(solution)/shard_map/reshape | solution.py:155
  4.7 0.7 %convert_element_type.168 = f32[2,2]{1,0:T(2,128)S(1)} convert(s32[2,2]{1,0:T(2,128)} %param.17) | non-fusion elementwise | flops 4 | bytes 32 | tf_op jit(solution)/shard_map/convert_element_type | solution.py:154
  5.6 3.8 %collective-permute-start.2 = (f32[12420]{0:T(1024)S(1)}, f32[12420]{0:T(1024)S(1)}, u32[]{:S(2)}, u32[]{:S(2)}) collective-permute-start(f32[12420]{0:T(1024)S(1)} %concatenate.60), channel_id=1, source_target_pairs={{0,12},{4,0},{8,4},{12,8},{1,13},{5,1},{9,5},{13,9},{2,14},{6,2},{... | collective-permute-start | bytes 149048 | tf_op jit(solution)/shard_map/ppermute | solution.py:37
  9.5 1.1 %collective-permute-start = (f32[12420]{0:T(1024)S(1)}, f32[12420]{0:T(1024)S(1)}, u32[]{:S(2)}, u32[]{:S(2)}) collective-permute-start(f32[12420]{0:T(1024)S(1)} %concatenate.60), channel_id=1, source_target_pairs={{0,4},{4,8},{8,12},{12,0},{1,5},{5,9},{9,13},{13,1},{2,6},{6,10},{... | collective-permute-start | bytes 149048 | tf_op jit(solution)/shard_map/ppermute | solution.py:37
  10.6 0.8 %select_select_fusion.3 = (bf16[2,32,192]{2,1,0:T(8,128)(2,1)S(1)}, bf16[2,32,192]{2,1,0:T(8,128)(2,1)S(1)}, bf16[2,32,192]{2,1,0:T(8,128)(2,1)S(1)}, bf16[2,32,192]{2,1,0:T(8,128)(2,1)S(1)}) fusion(bf16[2,32,192]{2,1,0:T(8,128)(2,1)S(1)} %collective-permute-done.3, bf16[2,32,192]{2,1,0:T(8,128)(2,1)S(1)} %collective-permute-done.4, ...), kind=kLoop, calls=%fused_computation.116 | loop fusion | flops 147456 | bytes 196620 | tf_op jit(solution)/shard_map/jit(_where)/select_n | solution.py:91
  11.4 0.2 convert_reduce_fusion.1
  11.6 0.2 fusion.23
  11.8 0.8 %fusion.25 = bf16[64,768]{1,0:T(8,128)(2,1)S(1)} fusion(bf16[64,768]{1,0:T(8,128)(2,1)S(1)} %get-tuple-element.28, f32[768]{0:T(1024)} %param.19, f32[64]{0:T(128)S(1)} %add_rsqrt_fusion.3, f32[64]{0:T(128)S(1)} %broadcast_multiply_fusion.3), kind=kLoop, calls=%fused_computation.57 | loop fusion | flops 245760 | bytes 200192 | tf_op jit(solution)/shard_map/convert_element_type | solution.py:16
  12.6 0.4 fusion.6
  13.2 0.2 fusion.78
  13.4 0.1 convolution_multiply_fusion.1
  13.6 0.2 fusion.8
  14.0 0.2 convolution_convert_fusion.6
  14.4 1.2 %collective-permute-done.1 = f32[12420]{0:T(1024)S(1)} collective-permute-done((f32[12420]{0:T(1024)S(1)}, f32[12420]{0:T(1024)S(1)}, u32[]{:S(2)}, u32[]{:S(2)}) %collective-permute-start.1) | collective-permute-done | bytes 49712 | tf_op jit(solution)/shard_map/ppermute | solution.py:37
  15.8 0.2 pad_maximum_fusion
  16.6 0.1 add_reduce_fusion
  16.7 0.2 select_reduce_fusion
  17.0 0.2 convolution_convert_fusion.1
  17.3 0.1 fusion.52
  17.4 0.1 reshape.472
  17.5 0.1 concatenate.69
  17.8 1.6 %collective-permute-start.7 = (bf16[32,768]{1,0:T(8,128)(2,1)S(1)}, bf16[32,768]{1,0:T(8,128)(2,1)S(1)}, u32[]{:S(2)}, u32[]{:S(2)}) collective-permute-start(bf16[32,768]{1,0:T(8,128)(2,1)S(1)} %add_convert_fusion.1), channel_id=1, source_target_pairs={{0,2},{1,3},{2,0},{3,1},{4,6},{5,7},{6,4},{7,5},{8,10},{9,11},{10,... | collective-permute-start | bytes 147464 | tf_op jit(solution)/shard_map/ppermute | solution.py:41
  19.3 0.1 maximum_select_fusion.4
  19.4 1.2 %collective-permute-start.10 = (bf16[4,32,384]{2,1,0:T(8,128)(2,1)S(1)}, bf16[4,32,384]{2,1,0:T(8,128)(2,1)S(1)}, u32[]{:S(2)}, u32[]{:S(2)}) collective-permute-start(bf16[4,32,384]{2,1,0:T(8,128)(2,1)S(1)} %maximum_select_fusion.4), channel_id=1, source_target_pairs={{0,2},{1,3},{2,0},{3,1},{4,6},{5,7},{6,4},{7,5},{8,10},{9,11},{10,... | collective-permute-start | bytes 294920 | tf_op jit(solution)/shard_map/ppermute | solution.py:41
  20.6 0.1 maximum_select_fusion.3
  20.7 1.2 %collective-permute-done.7 = bf16[32,768]{1,0:T(8,128)(2,1)S(1)} collective-permute-done((bf16[32,768]{1,0:T(8,128)(2,1)S(1)}, bf16[32,768]{1,0:T(8,128)(2,1)S(1)}, u32[]{:S(2)}, u32[]{:S(2)}) %collective-permute-start.7) | collective-permute-done | bytes 49184 | tf_op jit(solution)/shard_map/ppermute | solution.py:41
  22.0 2.4 %collective-permute-done.10 = bf16[4,32,384]{2,1,0:T(8,128)(2,1)S(1)} collective-permute-done((bf16[4,32,384]{2,1,0:T(8,128)(2,1)S(1)}, bf16[4,32,384]{2,1,0:T(8,128)(2,1)S(1)}, u32[]{:S(2)}, u32[]{:S(2)}) %collective-permute-start.10) | collective-permute-done | bytes 98336 | tf_op jit(solution)/shard_map/ppermute | solution.py:41
  24.4 0.1 convert_reduce_fusion
  24.6 0.2 fusion.10
  24.9 0.4 fusion.26
  25.4 0.1 reshape.586
  25.5 0.1 reshape.585
  25.7 0.1 pad_maximum_fusion.1
  25.8 0.2 multiply_reduce_fusion.1
  26.1 0.2 copy-done.5
  26.3 0.2 convolution_convert_fusion.8
  26.7 0.2 convolution_convert_fusion
  26.9 0.1 reshape_reshape_reshape.3
  27.1 0.2 convolution_multiply_fusion
  27.4 0.3 fusion.5
  27.7 0.1 reshape.473
  27.9 0.1 copy-done.3
  28.0 0.2 convolution_convert_fusion.3
  28.5 1.1 %collective-permute-done.11 = bf16[64,768]{1,0:T(8,128)(2,1)S(1)} collective-permute-done((bf16[64,768]{1,0:T(8,128)(2,1)S(1)}, bf16[64,768]{1,0:T(8,128)(2,1)S(1)}, u32[]{:S(2)}, u32[]{:S(2)}) %collective-permute-start.11) | collective-permute-done | bytes 98336 | tf_op jit(solution)/shard_map/ppermute | solution.py:41
  29.6 1.2 %collective-permute-start.12 = (bf16[64,768]{1,0:T(8,128)(2,1)S(1)}, bf16[64,768]{1,0:T(8,128)(2,1)S(1)}, u32[]{:S(2)}, u32[]{:S(2)}) collective-permute-start(bf16[64,768]{1,0:T(8,128)(2,1)S(1)} %add_convert_fusion), channel_id=1, source_target_pairs={{0,2},{1,3},{2,0},{3,1},{4,6},{5,7},{6,4},{7,5},{8,10},{9,11},{10,... | collective-permute-start | bytes 294920 | tf_op jit(solution)/shard_map/ppermute | solution.py:41
  30.9 3.7 %collective-permute-done.12 = bf16[64,768]{1,0:T(8,128)(2,1)S(1)} collective-permute-done((bf16[64,768]{1,0:T(8,128)(2,1)S(1)}, bf16[64,768]{1,0:T(8,128)(2,1)S(1)}, u32[]{:S(2)}, u32[]{:S(2)}) %collective-permute-start.12) | collective-permute-done | bytes 98336 | tf_op jit(solution)/shard_map/ppermute | solution.py:41
  34.8 0.6 %gather_fusion = f32[4,32,768]{2,1,0:T(8,128)S(1)} fusion(f32[2,32,768]{2,1,0:T(8,128)S(1)} %convert_add_fusion.2, s32[1024]{0:T(1024)S(1)} %pad_clamp_fusion), kind=kCustom, calls=%fused_computation | custom fusion | bytes 786448 | tf_op jit(solution)/shard_map/jit(_take)/gather | solution.py:204
  35.4 0.7 %collective-permute-done.13 = f32[64,768]{1,0:T(8,128)S(1)} collective-permute-done((f32[64,768]{1,0:T(8,128)S(1)}, f32[64,768]{1,0:T(8,128)S(1)}, u32[]{:S(2)}, u32[]{:S(2)}) %collective-permute-start.13) | collective-permute-done | bytes 196640 | tf_op jit(solution)/shard_map/ppermute | solution.py:41
  36.1 0.2 fusion.75
  36.4 0.2 multiply_reduce_fusion
  36.6 0.1 multiply_convert_fusion
  36.7 1.1 %fusion.13 = bf16[128,768]{1,0:T(8,128)(2,1)S(1)} fusion(bf16[128,768]{1,0:T(8,128)(2,1)S(1)} %multiply_convert_fusion, bf16[768,768]{1,0:T(8,128)(2,1)S(1)} %copy-done), kind=kOutput, calls=%fused_computation.28 | convolution fusion | flops 157384704 | bytes 1572864 | tf_op jit(solution)/shard_map/dot_general | solution.py:213
  37.8 0.2 copy-done.1
  38.0 0.3 convolution_convert_fusion.2
  38.3 0.2 copy.71
  38.9 1.0 %collective-permute-start.16 = (bf16[128,192]{1,0:T(8,128)(2,1)S(1)}, bf16[128,192]{1,0:T(8,128)(2,1)S(1)}, u32[]{:S(2)}, u32[]{:S(2)}) collective-permute-start(bf16[128,192]{1,0:T(8,128)(2,1)S(1)} %select_bitcast_fusion), channel_id=1, source_target_pairs={{0,3},{1,2},{2,1},{3,0},{4,7},{5,6},{6,5},{7,4},{8,11},{9,10},{10,... | collective-permute-start | bytes 147464 | tf_op jit(solution)/shard_map/ppermute | solution.py:41
  39.8 0.4 collective-permute-start.14
  40.3 0.9 %collective-permute-start.15 = (bf16[128,192]{1,0:T(8,128)(2,1)S(1)}, bf16[128,192]{1,0:T(8,128)(2,1)S(1)}, u32[]{:S(2)}, u32[]{:S(2)}) collective-permute-start(bf16[128,192]{1,0:T(8,128)(2,1)S(1)} %select_bitcast_fusion.1), channel_id=1, source_target_pairs={{0,2},{1,3},{2,0},{3,1},{4,6},{5,7},{6,4},{7,5},{8,10},{9,11},{10,... | collective-permute-start | bytes 147464 | tf_op jit(solution)/shard_map/ppermute | solution.py:41
  41.4 1.7 %collective-permute-done.16 = bf16[128,192]{1,0:T(8,128)(2,1)S(1)} collective-permute-done((bf16[128,192]{1,0:T(8,128)(2,1)S(1)}, bf16[128,192]{1,0:T(8,128)(2,1)S(1)}, u32[]{:S(2)}, u32[]{:S(2)}) %collective-permute-start.16) | collective-permute-done | bytes 49184 | tf_op jit(solution)/shard_map/ppermute | solution.py:41
  43.0 1.7 %collective-permute-done.15 = bf16[128,192]{1,0:T(8,128)(2,1)S(1)} collective-permute-done((bf16[128,192]{1,0:T(8,128)(2,1)S(1)}, bf16[128,192]{1,0:T(8,128)(2,1)S(1)}, u32[]{:S(2)}, u32[]{:S(2)}) %collective-permute-start.15) | collective-permute-done | bytes 49184 | tf_op jit(solution)/shard_map/ppermute | solution.py:41
  45.1 0.6 %pad_maximum_fusion.3 = bf16[64,192]{1,0:T(8,128)(2,1)} fusion(bf16[32,192]{1,0:T(8,128)(2,1)S(1)} %divide_convert_fusion.4, bf16[32,192]{1,0:T(8,128)(2,1)S(1)} %divide_convert_fusion.5), kind=kLoop, calls=%fused_computation.110 | loop fusion | flops 49152 | bytes 49152 | tf_op jit(solution)/shard_map/concatenate | solution.py:231
  (105 shorter events, 3.9 us)
Async XLA Ops:
  0.0 36.7 %copy-start = (bf16[768,768]{1,0:T(8,128)(2,1)S(1)}, bf16[768,768]{1,0:T(8,128)(2,1)}, u32[]{:S(2)}) copy-start(bf16[768,768]{1,0:T(8,128)(2,1)} %param.28) | copy-start | bytes 3538948
  0.0 12.6 %copy-start.2 = (bf16[3,768,192]{1,2,0:T(8,128)(2,1)S(1)}, bf16[3,768,192]{1,2,0:T(8,128)(2,1)}, u32[]{:S(2)}) copy-start(bf16[3,768,192]{1,2,0:T(8,128)(2,1)} %param.23) | copy-start | bytes 2654212
  0.0 9.5 %collective-permute-start.5 = (bf16[2,32,192]{2,1,0:T(8,128)(2,1)}, bf16[2,32,192]{2,1,0:T(8,128)(2,1)S(1)}, u32[]{:S(2)}, u32[]{:S(2)}) collective-permute-start(bf16[2,32,192]{2,1,0:T(8,128)(2,1)} %bitcast.79), channel_id=1, source_target_pairs={{0,1},{1,0},{2,3},{3,2},{4,5},{5,4},{6,7},{7,6},{8,9},{9,8},{10,11... | collective-permute-start | bytes 73736 | tf_op jit(solution)/shard_map/ppermute | solution.py:41
  0.5 10.1 %collective-permute-start.4 = (bf16[2,32,192]{2,1,0:T(8,128)(2,1)}, bf16[2,32,192]{2,1,0:T(8,128)(2,1)S(1)}, u32[]{:S(2)}, u32[]{:S(2)}) collective-permute-start(bf16[2,32,192]{2,1,0:T(8,128)(2,1)} %bitcast.80), channel_id=1, source_target_pairs={{0,2},{1,3},{2,0},{3,1},{4,6},{5,7},{6,4},{7,5},{8,10},{9,11},{10,... | collective-permute-start | bytes 73736 | tf_op jit(solution)/shard_map/ppermute | solution.py:41
  3.0 7.6 %collective-permute-start.3 = (bf16[2,32,192]{2,1,0:T(8,128)(2,1)}, bf16[2,32,192]{2,1,0:T(8,128)(2,1)S(1)}, u32[]{:S(2)}, u32[]{:S(2)}) collective-permute-start(bf16[2,32,192]{2,1,0:T(8,128)(2,1)} %bitcast.81), channel_id=1, source_target_pairs={{0,3},{1,2},{2,1},{3,0},{4,7},{5,6},{6,5},{7,4},{8,11},{9,10},{10,... | collective-permute-start | bytes 73736 | tf_op jit(solution)/shard_map/ppermute | solution.py:41
  5.6 8.7 %collective-permute-start.2 = (f32[12420]{0:T(1024)S(1)}, f32[12420]{0:T(1024)S(1)}, u32[]{:S(2)}, u32[]{:S(2)}) collective-permute-start(f32[12420]{0:T(1024)S(1)} %concatenate.60), channel_id=1, source_target_pairs={{0,12},{4,0},{8,4},{12,8},{1,13},{5,1},{9,5},{13,9},{2,14},{6,2},{... | collective-permute-start | bytes 149048 | tf_op jit(solution)/shard_map/ppermute | solution.py:37
  9.4 6.2 %collective-permute-start.1 = (f32[12420]{0:T(1024)S(1)}, f32[12420]{0:T(1024)S(1)}, u32[]{:S(2)}, u32[]{:S(2)}) collective-permute-start(f32[12420]{0:T(1024)S(1)} %concatenate.60), channel_id=1, source_target_pairs={{0,8},{4,12},{8,0},{12,4},{1,9},{5,13},{9,1},{13,5},{2,10},{6,14},... | collective-permute-start | bytes 149048 | tf_op jit(solution)/shard_map/ppermute | solution.py:37
  9.5 6.1 %collective-permute-start = (f32[12420]{0:T(1024)S(1)}, f32[12420]{0:T(1024)S(1)}, u32[]{:S(2)}, u32[]{:S(2)}) collective-permute-start(f32[12420]{0:T(1024)S(1)} %concatenate.60), channel_id=1, source_target_pairs={{0,4},{4,8},{8,12},{12,0},{1,5},{5,9},{9,13},{13,1},{2,6},{6,10},{... | collective-permute-start | bytes 149048 | tf_op jit(solution)/shard_map/ppermute | solution.py:37
  12.6 1.4 %copy-start.4 = (bf16[192,768]{1,0:T(8,128)(2,1)S(1)}, bf16[192,768]{1,0:T(8,128)(2,1)}, u32[]{:S(2)}) copy-start(bf16[192,768]{1,0:T(8,128)(2,1)} %param.24) | copy-start | bytes 884740
  14.2 3.5 %collective-permute-start.6 = (bf16[32,768]{1,0:T(8,128)(2,1)S(1)}, bf16[32,768]{1,0:T(8,128)(2,1)S(1)}, u32[]{:S(2)}, u32[]{:S(2)}) collective-permute-start(bf16[32,768]{1,0:T(8,128)(2,1)S(1)} %broadcast_select_fusion.5), channel_id=1, source_target_pairs={{0,1},{1,0},{2,3},{3,2},{4,5},{5,4},{6,7},{7,6},{8,9},{9,8},{10,11... | collective-permute-start | bytes 147464 | tf_op jit(solution)/shard_map/ppermute | solution.py:41
  16.0 8.9 %copy-start.8 = (bf16[2,768,192]{1,2,0:T(8,128)(2,1)S(1)}, bf16[2,768,192]{1,2,0:T(8,128)(2,1)}, u32[]{:S(2)}) copy-start(bf16[2,768,192]{1,2,0:T(8,128)(2,1)} %param.26) | copy-start | bytes 1769476
  16.0 8.9 %copy-start.9 = (f32[768]{0:T(1024)S(1)}, f32[768]{0:T(1024)}, u32[]{:S(2)}) copy-start(f32[768]{0:T(1024)} %param.21) | copy-start | bytes 9220
  17.6 1.7 %collective-permute-start.9 = (bf16[4,32,192]{2,1,0:T(8,128)(2,1)S(1)}, bf16[4,32,192]{2,1,0:T(8,128)(2,1)S(1)}, u32[]{:S(2)}, u32[]{:S(2)}) collective-permute-start(bf16[4,32,192]{2,1,0:T(8,128)(2,1)S(1)} %reshape.472), channel_id=1, source_target_pairs={{0,1},{1,0},{2,3},{3,2},{4,5},{5,4},{6,7},{7,6},{8,9},{9,8},{10,11... | collective-permute-start | bytes 147464 | tf_op jit(solution)/shard_map/ppermute | solution.py:41
  17.8 4.2 %collective-permute-start.7 = (bf16[32,768]{1,0:T(8,128)(2,1)S(1)}, bf16[32,768]{1,0:T(8,128)(2,1)S(1)}, u32[]{:S(2)}, u32[]{:S(2)}) collective-permute-start(bf16[32,768]{1,0:T(8,128)(2,1)S(1)} %add_convert_fusion.1), channel_id=1, source_target_pairs={{0,2},{1,3},{2,0},{3,1},{4,6},{5,7},{6,4},{7,5},{8,10},{9,11},{10,... | collective-permute-start | bytes 147464 | tf_op jit(solution)/shard_map/ppermute | solution.py:41
  19.4 5.0 %collective-permute-start.10 = (bf16[4,32,384]{2,1,0:T(8,128)(2,1)S(1)}, bf16[4,32,384]{2,1,0:T(8,128)(2,1)S(1)}, u32[]{:S(2)}, u32[]{:S(2)}) collective-permute-start(bf16[4,32,384]{2,1,0:T(8,128)(2,1)S(1)} %maximum_select_fusion.4), channel_id=1, source_target_pairs={{0,2},{1,3},{2,0},{3,1},{4,6},{5,7},{6,4},{7,5},{8,10},{9,11},{10,... | collective-permute-start | bytes 294920 | tf_op jit(solution)/shard_map/ppermute | solution.py:41
  22.0 3.7 %collective-permute-start.8 = (f32[32,768]{1,0:T(8,128)S(1)}, f32[32,768]{1,0:T(8,128)S(1)}, u32[]{:S(2)}, u32[]{:S(2)}) collective-permute-start(f32[32,768]{1,0:T(8,128)S(1)} %convert_add_fusion.3), channel_id=1, source_target_pairs={{0,1},{1,0},{2,3},{3,2},{4,5},{5,4},{6,7},{7,6},{8,9},{9,8},{10,11... | collective-permute-start | bytes 294920 | tf_op jit(solution)/shard_map/ppermute | solution.py:41
  25.3 0.7 %copy-start.6 = (f32[768]{0:T(1024)S(1)}, f32[768]{0:T(1024)}, u32[]{:S(2)}) copy-start(f32[768]{0:T(1024)} %param.20) | copy-start | bytes 9220
  25.3 1.0 %copy-start.5 = (bf16[768,192]{0,1:T(8,128)(2,1)S(1)}, bf16[768,192]{0,1:T(8,128)(2,1)}, u32[]{:S(2)}) copy-start(bf16[768,192]{0,1:T(8,128)(2,1)} %param.25) | copy-start | bytes 884740
  27.0 1.0 %copy-start.3 = (bf16[192,768]{1,0:T(8,128)(2,1)S(1)}, bf16[192,768]{1,0:T(8,128)(2,1)}, u32[]{:S(2)}) copy-start(bf16[192,768]{1,0:T(8,128)(2,1)} %param.27) | copy-start | bytes 884740
  28.2 1.4 %collective-permute-start.11 = (bf16[64,768]{1,0:T(8,128)(2,1)S(1)}, bf16[64,768]{1,0:T(8,128)(2,1)S(1)}, u32[]{:S(2)}, u32[]{:S(2)}) collective-permute-start(bf16[64,768]{1,0:T(8,128)(2,1)S(1)} %broadcast_select_fusion.2), channel_id=1, source_target_pairs={{0,1},{1,0},{2,3},{3,2},{4,5},{5,4},{6,7},{7,6},{8,9},{9,8},{10,11... | collective-permute-start | bytes 294920 | tf_op jit(solution)/shard_map/ppermute | solution.py:41
  29.6 4.9 %collective-permute-start.12 = (bf16[64,768]{1,0:T(8,128)(2,1)S(1)}, bf16[64,768]{1,0:T(8,128)(2,1)S(1)}, u32[]{:S(2)}, u32[]{:S(2)}) collective-permute-start(bf16[64,768]{1,0:T(8,128)(2,1)S(1)} %add_convert_fusion), channel_id=1, source_target_pairs={{0,2},{1,3},{2,0},{3,1},{4,6},{5,7},{6,4},{7,5},{8,10},{9,11},{10,... | collective-permute-start | bytes 294920 | tf_op jit(solution)/shard_map/ppermute | solution.py:41
  34.6 1.5 %collective-permute-start.13 = (f32[64,768]{1,0:T(8,128)S(1)}, f32[64,768]{1,0:T(8,128)S(1)}, u32[]{:S(2)}, u32[]{:S(2)}) collective-permute-start(f32[64,768]{1,0:T(8,128)S(1)} %convert_add_fusion.1), channel_id=1, source_target_pairs={{0,1},{1,0},{2,3},{3,2},{4,5},{5,4},{6,7},{7,6},{8,9},{9,8},{10,11... | collective-permute-start | bytes 589832 | tf_op jit(solution)/shard_map/ppermute | solution.py:41
  35.4 1.2 %copy-start.7 = (f32[768]{0:T(1024)S(1)}, f32[768]{0:T(1024)}, u32[]{:S(2)}) copy-start(f32[768]{0:T(1024)} %param.22) | copy-start | bytes 9220
  36.7 1.3 %copy-start.1 = (bf16[768,768]{1,0:T(8,128)(2,1)S(1)}, bf16[768,768]{1,0:T(8,128)(2,1)}, u32[]{:S(2)}) copy-start(bf16[768,768]{1,0:T(8,128)(2,1)} %param.29) | copy-start | bytes 3538948
  38.9 4.1 %collective-permute-start.16 = (bf16[128,192]{1,0:T(8,128)(2,1)S(1)}, bf16[128,192]{1,0:T(8,128)(2,1)S(1)}, u32[]{:S(2)}, u32[]{:S(2)}) collective-permute-start(bf16[128,192]{1,0:T(8,128)(2,1)S(1)} %select_bitcast_fusion), channel_id=1, source_target_pairs={{0,3},{1,2},{2,1},{3,0},{4,7},{5,6},{6,5},{7,4},{8,11},{9,10},{10,... | collective-permute-start | bytes 147464 | tf_op jit(solution)/shard_map/ppermute | solution.py:41
  39.8 3.2 %collective-permute-start.14 = (bf16[128,192]{1,0:T(8,128)(2,1)S(1)}, bf16[128,192]{1,0:T(8,128)(2,1)S(1)}, u32[]{:S(2)}, u32[]{:S(2)}) collective-permute-start(bf16[128,192]{1,0:T(8,128)(2,1)S(1)} %select_bitcast_fusion.2), channel_id=1, source_target_pairs={{0,1},{1,0},{2,3},{3,2},{4,5},{5,4},{6,7},{7,6},{8,9},{9,8},{10,11... | collective-permute-start | bytes 147464 | tf_op jit(solution)/shard_map/ppermute | solution.py:41
  40.3 4.4 %collective-permute-start.15 = (bf16[128,192]{1,0:T(8,128)(2,1)S(1)}, bf16[128,192]{1,0:T(8,128)(2,1)S(1)}, u32[]{:S(2)}, u32[]{:S(2)}) collective-permute-start(bf16[128,192]{1,0:T(8,128)(2,1)S(1)} %select_bitcast_fusion.1), channel_id=1, source_target_pairs={{0,2},{1,3},{2,0},{3,1},{4,6},{5,7},{6,4},{7,5},{8,10},{9,11},{10,... | collective-permute-start | bytes 147464 | tf_op jit(solution)/shard_map/ppermute | solution.py:41

commit v16 on v15

--- a/solution.py
+++ b/solution.py
@@ -193,9 +193,9 @@
     )
 
     rows_n = views_n * TOKS
-    context = layer_norm(mp_gather_steps(context_q).astype(jnp.float32), gain_context).reshape(
-        rows_n, width
-    )
+    context = lax.optimization_barrier(
+        layer_norm(mp_gather_steps(context_q).astype(jnp.float32), gain_context)
+    ).reshape(rows_n, width)
     keyval = jnp.einsum(
         "rd,kdc->krc", context, cross_kv, preferred_element_type=jnp.float32
     ).astype(jnp.bfloat16)

time: 46.1 us -> 45.9 us (level)
    convert_element_type x3 -> x4, other arithmetic: 1.02 us -> 1.15 us  [layer_norm(): return (center * lax.rsqrt(spread + EPSILON) * gain).astype(jnp.bfloat16)]
  transfers between devices with their start and end apart: 17 -> 17, of which waited for: 8 -> 8; matrix products, arithmetic and copies ran while one was open for 23% -> 22% of each run, Pallas kernels for 0% -> 0%
where the time goes in v16:
time: 45.9 us; the launch traced here: 45.5 us
  starting transfers between devices  14.5 us (32%)
  waiting for transfers between devices  14 us (31%)
  other arithmetic  6.23 us (14%)
  local copies, waits for them, and re-layouts  5.73 us (12%)
  matrix products  4.31 us (9%)
  between operations  0.74 us (2%)
    ppermute x14, waiting for transfers between devices, swap(): return lax.ppermute(values, 'mp', pairs)  12.8 us
    ppermute x14, starting transfers between devices, swap(): return lax.ppermute(values, 'mp', pairs)  9.61 us
    ppermute x3, starting transfers between devices, pairs_shift(): lax.ppermute(values, 'pairs', [(i, (i + step) % owners_n) for i in range(...  4.9 us
    ppermute x3, waiting for transfers between devices, pairs_shift(): lax.ppermute(values, 'pairs', [(i, (i + step) % owners_n) for i in range(...  1.25 us
    convert_element_type x4, other arithmetic, layer_norm(): return (center * lax.rsqrt(spread + EPSILON) * gain).astype(jnp.bfloat16)  1.15 us
    dot_general x1, matrix products, per_device(): jnp.dot(normed, mlp_up, preferred_element_type=jnp.float32)  1.06 us
    unnamed x24, local copies, waits for them, and re-layouts  0.95 us
  transfers between devices with their start and end apart: 17, of which 8 were waited for; matrix products, arithmetic and copies ran while one was open for 22% of the time, Pallas kernels for 0%

profile of v16, /device:TPU:0, one launch (start us, length us, event | category | flops | bytes accessed | tf_op | source)
XLA Modules:
  0.0 45.5 jit_solution(5529689056069933850)
XLA Ops:
  0.0 0.5 collective-permute-start.5
  0.5 2.6 %collective-permute-start.4 = (bf16[2,32,192]{2,1,0:T(8,128)(2,1)}, bf16[2,32,192]{2,1,0:T(8,128)(2,1)S(1)}, u32[]{:S(2)}, u32[]{:S(2)}) collective-permute-start(bf16[2,32,192]{2,1,0:T(8,128)(2,1)} %bitcast.80), channel_id=1, source_target_pairs={{0,2},{1,3},{2,0},{3,1},{4,6},{5,7},{6,4},{7,5},{8,10},{9,11},{10,... | collective-permute-start | bytes 73736 | tf_op jit(solution)/shard_map/ppermute | solution.py:41
  3.1 0.9 %reshape.521 = f32[12288]{0:T(1024)S(1)} reshape(bf16[64,192]{1,0:T(8,128)(2,1)} %param.16) | data formatting | bytes 73728 | tf_op jit(solution)/shard_map/reshape | solution.py:153
  4.0 0.8 %reshape.444 = f32[128]{0:T(128)S(1)} reshape(f32[2,64]{1,0:T(2,128)} %param.18) | data formatting | bytes 1024 | tf_op jit(solution)/shard_map/reshape | solution.py:155
  4.7 0.7 %convert_element_type.164 = f32[2,2]{1,0:T(2,128)S(1)} convert(s32[2,2]{1,0:T(2,128)} %param.17) | non-fusion elementwise | flops 4 | bytes 32 | tf_op jit(solution)/shard_map/convert_element_type | solution.py:154
  5.6 3.8 %collective-permute-start.2 = (f32[12420]{0:T(1024)S(1)}, f32[12420]{0:T(1024)S(1)}, u32[]{:S(2)}, u32[]{:S(2)}) collective-permute-start(f32[12420]{0:T(1024)S(1)} %concatenate.42), channel_id=1, source_target_pairs={{0,12},{4,0},{8,4},{12,8},{1,13},{5,1},{9,5},{13,9},{2,14},{6,2},{... | collective-permute-start | bytes 149048 | tf_op jit(solution)/shard_map/ppermute | solution.py:37
  9.5 1.1 %collective-permute-start = (f32[12420]{0:T(1024)S(1)}, f32[12420]{0:T(1024)S(1)}, u32[]{:S(2)}, u32[]{:S(2)}) collective-permute-start(f32[12420]{0:T(1024)S(1)} %concatenate.42), channel_id=1, source_target_pairs={{0,4},{4,8},{8,12},{12,0},{1,5},{5,9},{9,13},{13,1},{2,6},{6,10},{... | collective-permute-start | bytes 149048 | tf_op jit(solution)/shard_map/ppermute | solution.py:37
  10.6 0.8 %select_select_fusion.3 = (bf16[2,32,192]{2,1,0:T(8,128)(2,1)S(1)}, bf16[2,32,192]{2,1,0:T(8,128)(2,1)S(1)}, bf16[2,32,192]{2,1,0:T(8,128)(2,1)S(1)}, bf16[2,32,192]{2,1,0:T(8,128)(2,1)S(1)}) fusion(bf16[2,32,192]{2,1,0:T(8,128)(2,1)S(1)} %collective-permute-done.3, bf16[2,32,192]{2,1,0:T(8,128)(2,1)S(1)} %collective-permute-done.4, ...), kind=kLoop, calls=%fused_computation.106 | loop fusion | flops 147456 | bytes 196620 | tf_op jit(solution)/shard_map/jit(_where)/select_n | solution.py:91
  11.4 0.2 convert_reduce_fusion.1
  11.6 0.2 fusion.26
  11.8 0.8 %fusion.28 = bf16[64,768]{1,0:T(8,128)(2,1)S(1)} fusion(bf16[64,768]{1,0:T(8,128)(2,1)S(1)} %get-tuple-element.28, f32[768]{0:T(1024)} %param.19, f32[64]{0:T(128)S(1)} %add_rsqrt_fusion.3, f32[64]{0:T(128)S(1)} %broadcast_multiply_fusion.3), kind=kLoop, calls=%fused_computation.59 | loop fusion | flops 245760 | bytes 200192 | tf_op jit(solution)/shard_map/convert_element_type | solution.py:16
  12.6 0.4 fusion.6
  13.2 0.2 fusion.70
  13.4 0.1 convolution_multiply_fusion.1
  13.6 0.2 fusion.8
  14.0 0.2 convolution_convert_fusion.6
  14.4 1.2 %collective-permute-done.1 = f32[12420]{0:T(1024)S(1)} collective-permute-done((f32[12420]{0:T(1024)S(1)}, f32[12420]{0:T(1024)S(1)}, u32[]{:S(2)}, u32[]{:S(2)}) %collective-permute-start.1) | collective-permute-done | bytes 49712 | tf_op jit(solution)/shard_map/ppermute | solution.py:37
  15.8 0.2 pad_maximum_fusion
  16.6 0.1 add_reduce_fusion
  16.7 0.2 select_reduce_fusion
  17.0 0.2 convolution_convert_fusion.1
  17.3 0.1 reshape.451
  17.4 0.1 fusion.45
  17.6 1.6 %collective-permute-start.7 = (bf16[32,768]{1,0:T(8,128)(2,1)S(1)}, bf16[32,768]{1,0:T(8,128)(2,1)S(1)}, u32[]{:S(2)}, u32[]{:S(2)}) collective-permute-start(bf16[32,768]{1,0:T(8,128)(2,1)S(1)} %add_convert_fusion.1), channel_id=1, source_target_pairs={{0,2},{1,3},{2,0},{3,1},{4,6},{5,7},{6,4},{7,5},{8,10},{9,11},{10,... | collective-permute-start | bytes 147464 | tf_op jit(solution)/shard_map/ppermute | solution.py:41
  19.2 0.1 maximum_select_fusion.1
  19.3 1.1 %collective-permute-start.10 = (bf16[4,32,384]{2,1,0:T(8,128)(2,1)S(1)}, bf16[4,32,384]{2,1,0:T(8,128)(2,1)S(1)}, u32[]{:S(2)}, u32[]{:S(2)}) collective-permute-start(bf16[4,32,384]{2,1,0:T(8,128)(2,1)S(1)} %maximum_select_fusion.1), channel_id=1, source_target_pairs={{0,2},{1,3},{2,0},{3,1},{4,6},{5,7},{6,4},{7,5},{8,10},{9,11},{10,... | collective-permute-start | bytes 294920 | tf_op jit(solution)/shard_map/ppermute | solution.py:41
  20.4 1.5 %collective-permute-done.7 = bf16[32,768]{1,0:T(8,128)(2,1)S(1)} collective-permute-done((bf16[32,768]{1,0:T(8,128)(2,1)S(1)}, bf16[32,768]{1,0:T(8,128)(2,1)S(1)}, u32[]{:S(2)}, u32[]{:S(2)}) %collective-permute-start.7) | collective-permute-done | bytes 49184 | tf_op jit(solution)/shard_map/ppermute | solution.py:41
  21.9 2.4 %collective-permute-done.10 = bf16[4,32,384]{2,1,0:T(8,128)(2,1)S(1)} collective-permute-done((bf16[4,32,384]{2,1,0:T(8,128)(2,1)S(1)}, bf16[4,32,384]{2,1,0:T(8,128)(2,1)S(1)}, u32[]{:S(2)}, u32[]{:S(2)}) %collective-permute-start.10) | collective-permute-done | bytes 98336 | tf_op jit(solution)/shard_map/ppermute | solution.py:41
  24.3 0.1 convert_reduce_fusion
  24.4 0.2 fusion.11
  24.6 0.1 fusion.13
  24.8 0.3 fusion.76
  25.2 0.1 reshape.566
  25.3 0.1 reshape.565
  25.5 0.1 pad_maximum_fusion.1
  25.6 0.2 multiply_reduce_fusion.1
  25.9 0.2 copy-done.6
  26.1 0.2 convolution_convert_fusion.8
  26.3 0.1 reshape_reshape.3
  26.4 0.2 convolution_convert_fusion
  26.7 0.1 reshape_reshape_reshape.3
  26.8 0.2 convolution_multiply_fusion
  27.1 0.3 fusion.5
  27.5 0.1 reshape.453
  27.7 0.1 copy-done.4
  27.8 0.2 convolution_convert_fusion.3
  28.3 1.1 %collective-permute-done.11 = bf16[64,768]{1,0:T(8,128)(2,1)S(1)} collective-permute-done((bf16[64,768]{1,0:T(8,128)(2,1)S(1)}, bf16[64,768]{1,0:T(8,128)(2,1)S(1)}, u32[]{:S(2)}, u32[]{:S(2)}) %collective-permute-start.11) | collective-permute-done | bytes 98336 | tf_op jit(solution)/shard_map/ppermute | solution.py:41
  29.4 1.2 %collective-permute-start.12 = (bf16[64,768]{1,0:T(8,128)(2,1)S(1)}, bf16[64,768]{1,0:T(8,128)(2,1)S(1)}, u32[]{:S(2)}, u32[]{:S(2)}) collective-permute-start(bf16[64,768]{1,0:T(8,128)(2,1)S(1)} %add_convert_fusion), channel_id=1, source_target_pairs={{0,2},{1,3},{2,0},{3,1},{4,6},{5,7},{6,4},{7,5},{8,10},{9,11},{10,... | collective-permute-start | bytes 294920 | tf_op jit(solution)/shard_map/ppermute | solution.py:41
  30.6 3.7 %collective-permute-done.12 = bf16[64,768]{1,0:T(8,128)(2,1)S(1)} collective-permute-done((bf16[64,768]{1,0:T(8,128)(2,1)S(1)}, bf16[64,768]{1,0:T(8,128)(2,1)S(1)}, u32[]{:S(2)}, u32[]{:S(2)}) %collective-permute-start.12) | collective-permute-done | bytes 98336 | tf_op jit(solution)/shard_map/ppermute | solution.py:41
  34.5 0.6 %gather_fusion = f32[4,32,768]{2,1,0:T(8,128)S(1)} fusion(f32[2,32,768]{2,1,0:T(8,128)S(1)} %convert_add_fusion.2, s32[1024]{0:T(1024)S(1)} %pad_clamp_fusion), kind=kCustom, calls=%fused_computation | custom fusion | bytes 786448 | tf_op jit(solution)/shard_map/jit(_take)/gather | solution.py:204
  35.1 0.7 %collective-permute-done.13 = f32[64,768]{1,0:T(8,128)S(1)} collective-permute-done((f32[64,768]{1,0:T(8,128)S(1)}, f32[64,768]{1,0:T(8,128)S(1)}, u32[]{:S(2)}, u32[]{:S(2)}) %collective-permute-start.13) | collective-permute-done | bytes 196640 | tf_op jit(solution)/shard_map/ppermute | solution.py:41
  35.9 0.2 fusion.67
  36.1 0.2 multiply_reduce_fusion
  36.3 0.1 multiply_convert_fusion
  36.5 1.1 %fusion.16 = bf16[128,768]{1,0:T(8,128)(2,1)S(1)} fusion(bf16[128,768]{1,0:T(8,128)(2,1)S(1)} %multiply_convert_fusion, bf16[768,768]{1,0:T(8,128)(2,1)S(1)} %copy-done), kind=kOutput, calls=%fused_computation.31 | convolution fusion | flops 157384704 | bytes 1572864 | tf_op jit(solution)/shard_map/dot_general | solution.py:213
  37.6 0.2 copy-done.1
  37.8 0.3 convolution_convert_fusion.2
  38.1 0.2 copy.71
  38.7 1.0 %collective-permute-start.16 = (bf16[128,192]{1,0:T(8,128)(2,1)S(1)}, bf16[128,192]{1,0:T(8,128)(2,1)S(1)}, u32[]{:S(2)}, u32[]{:S(2)}) collective-permute-start(bf16[128,192]{1,0:T(8,128)(2,1)S(1)} %select_bitcast_fusion), channel_id=1, source_target_pairs={{0,3},{1,2},{2,1},{3,0},{4,7},{5,6},{6,5},{7,4},{8,11},{9,10},{10,... | collective-permute-start | bytes 147464 | tf_op jit(solution)/shard_map/ppermute | solution.py:41
  39.6 0.4 collective-permute-start.14
  40.1 0.9 %collective-permute-start.15 = (bf16[128,192]{1,0:T(8,128)(2,1)S(1)}, bf16[128,192]{1,0:T(8,128)(2,1)S(1)}, u32[]{:S(2)}, u32[]{:S(2)}) collective-permute-start(bf16[128,192]{1,0:T(8,128)(2,1)S(1)} %select_bitcast_fusion.1), channel_id=1, source_target_pairs={{0,2},{1,3},{2,0},{3,1},{4,6},{5,7},{6,4},{7,5},{8,10},{9,11},{10,... | collective-permute-start | bytes 147464 | tf_op jit(solution)/shard_map/ppermute | solution.py:41
  41.1 1.7 %collective-permute-done.16 = bf16[128,192]{1,0:T(8,128)(2,1)S(1)} collective-permute-done((bf16[128,192]{1,0:T(8,128)(2,1)S(1)}, bf16[128,192]{1,0:T(8,128)(2,1)S(1)}, u32[]{:S(2)}, u32[]{:S(2)}) %collective-permute-start.16) | collective-permute-done | bytes 49184 | tf_op jit(solution)/shard_map/ppermute | solution.py:41
  42.8 1.7 %collective-permute-done.15 = bf16[128,192]{1,0:T(8,128)(2,1)S(1)} collective-permute-done((bf16[128,192]{1,0:T(8,128)(2,1)S(1)}, bf16[128,192]{1,0:T(8,128)(2,1)S(1)}, u32[]{:S(2)}, u32[]{:S(2)}) %collective-permute-start.15) | collective-permute-done | bytes 49184 | tf_op jit(solution)/shard_map/ppermute | solution.py:41
  44.9 0.6 %pad_maximum_fusion.3 = bf16[64,192]{1,0:T(8,128)(2,1)} fusion(bf16[32,192]{1,0:T(8,128)(2,1)S(1)} %divide_convert_fusion.4, bf16[32,192]{1,0:T(8,128)(2,1)S(1)} %divide_convert_fusion.5), kind=kLoop, calls=%fused_computation.100 | loop fusion | flops 49152 | bytes 49152 | tf_op jit(solution)/shard_map/concatenate | solution.py:231
  (102 shorter events, 3.7 us)
Async XLA Ops:
  0.0 36.5 %copy-start = (bf16[768,768]{1,0:T(8,128)(2,1)S(1)}, bf16[768,768]{1,0:T(8,128)(2,1)}, u32[]{:S(2)}) copy-start(bf16[768,768]{1,0:T(8,128)(2,1)} %param.28) | copy-start | bytes 3538948
  0.0 12.6 %copy-start.2 = (bf16[3,768,192]{1,2,0:T(8,128)(2,1)S(1)}, bf16[3,768,192]{1,2,0:T(8,128)(2,1)}, u32[]{:S(2)}) copy-start(bf16[3,768,192]{1,2,0:T(8,128)(2,1)} %param.23) | copy-start | bytes 2654212
  0.0 9.5 %collective-permute-start.5 = (bf16[2,32,192]{2,1,0:T(8,128)(2,1)}, bf16[2,32,192]{2,1,0:T(8,128)(2,1)S(1)}, u32[]{:S(2)}, u32[]{:S(2)}) collective-permute-start(bf16[2,32,192]{2,1,0:T(8,128)(2,1)} %bitcast.79), channel_id=1, source_target_pairs={{0,1},{1,0},{2,3},{3,2},{4,5},{5,4},{6,7},{7,6},{8,9},{9,8},{10,11... | collective-permute-start | bytes 73736 | tf_op jit(solution)/shard_map/ppermute | solution.py:41
  0.5 10.1 %collective-permute-start.4 = (bf16[2,32,192]{2,1,0:T(8,128)(2,1)}, bf16[2,32,192]{2,1,0:T(8,128)(2,1)S(1)}, u32[]{:S(2)}, u32[]{:S(2)}) collective-permute-start(bf16[2,32,192]{2,1,0:T(8,128)(2,1)} %bitcast.80), channel_id=1, source_target_pairs={{0,2},{1,3},{2,0},{3,1},{4,6},{5,7},{6,4},{7,5},{8,10},{9,11},{10,... | collective-permute-start | bytes 73736 | tf_op jit(solution)/shard_map/ppermute | solution.py:41
  3.0 7.6 %collective-permute-start.3 = (bf16[2,32,192]{2,1,0:T(8,128)(2,1)}, bf16[2,32,192]{2,1,0:T(8,128)(2,1)S(1)}, u32[]{:S(2)}, u32[]{:S(2)}) collective-permute-start(bf16[2,32,192]{2,1,0:T(8,128)(2,1)} %bitcast.81), channel_id=1, source_target_pairs={{0,3},{1,2},{2,1},{3,0},{4,7},{5,6},{6,5},{7,4},{8,11},{9,10},{10,... | collective-permute-start | bytes 73736 | tf_op jit(solution)/shard_map/ppermute | solution.py:41
  5.6 8.7 %collective-permute-start.2 = (f32[12420]{0:T(1024)S(1)}, f32[12420]{0:T(1024)S(1)}, u32[]{:S(2)}, u32[]{:S(2)}) collective-permute-start(f32[12420]{0:T(1024)S(1)} %concatenate.42), channel_id=1, source_target_pairs={{0,12},{4,0},{8,4},{12,8},{1,13},{5,1},{9,5},{13,9},{2,14},{6,2},{... | collective-permute-start | bytes 149048 | tf_op jit(solution)/shard_map/ppermute | solution.py:37
  9.4 6.2 %collective-permute-start.1 = (f32[12420]{0:T(1024)S(1)}, f32[12420]{0:T(1024)S(1)}, u32[]{:S(2)}, u32[]{:S(2)}) collective-permute-start(f32[12420]{0:T(1024)S(1)} %concatenate.42), channel_id=1, source_target_pairs={{0,8},{4,12},{8,0},{12,4},{1,9},{5,13},{9,1},{13,5},{2,10},{6,14},... | collective-permute-start | bytes 149048 | tf_op jit(solution)/shard_map/ppermute | solution.py:37
  9.5 6.1 %collective-permute-start = (f32[12420]{0:T(1024)S(1)}, f32[12420]{0:T(1024)S(1)}, u32[]{:S(2)}, u32[]{:S(2)}) collective-permute-start(f32[12420]{0:T(1024)S(1)} %concatenate.42), channel_id=1, source_target_pairs={{0,4},{4,8},{8,12},{12,0},{1,5},{5,9},{9,13},{13,1},{2,6},{6,10},{... | collective-permute-start | bytes 149048 | tf_op jit(solution)/shard_map/ppermute | solution.py:37
  12.6 1.4 %copy-start.5 = (bf16[192,768]{1,0:T(8,128)(2,1)S(1)}, bf16[192,768]{1,0:T(8,128)(2,1)}, u32[]{:S(2)}) copy-start(bf16[192,768]{1,0:T(8,128)(2,1)} %param.24) | copy-start | bytes 884740
  14.2 3.4 %collective-permute-start.6 = (bf16[32,768]{1,0:T(8,128)(2,1)S(1)}, bf16[32,768]{1,0:T(8,128)(2,1)S(1)}, u32[]{:S(2)}, u32[]{:S(2)}) collective-permute-start(bf16[32,768]{1,0:T(8,128)(2,1)S(1)} %broadcast_select_fusion.5), channel_id=1, source_target_pairs={{0,1},{1,0},{2,3},{3,2},{4,5},{5,4},{6,7},{7,6},{8,9},{9,8},{10,11... | collective-permute-start | bytes 147464 | tf_op jit(solution)/shard_map/ppermute | solution.py:41
  15.8 8.8 %copy-start.7 = (f32[768]{0:T(1024)S(1)}, f32[768]{0:T(1024)}, u32[]{:S(2)}) copy-start(f32[768]{0:T(1024)} %param.21) | copy-start | bytes 9220
  16.0 8.8 %copy-start.3 = (bf16[2,768,192]{1,2,0:T(8,128)(2,1)S(1)}, bf16[2,768,192]{1,2,0:T(8,128)(2,1)}, u32[]{:S(2)}) copy-start(bf16[2,768,192]{1,2,0:T(8,128)(2,1)} %param.26) | copy-start | bytes 1769476
  17.4 1.8 %collective-permute-start.9 = (bf16[4,32,192]{2,1,0:T(8,128)(2,1)S(1)}, bf16[4,32,192]{2,1,0:T(8,128)(2,1)S(1)}, u32[]{:S(2)}, u32[]{:S(2)}) collective-permute-start(bf16[4,32,192]{2,1,0:T(8,128)(2,1)S(1)} %reshape.451), channel_id=1, source_target_pairs={{0,1},{1,0},{2,3},{3,2},{4,5},{5,4},{6,7},{7,6},{8,9},{9,8},{10,11... | collective-permute-start | bytes 147464 | tf_op jit(solution)/shard_map/ppermute | solution.py:41
  17.6 4.2 %collective-permute-start.7 = (bf16[32,768]{1,0:T(8,128)(2,1)S(1)}, bf16[32,768]{1,0:T(8,128)(2,1)S(1)}, u32[]{:S(2)}, u32[]{:S(2)}) collective-permute-start(bf16[32,768]{1,0:T(8,128)(2,1)S(1)} %add_convert_fusion.1), channel_id=1, source_target_pairs={{0,2},{1,3},{2,0},{3,1},{4,6},{5,7},{6,4},{7,5},{8,10},{9,11},{10,... | collective-permute-start | bytes 147464 | tf_op jit(solution)/shard_map/ppermute | solution.py:41
  19.3 5.0 %collective-permute-start.10 = (bf16[4,32,384]{2,1,0:T(8,128)(2,1)S(1)}, bf16[4,32,384]{2,1,0:T(8,128)(2,1)S(1)}, u32[]{:S(2)}, u32[]{:S(2)}) collective-permute-start(bf16[4,32,384]{2,1,0:T(8,128)(2,1)S(1)} %maximum_select_fusion.1), channel_id=1, source_target_pairs={{0,2},{1,3},{2,0},{3,1},{4,6},{5,7},{6,4},{7,5},{8,10},{9,11},{10,... | collective-permute-start | bytes 294920 | tf_op jit(solution)/shard_map/ppermute | solution.py:41
  21.8 3.6 %collective-permute-start.8 = (f32[32,768]{1,0:T(8,128)S(1)}, f32[32,768]{1,0:T(8,128)S(1)}, u32[]{:S(2)}, u32[]{:S(2)}) collective-permute-start(f32[32,768]{1,0:T(8,128)S(1)} %convert_add_fusion.3), channel_id=1, source_target_pairs={{0,1},{1,0},{2,3},{3,2},{4,5},{5,4},{6,7},{7,6},{8,9},{9,8},{10,11... | collective-permute-start | bytes 294920 | tf_op jit(solution)/shard_map/ppermute | solution.py:41
  25.1 0.7 %copy-start.8 = (f32[768]{0:T(1024)S(1)}, f32[768]{0:T(1024)}, u32[]{:S(2)}) copy-start(f32[768]{0:T(1024)} %param.20) | copy-start | bytes 9220
  25.1 1.0 %copy-start.6 = (bf16[768,192]{0,1:T(8,128)(2,1)S(1)}, bf16[768,192]{0,1:T(8,128)(2,1)}, u32[]{:S(2)}) copy-start(bf16[768,192]{0,1:T(8,128)(2,1)} %param.25) | copy-start | bytes 884740
  26.8 1.0 %copy-start.4 = (bf16[192,768]{1,0:T(8,128)(2,1)S(1)}, bf16[192,768]{1,0:T(8,128)(2,1)}, u32[]{:S(2)}) copy-start(bf16[192,768]{1,0:T(8,128)(2,1)} %param.27) | copy-start | bytes 884740
  28.0 1.4 %collective-permute-start.11 = (bf16[64,768]{1,0:T(8,128)(2,1)S(1)}, bf16[64,768]{1,0:T(8,128)(2,1)S(1)}, u32[]{:S(2)}, u32[]{:S(2)}) collective-permute-start(bf16[64,768]{1,0:T(8,128)(2,1)S(1)} %broadcast_select_fusion.2), channel_id=1, source_target_pairs={{0,1},{1,0},{2,3},{3,2},{4,5},{5,4},{6,7},{7,6},{8,9},{9,8},{10,11... | collective-permute-start | bytes 294920 | tf_op jit(solution)/shard_map/ppermute | solution.py:41
  29.4 4.9 %collective-permute-start.12 = (bf16[64,768]{1,0:T(8,128)(2,1)S(1)}, bf16[64,768]{1,0:T(8,128)(2,1)S(1)}, u32[]{:S(2)}, u32[]{:S(2)}) collective-permute-start(bf16[64,768]{1,0:T(8,128)(2,1)S(1)} %add_convert_fusion), channel_id=1, source_target_pairs={{0,2},{1,3},{2,0},{3,1},{4,6},{5,7},{6,4},{7,5},{8,10},{9,11},{10,... | collective-permute-start | bytes 294920 | tf_op jit(solution)/shard_map/ppermute | solution.py:41
  34.4 1.5 %collective-permute-start.13 = (f32[64,768]{1,0:T(8,128)S(1)}, f32[64,768]{1,0:T(8,128)S(1)}, u32[]{:S(2)}, u32[]{:S(2)}) collective-permute-start(f32[64,768]{1,0:T(8,128)S(1)} %convert_add_fusion.1), channel_id=1, source_target_pairs={{0,1},{1,0},{2,3},{3,2},{4,5},{5,4},{6,7},{7,6},{8,9},{9,8},{10,11... | collective-permute-start | bytes 589832 | tf_op jit(solution)/shard_map/ppermute | solution.py:41
  35.1 1.2 %copy-start.9 = (f32[768]{0:T(1024)S(1)}, f32[768]{0:T(1024)}, u32[]{:S(2)}) copy-start(f32[768]{0:T(1024)} %param.22) | copy-start | bytes 9220
  36.5 1.3 %copy-start.1 = (bf16[768,768]{1,0:T(8,128)(2,1)S(1)}, bf16[768,768]{1,0:T(8,128)(2,1)}, u32[]{:S(2)}) copy-start(bf16[768,768]{1,0:T(8,128)(2,1)} %param.29) | copy-start | bytes 3538948
  38.7 4.1 %collective-permute-start.16 = (bf16[128,192]{1,0:T(8,128)(2,1)S(1)}, bf16[128,192]{1,0:T(8,128)(2,1)S(1)}, u32[]{:S(2)}, u32[]{:S(2)}) collective-permute-start(bf16[128,192]{1,0:T(8,128)(2,1)S(1)} %select_bitcast_fusion), channel_id=1, source_target_pairs={{0,3},{1,2},{2,1},{3,0},{4,7},{5,6},{6,5},{7,4},{8,11},{9,10},{10,... | collective-permute-start | bytes 147464 | tf_op jit(solution)/shard_map/ppermute | solution.py:41
  39.6 3.2 %collective-permute-start.14 = (bf16[128,192]{1,0:T(8,128)(2,1)S(1)}, bf16[128,192]{1,0:T(8,128)(2,1)S(1)}, u32[]{:S(2)}, u32[]{:S(2)}) collective-permute-start(bf16[128,192]{1,0:T(8,128)(2,1)S(1)} %select_bitcast_fusion.2), channel_id=1, source_target_pairs={{0,1},{1,0},{2,3},{3,2},{4,5},{5,4},{6,7},{7,6},{8,9},{9,8},{10,11... | collective-permute-start | bytes 147464 | tf_op jit(solution)/shard_map/ppermute | solution.py:41
  40.1 4.4 %collective-permute-start.15 = (bf16[128,192]{1,0:T(8,128)(2,1)S(1)}, bf16[128,192]{1,0:T(8,128)(2,1)S(1)}, u32[]{:S(2)}, u32[]{:S(2)}) collective-permute-start(bf16[128,192]{1,0:T(8,128)(2,1)S(1)} %select_bitcast_fusion.1), channel_id=1, source_target_pairs={{0,2},{1,3},{2,0},{3,1},{4,6},{5,7},{6,4},{7,5},{8,10},{9,11},{10,... | collective-permute-start | bytes 147464 | tf_op jit(solution)/shard_map/ppermute | solution.py:41

commit v17 on v16

--- a/solution.py
+++ b/solution.py
@@ -106,6 +106,38 @@
     return jnp.where(
         chip == 0, jnp.concatenate([pair, other], axis=2), jnp.concatenate([other, pair], axis=2)
     )
+
+
+def allreduce_with_context(term, context_q):
+    if lax.axis_size("mp") != 4:
+        return mp_allreduce(term), mp_gather_steps(context_q)
+    index = lax.axis_index("mp")
+    core = index % 2
+    chip = index // 2
+    rows_n = term.shape[0]
+    halves = term.reshape(2, rows_n // 2, term.shape[1])
+    keep = jnp.where(core == 0, halves[0], halves[1])
+    send = jnp.where(core == 0, halves[1], halves[0])
+    got = swap(send, mp_pairs(1))
+    chip_sum = (keep.astype(jnp.float32) + got.astype(jnp.float32)).astype(jnp.bfloat16)
+    near = swap(context_q, mp_pairs(1))
+    pair = jnp.where(
+        core == 0,
+        jnp.concatenate([context_q, near], axis=2),
+        jnp.concatenate([near, context_q], axis=2),
+    )
+    cut = chip_sum.size
+    both = swap(jnp.concatenate([chip_sum.reshape(-1), pair.reshape(-1)]), mp_pairs(2))
+    other = both[:cut].reshape(chip_sum.shape)
+    far = both[cut:].reshape(pair.shape)
+    total = chip_sum.astype(jnp.float32) + other.astype(jnp.float32)
+    rest = swap(total, mp_pairs(1))
+    first = jnp.where(core == 0, total, rest)
+    second = jnp.where(core == 0, rest, total)
+    context = jnp.where(
+        chip == 0, jnp.concatenate([pair, far], axis=2), jnp.concatenate([far, pair], axis=2)
+    )
+    return jnp.concatenate([first, second], axis=0), context
 
 
 def pairs_gather(payload, owners_n):
@@ -186,7 +218,8 @@
     term = jnp.dot(
         attend(qkv[0], qkv[1], qkv[2], img_dev), self_out, preferred_element_type=jnp.float32
     )
-    resid_img = begin + mp_allreduce(term.astype(jnp.bfloat16))
+    summed, context_full = allreduce_with_context(term.astype(jnp.bfloat16), context_q)
+    resid_img = begin + summed
     normed = lax.optimization_barrier(layer_norm(resid_img, gain_query))
     query_img = jnp.dot(normed, cross_query, preferred_element_type=jnp.float32).astype(
         jnp.bfloat16
@@ -194,7 +227,7 @@
 
     rows_n = views_n * TOKS
     context = lax.optimization_barrier(
-        layer_norm(mp_gather_steps(context_q).astype(jnp.float32), gain_context)
+        layer_norm(context_full.astype(jnp.float32), gain_context)
     ).reshape(rows_n, width)
     keyval = jnp.einsum(
         "rd,kdc->krc", context, cross_kv, preferred_element_type=jnp.float32

time: 45.9 us -> 47.8 us (1.041)
  waiting for transfers between devices: 14 us -> 16.3 us
  starting transfers between devices: 14.5 us -> 13.9 us
    ppermute x14 -> x13, waiting for transfers between devices: 12.8 us -> 15.1 us  [swap(): return lax.ppermute(values, 'mp', pairs)]
    ppermute x14 -> x13, starting transfers between devices: 9.61 us -> 9.04 us  [swap(): return lax.ppermute(values, 'mp', pairs)]
  transfers between devices with their start and end apart: 17 -> 16, of which waited for: 8 -> 9; matrix products, arithmetic and copies ran while one was open for 22% -> 19% of each run, Pallas kernels for 0% -> 0%
where the time goes in v17:
time: 47.8 us; the launch traced here: 47.4 us
  waiting for transfers between devices  16.3 us (34%)
  starting transfers between devices  13.9 us (29%)
  other arithmetic  6.25 us (13%)
  local copies, waits for them, and re-layouts  5.77 us (12%)
  matrix products  4.3 us (9%)
  between operations  0.79 us (2%)
    ppermute x13, waiting for transfers between devices, swap(): return lax.ppermute(values, 'mp', pairs)  15.1 us
    ppermute x13, starting transfers between devices, swap(): return lax.ppermute(values, 'mp', pairs)  9.04 us
    ppermute x3, starting transfers between devices, pairs_shift(): lax.ppermute(values, 'pairs', [(i, (i + step) % owners_n) for i in range(...  4.9 us
    ppermute x3, waiting for transfers between devices, pairs_shift(): lax.ppermute(values, 'pairs', [(i, (i + step) % owners_n) for i in range(...  1.25 us
    convert_element_type x4, other arithmetic, layer_norm(): return (center * lax.rsqrt(spread + EPSILON) * gain).astype(jnp.bfloat16)  1.15 us
    dot_general x1, matrix products, per_device(): jnp.dot(normed, mlp_up, preferred_element_type=jnp.float32)  1.06 us
  transfers between devices with their start and end apart: 16, of which 9 were waited for; matrix products, arithmetic and copies ran while one was open for 19% of the time, Pallas kernels for 0%

profile of v17, /device:TPU:0, one launch (start us, length us, event | category | flops | bytes accessed | tf_op | source)
XLA Modules:
  0.0 47.4 jit_solution(1978011873376357209)
XLA Ops:
  0.0 0.5 collective-permute-start.5
  0.5 2.6 %collective-permute-start.4 = (bf16[2,32,192]{2,1,0:T(8,128)(2,1)}, bf16[2,32,192]{2,1,0:T(8,128)(2,1)S(1)}, u32[]{:S(2)}, u32[]{:S(2)}) collective-permute-start(bf16[2,32,192]{2,1,0:T(8,128)(2,1)} %bitcast.80), channel_id=1, source_target_pairs={{0,2},{1,3},{2,0},{3,1},{4,6},{5,7},{6,4},{7,5},{8,10},{9,11},{10,... | collective-permute-start | bytes 73736 | tf_op jit(solution)/shard_map/ppermute | solution.py:41
  3.1 0.9 %reshape.550 = f32[12288]{0:T(1024)S(1)} reshape(bf16[64,192]{1,0:T(8,128)(2,1)} %param.16) | data formatting | bytes 73728 | tf_op jit(solution)/shard_map/reshape | solution.py:185
  4.0 0.8 %reshape.472 = f32[128]{0:T(128)S(1)} reshape(f32[2,64]{1,0:T(2,128)} %param.18) | data formatting | bytes 1024 | tf_op jit(solution)/shard_map/reshape | solution.py:187
  4.7 0.7 %convert_element_type.167 = f32[2,2]{1,0:T(2,128)S(1)} convert(s32[2,2]{1,0:T(2,128)} %param.17) | non-fusion elementwise | flops 4 | bytes 32 | tf_op jit(solution)/shard_map/convert_element_type | solution.py:186
  5.6 3.8 %collective-permute-start.2 = (f32[12420]{0:T(1024)S(1)}, f32[12420]{0:T(1024)S(1)}, u32[]{:S(2)}, u32[]{:S(2)}) collective-permute-start(f32[12420]{0:T(1024)S(1)} %concatenate.45), channel_id=1, source_target_pairs={{0,12},{4,0},{8,4},{12,8},{1,13},{5,1},{9,5},{13,9},{2,14},{6,2},{... | collective-permute-start | bytes 149048 | tf_op jit(solution)/shard_map/ppermute | solution.py:37
  9.5 1.1 %collective-permute-start = (f32[12420]{0:T(1024)S(1)}, f32[12420]{0:T(1024)S(1)}, u32[]{:S(2)}, u32[]{:S(2)}) collective-permute-start(f32[12420]{0:T(1024)S(1)} %concatenate.45), channel_id=1, source_target_pairs={{0,4},{4,8},{8,12},{12,0},{1,5},{5,9},{9,13},{13,1},{2,6},{6,10},{... | collective-permute-start | bytes 149048 | tf_op jit(solution)/shard_map/ppermute | solution.py:37
  10.6 0.8 %select_select_fusion.3 = (bf16[2,32,192]{2,1,0:T(8,128)(2,1)S(1)}, bf16[2,32,192]{2,1,0:T(8,128)(2,1)S(1)}, bf16[2,32,192]{2,1,0:T(8,128)(2,1)S(1)}, bf16[2,32,192]{2,1,0:T(8,128)(2,1)S(1)}) fusion(bf16[2,32,192]{2,1,0:T(8,128)(2,1)S(1)} %collective-permute-done.3, bf16[2,32,192]{2,1,0:T(8,128)(2,1)S(1)} %collective-permute-done.4, ...), kind=kLoop, calls=%fused_computation.108 | loop fusion | flops 147456 | bytes 196620 | tf_op jit(solution)/shard_map/jit(_where)/select_n | solution.py:91
  11.4 0.2 convert_reduce_fusion.1
  11.6 0.2 fusion.26
  11.8 0.8 %fusion.28 = bf16[64,768]{1,0:T(8,128)(2,1)S(1)} fusion(bf16[64,768]{1,0:T(8,128)(2,1)S(1)} %get-tuple-element.28, f32[768]{0:T(1024)} %param.19, f32[64]{0:T(128)S(1)} %add_rsqrt_fusion.3, f32[64]{0:T(128)S(1)} %broadcast_multiply_fusion.3), kind=kLoop, calls=%fused_computation.59 | loop fusion | flops 245760 | bytes 200192 | tf_op jit(solution)/shard_map/convert_element_type | solution.py:16
  12.6 0.4 fusion.6
  13.2 0.2 fusion.70
  13.4 0.1 convolution_multiply_fusion.1
  13.6 0.2 fusion.8
  14.0 0.2 convolution_convert_fusion.6
  14.4 1.2 %collective-permute-done.1 = f32[12420]{0:T(1024)S(1)} collective-permute-done((f32[12420]{0:T(1024)S(1)}, f32[12420]{0:T(1024)S(1)}, u32[]{:S(2)}, u32[]{:S(2)}) %collective-permute-start.1) | collective-permute-done | bytes 49712 | tf_op jit(solution)/shard_map/ppermute | solution.py:37
  15.7 0.2 pad_maximum_fusion
  16.5 0.1 add_reduce_fusion
  16.6 0.2 select_reduce_fusion
  16.9 0.2 convolution_convert_fusion.1
  17.2 0.1 reshape.480
  17.6 1.1 %collective-permute-done.7 = bf16[4,32,192]{2,1,0:T(8,128)(2,1)S(1)} collective-permute-done((bf16[4,32,192]{2,1,0:T(8,128)(2,1)S(1)}, bf16[4,32,192]{2,1,0:T(8,128)(2,1)S(1)}, u32[]{:S(2)}, u32[]{:S(2)}) %collective-permute-start.7) | collective-permute-done | bytes 49184 | tf_op jit(solution)/shard_map/ppermute | solution.py:41
  18.7 0.1 maximum_select_fusion.1
  18.9 1.6 %collective-permute-start.8 = (bf16[73728]{0:T(1024)(128)(2,1)S(1)}, bf16[73728]{0:T(1024)(128)(2,1)S(1)}, u32[]{:S(2)}, u32[]{:S(2)}) collective-permute-start(bf16[73728]{0:T(1024)(128)(2,1)S(1)} %pad_maximum_fusion.2), channel_id=1, source_target_pairs={{0,2},{1,3},{2,0},{3,1},{4,6},{5,7},{6,4},{7,5},{8,10},{9,11},{10,... | collective-permute-start | bytes 442376 | tf_op jit(solution)/shard_map/ppermute | solution.py:41
  20.4 0.1 fusion.45
  20.6 4.3 %collective-permute-done.8 = bf16[73728]{0:T(1024)(128)(2,1)S(1)} collective-permute-done((bf16[73728]{0:T(1024)(128)(2,1)S(1)}, bf16[73728]{0:T(1024)(128)(2,1)S(1)}, u32[]{:S(2)}, u32[]{:S(2)}) %collective-permute-start.8) | collective-permute-done | bytes 147488 | tf_op jit(solution)/shard_map/ppermute | solution.py:41
  25.0 0.1 convert_reduce_fusion
  25.1 0.2 fusion.11
  25.4 0.1 fusion.13
  25.5 0.3 fusion.76
  26.0 0.1 reshape.596
  26.1 0.1 reshape.595
  26.2 1.0 %collective-permute-done.9 = f32[32,768]{1,0:T(8,128)S(1)} collective-permute-done((f32[32,768]{1,0:T(8,128)S(1)}, f32[32,768]{1,0:T(8,128)S(1)}, u32[]{:S(2)}, u32[]{:S(2)}) %collective-permute-start.9) | collective-permute-done | bytes 98336 | tf_op jit(solution)/shard_map/ppermute | solution.py:41
  27.2 0.1 pad_maximum_fusion.1
  27.4 0.2 multiply_reduce_fusion.1
  27.7 0.2 convolution_convert_fusion.8
  28.0 0.1 reshape_reshape.3
  28.1 0.2 convolution_convert_fusion
  28.3 0.1 reshape_reshape_reshape.3
  28.5 0.2 convolution_multiply_fusion
  28.8 0.3 fusion.5
  29.1 0.1 reshape.482
  29.3 0.1 copy-done.4
  29.4 0.2 convolution_convert_fusion.3
  29.6 0.2 collective-permute-start.10
  30.0 1.0 %collective-permute-done.10 = bf16[64,768]{1,0:T(8,128)(2,1)S(1)} collective-permute-done((bf16[64,768]{1,0:T(8,128)(2,1)S(1)}, bf16[64,768]{1,0:T(8,128)(2,1)S(1)}, u32[]{:S(2)}, u32[]{:S(2)}) %collective-permute-start.10) | collective-permute-done | bytes 98336 | tf_op jit(solution)/shard_map/ppermute | solution.py:41
  31.1 1.6 %collective-permute-start.11 = (bf16[64,768]{1,0:T(8,128)(2,1)S(1)}, bf16[64,768]{1,0:T(8,128)(2,1)S(1)}, u32[]{:S(2)}, u32[]{:S(2)}) collective-permute-start(bf16[64,768]{1,0:T(8,128)(2,1)S(1)} %add_convert_fusion), channel_id=1, source_target_pairs={{0,2},{1,3},{2,0},{3,1},{4,6},{5,7},{6,4},{7,5},{8,10},{9,11},{10,... | collective-permute-start | bytes 294920 | tf_op jit(solution)/shard_map/ppermute | solution.py:41
  32.6 3.4 %collective-permute-done.11 = bf16[64,768]{1,0:T(8,128)(2,1)S(1)} collective-permute-done((bf16[64,768]{1,0:T(8,128)(2,1)S(1)}, bf16[64,768]{1,0:T(8,128)(2,1)S(1)}, u32[]{:S(2)}, u32[]{:S(2)}) %collective-permute-start.11) | collective-permute-done | bytes 98336 | tf_op jit(solution)/shard_map/ppermute | solution.py:41
  36.2 0.6 %gather_fusion = f32[4,32,768]{2,1,0:T(8,128)S(1)} fusion(f32[2,32,768]{2,1,0:T(8,128)S(1)} %convert_add_fusion.2, s32[1024]{0:T(1024)S(1)} %pad_clamp_fusion), kind=kCustom, calls=%fused_computation | custom fusion | bytes 786448 | tf_op jit(solution)/shard_map/jit(_take)/gather | solution.py:237
  36.8 0.7 %collective-permute-done.12 = f32[64,768]{1,0:T(8,128)S(1)} collective-permute-done((f32[64,768]{1,0:T(8,128)S(1)}, f32[64,768]{1,0:T(8,128)S(1)}, u32[]{:S(2)}, u32[]{:S(2)}) %collective-permute-start.12) | collective-permute-done | bytes 196640 | tf_op jit(solution)/shard_map/ppermute | solution.py:41
  37.5 0.2 fusion.67
  37.8 0.2 multiply_reduce_fusion
  38.0 0.1 multiply_convert_fusion
  38.1 1.1 %fusion.16 = bf16[128,768]{1,0:T(8,128)(2,1)S(1)} fusion(bf16[128,768]{1,0:T(8,128)(2,1)S(1)} %multiply_convert_fusion, bf16[768,768]{1,0:T(8,128)(2,1)S(1)} %copy-done), kind=kOutput, calls=%fused_computation.31 | convolution fusion | flops 157384704 | bytes 1572864 | tf_op jit(solution)/shard_map/dot_general | solution.py:246
  39.2 0.2 copy-done.1
  39.4 0.3 convolution_convert_fusion.2
  39.7 0.2 copy.71
  40.3 1.3 %collective-permute-start.15 = (bf16[128,192]{1,0:T(8,128)(2,1)S(1)}, bf16[128,192]{1,0:T(8,128)(2,1)S(1)}, u32[]{:S(2)}, u32[]{:S(2)}) collective-permute-start(bf16[128,192]{1,0:T(8,128)(2,1)S(1)} %select_bitcast_fusion), channel_id=1, source_target_pairs={{0,3},{1,2},{2,1},{3,0},{4,7},{5,6},{6,5},{7,4},{8,11},{9,10},{10,... | collective-permute-start | bytes 147464 | tf_op jit(solution)/shard_map/ppermute | solution.py:41
  41.6 0.4 collective-permute-start.13
  42.0 0.6 %collective-permute-start.14 = (bf16[128,192]{1,0:T(8,128)(2,1)S(1)}, bf16[128,192]{1,0:T(8,128)(2,1)S(1)}, u32[]{:S(2)}, u32[]{:S(2)}) collective-permute-start(bf16[128,192]{1,0:T(8,128)(2,1)S(1)} %select_bitcast_fusion.1), channel_id=1, source_target_pairs={{0,2},{1,3},{2,0},{3,1},{4,6},{5,7},{6,4},{7,5},{8,10},{9,11},{10,... | collective-permute-start | bytes 147464 | tf_op jit(solution)/shard_map/ppermute | solution.py:41
  42.8 1.7 %collective-permute-done.15 = bf16[128,192]{1,0:T(8,128)(2,1)S(1)} collective-permute-done((bf16[128,192]{1,0:T(8,128)(2,1)S(1)}, bf16[128,192]{1,0:T(8,128)(2,1)S(1)}, u32[]{:S(2)}, u32[]{:S(2)}) %collective-permute-start.15) | collective-permute-done | bytes 49184 | tf_op jit(solution)/shard_map/ppermute | solution.py:41
  44.4 1.9 %collective-permute-done.14 = bf16[128,192]{1,0:T(8,128)(2,1)S(1)} collective-permute-done((bf16[128,192]{1,0:T(8,128)(2,1)S(1)}, bf16[128,192]{1,0:T(8,128)(2,1)S(1)}, u32[]{:S(2)}, u32[]{:S(2)}) %collective-permute-start.14) | collective-permute-done | bytes 49184 | tf_op jit(solution)/shard_map/ppermute | solution.py:41
  46.8 0.6 %pad_maximum_fusion.4 = bf16[64,192]{1,0:T(8,128)(2,1)} fusion(bf16[32,192]{1,0:T(8,128)(2,1)S(1)} %divide_convert_fusion.4, bf16[32,192]{1,0:T(8,128)(2,1)S(1)} %divide_convert_fusion.5), kind=kLoop, calls=%fused_computation.102 | loop fusion | flops 49152 | bytes 49152 | tf_op jit(solution)/shard_map/concatenate | solution.py:264
  (107 shorter events, 3.8 us)
Async XLA Ops:
  0.0 38.1 %copy-start = (bf16[768,768]{1,0:T(8,128)(2,1)S(1)}, bf16[768,768]{1,0:T(8,128)(2,1)}, u32[]{:S(2)}) copy-start(bf16[768,768]{1,0:T(8,128)(2,1)} %param.28) | copy-start | bytes 3538948
  0.0 12.6 %copy-start.2 = (bf16[3,768,192]{1,2,0:T(8,128)(2,1)S(1)}, bf16[3,768,192]{1,2,0:T(8,128)(2,1)}, u32[]{:S(2)}) copy-start(bf16[3,768,192]{1,2,0:T(8,128)(2,1)} %param.23) | copy-start | bytes 2654212
  0.0 9.5 %collective-permute-start.5 = (bf16[2,32,192]{2,1,0:T(8,128)(2,1)}, bf16[2,32,192]{2,1,0:T(8,128)(2,1)S(1)}, u32[]{:S(2)}, u32[]{:S(2)}) collective-permute-start(bf16[2,32,192]{2,1,0:T(8,128)(2,1)} %bitcast.79), channel_id=1, source_target_pairs={{0,1},{1,0},{2,3},{3,2},{4,5},{5,4},{6,7},{7,6},{8,9},{9,8},{10,11... | collective-permute-start | bytes 73736 | tf_op jit(solution)/shard_map/ppermute | solution.py:41
  0.5 10.1 %collective-permute-start.4 = (bf16[2,32,192]{2,1,0:T(8,128)(2,1)}, bf16[2,32,192]{2,1,0:T(8,128)(2,1)S(1)}, u32[]{:S(2)}, u32[]{:S(2)}) collective-permute-start(bf16[2,32,192]{2,1,0:T(8,128)(2,1)} %bitcast.80), channel_id=1, source_target_pairs={{0,2},{1,3},{2,0},{3,1},{4,6},{5,7},{6,4},{7,5},{8,10},{9,11},{10,... | collective-permute-start | bytes 73736 | tf_op jit(solution)/shard_map/ppermute | solution.py:41
  3.0 7.6 %collective-permute-start.3 = (bf16[2,32,192]{2,1,0:T(8,128)(2,1)}, bf16[2,32,192]{2,1,0:T(8,128)(2,1)S(1)}, u32[]{:S(2)}, u32[]{:S(2)}) collective-permute-start(bf16[2,32,192]{2,1,0:T(8,128)(2,1)} %bitcast.81), channel_id=1, source_target_pairs={{0,3},{1,2},{2,1},{3,0},{4,7},{5,6},{6,5},{7,4},{8,11},{9,10},{10,... | collective-permute-start | bytes 73736 | tf_op jit(solution)/shard_map/ppermute | solution.py:41
  5.6 8.7 %collective-permute-start.2 = (f32[12420]{0:T(1024)S(1)}, f32[12420]{0:T(1024)S(1)}, u32[]{:S(2)}, u32[]{:S(2)}) collective-permute-start(f32[12420]{0:T(1024)S(1)} %concatenate.45), channel_id=1, source_target_pairs={{0,12},{4,0},{8,4},{12,8},{1,13},{5,1},{9,5},{13,9},{2,14},{6,2},{... | collective-permute-start | bytes 149048 | tf_op jit(solution)/shard_map/ppermute | solution.py:37
  9.4 6.2 %collective-permute-start.1 = (f32[12420]{0:T(1024)S(1)}, f32[12420]{0:T(1024)S(1)}, u32[]{:S(2)}, u32[]{:S(2)}) collective-permute-start(f32[12420]{0:T(1024)S(1)} %concatenate.45), channel_id=1, source_target_pairs={{0,8},{4,12},{8,0},{12,4},{1,9},{5,13},{9,1},{13,5},{2,10},{6,14},... | collective-permute-start | bytes 149048 | tf_op jit(solution)/shard_map/ppermute | solution.py:37
  9.5 6.1 %collective-permute-start = (f32[12420]{0:T(1024)S(1)}, f32[12420]{0:T(1024)S(1)}, u32[]{:S(2)}, u32[]{:S(2)}) collective-permute-start(f32[12420]{0:T(1024)S(1)} %concatenate.45), channel_id=1, source_target_pairs={{0,4},{4,8},{8,12},{12,0},{1,5},{5,9},{9,13},{13,1},{2,6},{6,10},{... | collective-permute-start | bytes 149048 | tf_op jit(solution)/shard_map/ppermute | solution.py:37
  12.6 1.4 %copy-start.5 = (bf16[192,768]{1,0:T(8,128)(2,1)S(1)}, bf16[192,768]{1,0:T(8,128)(2,1)}, u32[]{:S(2)}) copy-start(bf16[192,768]{1,0:T(8,128)(2,1)} %param.24) | copy-start | bytes 884740
  14.2 3.2 %collective-permute-start.6 = (bf16[32,768]{1,0:T(8,128)(2,1)S(1)}, bf16[32,768]{1,0:T(8,128)(2,1)S(1)}, u32[]{:S(2)}, u32[]{:S(2)}) collective-permute-start(bf16[32,768]{1,0:T(8,128)(2,1)S(1)} %broadcast_select_fusion.5), channel_id=1, source_target_pairs={{0,1},{1,0},{2,3},{3,2},{4,5},{5,4},{6,7},{7,6},{8,9},{9,8},{10,11... | collective-permute-start | bytes 147464 | tf_op jit(solution)/shard_map/ppermute | solution.py:41
  17.4 1.3 %collective-permute-start.7 = (bf16[4,32,192]{2,1,0:T(8,128)(2,1)S(1)}, bf16[4,32,192]{2,1,0:T(8,128)(2,1)S(1)}, u32[]{:S(2)}, u32[]{:S(2)}) collective-permute-start(bf16[4,32,192]{2,1,0:T(8,128)(2,1)S(1)} %reshape.480), channel_id=1, source_target_pairs={{0,1},{1,0},{2,3},{3,2},{4,5},{5,4},{6,7},{7,6},{8,9},{9,8},{10,11... | collective-permute-start | bytes 147464 | tf_op jit(solution)/shard_map/ppermute | solution.py:41
  17.5 7.9 %copy-start.7 = (f32[768]{0:T(1024)S(1)}, f32[768]{0:T(1024)}, u32[]{:S(2)}) copy-start(f32[768]{0:T(1024)} %param.21) | copy-start | bytes 9220
  18.8 6.7 %copy-start.3 = (bf16[2,768,192]{1,2,0:T(8,128)(2,1)S(1)}, bf16[2,768,192]{1,2,0:T(8,128)(2,1)}, u32[]{:S(2)}) copy-start(bf16[2,768,192]{1,2,0:T(8,128)(2,1)} %param.26) | copy-start | bytes 1769476
  18.9 6.0 %collective-permute-start.8 = (bf16[73728]{0:T(1024)(128)(2,1)S(1)}, bf16[73728]{0:T(1024)(128)(2,1)S(1)}, u32[]{:S(2)}, u32[]{:S(2)}) collective-permute-start(bf16[73728]{0:T(1024)(128)(2,1)S(1)} %pad_maximum_fusion.2), channel_id=1, source_target_pairs={{0,2},{1,3},{2,0},{3,1},{4,6},{5,7},{6,4},{7,5},{8,10},{9,11},{10,... | collective-permute-start | bytes 442376 | tf_op jit(solution)/shard_map/ppermute | solution.py:41
  25.8 1.8 %copy-start.8 = (f32[768]{0:T(1024)S(1)}, f32[768]{0:T(1024)}, u32[]{:S(2)}) copy-start(f32[768]{0:T(1024)} %param.20) | copy-start | bytes 9220
  25.9 1.9 %copy-start.6 = (bf16[768,192]{0,1:T(8,128)(2,1)S(1)}, bf16[768,192]{0,1:T(8,128)(2,1)}, u32[]{:S(2)}) copy-start(bf16[768,192]{0,1:T(8,128)(2,1)} %param.25) | copy-start | bytes 884740
  25.9 1.4 %collective-permute-start.9 = (f32[32,768]{1,0:T(8,128)S(1)}, f32[32,768]{1,0:T(8,128)S(1)}, u32[]{:S(2)}, u32[]{:S(2)}) collective-permute-start(f32[32,768]{1,0:T(8,128)S(1)} %convert_add_fusion.3), channel_id=1, source_target_pairs={{0,1},{1,0},{2,3},{3,2},{4,5},{5,4},{6,7},{7,6},{8,9},{9,8},{10,11... | collective-permute-start | bytes 294920 | tf_op jit(solution)/shard_map/ppermute | solution.py:41
  28.4 1.0 %copy-start.4 = (bf16[192,768]{1,0:T(8,128)(2,1)S(1)}, bf16[192,768]{1,0:T(8,128)(2,1)}, u32[]{:S(2)}) copy-start(bf16[192,768]{1,0:T(8,128)(2,1)} %param.27) | copy-start | bytes 884740
  29.6 1.4 %collective-permute-start.10 = (bf16[64,768]{1,0:T(8,128)(2,1)S(1)}, bf16[64,768]{1,0:T(8,128)(2,1)S(1)}, u32[]{:S(2)}, u32[]{:S(2)}) collective-permute-start(bf16[64,768]{1,0:T(8,128)(2,1)S(1)} %broadcast_select_fusion.2), channel_id=1, source_target_pairs={{0,1},{1,0},{2,3},{3,2},{4,5},{5,4},{6,7},{7,6},{8,9},{9,8},{10,11... | collective-permute-start | bytes 294920 | tf_op jit(solution)/shard_map/ppermute | solution.py:41
  31.1 4.9 %collective-permute-start.11 = (bf16[64,768]{1,0:T(8,128)(2,1)S(1)}, bf16[64,768]{1,0:T(8,128)(2,1)S(1)}, u32[]{:S(2)}, u32[]{:S(2)}) collective-permute-start(bf16[64,768]{1,0:T(8,128)(2,1)S(1)} %add_convert_fusion), channel_id=1, source_target_pairs={{0,2},{1,3},{2,0},{3,1},{4,6},{5,7},{6,4},{7,5},{8,10},{9,11},{10,... | collective-permute-start | bytes 294920 | tf_op jit(solution)/shard_map/ppermute | solution.py:41
  36.0 1.5 %collective-permute-start.12 = (f32[64,768]{1,0:T(8,128)S(1)}, f32[64,768]{1,0:T(8,128)S(1)}, u32[]{:S(2)}, u32[]{:S(2)}) collective-permute-start(f32[64,768]{1,0:T(8,128)S(1)} %convert_add_fusion.1), channel_id=1, source_target_pairs={{0,1},{1,0},{2,3},{3,2},{4,5},{5,4},{6,7},{7,6},{8,9},{9,8},{10,11... | collective-permute-start | bytes 589832 | tf_op jit(solution)/shard_map/ppermute | solution.py:41
  36.8 1.2 %copy-start.9 = (f32[768]{0:T(1024)S(1)}, f32[768]{0:T(1024)}, u32[]{:S(2)}) copy-start(f32[768]{0:T(1024)} %param.22) | copy-start | bytes 9220
  38.1 1.3 %copy-start.1 = (bf16[768,768]{1,0:T(8,128)(2,1)S(1)}, bf16[768,768]{1,0:T(8,128)(2,1)}, u32[]{:S(2)}) copy-start(bf16[768,768]{1,0:T(8,128)(2,1)} %param.29) | copy-start | bytes 3538948
  40.3 4.1 %collective-permute-start.15 = (bf16[128,192]{1,0:T(8,128)(2,1)S(1)}, bf16[128,192]{1,0:T(8,128)(2,1)S(1)}, u32[]{:S(2)}, u32[]{:S(2)}) collective-permute-start(bf16[128,192]{1,0:T(8,128)(2,1)S(1)} %select_bitcast_fusion), channel_id=1, source_target_pairs={{0,3},{1,2},{2,1},{3,0},{4,7},{5,6},{6,5},{7,4},{8,11},{9,10},{10,... | collective-permute-start | bytes 147464 | tf_op jit(solution)/shard_map/ppermute | solution.py:41
  41.6 2.8 %collective-permute-start.13 = (bf16[128,192]{1,0:T(8,128)(2,1)S(1)}, bf16[128,192]{1,0:T(8,128)(2,1)S(1)}, u32[]{:S(2)}, u32[]{:S(2)}) collective-permute-start(bf16[128,192]{1,0:T(8,128)(2,1)S(1)} %select_bitcast_fusion.2), channel_id=1, source_target_pairs={{0,1},{1,0},{2,3},{3,2},{4,5},{5,4},{6,7},{7,6},{8,9},{9,8},{10,11... | collective-permute-start | bytes 147464 | tf_op jit(solution)/shard_map/ppermute | solution.py:41
  42.0 4.3 %collective-permute-start.14 = (bf16[128,192]{1,0:T(8,128)(2,1)S(1)}, bf16[128,192]{1,0:T(8,128)(2,1)S(1)}, u32[]{:S(2)}, u32[]{:S(2)}) collective-permute-start(bf16[128,192]{1,0:T(8,128)(2,1)S(1)} %select_bitcast_fusion.1), channel_id=1, source_target_pairs={{0,2},{1,3},{2,0},{3,1},{4,6},{5,7},{6,4},{7,5},{8,10},{9,11},{10,... | collective-permute-start | bytes 147464 | tf_op jit(solution)/shard_map/ppermute | solution.py:41

commit v18 on v16

--- a/solution.py
+++ b/solution.py
@@ -210,7 +210,8 @@
     resid = resid + mp_allreduce(term.astype(jnp.bfloat16))
     normed = lax.optimization_barrier(layer_norm(resid, gain_mlp))
     hidden = jax.nn.gelu(
-        jnp.dot(normed, mlp_up, preferred_element_type=jnp.float32), approximate=False
+        lax.optimization_barrier(jnp.dot(normed, mlp_up, preferred_element_type=jnp.float32)),
+        approximate=False,
     )
     hidden = lax.optimization_barrier(hidden.astype(jnp.bfloat16))
     term = jnp.dot(hidden, mlp_down, preferred_element_type=jnp.float32)

time: 45.9 us -> 45.9 us (level)
  other arithmetic: 6.23 us -> 7.08 us
  matrix products: 4.31 us -> 3.57 us
    convert_element_type x0 -> x1, other arithmetic: none -> 0.84 us  [per_device(): hidden = lax.optimization_barrier(hidden.astype(jnp.bfloat16))]
    dot_general x1, matrix products: 1.06 us -> 0.33 us  [per_device(): jnp.dot(normed, mlp_up, preferred_element_type=jnp.float32)]
where the time goes in v18:
time: 45.9 us; the launch traced here: 45.5 us
  starting transfers between devices  14.5 us (32%)
  waiting for transfers between devices  14 us (31%)
  other arithmetic  7.08 us (15%)
  local copies, waits for them, and re-layouts  5.61 us (12%)
  matrix products  3.57 us (8%)
  between operations  0.74 us (2%)
    ppermute x14, waiting for transfers between devices, swap(): return lax.ppermute(values, 'mp', pairs)  12.8 us
    ppermute x14, starting transfers between devices, swap(): return lax.ppermute(values, 'mp', pairs)  9.61 us
    ppermute x3, starting transfers between devices, pairs_shift(): lax.ppermute(values, 'pairs', [(i, (i + step) % owners_n) for i in range(...  4.9 us
    ppermute x3, waiting for transfers between devices, pairs_shift(): lax.ppermute(values, 'pairs', [(i, (i + step) % owners_n) for i in range(...  1.25 us
    convert_element_type x4, other arithmetic, layer_norm(): return (center * lax.rsqrt(spread + EPSILON) * gain).astype(jnp.bfloat16)  1.15 us
  transfers between devices with their start and end apart: 17, of which 8 were waited for; matrix products, arithmetic and copies ran while one was open for 22% of the time, Pallas kernels for 0%

profile of v18, /device:TPU:0, one launch (start us, length us, event | category | flops | bytes accessed | tf_op | source)
XLA Modules:
  0.0 45.5 jit_solution(15105124621857970721)
XLA Ops:
  0.0 0.5 collective-permute-start.5
  0.5 2.6 %collective-permute-start.4 = (bf16[2,32,192]{2,1,0:T(8,128)(2,1)}, bf16[2,32,192]{2,1,0:T(8,128)(2,1)S(1)}, u32[]{:S(2)}, u32[]{:S(2)}) collective-permute-start(bf16[2,32,192]{2,1,0:T(8,128)(2,1)} %bitcast.80), channel_id=1, source_target_pairs={{0,2},{1,3},{2,0},{3,1},{4,6},{5,7},{6,4},{7,5},{8,10},{9,11},{10,... | collective-permute-start | bytes 73736 | tf_op jit(solution)/shard_map/ppermute | solution.py:41
  3.1 0.9 %reshape.521 = f32[12288]{0:T(1024)S(1)} reshape(bf16[64,192]{1,0:T(8,128)(2,1)} %param.16) | data formatting | bytes 73728 | tf_op jit(solution)/shard_map/reshape | solution.py:153
  4.0 0.8 %reshape.444 = f32[128]{0:T(128)S(1)} reshape(f32[2,64]{1,0:T(2,128)} %param.18) | data formatting | bytes 1024 | tf_op jit(solution)/shard_map/reshape | solution.py:155
  4.7 0.7 %convert_element_type.164 = f32[2,2]{1,0:T(2,128)S(1)} convert(s32[2,2]{1,0:T(2,128)} %param.17) | non-fusion elementwise | flops 4 | bytes 32 | tf_op jit(solution)/shard_map/convert_element_type | solution.py:154
  5.6 3.8 %collective-permute-start.2 = (f32[12420]{0:T(1024)S(1)}, f32[12420]{0:T(1024)S(1)}, u32[]{:S(2)}, u32[]{:S(2)}) collective-permute-start(f32[12420]{0:T(1024)S(1)} %concatenate.42), channel_id=1, source_target_pairs={{0,12},{4,0},{8,4},{12,8},{1,13},{5,1},{9,5},{13,9},{2,14},{6,2},{... | collective-permute-start | bytes 149048 | tf_op jit(solution)/shard_map/ppermute | solution.py:37
  9.5 1.1 %collective-permute-start = (f32[12420]{0:T(1024)S(1)}, f32[12420]{0:T(1024)S(1)}, u32[]{:S(2)}, u32[]{:S(2)}) collective-permute-start(f32[12420]{0:T(1024)S(1)} %concatenate.42), channel_id=1, source_target_pairs={{0,4},{4,8},{8,12},{12,0},{1,5},{5,9},{9,13},{13,1},{2,6},{6,10},{... | collective-permute-start | bytes 149048 | tf_op jit(solution)/shard_map/ppermute | solution.py:37
  10.6 0.8 %select_select_fusion.3 = (bf16[2,32,192]{2,1,0:T(8,128)(2,1)S(1)}, bf16[2,32,192]{2,1,0:T(8,128)(2,1)S(1)}, bf16[2,32,192]{2,1,0:T(8,128)(2,1)S(1)}, bf16[2,32,192]{2,1,0:T(8,128)(2,1)S(1)}) fusion(bf16[2,32,192]{2,1,0:T(8,128)(2,1)S(1)} %collective-permute-done.3, bf16[2,32,192]{2,1,0:T(8,128)(2,1)S(1)} %collective-permute-done.4, ...), kind=kLoop, calls=%fused_computation.106 | loop fusion | flops 147456 | bytes 196620 | tf_op jit(solution)/shard_map/jit(_where)/select_n | solution.py:91
  11.4 0.2 convert_reduce_fusion.1
  11.6 0.2 fusion.26
  11.8 0.8 %fusion.28 = bf16[64,768]{1,0:T(8,128)(2,1)S(1)} fusion(bf16[64,768]{1,0:T(8,128)(2,1)S(1)} %get-tuple-element.28, f32[768]{0:T(1024)} %param.19, f32[64]{0:T(128)S(1)} %add_rsqrt_fusion.3, f32[64]{0:T(128)S(1)} %broadcast_multiply_fusion.3), kind=kLoop, calls=%fused_computation.59 | loop fusion | flops 245760 | bytes 200192 | tf_op jit(solution)/shard_map/convert_element_type | solution.py:16
  12.6 0.4 fusion.6
  13.2 0.2 fusion.70
  13.4 0.1 convolution_multiply_fusion.1
  13.6 0.2 fusion.8
  14.0 0.2 convolution_convert_fusion.6
  14.4 1.2 %collective-permute-done.1 = f32[12420]{0:T(1024)S(1)} collective-permute-done((f32[12420]{0:T(1024)S(1)}, f32[12420]{0:T(1024)S(1)}, u32[]{:S(2)}, u32[]{:S(2)}) %collective-permute-start.1) | collective-permute-done | bytes 49712 | tf_op jit(solution)/shard_map/ppermute | solution.py:37
  15.8 0.2 pad_maximum_fusion
  16.6 0.1 add_reduce_fusion
  16.7 0.2 select_reduce_fusion
  17.0 0.2 convolution_convert_fusion.1
  17.3 0.1 reshape.451
  17.4 0.1 fusion.45
  17.6 1.6 %collective-permute-start.7 = (bf16[32,768]{1,0:T(8,128)(2,1)S(1)}, bf16[32,768]{1,0:T(8,128)(2,1)S(1)}, u32[]{:S(2)}, u32[]{:S(2)}) collective-permute-start(bf16[32,768]{1,0:T(8,128)(2,1)S(1)} %add_convert_fusion.1), channel_id=1, source_target_pairs={{0,2},{1,3},{2,0},{3,1},{4,6},{5,7},{6,4},{7,5},{8,10},{9,11},{10,... | collective-permute-start | bytes 147464 | tf_op jit(solution)/shard_map/ppermute | solution.py:41
  19.2 0.1 maximum_select_fusion.1
  19.3 1.1 %collective-permute-start.10 = (bf16[4,32,384]{2,1,0:T(8,128)(2,1)S(1)}, bf16[4,32,384]{2,1,0:T(8,128)(2,1)S(1)}, u32[]{:S(2)}, u32[]{:S(2)}) collective-permute-start(bf16[4,32,384]{2,1,0:T(8,128)(2,1)S(1)} %maximum_select_fusion.1), channel_id=1, source_target_pairs={{0,2},{1,3},{2,0},{3,1},{4,6},{5,7},{6,4},{7,5},{8,10},{9,11},{10,... | collective-permute-start | bytes 294920 | tf_op jit(solution)/shard_map/ppermute | solution.py:41
  20.4 1.5 %collective-permute-done.7 = bf16[32,768]{1,0:T(8,128)(2,1)S(1)} collective-permute-done((bf16[32,768]{1,0:T(8,128)(2,1)S(1)}, bf16[32,768]{1,0:T(8,128)(2,1)S(1)}, u32[]{:S(2)}, u32[]{:S(2)}) %collective-permute-start.7) | collective-permute-done | bytes 49184 | tf_op jit(solution)/shard_map/ppermute | solution.py:41
  21.9 2.4 %collective-permute-done.10 = bf16[4,32,384]{2,1,0:T(8,128)(2,1)S(1)} collective-permute-done((bf16[4,32,384]{2,1,0:T(8,128)(2,1)S(1)}, bf16[4,32,384]{2,1,0:T(8,128)(2,1)S(1)}, u32[]{:S(2)}, u32[]{:S(2)}) %collective-permute-start.10) | collective-permute-done | bytes 98336 | tf_op jit(solution)/shard_map/ppermute | solution.py:41
  24.3 0.1 convert_reduce_fusion
  24.4 0.2 fusion.11
  24.6 0.1 fusion.13
  24.8 0.3 fusion.76
  25.2 0.1 reshape.566
  25.3 0.1 reshape.565
  25.5 0.1 pad_maximum_fusion.1
  25.6 0.2 multiply_reduce_fusion.1
  25.9 0.2 copy-done.6
  26.1 0.2 convolution_convert_fusion.8
  26.3 0.1 reshape_reshape.3
  26.4 0.2 convolution_convert_fusion
  26.7 0.1 reshape_reshape_reshape.3
  26.8 0.2 convolution_multiply_fusion
  27.1 0.3 fusion.5
  27.5 0.1 reshape.453
  27.7 0.1 copy-done.4
  27.8 0.2 convolution_convert_fusion.3
  28.3 1.1 %collective-permute-done.11 = bf16[64,768]{1,0:T(8,128)(2,1)S(1)} collective-permute-done((bf16[64,768]{1,0:T(8,128)(2,1)S(1)}, bf16[64,768]{1,0:T(8,128)(2,1)S(1)}, u32[]{:S(2)}, u32[]{:S(2)}) %collective-permute-start.11) | collective-permute-done | bytes 98336 | tf_op jit(solution)/shard_map/ppermute | solution.py:41
  29.4 1.2 %collective-permute-start.12 = (bf16[64,768]{1,0:T(8,128)(2,1)S(1)}, bf16[64,768]{1,0:T(8,128)(2,1)S(1)}, u32[]{:S(2)}, u32[]{:S(2)}) collective-permute-start(bf16[64,768]{1,0:T(8,128)(2,1)S(1)} %add_convert_fusion), channel_id=1, source_target_pairs={{0,2},{1,3},{2,0},{3,1},{4,6},{5,7},{6,4},{7,5},{8,10},{9,11},{10,... | collective-permute-start | bytes 294920 | tf_op jit(solution)/shard_map/ppermute | solution.py:41
  30.6 3.7 %collective-permute-done.12 = bf16[64,768]{1,0:T(8,128)(2,1)S(1)} collective-permute-done((bf16[64,768]{1,0:T(8,128)(2,1)S(1)}, bf16[64,768]{1,0:T(8,128)(2,1)S(1)}, u32[]{:S(2)}, u32[]{:S(2)}) %collective-permute-start.12) | collective-permute-done | bytes 98336 | tf_op jit(solution)/shard_map/ppermute | solution.py:41
  34.5 0.6 %gather_fusion = f32[4,32,768]{2,1,0:T(8,128)S(1)} fusion(f32[2,32,768]{2,1,0:T(8,128)S(1)} %convert_add_fusion.2, s32[1024]{0:T(1024)S(1)} %pad_clamp_fusion), kind=kCustom, calls=%fused_computation | custom fusion | bytes 786448 | tf_op jit(solution)/shard_map/jit(_take)/gather | solution.py:204
  35.1 0.7 %collective-permute-done.13 = f32[64,768]{1,0:T(8,128)S(1)} collective-permute-done((f32[64,768]{1,0:T(8,128)S(1)}, f32[64,768]{1,0:T(8,128)S(1)}, u32[]{:S(2)}, u32[]{:S(2)}) %collective-permute-start.13) | collective-permute-done | bytes 196640 | tf_op jit(solution)/shard_map/ppermute | solution.py:41
  35.9 0.2 fusion.67
  36.1 0.2 multiply_reduce_fusion
  36.3 0.1 multiply_convert_fusion
  36.5 0.3 fusion.77
  36.8 0.8 %fusion.16 = bf16[128,768]{1,0:T(8,128)(2,1)S(1)} fusion(f32[128,768]{1,0:T(8,128)S(1)} %fusion.77), kind=kLoop, calls=%fused_computation.31 | loop fusion | flops 6389760 | bytes 589824 | tf_op jit(solution)/shard_map/convert_element_type | solution.py:216
  37.8 0.3 convolution_convert_fusion.2
  38.1 0.2 copy.71
  38.7 1.0 %collective-permute-start.16 = (bf16[128,192]{1,0:T(8,128)(2,1)S(1)}, bf16[128,192]{1,0:T(8,128)(2,1)S(1)}, u32[]{:S(2)}, u32[]{:S(2)}) collective-permute-start(bf16[128,192]{1,0:T(8,128)(2,1)S(1)} %select_bitcast_fusion), channel_id=1, source_target_pairs={{0,3},{1,2},{2,1},{3,0},{4,7},{5,6},{6,5},{7,4},{8,11},{9,10},{10,... | collective-permute-start | bytes 147464 | tf_op jit(solution)/shard_map/ppermute | solution.py:41
  39.6 0.4 collective-permute-start.14
  40.1 0.9 %collective-permute-start.15 = (bf16[128,192]{1,0:T(8,128)(2,1)S(1)}, bf16[128,192]{1,0:T(8,128)(2,1)S(1)}, u32[]{:S(2)}, u32[]{:S(2)}) collective-permute-start(bf16[128,192]{1,0:T(8,128)(2,1)S(1)} %select_bitcast_fusion.1), channel_id=1, source_target_pairs={{0,2},{1,3},{2,0},{3,1},{4,6},{5,7},{6,4},{7,5},{8,10},{9,11},{10,... | collective-permute-start | bytes 147464 | tf_op jit(solution)/shard_map/ppermute | solution.py:41
  41.1 1.7 %collective-permute-done.16 = bf16[128,192]{1,0:T(8,128)(2,1)S(1)} collective-permute-done((bf16[128,192]{1,0:T(8,128)(2,1)S(1)}, bf16[128,192]{1,0:T(8,128)(2,1)S(1)}, u32[]{:S(2)}, u32[]{:S(2)}) %collective-permute-start.16) | collective-permute-done | bytes 49184 | tf_op jit(solution)/shard_map/ppermute | solution.py:41
  42.8 1.7 %collective-permute-done.15 = bf16[128,192]{1,0:T(8,128)(2,1)S(1)} collective-permute-done((bf16[128,192]{1,0:T(8,128)(2,1)S(1)}, bf16[128,192]{1,0:T(8,128)(2,1)S(1)}, u32[]{:S(2)}, u32[]{:S(2)}) %collective-permute-start.15) | collective-permute-done | bytes 49184 | tf_op jit(solution)/shard_map/ppermute | solution.py:41
  44.9 0.6 %pad_maximum_fusion.3 = bf16[64,192]{1,0:T(8,128)(2,1)} fusion(bf16[32,192]{1,0:T(8,128)(2,1)S(1)} %divide_convert_fusion.4, bf16[32,192]{1,0:T(8,128)(2,1)S(1)} %divide_convert_fusion.5), kind=kLoop, calls=%fused_computation.100 | loop fusion | flops 49152 | bytes 49152 | tf_op jit(solution)/shard_map/concatenate | solution.py:232
  (103 shorter events, 3.7 us)
Async XLA Ops:
  0.0 36.5 %copy-start = (bf16[768,768]{1,0:T(8,128)(2,1)S(1)}, bf16[768,768]{1,0:T(8,128)(2,1)}, u32[]{:S(2)}) copy-start(bf16[768,768]{1,0:T(8,128)(2,1)} %param.28) | copy-start | bytes 3538948
  0.0 12.6 %copy-start.2 = (bf16[3,768,192]{1,2,0:T(8,128)(2,1)S(1)}, bf16[3,768,192]{1,2,0:T(8,128)(2,1)}, u32[]{:S(2)}) copy-start(bf16[3,768,192]{1,2,0:T(8,128)(2,1)} %param.23) | copy-start | bytes 2654212
  0.0 9.5 %collective-permute-start.5 = (bf16[2,32,192]{2,1,0:T(8,128)(2,1)}, bf16[2,32,192]{2,1,0:T(8,128)(2,1)S(1)}, u32[]{:S(2)}, u32[]{:S(2)}) collective-permute-start(bf16[2,32,192]{2,1,0:T(8,128)(2,1)} %bitcast.79), channel_id=1, source_target_pairs={{0,1},{1,0},{2,3},{3,2},{4,5},{5,4},{6,7},{7,6},{8,9},{9,8},{10,11... | collective-permute-start | bytes 73736 | tf_op jit(solution)/shard_map/ppermute | solution.py:41
  0.5 10.1 %collective-permute-start.4 = (bf16[2,32,192]{2,1,0:T(8,128)(2,1)}, bf16[2,32,192]{2,1,0:T(8,128)(2,1)S(1)}, u32[]{:S(2)}, u32[]{:S(2)}) collective-permute-start(bf16[2,32,192]{2,1,0:T(8,128)(2,1)} %bitcast.80), channel_id=1, source_target_pairs={{0,2},{1,3},{2,0},{3,1},{4,6},{5,7},{6,4},{7,5},{8,10},{9,11},{10,... | collective-permute-start | bytes 73736 | tf_op jit(solution)/shard_map/ppermute | solution.py:41
  3.0 7.6 %collective-permute-start.3 = (bf16[2,32,192]{2,1,0:T(8,128)(2,1)}, bf16[2,32,192]{2,1,0:T(8,128)(2,1)S(1)}, u32[]{:S(2)}, u32[]{:S(2)}) collective-permute-start(bf16[2,32,192]{2,1,0:T(8,128)(2,1)} %bitcast.81), channel_id=1, source_target_pairs={{0,3},{1,2},{2,1},{3,0},{4,7},{5,6},{6,5},{7,4},{8,11},{9,10},{10,... | collective-permute-start | bytes 73736 | tf_op jit(solution)/shard_map/ppermute | solution.py:41
  5.6 8.7 %collective-permute-start.2 = (f32[12420]{0:T(1024)S(1)}, f32[12420]{0:T(1024)S(1)}, u32[]{:S(2)}, u32[]{:S(2)}) collective-permute-start(f32[12420]{0:T(1024)S(1)} %concatenate.42), channel_id=1, source_target_pairs={{0,12},{4,0},{8,4},{12,8},{1,13},{5,1},{9,5},{13,9},{2,14},{6,2},{... | collective-permute-start | bytes 149048 | tf_op jit(solution)/shard_map/ppermute | solution.py:37
  9.4 6.2 %collective-permute-start.1 = (f32[12420]{0:T(1024)S(1)}, f32[12420]{0:T(1024)S(1)}, u32[]{:S(2)}, u32[]{:S(2)}) collective-permute-start(f32[12420]{0:T(1024)S(1)} %concatenate.42), channel_id=1, source_target_pairs={{0,8},{4,12},{8,0},{12,4},{1,9},{5,13},{9,1},{13,5},{2,10},{6,14},... | collective-permute-start | bytes 149048 | tf_op jit(solution)/shard_map/ppermute | solution.py:37
  9.5 6.1 %collective-permute-start = (f32[12420]{0:T(1024)S(1)}, f32[12420]{0:T(1024)S(1)}, u32[]{:S(2)}, u32[]{:S(2)}) collective-permute-start(f32[12420]{0:T(1024)S(1)} %concatenate.42), channel_id=1, source_target_pairs={{0,4},{4,8},{8,12},{12,0},{1,5},{5,9},{9,13},{13,1},{2,6},{6,10},{... | collective-permute-start | bytes 149048 | tf_op jit(solution)/shard_map/ppermute | solution.py:37
  12.6 1.4 %copy-start.5 = (bf16[192,768]{1,0:T(8,128)(2,1)S(1)}, bf16[192,768]{1,0:T(8,128)(2,1)}, u32[]{:S(2)}) copy-start(bf16[192,768]{1,0:T(8,128)(2,1)} %param.24) | copy-start | bytes 884740
  14.2 3.4 %collective-permute-start.6 = (bf16[32,768]{1,0:T(8,128)(2,1)S(1)}, bf16[32,768]{1,0:T(8,128)(2,1)S(1)}, u32[]{:S(2)}, u32[]{:S(2)}) collective-permute-start(bf16[32,768]{1,0:T(8,128)(2,1)S(1)} %broadcast_select_fusion.5), channel_id=1, source_target_pairs={{0,1},{1,0},{2,3},{3,2},{4,5},{5,4},{6,7},{7,6},{8,9},{9,8},{10,11... | collective-permute-start | bytes 147464 | tf_op jit(solution)/shard_map/ppermute | solution.py:41
  15.8 8.8 %copy-start.7 = (f32[768]{0:T(1024)S(1)}, f32[768]{0:T(1024)}, u32[]{:S(2)}) copy-start(f32[768]{0:T(1024)} %param.21) | copy-start | bytes 9220
  16.0 8.8 %copy-start.3 = (bf16[2,768,192]{1,2,0:T(8,128)(2,1)S(1)}, bf16[2,768,192]{1,2,0:T(8,128)(2,1)}, u32[]{:S(2)}) copy-start(bf16[2,768,192]{1,2,0:T(8,128)(2,1)} %param.26) | copy-start | bytes 1769476
  17.4 1.8 %collective-permute-start.9 = (bf16[4,32,192]{2,1,0:T(8,128)(2,1)S(1)}, bf16[4,32,192]{2,1,0:T(8,128)(2,1)S(1)}, u32[]{:S(2)}, u32[]{:S(2)}) collective-permute-start(bf16[4,32,192]{2,1,0:T(8,128)(2,1)S(1)} %reshape.451), channel_id=1, source_target_pairs={{0,1},{1,0},{2,3},{3,2},{4,5},{5,4},{6,7},{7,6},{8,9},{9,8},{10,11... | collective-permute-start | bytes 147464 | tf_op jit(solution)/shard_map/ppermute | solution.py:41
  17.6 4.2 %collective-permute-start.7 = (bf16[32,768]{1,0:T(8,128)(2,1)S(1)}, bf16[32,768]{1,0:T(8,128)(2,1)S(1)}, u32[]{:S(2)}, u32[]{:S(2)}) collective-permute-start(bf16[32,768]{1,0:T(8,128)(2,1)S(1)} %add_convert_fusion.1), channel_id=1, source_target_pairs={{0,2},{1,3},{2,0},{3,1},{4,6},{5,7},{6,4},{7,5},{8,10},{9,11},{10,... | collective-permute-start | bytes 147464 | tf_op jit(solution)/shard_map/ppermute | solution.py:41
  19.3 5.0 %collective-permute-start.10 = (bf16[4,32,384]{2,1,0:T(8,128)(2,1)S(1)}, bf16[4,32,384]{2,1,0:T(8,128)(2,1)S(1)}, u32[]{:S(2)}, u32[]{:S(2)}) collective-permute-start(bf16[4,32,384]{2,1,0:T(8,128)(2,1)S(1)} %maximum_select_fusion.1), channel_id=1, source_target_pairs={{0,2},{1,3},{2,0},{3,1},{4,6},{5,7},{6,4},{7,5},{8,10},{9,11},{10,... | collective-permute-start | bytes 294920 | tf_op jit(solution)/shard_map/ppermute | solution.py:41
  21.8 3.6 %collective-permute-start.8 = (f32[32,768]{1,0:T(8,128)S(1)}, f32[32,768]{1,0:T(8,128)S(1)}, u32[]{:S(2)}, u32[]{:S(2)}) collective-permute-start(f32[32,768]{1,0:T(8,128)S(1)} %convert_add_fusion.3), channel_id=1, source_target_pairs={{0,1},{1,0},{2,3},{3,2},{4,5},{5,4},{6,7},{7,6},{8,9},{9,8},{10,11... | collective-permute-start | bytes 294920 | tf_op jit(solution)/shard_map/ppermute | solution.py:41
  25.1 0.7 %copy-start.8 = (f32[768]{0:T(1024)S(1)}, f32[768]{0:T(1024)}, u32[]{:S(2)}) copy-start(f32[768]{0:T(1024)} %param.20) | copy-start | bytes 9220
  25.1 1.0 %copy-start.6 = (bf16[768,192]{0,1:T(8,128)(2,1)S(1)}, bf16[768,192]{0,1:T(8,128)(2,1)}, u32[]{:S(2)}) copy-start(bf16[768,192]{0,1:T(8,128)(2,1)} %param.25) | copy-start | bytes 884740
  26.8 1.0 %copy-start.4 = (bf16[192,768]{1,0:T(8,128)(2,1)S(1)}, bf16[192,768]{1,0:T(8,128)(2,1)}, u32[]{:S(2)}) copy-start(bf16[192,768]{1,0:T(8,128)(2,1)} %param.27) | copy-start | bytes 884740
  28.0 1.4 %collective-permute-start.11 = (bf16[64,768]{1,0:T(8,128)(2,1)S(1)}, bf16[64,768]{1,0:T(8,128)(2,1)S(1)}, u32[]{:S(2)}, u32[]{:S(2)}) collective-permute-start(bf16[64,768]{1,0:T(8,128)(2,1)S(1)} %broadcast_select_fusion.2), channel_id=1, source_target_pairs={{0,1},{1,0},{2,3},{3,2},{4,5},{5,4},{6,7},{7,6},{8,9},{9,8},{10,11... | collective-permute-start | bytes 294920 | tf_op jit(solution)/shard_map/ppermute | solution.py:41
  29.4 4.9 %collective-permute-start.12 = (bf16[64,768]{1,0:T(8,128)(2,1)S(1)}, bf16[64,768]{1,0:T(8,128)(2,1)S(1)}, u32[]{:S(2)}, u32[]{:S(2)}) collective-permute-start(bf16[64,768]{1,0:T(8,128)(2,1)S(1)} %add_convert_fusion), channel_id=1, source_target_pairs={{0,2},{1,3},{2,0},{3,1},{4,6},{5,7},{6,4},{7,5},{8,10},{9,11},{10,... | collective-permute-start | bytes 294920 | tf_op jit(solution)/shard_map/ppermute | solution.py:41
  34.4 1.5 %collective-permute-start.13 = (f32[64,768]{1,0:T(8,128)S(1)}, f32[64,768]{1,0:T(8,128)S(1)}, u32[]{:S(2)}, u32[]{:S(2)}) collective-permute-start(f32[64,768]{1,0:T(8,128)S(1)} %convert_add_fusion.1), channel_id=1, source_target_pairs={{0,1},{1,0},{2,3},{3,2},{4,5},{5,4},{6,7},{7,6},{8,9},{9,8},{10,11... | collective-permute-start | bytes 589832 | tf_op jit(solution)/shard_map/ppermute | solution.py:41
  35.1 1.2 %copy-start.9 = (f32[768]{0:T(1024)S(1)}, f32[768]{0:T(1024)}, u32[]{:S(2)}) copy-start(f32[768]{0:T(1024)} %param.22) | copy-start | bytes 9220
  36.5 1.3 %copy-start.1 = (bf16[768,768]{1,0:T(8,128)(2,1)S(1)}, bf16[768,768]{1,0:T(8,128)(2,1)}, u32[]{:S(2)}) copy-start(bf16[768,768]{1,0:T(8,128)(2,1)} %param.29) | copy-start | bytes 3538948
  38.7 4.1 %collective-permute-start.16 = (bf16[128,192]{1,0:T(8,128)(2,1)S(1)}, bf16[128,192]{1,0:T(8,128)(2,1)S(1)}, u32[]{:S(2)}, u32[]{:S(2)}) collective-permute-start(bf16[128,192]{1,0:T(8,128)(2,1)S(1)} %select_bitcast_fusion), channel_id=1, source_target_pairs={{0,3},{1,2},{2,1},{3,0},{4,7},{5,6},{6,5},{7,4},{8,11},{9,10},{10,... | collective-permute-start | bytes 147464 | tf_op jit(solution)/shard_map/ppermute | solution.py:41
  39.6 3.2 %collective-permute-start.14 = (bf16[128,192]{1,0:T(8,128)(2,1)S(1)}, bf16[128,192]{1,0:T(8,128)(2,1)S(1)}, u32[]{:S(2)}, u32[]{:S(2)}) collective-permute-start(bf16[128,192]{1,0:T(8,128)(2,1)S(1)} %select_bitcast_fusion.2), channel_id=1, source_target_pairs={{0,1},{1,0},{2,3},{3,2},{4,5},{5,4},{6,7},{7,6},{8,9},{9,8},{10,11... | collective-permute-start | bytes 147464 | tf_op jit(solution)/shard_map/ppermute | solution.py:41
  40.1 4.4 %collective-permute-start.15 = (bf16[128,192]{1,0:T(8,128)(2,1)S(1)}, bf16[128,192]{1,0:T(8,128)(2,1)S(1)}, u32[]{:S(2)}, u32[]{:S(2)}) collective-permute-start(bf16[128,192]{1,0:T(8,128)(2,1)S(1)} %select_bitcast_fusion.1), channel_id=1, source_target_pairs={{0,2},{1,3},{2,0},{3,1},{4,6},{5,7},{6,4},{7,5},{8,10},{9,11},{10,... | collective-permute-start | bytes 147464 | tf_op jit(solution)/shard_map/ppermute | solution.py:41

commit v19 on v18

--- a/solution.py
+++ b/solution.py
@@ -148,19 +148,26 @@
     owners_n = lax.axis_size("pairs")
     own = lax.axis_index("pairs")
 
-    payload = jnp.concatenate(
+    high = lax.optimization_barrier(confidence.astype(jnp.bfloat16))
+    rest = confidence - high.astype(jnp.float32)
+    mid = lax.optimization_barrier(rest.astype(jnp.bfloat16))
+    low = (rest - mid.astype(jnp.float32)).astype(jnp.bfloat16)
+    conf_w = confidence.shape[1]
+    tok_rows = img_dev * TOKS
+    extra_n = -(-(3 * pair_dev + 1) // 8) * 8
+    extra = jnp.concatenate(
         [
-            tokens.astype(jnp.float32).reshape(-1),
-            pair_list.astype(jnp.float32).reshape(-1),
-            confidence.reshape(-1),
+            jnp.pad(jnp.concatenate([high, mid, low]), ((0, 0), (0, quarter - conf_w))),
+            jnp.pad(pair_list.reshape(1, views_n).astype(jnp.bfloat16), ((0, 0), (0, quarter - views_n))),
+            jnp.zeros((extra_n - 3 * pair_dev - 1, quarter), jnp.bfloat16),
         ]
     )
-    table = pairs_gather(payload, owners_n)
-    cut_tok = img_dev * TOKS * quarter
-    cut_ids = cut_tok + views_n
-    all_tok = table[:, :cut_tok].astype(jnp.bfloat16).reshape(owners_n * img_dev, TOKS * quarter)
-    all_ids = table[:, cut_tok:cut_ids].astype(jnp.int32)
-    all_conf = table[:, cut_ids:].reshape(owners_n * views_n, TOKS)
+    table = pairs_gather(jnp.concatenate([tokens, extra]), owners_n)
+    all_tok = table[:, :tok_rows].reshape(owners_n * img_dev, TOKS * quarter)
+    pieces = table[:, tok_rows : tok_rows + 3 * pair_dev, :conf_w].astype(jnp.float32)
+    pieces = pieces.reshape(owners_n, 3, pair_dev, conf_w)
+    all_conf = (pieces[:, 0] + pieces[:, 1] + pieces[:, 2]).reshape(owners_n * views_n, TOKS)
+    all_ids = table[:, tok_rows + 3 * pair_dev, :views_n].astype(jnp.int32)
     partner_ids = all_ids.reshape(owners_n, pair_dev, 2)[:, :, ::-1].reshape(-1)
     all_ids = all_ids.reshape(-1)
 

time: 45.9 us -> 50 us (1.089)
  other arithmetic: 7.08 us -> 11.2 us
  starting transfers between devices: 14.5 us -> 16.8 us
  waiting for transfers between devices: 14 us -> 12.7 us
  local copies, waits for them, and re-layouts: 5.61 us -> 4.46 us
    convert_element_type x2 -> x5, other arithmetic: 0.69 us -> 3.4 us  [the longest x1 0.68 us: per_device(): low = (rest - mid.astype(jnp.float32)).astype(jnp.bfloat16)]
    ppermute x3, starting transfers between devices: 4.9 us -> 6.77 us  [pairs_shift(): lax.ppermute(values, 'pairs', [(i, (i + step) % owners_n) for i in range(...]
    reshape x7 -> x2, local copies, waits for them, and re-layouts: 1.99 us -> 0.17 us  [the longest x1 0.16 us: per_device(): all_tok = table[:, :tok_rows].reshape(owners_n * img_dev, TOKS * quarter)]
    ppermute x3, waiting for transfers between devices: 1.25 us -> 0.01 us  [pairs_shift(): lax.ppermute(values, 'pairs', [(i, (i + step) % owners_n) for i in range(...]
    concatenate x0 -> x2, other arithmetic: none -> 0.85 us  [the longest x1 0.84 us: per_device(): table = pairs_gather(jnp.concatenate([tokens, extra]), owners_n)]
    convert_element_type x1 -> x5, local copies, waits for them, and re-layouts: 0.09 us -> 0.85 us  [the longest x4 0.77 us: per_device(): all_ids = table[:, tok_rows + 3 * pair_dev, :views_n].astype(jnp.int32)]
    another operation x1 -> x2, other arithmetic: 0.19 us -> 0.88 us  [pairs_gather(): jnp.stack([payload] + [pairs_shift(payload, step, owners_n) for step in r...]
  transfers between devices with their start and end apart: 17 -> 17, of which waited for: 8 -> 7; matrix products, arithmetic and copies ran while one was open for 22% -> 26% of each run, Pallas kernels for 0% -> 0%
where the time goes in v19:
time: 50 us; the launch traced here: 49.5 us
  starting transfers between devices  16.8 us (34%)
  waiting for transfers between devices  12.7 us (25%)
  other arithmetic  11.2 us (22%)
  local copies, waits for them, and re-layouts  4.46 us (9%)
  matrix products  3.56 us (7%)
  between operations  0.79 us (2%)
    ppermute x14, waiting for transfers between devices, swap(): return lax.ppermute(values, 'mp', pairs)  12.7 us
    ppermute x14, starting transfers between devices, swap(): return lax.ppermute(values, 'mp', pairs)  9.99 us
    ppermute x3, starting transfers between devices, pairs_shift(): lax.ppermute(values, 'pairs', [(i, (i + step) % owners_n) for i in range(...  6.77 us
    convert_element_type x4, other arithmetic, layer_norm(): return (center * lax.rsqrt(spread + EPSILON) * gain).astype(jnp.bfloat16)  1.15 us
  transfers between devices with their start and end apart: 17, of which 7 were waited for; matrix products, arithmetic and copies ran while one was open for 26% of the time, Pallas kernels for 0%

profile of v19, /device:TPU:0, one launch (start us, length us, event | category | flops | bytes accessed | tf_op | source)
XLA Modules:
  0.0 49.5 jit_solution(7331375199298537301)
XLA Ops:
  0.0 0.5 collective-permute-start.5
  0.5 2.6 %collective-permute-start.4 = (bf16[2,32,192]{2,1,0:T(8,128)(2,1)}, bf16[2,32,192]{2,1,0:T(8,128)(2,1)S(1)}, u32[]{:S(2)}, u32[]{:S(2)}) collective-permute-start(bf16[2,32,192]{2,1,0:T(8,128)(2,1)} %bitcast.99), channel_id=1, source_target_pairs={{0,2},{1,3},{2,0},{3,1},{4,6},{5,7},{6,4},{7,5},{8,10},{9,11},{10,... | collective-permute-start | bytes 73736 | tf_op jit(solution)/shard_map/ppermute | solution.py:41
  3.1 0.7 %convert_element_type.229 = bf16[2,2]{1,0:T(2,128)(2,1)S(1)} convert(s32[2,2]{1,0:T(2,128)} %param.17) | non-fusion elementwise | flops 4 | bytes 24 | tf_op jit(solution)/shard_map/convert_element_type | solution.py:161
  3.9 0.7 %convert_element_type.224 = bf16[2,64]{1,0:T(2,128)(2,1)S(1)} convert(f32[2,64]{1,0:T(2,128)} %param.18) | non-fusion elementwise | flops 128 | bytes 768 | tf_op jit(solution)/shard_map/convert_element_type | solution.py:151
  4.5 0.7 %fusion.59 = bf16[2,64]{1,0:T(2,128)(2,1)S(1)} fusion(f32[2,64]{1,0:T(2,128)} %param.18, bf16[2,64]{1,0:T(2,128)(2,1)S(1)} %convert_element_type.224), kind=kLoop, calls=%fused_computation.176 | loop fusion | flops 384 | bytes 1024 | tf_op jit(solution)/shard_map/convert_element_type | solution.py:153
  5.2 0.7 %subtract_convert_fusion = bf16[2,64]{1,0:T(2,128)(2,1)S(1)} fusion(bf16[2,64]{1,0:T(2,128)(2,1)S(1)} %fusion.59, f32[2,64]{1,0:T(2,128)} %param.18, bf16[2,64]{1,0:T(2,128)(2,1)S(1)} %convert_element_type.224), kind=kLoop, calls=%fused_computation.174 | loop fusion | flops 640 | bytes 1280 | tf_op jit(solution)/shard_map/convert_element_type | solution.py:154
  6.0 0.8 %fusion.44 = bf16[72,192]{1,0:T(8,128)(2,1)S(1)} fusion(bf16[1,4]{1,0:T(2,128)(2,1)S(1)} %convert_element_type.230, bf16[6,192]{1,0:T(8,128)(2,1)S(1)} %fusion.53, bf16[64,192]{1,0:T(8,128)(2,1)} %param.16, bf16[72]{0:T(256)(128)(2,1)S(1)} %pad.41.clone), kind=kLoop, calls=%fused_computation.104 | loop fusion | flops 165888 | bytes 54680 | tf_op jit(solution)/shard_map/concatenate | solution.py:165
  6.8 2.9 %collective-permute-start.1 = (bf16[72,192]{1,0:T(8,128)(2,1)S(1)}, bf16[72,192]{1,0:T(8,128)(2,1)S(1)}, u32[]{:S(2)}, u32[]{:S(2)}) collective-permute-start(bf16[72,192]{1,0:T(8,128)(2,1)S(1)} %fusion.44), channel_id=1, source_target_pairs={{0,8},{4,12},{8,0},{12,4},{1,9},{5,13},{9,1},{13,5},{2,10},{6,14},... | collective-permute-start | bytes 82952 | tf_op jit(solution)/shard_map/ppermute | solution.py:37
  9.7 1.6 %collective-permute-start = (bf16[72,192]{1,0:T(8,128)(2,1)S(1)}, bf16[72,192]{1,0:T(8,128)(2,1)S(1)}, u32[]{:S(2)}, u32[]{:S(2)}) collective-permute-start(bf16[72,192]{1,0:T(8,128)(2,1)S(1)} %fusion.44), channel_id=1, source_target_pairs={{0,4},{4,8},{8,12},{12,0},{1,5},{5,9},{9,13},{13,1},{2,6},{6,10},{... | collective-permute-start | bytes 82952 | tf_op jit(solution)/shard_map/ppermute | solution.py:37
  11.3 0.8 %fusion.108 = bf16[1,72,192]{2,1,0:T(8,128)(2,1)S(1)} fusion(bf16[72]{0:T(256)(128)(2,1)S(1)} %pad.41.clone, bf16[1,4]{1,0:T(2,128)(2,1)S(1)} %convert_element_type.230, bf16[6,192]{1,0:T(8,128)(2,1)S(1)} %fusion.53, bf16[64,192]{1,0:T(8,128)(2,1)} %param.16), kind=kLoop, calls=%fused_computation.207 | loop fusion | flops 165888 | bytes 54680 | tf_op jit(solution)/shard_map/stack | solution.py:113
  12.2 2.3 %collective-permute-start.2 = (bf16[72,192]{1,0:T(8,128)(2,1)S(1)}, bf16[72,192]{1,0:T(8,128)(2,1)S(1)}, u32[]{:S(2)}, u32[]{:S(2)}) collective-permute-start(bf16[72,192]{1,0:T(8,128)(2,1)S(1)} %fusion.44), channel_id=1, source_target_pairs={{0,12},{4,0},{8,4},{12,8},{1,13},{5,1},{9,5},{13,9},{2,14},{6,2},{... | collective-permute-start | bytes 82952 | tf_op jit(solution)/shard_map/ppermute | solution.py:37
  14.5 0.8 %select_select_fusion.3 = (bf16[2,32,192]{2,1,0:T(8,128)(2,1)S(1)}, bf16[2,32,192]{2,1,0:T(8,128)(2,1)S(1)}, bf16[2,32,192]{2,1,0:T(8,128)(2,1)S(1)}, bf16[2,32,192]{2,1,0:T(8,128)(2,1)S(1)}) fusion(bf16[2,32,192]{2,1,0:T(8,128)(2,1)S(1)} %collective-permute-done.3, bf16[2,32,192]{2,1,0:T(8,128)(2,1)S(1)} %collective-permute-done.4, ...), kind=kLoop, calls=%fused_computation.111 | loop fusion | flops 147456 | bytes 196620 | tf_op jit(solution)/shard_map/jit(_where)/select_n | solution.py:91
  15.3 0.2 convert_reduce_fusion.1
  15.5 0.2 fusion.26
  15.7 0.8 %fusion.28 = bf16[64,768]{1,0:T(8,128)(2,1)S(1)} fusion(bf16[64,768]{1,0:T(8,128)(2,1)S(1)} %get-tuple-element.28, f32[768]{0:T(1024)} %param.19, f32[64]{0:T(128)S(1)} %add_rsqrt_fusion.3, f32[64]{0:T(128)S(1)} %broadcast_multiply_fusion.3), kind=kLoop, calls=%fused_computation.58 | loop fusion | flops 245760 | bytes 200192 | tf_op jit(solution)/shard_map/convert_element_type | solution.py:16
  16.6 0.4 fusion.6
  17.2 0.2 fusion.81
  17.4 0.1 convolution_multiply_fusion.1
  17.6 0.2 fusion.8
  18.0 0.2 convolution_convert_fusion.6
  18.4 0.5 %broadcast.594 = s32[]{:T(128)} broadcast(s32[]{:T(128)} %constant.161.clone.1), dimensions={} | broadcast | bytes 8 | tf_op jit(solution)/shard_map/convert_element_type | solution.py:170
  18.9 0.7 %fusion.78 = (s32[4,4]{1,0:T(4,128)S(1)}, s32[4,1,4]{2,1,0:T(1,128)S(1)}) fusion(s32[]{:T(128)} %broadcast.594, bf16[1,72,192]{2,1,0:T(8,128)(2,1)S(1)} %bitcast.93, bf16[1,72,192]{2,1,0:T(8,128)(2,1)S(1)} %bitcast.87, bf16[1,72,192]{2,1,0:T(8,128)(2,1)S(1)} %bitcast.90, bf16[1,72,192]{2,1,0:T(8,128)(2,1)S(1)} %fusion.108), kind=kLoop, calls=%fused_computation.200 | loop fusion | flops 128 | bytes 110724 | tf_op jit(solution)/shard_map/convert_element_type | solution.py:170
  20.2 0.2 select_reduce_fusion
  20.5 0.2 reshape.429
  20.7 0.2 convolution_convert_fusion.1
  21.1 0.5 %collective-permute-start.9 = (bf16[4,32,192]{2,1,0:T(8,128)(2,1)S(1)}, bf16[4,32,192]{2,1,0:T(8,128)(2,1)S(1)}, u32[]{:S(2)}, u32[]{:S(2)}) collective-permute-start(bf16[4,32,192]{2,1,0:T(8,128)(2,1)S(1)} %reshape.430), channel_id=1, source_target_pairs={{0,1},{1,0},{2,3},{3,2},{4,5},{5,4},{6,7},{7,6},{8,9},{9,8},{10,11... | collective-permute-start | bytes 147464 | tf_op jit(solution)/shard_map/ppermute | solution.py:41
  21.8 1.6 %collective-permute-start.7 = (bf16[32,768]{1,0:T(8,128)(2,1)S(1)}, bf16[32,768]{1,0:T(8,128)(2,1)S(1)}, u32[]{:S(2)}, u32[]{:S(2)}) collective-permute-start(bf16[32,768]{1,0:T(8,128)(2,1)S(1)} %add_convert_fusion.1), channel_id=1, source_target_pairs={{0,2},{1,3},{2,0},{3,1},{4,6},{5,7},{6,4},{7,5},{8,10},{9,11},{10,... | collective-permute-start | bytes 147464 | tf_op jit(solution)/shard_map/ppermute | solution.py:41
  23.5 0.7 %collective-permute-start.10 = (bf16[4,32,384]{2,1,0:T(8,128)(2,1)S(1)}, bf16[4,32,384]{2,1,0:T(8,128)(2,1)S(1)}, u32[]{:S(2)}, u32[]{:S(2)}) collective-permute-start(bf16[4,32,384]{2,1,0:T(8,128)(2,1)S(1)} %maximum_select_fusion.1), channel_id=1, source_target_pairs={{0,2},{1,3},{2,0},{3,1},{4,6},{5,7},{6,4},{7,5},{8,10},{9,11},{10,... | collective-permute-start | bytes 294920 | tf_op jit(solution)/shard_map/ppermute | solution.py:41
  24.2 1.9 %collective-permute-done.7 = bf16[32,768]{1,0:T(8,128)(2,1)S(1)} collective-permute-done((bf16[32,768]{1,0:T(8,128)(2,1)S(1)}, bf16[32,768]{1,0:T(8,128)(2,1)S(1)}, u32[]{:S(2)}, u32[]{:S(2)}) %collective-permute-start.7) | collective-permute-done | bytes 49184 | tf_op jit(solution)/shard_map/ppermute | solution.py:41
  26.2 2.0 %collective-permute-done.10 = bf16[4,32,384]{2,1,0:T(8,128)(2,1)S(1)} collective-permute-done((bf16[4,32,384]{2,1,0:T(8,128)(2,1)S(1)}, bf16[4,32,384]{2,1,0:T(8,128)(2,1)S(1)}, u32[]{:S(2)}, u32[]{:S(2)}) %collective-permute-start.10) | collective-permute-done | bytes 98336 | tf_op jit(solution)/shard_map/ppermute | solution.py:41
  28.3 0.2 fusion.11
  28.5 0.1 fusion.13
  28.6 0.3 fusion.87
  29.0 0.1 reshape.549
  29.2 0.1 reshape.548
  29.3 0.1 pad_maximum_fusion
  29.5 0.2 multiply_reduce_fusion.1
  29.8 0.2 copy-done.6
  30.0 0.2 convolution_convert_fusion.8
  30.3 0.2 convolution_convert_fusion
  30.5 0.1 reshape_reshape_reshape.3
  30.7 0.2 convolution_multiply_fusion
  31.0 0.3 fusion.5
  31.4 0.1 reshape.432
  31.5 0.1 copy-done.4
  31.7 0.2 convolution_convert_fusion.3
  32.1 1.1 %collective-permute-done.11 = bf16[64,768]{1,0:T(8,128)(2,1)S(1)} collective-permute-done((bf16[64,768]{1,0:T(8,128)(2,1)S(1)}, bf16[64,768]{1,0:T(8,128)(2,1)S(1)}, u32[]{:S(2)}, u32[]{:S(2)}) %collective-permute-start.11) | collective-permute-done | bytes 98336 | tf_op jit(solution)/shard_map/ppermute | solution.py:41
  33.3 1.5 %collective-permute-start.12 = (bf16[64,768]{1,0:T(8,128)(2,1)S(1)}, bf16[64,768]{1,0:T(8,128)(2,1)S(1)}, u32[]{:S(2)}, u32[]{:S(2)}) collective-permute-start(bf16[64,768]{1,0:T(8,128)(2,1)S(1)} %add_convert_fusion), channel_id=1, source_target_pairs={{0,2},{1,3},{2,0},{3,1},{4,6},{5,7},{6,4},{7,5},{8,10},{9,11},{10,... | collective-permute-start | bytes 294920 | tf_op jit(solution)/shard_map/ppermute | solution.py:41
  34.8 3.5 %collective-permute-done.12 = bf16[64,768]{1,0:T(8,128)(2,1)S(1)} collective-permute-done((bf16[64,768]{1,0:T(8,128)(2,1)S(1)}, bf16[64,768]{1,0:T(8,128)(2,1)S(1)}, u32[]{:S(2)}, u32[]{:S(2)}) %collective-permute-start.12) | collective-permute-done | bytes 98336 | tf_op jit(solution)/shard_map/ppermute | solution.py:41
  38.4 0.6 %gather_fusion = f32[4,32,768]{2,1,0:T(8,128)S(1)} fusion(f32[2,32,768]{2,1,0:T(8,128)S(1)} %convert_add_fusion.2, s32[1024]{0:T(1024)S(1)} %pad_clamp_fusion), kind=kCustom, calls=%fused_computation | custom fusion | bytes 786448 | tf_op jit(solution)/shard_map/jit(_take)/gather | solution.py:211
  39.0 0.7 %collective-permute-done.13 = f32[64,768]{1,0:T(8,128)S(1)} collective-permute-done((f32[64,768]{1,0:T(8,128)S(1)}, f32[64,768]{1,0:T(8,128)S(1)}, u32[]{:S(2)}, u32[]{:S(2)}) %collective-permute-start.13) | collective-permute-done | bytes 196640 | tf_op jit(solution)/shard_map/ppermute | solution.py:41
  39.8 0.2 fusion.77
  40.0 0.2 multiply_reduce_fusion
  40.2 0.1 multiply_convert_fusion
  40.4 0.3 fusion.88
  40.7 0.8 %fusion.16 = bf16[128,768]{1,0:T(8,128)(2,1)S(1)} fusion(f32[128,768]{1,0:T(8,128)S(1)} %fusion.88), kind=kLoop, calls=%fused_computation.31 | loop fusion | flops 6389760 | bytes 589824 | tf_op jit(solution)/shard_map/convert_element_type | solution.py:223
  41.6 0.3 convolution_convert_fusion.2
  42.0 0.2 copy.96
  42.5 1.2 %collective-permute-start.16 = (bf16[128,192]{1,0:T(8,128)(2,1)S(1)}, bf16[128,192]{1,0:T(8,128)(2,1)S(1)}, u32[]{:S(2)}, u32[]{:S(2)}) collective-permute-start(bf16[128,192]{1,0:T(8,128)(2,1)S(1)} %select_bitcast_fusion), channel_id=1, source_target_pairs={{0,3},{1,2},{2,1},{3,0},{4,7},{5,6},{6,5},{7,4},{8,11},{9,10},{10,... | collective-permute-start | bytes 147464 | tf_op jit(solution)/shard_map/ppermute | solution.py:41
  43.7 0.4 collective-permute-start.14
  44.2 0.7 %collective-permute-start.15 = (bf16[128,192]{1,0:T(8,128)(2,1)S(1)}, bf16[128,192]{1,0:T(8,128)(2,1)S(1)}, u32[]{:S(2)}, u32[]{:S(2)}) collective-permute-start(bf16[128,192]{1,0:T(8,128)(2,1)S(1)} %select_bitcast_fusion.1), channel_id=1, source_target_pairs={{0,2},{1,3},{2,0},{3,1},{4,6},{5,7},{6,4},{7,5},{8,10},{9,11},{10,... | collective-permute-start | bytes 147464 | tf_op jit(solution)/shard_map/ppermute | solution.py:41
  45.0 1.7 %collective-permute-done.16 = bf16[128,192]{1,0:T(8,128)(2,1)S(1)} collective-permute-done((bf16[128,192]{1,0:T(8,128)(2,1)S(1)}, bf16[128,192]{1,0:T(8,128)(2,1)S(1)}, u32[]{:S(2)}, u32[]{:S(2)}) %collective-permute-start.16) | collective-permute-done | bytes 49184 | tf_op jit(solution)/shard_map/ppermute | solution.py:41
  46.7 1.9 %collective-permute-done.15 = bf16[128,192]{1,0:T(8,128)(2,1)S(1)} collective-permute-done((bf16[128,192]{1,0:T(8,128)(2,1)S(1)}, bf16[128,192]{1,0:T(8,128)(2,1)S(1)}, u32[]{:S(2)}, u32[]{:S(2)}) %collective-permute-start.15) | collective-permute-done | bytes 49184 | tf_op jit(solution)/shard_map/ppermute | solution.py:41
  48.9 0.6 %pad_maximum_fusion.3 = bf16[64,192]{1,0:T(8,128)(2,1)} fusion(bf16[32,192]{1,0:T(8,128)(2,1)S(1)} %divide_convert_fusion.4, bf16[32,192]{1,0:T(8,128)(2,1)S(1)} %divide_convert_fusion.5), kind=kLoop, calls=%fused_computation.105 | loop fusion | flops 49152 | bytes 49152 | tf_op jit(solution)/shard_map/concatenate | solution.py:239
  (107 shorter events, 4.2 us)
Async XLA Ops:
  0.0 40.4 %copy-start = (bf16[768,768]{1,0:T(8,128)(2,1)S(1)}, bf16[768,768]{1,0:T(8,128)(2,1)}, u32[]{:S(2)}) copy-start(bf16[768,768]{1,0:T(8,128)(2,1)} %param.28) | copy-start | bytes 3538948
  0.0 16.5 %copy-start.2 = (bf16[3,768,192]{1,2,0:T(8,128)(2,1)S(1)}, bf16[3,768,192]{1,2,0:T(8,128)(2,1)}, u32[]{:S(2)}) copy-start(bf16[3,768,192]{1,2,0:T(8,128)(2,1)} %param.23) | copy-start | bytes 2654212
  0.0 12.2 %collective-permute-start.5 = (bf16[2,32,192]{2,1,0:T(8,128)(2,1)}, bf16[2,32,192]{2,1,0:T(8,128)(2,1)S(1)}, u32[]{:S(2)}, u32[]{:S(2)}) collective-permute-start(bf16[2,32,192]{2,1,0:T(8,128)(2,1)} %bitcast.98), channel_id=1, source_target_pairs={{0,1},{1,0},{2,3},{3,2},{4,5},{5,4},{6,7},{7,6},{8,9},{9,8},{10,11... | collective-permute-start | bytes 73736 | tf_op jit(solution)/shard_map/ppermute | solution.py:41
  0.5 14.1 %collective-permute-start.4 = (bf16[2,32,192]{2,1,0:T(8,128)(2,1)}, bf16[2,32,192]{2,1,0:T(8,128)(2,1)S(1)}, u32[]{:S(2)}, u32[]{:S(2)}) collective-permute-start(bf16[2,32,192]{2,1,0:T(8,128)(2,1)} %bitcast.99), channel_id=1, source_target_pairs={{0,2},{1,3},{2,0},{3,1},{4,6},{5,7},{6,4},{7,5},{8,10},{9,11},{10,... | collective-permute-start | bytes 73736 | tf_op jit(solution)/shard_map/ppermute | solution.py:41
  3.0 11.5 %collective-permute-start.3 = (bf16[2,32,192]{2,1,0:T(8,128)(2,1)}, bf16[2,32,192]{2,1,0:T(8,128)(2,1)S(1)}, u32[]{:S(2)}, u32[]{:S(2)}) collective-permute-start(bf16[2,32,192]{2,1,0:T(8,128)(2,1)} %bitcast.100), channel_id=1, source_target_pairs={{0,3},{1,2},{2,1},{3,0},{4,7},{5,6},{6,5},{7,4},{8,11},{9,10},{10,... | collective-permute-start | bytes 73736 | tf_op jit(solution)/shard_map/ppermute | solution.py:41
  6.8 11.4 %collective-permute-start.1 = (bf16[72,192]{1,0:T(8,128)(2,1)S(1)}, bf16[72,192]{1,0:T(8,128)(2,1)S(1)}, u32[]{:S(2)}, u32[]{:S(2)}) collective-permute-start(bf16[72,192]{1,0:T(8,128)(2,1)S(1)} %fusion.44), channel_id=1, source_target_pairs={{0,8},{4,12},{8,0},{12,4},{1,9},{5,13},{9,1},{13,5},{2,10},{6,14},... | collective-permute-start | bytes 82952 | tf_op jit(solution)/shard_map/ppermute | solution.py:37
  9.7 8.5 %collective-permute-start = (bf16[72,192]{1,0:T(8,128)(2,1)S(1)}, bf16[72,192]{1,0:T(8,128)(2,1)S(1)}, u32[]{:S(2)}, u32[]{:S(2)}) collective-permute-start(bf16[72,192]{1,0:T(8,128)(2,1)S(1)} %fusion.44), channel_id=1, source_target_pairs={{0,4},{4,8},{8,12},{12,0},{1,5},{5,9},{9,13},{13,1},{2,6},{6,10},{... | collective-permute-start | bytes 82952 | tf_op jit(solution)/shard_map/ppermute | solution.py:37
  12.2 6.0 %collective-permute-start.2 = (bf16[72,192]{1,0:T(8,128)(2,1)S(1)}, bf16[72,192]{1,0:T(8,128)(2,1)S(1)}, u32[]{:S(2)}, u32[]{:S(2)}) collective-permute-start(bf16[72,192]{1,0:T(8,128)(2,1)S(1)} %fusion.44), channel_id=1, source_target_pairs={{0,12},{4,0},{8,4},{12,8},{1,13},{5,1},{9,5},{13,9},{2,14},{6,2},{... | collective-permute-start | bytes 82952 | tf_op jit(solution)/shard_map/ppermute | solution.py:37
  16.5 1.4 %copy-start.5 = (bf16[192,768]{1,0:T(8,128)(2,1)S(1)}, bf16[192,768]{1,0:T(8,128)(2,1)}, u32[]{:S(2)}) copy-start(bf16[192,768]{1,0:T(8,128)(2,1)} %param.24) | copy-start | bytes 884740
  18.2 3.6 %collective-permute-start.6 = (bf16[32,768]{1,0:T(8,128)(2,1)S(1)}, bf16[32,768]{1,0:T(8,128)(2,1)S(1)}, u32[]{:S(2)}, u32[]{:S(2)}) collective-permute-start(bf16[32,768]{1,0:T(8,128)(2,1)S(1)} %broadcast_select_fusion.5), channel_id=1, source_target_pairs={{0,1},{1,0},{2,3},{3,2},{4,5},{5,4},{6,7},{7,6},{8,9},{9,8},{10,11... | collective-permute-start | bytes 147464 | tf_op jit(solution)/shard_map/ppermute | solution.py:41
  18.3 10.1 %copy-start.7 = (f32[768]{0:T(1024)S(1)}, f32[768]{0:T(1024)}, u32[]{:S(2)}) copy-start(f32[768]{0:T(1024)} %param.21) | copy-start | bytes 9220
  20.4 8.2 %copy-start.3 = (bf16[2,768,192]{1,2,0:T(8,128)(2,1)S(1)}, bf16[2,768,192]{1,2,0:T(8,128)(2,1)}, u32[]{:S(2)}) copy-start(bf16[2,768,192]{1,2,0:T(8,128)(2,1)} %param.26) | copy-start | bytes 1769476
  21.1 2.3 %collective-permute-start.9 = (bf16[4,32,192]{2,1,0:T(8,128)(2,1)S(1)}, bf16[4,32,192]{2,1,0:T(8,128)(2,1)S(1)}, u32[]{:S(2)}, u32[]{:S(2)}) collective-permute-start(bf16[4,32,192]{2,1,0:T(8,128)(2,1)S(1)} %reshape.430), channel_id=1, source_target_pairs={{0,1},{1,0},{2,3},{3,2},{4,5},{5,4},{6,7},{7,6},{8,9},{9,8},{10,11... | collective-permute-start | bytes 147464 | tf_op jit(solution)/shard_map/ppermute | solution.py:41
  21.8 4.3 %collective-permute-start.7 = (bf16[32,768]{1,0:T(8,128)(2,1)S(1)}, bf16[32,768]{1,0:T(8,128)(2,1)S(1)}, u32[]{:S(2)}, u32[]{:S(2)}) collective-permute-start(bf16[32,768]{1,0:T(8,128)(2,1)S(1)} %add_convert_fusion.1), channel_id=1, source_target_pairs={{0,2},{1,3},{2,0},{3,1},{4,6},{5,7},{6,4},{7,5},{8,10},{9,11},{10,... | collective-permute-start | bytes 147464 | tf_op jit(solution)/shard_map/ppermute | solution.py:41
  23.5 4.7 %collective-permute-start.10 = (bf16[4,32,384]{2,1,0:T(8,128)(2,1)S(1)}, bf16[4,32,384]{2,1,0:T(8,128)(2,1)S(1)}, u32[]{:S(2)}, u32[]{:S(2)}) collective-permute-start(bf16[4,32,384]{2,1,0:T(8,128)(2,1)S(1)} %maximum_select_fusion.1), channel_id=1, source_target_pairs={{0,2},{1,3},{2,0},{3,1},{4,6},{5,7},{6,4},{7,5},{8,10},{9,11},{10,... | collective-permute-start | bytes 294920 | tf_op jit(solution)/shard_map/ppermute | solution.py:41
  26.1 3.2 %collective-permute-start.8 = (f32[32,768]{1,0:T(8,128)S(1)}, f32[32,768]{1,0:T(8,128)S(1)}, u32[]{:S(2)}, u32[]{:S(2)}) collective-permute-start(f32[32,768]{1,0:T(8,128)S(1)} %convert_add_fusion.3), channel_id=1, source_target_pairs={{0,1},{1,0},{2,3},{3,2},{4,5},{5,4},{6,7},{7,6},{8,9},{9,8},{10,11... | collective-permute-start | bytes 294920 | tf_op jit(solution)/shard_map/ppermute | solution.py:41
  29.0 0.7 %copy-start.8 = (f32[768]{0:T(1024)S(1)}, f32[768]{0:T(1024)}, u32[]{:S(2)}) copy-start(f32[768]{0:T(1024)} %param.20) | copy-start | bytes 9220
  29.0 1.0 %copy-start.6 = (bf16[768,192]{0,1:T(8,128)(2,1)S(1)}, bf16[768,192]{0,1:T(8,128)(2,1)}, u32[]{:S(2)}) copy-start(bf16[768,192]{0,1:T(8,128)(2,1)} %param.25) | copy-start | bytes 884740
  30.7 1.0 %copy-start.4 = (bf16[192,768]{1,0:T(8,128)(2,1)S(1)}, bf16[192,768]{1,0:T(8,128)(2,1)}, u32[]{:S(2)}) copy-start(bf16[192,768]{1,0:T(8,128)(2,1)} %param.27) | copy-start | bytes 884740
  31.9 1.4 %collective-permute-start.11 = (bf16[64,768]{1,0:T(8,128)(2,1)S(1)}, bf16[64,768]{1,0:T(8,128)(2,1)S(1)}, u32[]{:S(2)}, u32[]{:S(2)}) collective-permute-start(bf16[64,768]{1,0:T(8,128)(2,1)S(1)} %broadcast_select_fusion.2), channel_id=1, source_target_pairs={{0,1},{1,0},{2,3},{3,2},{4,5},{5,4},{6,7},{7,6},{8,9},{9,8},{10,11... | collective-permute-start | bytes 294920 | tf_op jit(solution)/shard_map/ppermute | solution.py:41
  33.3 4.9 %collective-permute-start.12 = (bf16[64,768]{1,0:T(8,128)(2,1)S(1)}, bf16[64,768]{1,0:T(8,128)(2,1)S(1)}, u32[]{:S(2)}, u32[]{:S(2)}) collective-permute-start(bf16[64,768]{1,0:T(8,128)(2,1)S(1)} %add_convert_fusion), channel_id=1, source_target_pairs={{0,2},{1,3},{2,0},{3,1},{4,6},{5,7},{6,4},{7,5},{8,10},{9,11},{10,... | collective-permute-start | bytes 294920 | tf_op jit(solution)/shard_map/ppermute | solution.py:41
  38.2 1.5 %collective-permute-start.13 = (f32[64,768]{1,0:T(8,128)S(1)}, f32[64,768]{1,0:T(8,128)S(1)}, u32[]{:S(2)}, u32[]{:S(2)}) collective-permute-start(f32[64,768]{1,0:T(8,128)S(1)} %convert_add_fusion.1), channel_id=1, source_target_pairs={{0,1},{1,0},{2,3},{3,2},{4,5},{5,4},{6,7},{7,6},{8,9},{9,8},{10,11... | collective-permute-start | bytes 589832 | tf_op jit(solution)/shard_map/ppermute | solution.py:41
  39.0 1.2 %copy-start.9 = (f32[768]{0:T(1024)S(1)}, f32[768]{0:T(1024)}, u32[]{:S(2)}) copy-start(f32[768]{0:T(1024)} %param.22) | copy-start | bytes 9220
  40.4 1.3 %copy-start.1 = (bf16[768,768]{1,0:T(8,128)(2,1)S(1)}, bf16[768,768]{1,0:T(8,128)(2,1)}, u32[]{:S(2)}) copy-start(bf16[768,768]{1,0:T(8,128)(2,1)} %param.29) | copy-start | bytes 3538948
  42.5 4.1 %collective-permute-start.16 = (bf16[128,192]{1,0:T(8,128)(2,1)S(1)}, bf16[128,192]{1,0:T(8,128)(2,1)S(1)}, u32[]{:S(2)}, u32[]{:S(2)}) collective-permute-start(bf16[128,192]{1,0:T(8,128)(2,1)S(1)} %select_bitcast_fusion), channel_id=1, source_target_pairs={{0,3},{1,2},{2,1},{3,0},{4,7},{5,6},{6,5},{7,4},{8,11},{9,10},{10,... | collective-permute-start | bytes 147464 | tf_op jit(solution)/shard_map/ppermute | solution.py:41
  43.7 2.9 %collective-permute-start.14 = (bf16[128,192]{1,0:T(8,128)(2,1)S(1)}, bf16[128,192]{1,0:T(8,128)(2,1)S(1)}, u32[]{:S(2)}, u32[]{:S(2)}) collective-permute-start(bf16[128,192]{1,0:T(8,128)(2,1)S(1)} %select_bitcast_fusion.2), channel_id=1, source_target_pairs={{0,1},{1,0},{2,3},{3,2},{4,5},{5,4},{6,7},{7,6},{8,9},{9,8},{10,11... | collective-permute-start | bytes 147464 | tf_op jit(solution)/shard_map/ppermute | solution.py:41
  44.2 4.3 %collective-permute-start.15 = (bf16[128,192]{1,0:T(8,128)(2,1)S(1)}, bf16[128,192]{1,0:T(8,128)(2,1)S(1)}, u32[]{:S(2)}, u32[]{:S(2)}) collective-permute-start(bf16[128,192]{1,0:T(8,128)(2,1)S(1)} %select_bitcast_fusion.1), channel_id=1, source_target_pairs={{0,2},{1,3},{2,0},{3,1},{4,6},{5,7},{6,4},{7,5},{8,10},{9,11},{10,... | collective-permute-start | bytes 147464 | tf_op jit(solution)/shard_map/ppermute | solution.py:41

commit v20 on v18

--- a/solution.py
+++ b/solution.py
@@ -110,9 +110,8 @@
 
 def pairs_gather(payload, owners_n):
     if owners_n <= SHIFTS_MAX:
-        return jnp.stack(
-            [payload] + [pairs_shift(payload, step, owners_n) for step in range(1, owners_n)]
-        )
+        moved = {step: pairs_shift(payload, step, owners_n) for step in range(owners_n - 1, 0, -1)}
+        return jnp.stack([payload] + [moved[step] for step in range(1, owners_n)])
     own = lax.axis_index("pairs")
     every = lax.all_gather(payload, "pairs", axis=0)
     return jnp.roll(every[::-1], own + 1, axis=0)

time: 45.9 us -> 45.9 us (level)
  no operation moved by 1% of the time
where the time goes in v20:
time: 45.9 us; the launch traced here: 45.5 us
  starting transfers between devices  14.5 us (32%)
  waiting for transfers between devices  14 us (31%)
  other arithmetic  7.08 us (15%)
  local copies, waits for them, and re-layouts  5.61 us (12%)
  matrix products  3.57 us (8%)
  between operations  0.74 us (2%)
    ppermute x14, waiting for transfers between devices, swap(): return lax.ppermute(values, 'mp', pairs)  12.8 us
    ppermute x14, starting transfers between devices, swap(): return lax.ppermute(values, 'mp', pairs)  9.61 us
    ppermute x3, starting transfers between devices, pairs_shift(): lax.ppermute(values, 'pairs', [(i, (i + step) % owners_n) for i in range(...  4.9 us
    ppermute x3, waiting for transfers between devices, pairs_shift(): lax.ppermute(values, 'pairs', [(i, (i + step) % owners_n) for i in range(...  1.25 us
    convert_element_type x4, other arithmetic, layer_norm(): return (center * lax.rsqrt(spread + EPSILON) * gain).astype(jnp.bfloat16)  1.15 us
  transfers between devices with their start and end apart: 17, of which 8 were waited for; matrix products, arithmetic and copies ran while one was open for 22% of the time, Pallas kernels for 0%

profile of v20, /device:TPU:0, one launch (start us, length us, event | category | flops | bytes accessed | tf_op | source)
XLA Modules:
  0.0 45.5 jit_solution(15105124621857970721)
XLA Ops:
  0.0 0.5 collective-permute-start.5
  0.5 2.6 %collective-permute-start.4 = (bf16[2,32,192]{2,1,0:T(8,128)(2,1)}, bf16[2,32,192]{2,1,0:T(8,128)(2,1)S(1)}, u32[]{:S(2)}, u32[]{:S(2)}) collective-permute-start(bf16[2,32,192]{2,1,0:T(8,128)(2,1)} %bitcast.80), channel_id=1, source_target_pairs={{0,2},{1,3},{2,0},{3,1},{4,6},{5,7},{6,4},{7,5},{8,10},{9,11},{10,... | collective-permute-start | bytes 73736 | tf_op jit(solution)/shard_map/ppermute | solution.py:41
  3.1 0.9 %reshape.521 = f32[12288]{0:T(1024)S(1)} reshape(bf16[64,192]{1,0:T(8,128)(2,1)} %param.16) | data formatting | bytes 73728 | tf_op jit(solution)/shard_map/reshape | solution.py:152
  4.0 0.8 %reshape.444 = f32[128]{0:T(128)S(1)} reshape(f32[2,64]{1,0:T(2,128)} %param.18) | data formatting | bytes 1024 | tf_op jit(solution)/shard_map/reshape | solution.py:154
  4.7 0.7 %convert_element_type.164 = f32[2,2]{1,0:T(2,128)S(1)} convert(s32[2,2]{1,0:T(2,128)} %param.17) | non-fusion elementwise | flops 4 | bytes 32 | tf_op jit(solution)/shard_map/convert_element_type | solution.py:153
  5.6 3.8 %collective-permute-start.2 = (f32[12420]{0:T(1024)S(1)}, f32[12420]{0:T(1024)S(1)}, u32[]{:S(2)}, u32[]{:S(2)}) collective-permute-start(f32[12420]{0:T(1024)S(1)} %concatenate.42), channel_id=1, source_target_pairs={{0,12},{4,0},{8,4},{12,8},{1,13},{5,1},{9,5},{13,9},{2,14},{6,2},{... | collective-permute-start | bytes 149048 | tf_op jit(solution)/shard_map/ppermute | solution.py:37
  9.5 1.1 %collective-permute-start = (f32[12420]{0:T(1024)S(1)}, f32[12420]{0:T(1024)S(1)}, u32[]{:S(2)}, u32[]{:S(2)}) collective-permute-start(f32[12420]{0:T(1024)S(1)} %concatenate.42), channel_id=1, source_target_pairs={{0,4},{4,8},{8,12},{12,0},{1,5},{5,9},{9,13},{13,1},{2,6},{6,10},{... | collective-permute-start | bytes 149048 | tf_op jit(solution)/shard_map/ppermute | solution.py:37
  10.6 0.8 %select_select_fusion.3 = (bf16[2,32,192]{2,1,0:T(8,128)(2,1)S(1)}, bf16[2,32,192]{2,1,0:T(8,128)(2,1)S(1)}, bf16[2,32,192]{2,1,0:T(8,128)(2,1)S(1)}, bf16[2,32,192]{2,1,0:T(8,128)(2,1)S(1)}) fusion(bf16[2,32,192]{2,1,0:T(8,128)(2,1)S(1)} %collective-permute-done.3, bf16[2,32,192]{2,1,0:T(8,128)(2,1)S(1)} %collective-permute-done.4, ...), kind=kLoop, calls=%fused_computation.106 | loop fusion | flops 147456 | bytes 196620 | tf_op jit(solution)/shard_map/jit(_where)/select_n | solution.py:91
  11.4 0.2 convert_reduce_fusion.1
  11.6 0.2 fusion.26
  11.8 0.8 %fusion.28 = bf16[64,768]{1,0:T(8,128)(2,1)S(1)} fusion(bf16[64,768]{1,0:T(8,128)(2,1)S(1)} %get-tuple-element.28, f32[768]{0:T(1024)} %param.19, f32[64]{0:T(128)S(1)} %add_rsqrt_fusion.3, f32[64]{0:T(128)S(1)} %broadcast_multiply_fusion.3), kind=kLoop, calls=%fused_computation.59 | loop fusion | flops 245760 | bytes 200192 | tf_op jit(solution)/shard_map/convert_element_type | solution.py:16
  12.6 0.4 fusion.6
  13.2 0.2 fusion.70
  13.4 0.1 convolution_multiply_fusion.1
  13.6 0.2 fusion.8
  14.0 0.2 convolution_convert_fusion.6
  14.4 1.2 %collective-permute-done.1 = f32[12420]{0:T(1024)S(1)} collective-permute-done((f32[12420]{0:T(1024)S(1)}, f32[12420]{0:T(1024)S(1)}, u32[]{:S(2)}, u32[]{:S(2)}) %collective-permute-start.1) | collective-permute-done | bytes 49712 | tf_op jit(solution)/shard_map/ppermute | solution.py:37
  15.8 0.2 pad_maximum_fusion
  16.6 0.1 add_reduce_fusion
  16.7 0.2 select_reduce_fusion
  17.0 0.2 convolution_convert_fusion.1
  17.3 0.1 reshape.451
  17.4 0.1 fusion.45
  17.6 1.6 %collective-permute-start.7 = (bf16[32,768]{1,0:T(8,128)(2,1)S(1)}, bf16[32,768]{1,0:T(8,128)(2,1)S(1)}, u32[]{:S(2)}, u32[]{:S(2)}) collective-permute-start(bf16[32,768]{1,0:T(8,128)(2,1)S(1)} %add_convert_fusion.1), channel_id=1, source_target_pairs={{0,2},{1,3},{2,0},{3,1},{4,6},{5,7},{6,4},{7,5},{8,10},{9,11},{10,... | collective-permute-start | bytes 147464 | tf_op jit(solution)/shard_map/ppermute | solution.py:41
  19.2 0.1 maximum_select_fusion.1
  19.3 1.1 %collective-permute-start.10 = (bf16[4,32,384]{2,1,0:T(8,128)(2,1)S(1)}, bf16[4,32,384]{2,1,0:T(8,128)(2,1)S(1)}, u32[]{:S(2)}, u32[]{:S(2)}) collective-permute-start(bf16[4,32,384]{2,1,0:T(8,128)(2,1)S(1)} %maximum_select_fusion.1), channel_id=1, source_target_pairs={{0,2},{1,3},{2,0},{3,1},{4,6},{5,7},{6,4},{7,5},{8,10},{9,11},{10,... | collective-permute-start | bytes 294920 | tf_op jit(solution)/shard_map/ppermute | solution.py:41
  20.4 1.5 %collective-permute-done.7 = bf16[32,768]{1,0:T(8,128)(2,1)S(1)} collective-permute-done((bf16[32,768]{1,0:T(8,128)(2,1)S(1)}, bf16[32,768]{1,0:T(8,128)(2,1)S(1)}, u32[]{:S(2)}, u32[]{:S(2)}) %collective-permute-start.7) | collective-permute-done | bytes 49184 | tf_op jit(solution)/shard_map/ppermute | solution.py:41
  21.9 2.4 %collective-permute-done.10 = bf16[4,32,384]{2,1,0:T(8,128)(2,1)S(1)} collective-permute-done((bf16[4,32,384]{2,1,0:T(8,128)(2,1)S(1)}, bf16[4,32,384]{2,1,0:T(8,128)(2,1)S(1)}, u32[]{:S(2)}, u32[]{:S(2)}) %collective-permute-start.10) | collective-permute-done | bytes 98336 | tf_op jit(solution)/shard_map/ppermute | solution.py:41
  24.3 0.1 convert_reduce_fusion
  24.4 0.2 fusion.11
  24.6 0.1 fusion.13
  24.8 0.3 fusion.76
  25.2 0.1 reshape.566
  25.3 0.1 reshape.565
  25.5 0.1 pad_maximum_fusion.1
  25.6 0.2 multiply_reduce_fusion.1
  25.9 0.2 copy-done.6
  26.1 0.2 convolution_convert_fusion.8
  26.3 0.1 reshape_reshape.3
  26.4 0.2 convolution_convert_fusion
  26.7 0.1 reshape_reshape_reshape.3
  26.8 0.2 convolution_multiply_fusion
  27.1 0.3 fusion.5
  27.5 0.1 reshape.453
  27.7 0.1 copy-done.4
  27.8 0.2 convolution_convert_fusion.3
  28.3 1.1 %collective-permute-done.11 = bf16[64,768]{1,0:T(8,128)(2,1)S(1)} collective-permute-done((bf16[64,768]{1,0:T(8,128)(2,1)S(1)}, bf16[64,768]{1,0:T(8,128)(2,1)S(1)}, u32[]{:S(2)}, u32[]{:S(2)}) %collective-permute-start.11) | collective-permute-done | bytes 98336 | tf_op jit(solution)/shard_map/ppermute | solution.py:41
  29.4 1.2 %collective-permute-start.12 = (bf16[64,768]{1,0:T(8,128)(2,1)S(1)}, bf16[64,768]{1,0:T(8,128)(2,1)S(1)}, u32[]{:S(2)}, u32[]{:S(2)}) collective-permute-start(bf16[64,768]{1,0:T(8,128)(2,1)S(1)} %add_convert_fusion), channel_id=1, source_target_pairs={{0,2},{1,3},{2,0},{3,1},{4,6},{5,7},{6,4},{7,5},{8,10},{9,11},{10,... | collective-permute-start | bytes 294920 | tf_op jit(solution)/shard_map/ppermute | solution.py:41
  30.6 3.7 %collective-permute-done.12 = bf16[64,768]{1,0:T(8,128)(2,1)S(1)} collective-permute-done((bf16[64,768]{1,0:T(8,128)(2,1)S(1)}, bf16[64,768]{1,0:T(8,128)(2,1)S(1)}, u32[]{:S(2)}, u32[]{:S(2)}) %collective-permute-start.12) | collective-permute-done | bytes 98336 | tf_op jit(solution)/shard_map/ppermute | solution.py:41
  34.5 0.6 %gather_fusion = f32[4,32,768]{2,1,0:T(8,128)S(1)} fusion(f32[2,32,768]{2,1,0:T(8,128)S(1)} %convert_add_fusion.2, s32[1024]{0:T(1024)S(1)} %pad_clamp_fusion), kind=kCustom, calls=%fused_computation | custom fusion | bytes 786448 | tf_op jit(solution)/shard_map/jit(_take)/gather | solution.py:203
  35.1 0.7 %collective-permute-done.13 = f32[64,768]{1,0:T(8,128)S(1)} collective-permute-done((f32[64,768]{1,0:T(8,128)S(1)}, f32[64,768]{1,0:T(8,128)S(1)}, u32[]{:S(2)}, u32[]{:S(2)}) %collective-permute-start.13) | collective-permute-done | bytes 196640 | tf_op jit(solution)/shard_map/ppermute | solution.py:41
  35.9 0.2 fusion.67
  36.1 0.2 multiply_reduce_fusion
  36.3 0.1 multiply_convert_fusion
  36.5 0.3 fusion.77
  36.8 0.8 %fusion.16 = bf16[128,768]{1,0:T(8,128)(2,1)S(1)} fusion(f32[128,768]{1,0:T(8,128)S(1)} %fusion.77), kind=kLoop, calls=%fused_computation.31 | loop fusion | flops 6389760 | bytes 589824 | tf_op jit(solution)/shard_map/convert_element_type | solution.py:215
  37.8 0.3 convolution_convert_fusion.2
  38.1 0.2 copy.71
  38.7 1.0 %collective-permute-start.16 = (bf16[128,192]{1,0:T(8,128)(2,1)S(1)}, bf16[128,192]{1,0:T(8,128)(2,1)S(1)}, u32[]{:S(2)}, u32[]{:S(2)}) collective-permute-start(bf16[128,192]{1,0:T(8,128)(2,1)S(1)} %select_bitcast_fusion), channel_id=1, source_target_pairs={{0,3},{1,2},{2,1},{3,0},{4,7},{5,6},{6,5},{7,4},{8,11},{9,10},{10,... | collective-permute-start | bytes 147464 | tf_op jit(solution)/shard_map/ppermute | solution.py:41
  39.6 0.4 collective-permute-start.14
  40.1 0.9 %collective-permute-start.15 = (bf16[128,192]{1,0:T(8,128)(2,1)S(1)}, bf16[128,192]{1,0:T(8,128)(2,1)S(1)}, u32[]{:S(2)}, u32[]{:S(2)}) collective-permute-start(bf16[128,192]{1,0:T(8,128)(2,1)S(1)} %select_bitcast_fusion.1), channel_id=1, source_target_pairs={{0,2},{1,3},{2,0},{3,1},{4,6},{5,7},{6,4},{7,5},{8,10},{9,11},{10,... | collective-permute-start | bytes 147464 | tf_op jit(solution)/shard_map/ppermute | solution.py:41
  41.1 1.7 %collective-permute-done.16 = bf16[128,192]{1,0:T(8,128)(2,1)S(1)} collective-permute-done((bf16[128,192]{1,0:T(8,128)(2,1)S(1)}, bf16[128,192]{1,0:T(8,128)(2,1)S(1)}, u32[]{:S(2)}, u32[]{:S(2)}) %collective-permute-start.16) | collective-permute-done | bytes 49184 | tf_op jit(solution)/shard_map/ppermute | solution.py:41
  42.8 1.7 %collective-permute-done.15 = bf16[128,192]{1,0:T(8,128)(2,1)S(1)} collective-permute-done((bf16[128,192]{1,0:T(8,128)(2,1)S(1)}, bf16[128,192]{1,0:T(8,128)(2,1)S(1)}, u32[]{:S(2)}, u32[]{:S(2)}) %collective-permute-start.15) | collective-permute-done | bytes 49184 | tf_op jit(solution)/shard_map/ppermute | solution.py:41
  44.9 0.6 %pad_maximum_fusion.3 = bf16[64,192]{1,0:T(8,128)(2,1)} fusion(bf16[32,192]{1,0:T(8,128)(2,1)S(1)} %divide_convert_fusion.4, bf16[32,192]{1,0:T(8,128)(2,1)S(1)} %divide_convert_fusion.5), kind=kLoop, calls=%fused_computation.100 | loop fusion | flops 49152 | bytes 49152 | tf_op jit(solution)/shard_map/concatenate | solution.py:231
  (103 shorter events, 3.7 us)
Async XLA Ops:
  0.0 36.5 %copy-start = (bf16[768,768]{1,0:T(8,128)(2,1)S(1)}, bf16[768,768]{1,0:T(8,128)(2,1)}, u32[]{:S(2)}) copy-start(bf16[768,768]{1,0:T(8,128)(2,1)} %param.28) | copy-start | bytes 3538948
  0.0 12.6 %copy-start.2 = (bf16[3,768,192]{1,2,0:T(8,128)(2,1)S(1)}, bf16[3,768,192]{1,2,0:T(8,128)(2,1)}, u32[]{:S(2)}) copy-start(bf16[3,768,192]{1,2,0:T(8,128)(2,1)} %param.23) | copy-start | bytes 2654212
  0.0 9.5 %collective-permute-start.5 = (bf16[2,32,192]{2,1,0:T(8,128)(2,1)}, bf16[2,32,192]{2,1,0:T(8,128)(2,1)S(1)}, u32[]{:S(2)}, u32[]{:S(2)}) collective-permute-start(bf16[2,32,192]{2,1,0:T(8,128)(2,1)} %bitcast.79), channel_id=1, source_target_pairs={{0,1},{1,0},{2,3},{3,2},{4,5},{5,4},{6,7},{7,6},{8,9},{9,8},{10,11... | collective-permute-start | bytes 73736 | tf_op jit(solution)/shard_map/ppermute | solution.py:41
  0.5 10.1 %collective-permute-start.4 = (bf16[2,32,192]{2,1,0:T(8,128)(2,1)}, bf16[2,32,192]{2,1,0:T(8,128)(2,1)S(1)}, u32[]{:S(2)}, u32[]{:S(2)}) collective-permute-start(bf16[2,32,192]{2,1,0:T(8,128)(2,1)} %bitcast.80), channel_id=1, source_target_pairs={{0,2},{1,3},{2,0},{3,1},{4,6},{5,7},{6,4},{7,5},{8,10},{9,11},{10,... | collective-permute-start | bytes 73736 | tf_op jit(solution)/shard_map/ppermute | solution.py:41
  3.0 7.6 %collective-permute-start.3 = (bf16[2,32,192]{2,1,0:T(8,128)(2,1)}, bf16[2,32,192]{2,1,0:T(8,128)(2,1)S(1)}, u32[]{:S(2)}, u32[]{:S(2)}) collective-permute-start(bf16[2,32,192]{2,1,0:T(8,128)(2,1)} %bitcast.81), channel_id=1, source_target_pairs={{0,3},{1,2},{2,1},{3,0},{4,7},{5,6},{6,5},{7,4},{8,11},{9,10},{10,... | collective-permute-start | bytes 73736 | tf_op jit(solution)/shard_map/ppermute | solution.py:41
  5.6 8.7 %collective-permute-start.2 = (f32[12420]{0:T(1024)S(1)}, f32[12420]{0:T(1024)S(1)}, u32[]{:S(2)}, u32[]{:S(2)}) collective-permute-start(f32[12420]{0:T(1024)S(1)} %concatenate.42), channel_id=1, source_target_pairs={{0,12},{4,0},{8,4},{12,8},{1,13},{5,1},{9,5},{13,9},{2,14},{6,2},{... | collective-permute-start | bytes 149048 | tf_op jit(solution)/shard_map/ppermute | solution.py:37
  9.4 6.2 %collective-permute-start.1 = (f32[12420]{0:T(1024)S(1)}, f32[12420]{0:T(1024)S(1)}, u32[]{:S(2)}, u32[]{:S(2)}) collective-permute-start(f32[12420]{0:T(1024)S(1)} %concatenate.42), channel_id=1, source_target_pairs={{0,8},{4,12},{8,0},{12,4},{1,9},{5,13},{9,1},{13,5},{2,10},{6,14},... | collective-permute-start | bytes 149048 | tf_op jit(solution)/shard_map/ppermute | solution.py:37
  9.5 6.1 %collective-permute-start = (f32[12420]{0:T(1024)S(1)}, f32[12420]{0:T(1024)S(1)}, u32[]{:S(2)}, u32[]{:S(2)}) collective-permute-start(f32[12420]{0:T(1024)S(1)} %concatenate.42), channel_id=1, source_target_pairs={{0,4},{4,8},{8,12},{12,0},{1,5},{5,9},{9,13},{13,1},{2,6},{6,10},{... | collective-permute-start | bytes 149048 | tf_op jit(solution)/shard_map/ppermute | solution.py:37
  12.6 1.4 %copy-start.5 = (bf16[192,768]{1,0:T(8,128)(2,1)S(1)}, bf16[192,768]{1,0:T(8,128)(2,1)}, u32[]{:S(2)}) copy-start(bf16[192,768]{1,0:T(8,128)(2,1)} %param.24) | copy-start | bytes 884740
  14.2 3.4 %collective-permute-start.6 = (bf16[32,768]{1,0:T(8,128)(2,1)S(1)}, bf16[32,768]{1,0:T(8,128)(2,1)S(1)}, u32[]{:S(2)}, u32[]{:S(2)}) collective-permute-start(bf16[32,768]{1,0:T(8,128)(2,1)S(1)} %broadcast_select_fusion.5), channel_id=1, source_target_pairs={{0,1},{1,0},{2,3},{3,2},{4,5},{5,4},{6,7},{7,6},{8,9},{9,8},{10,11... | collective-permute-start | bytes 147464 | tf_op jit(solution)/shard_map/ppermute | solution.py:41
  15.8 8.8 %copy-start.7 = (f32[768]{0:T(1024)S(1)}, f32[768]{0:T(1024)}, u32[]{:S(2)}) copy-start(f32[768]{0:T(1024)} %param.21) | copy-start | bytes 9220
  16.0 8.8 %copy-start.3 = (bf16[2,768,192]{1,2,0:T(8,128)(2,1)S(1)}, bf16[2,768,192]{1,2,0:T(8,128)(2,1)}, u32[]{:S(2)}) copy-start(bf16[2,768,192]{1,2,0:T(8,128)(2,1)} %param.26) | copy-start | bytes 1769476
  17.4 1.8 %collective-permute-start.9 = (bf16[4,32,192]{2,1,0:T(8,128)(2,1)S(1)}, bf16[4,32,192]{2,1,0:T(8,128)(2,1)S(1)}, u32[]{:S(2)}, u32[]{:S(2)}) collective-permute-start(bf16[4,32,192]{2,1,0:T(8,128)(2,1)S(1)} %reshape.451), channel_id=1, source_target_pairs={{0,1},{1,0},{2,3},{3,2},{4,5},{5,4},{6,7},{7,6},{8,9},{9,8},{10,11... | collective-permute-start | bytes 147464 | tf_op jit(solution)/shard_map/ppermute | solution.py:41
  17.6 4.2 %collective-permute-start.7 = (bf16[32,768]{1,0:T(8,128)(2,1)S(1)}, bf16[32,768]{1,0:T(8,128)(2,1)S(1)}, u32[]{:S(2)}, u32[]{:S(2)}) collective-permute-start(bf16[32,768]{1,0:T(8,128)(2,1)S(1)} %add_convert_fusion.1), channel_id=1, source_target_pairs={{0,2},{1,3},{2,0},{3,1},{4,6},{5,7},{6,4},{7,5},{8,10},{9,11},{10,... | collective-permute-start | bytes 147464 | tf_op jit(solution)/shard_map/ppermute | solution.py:41
  19.3 5.0 %collective-permute-start.10 = (bf16[4,32,384]{2,1,0:T(8,128)(2,1)S(1)}, bf16[4,32,384]{2,1,0:T(8,128)(2,1)S(1)}, u32[]{:S(2)}, u32[]{:S(2)}) collective-permute-start(bf16[4,32,384]{2,1,0:T(8,128)(2,1)S(1)} %maximum_select_fusion.1), channel_id=1, source_target_pairs={{0,2},{1,3},{2,0},{3,1},{4,6},{5,7},{6,4},{7,5},{8,10},{9,11},{10,... | collective-permute-start | bytes 294920 | tf_op jit(solution)/shard_map/ppermute | solution.py:41
  21.8 3.6 %collective-permute-start.8 = (f32[32,768]{1,0:T(8,128)S(1)}, f32[32,768]{1,0:T(8,128)S(1)}, u32[]{:S(2)}, u32[]{:S(2)}) collective-permute-start(f32[32,768]{1,0:T(8,128)S(1)} %convert_add_fusion.3), channel_id=1, source_target_pairs={{0,1},{1,0},{2,3},{3,2},{4,5},{5,4},{6,7},{7,6},{8,9},{9,8},{10,11... | collective-permute-start | bytes 294920 | tf_op jit(solution)/shard_map/ppermute | solution.py:41
  25.1 0.7 %copy-start.8 = (f32[768]{0:T(1024)S(1)}, f32[768]{0:T(1024)}, u32[]{:S(2)}) copy-start(f32[768]{0:T(1024)} %param.20) | copy-start | bytes 9220
  25.1 1.0 %copy-start.6 = (bf16[768,192]{0,1:T(8,128)(2,1)S(1)}, bf16[768,192]{0,1:T(8,128)(2,1)}, u32[]{:S(2)}) copy-start(bf16[768,192]{0,1:T(8,128)(2,1)} %param.25) | copy-start | bytes 884740
  26.8 1.0 %copy-start.4 = (bf16[192,768]{1,0:T(8,128)(2,1)S(1)}, bf16[192,768]{1,0:T(8,128)(2,1)}, u32[]{:S(2)}) copy-start(bf16[192,768]{1,0:T(8,128)(2,1)} %param.27) | copy-start | bytes 884740
  28.0 1.4 %collective-permute-start.11 = (bf16[64,768]{1,0:T(8,128)(2,1)S(1)}, bf16[64,768]{1,0:T(8,128)(2,1)S(1)}, u32[]{:S(2)}, u32[]{:S(2)}) collective-permute-start(bf16[64,768]{1,0:T(8,128)(2,1)S(1)} %broadcast_select_fusion.2), channel_id=1, source_target_pairs={{0,1},{1,0},{2,3},{3,2},{4,5},{5,4},{6,7},{7,6},{8,9},{9,8},{10,11... | collective-permute-start | bytes 294920 | tf_op jit(solution)/shard_map/ppermute | solution.py:41
  29.4 4.9 %collective-permute-start.12 = (bf16[64,768]{1,0:T(8,128)(2,1)S(1)}, bf16[64,768]{1,0:T(8,128)(2,1)S(1)}, u32[]{:S(2)}, u32[]{:S(2)}) collective-permute-start(bf16[64,768]{1,0:T(8,128)(2,1)S(1)} %add_convert_fusion), channel_id=1, source_target_pairs={{0,2},{1,3},{2,0},{3,1},{4,6},{5,7},{6,4},{7,5},{8,10},{9,11},{10,... | collective-permute-start | bytes 294920 | tf_op jit(solution)/shard_map/ppermute | solution.py:41
  34.4 1.5 %collective-permute-start.13 = (f32[64,768]{1,0:T(8,128)S(1)}, f32[64,768]{1,0:T(8,128)S(1)}, u32[]{:S(2)}, u32[]{:S(2)}) collective-permute-start(f32[64,768]{1,0:T(8,128)S(1)} %convert_add_fusion.1), channel_id=1, source_target_pairs={{0,1},{1,0},{2,3},{3,2},{4,5},{5,4},{6,7},{7,6},{8,9},{9,8},{10,11... | collective-permute-start | bytes 589832 | tf_op jit(solution)/shard_map/ppermute | solution.py:41
  35.1 1.2 %copy-start.9 = (f32[768]{0:T(1024)S(1)}, f32[768]{0:T(1024)}, u32[]{:S(2)}) copy-start(f32[768]{0:T(1024)} %param.22) | copy-start | bytes 9220
  36.5 1.3 %copy-start.1 = (bf16[768,768]{1,0:T(8,128)(2,1)S(1)}, bf16[768,768]{1,0:T(8,128)(2,1)}, u32[]{:S(2)}) copy-start(bf16[768,768]{1,0:T(8,128)(2,1)} %param.29) | copy-start | bytes 3538948
  38.7 4.1 %collective-permute-start.16 = (bf16[128,192]{1,0:T(8,128)(2,1)S(1)}, bf16[128,192]{1,0:T(8,128)(2,1)S(1)}, u32[]{:S(2)}, u32[]{:S(2)}) collective-permute-start(bf16[128,192]{1,0:T(8,128)(2,1)S(1)} %select_bitcast_fusion), channel_id=1, source_target_pairs={{0,3},{1,2},{2,1},{3,0},{4,7},{5,6},{6,5},{7,4},{8,11},{9,10},{10,... | collective-permute-start | bytes 147464 | tf_op jit(solution)/shard_map/ppermute | solution.py:41
  39.6 3.2 %collective-permute-start.14 = (bf16[128,192]{1,0:T(8,128)(2,1)S(1)}, bf16[128,192]{1,0:T(8,128)(2,1)S(1)}, u32[]{:S(2)}, u32[]{:S(2)}) collective-permute-start(bf16[128,192]{1,0:T(8,128)(2,1)S(1)} %select_bitcast_fusion.2), channel_id=1, source_target_pairs={{0,1},{1,0},{2,3},{3,2},{4,5},{5,4},{6,7},{7,6},{8,9},{9,8},{10,11... | collective-permute-start | bytes 147464 | tf_op jit(solution)/shard_map/ppermute | solution.py:41
  40.1 4.4 %collective-permute-start.15 = (bf16[128,192]{1,0:T(8,128)(2,1)S(1)}, bf16[128,192]{1,0:T(8,128)(2,1)S(1)}, u32[]{:S(2)}, u32[]{:S(2)}) collective-permute-start(bf16[128,192]{1,0:T(8,128)(2,1)S(1)} %select_bitcast_fusion.1), channel_id=1, source_target_pairs={{0,2},{1,3},{2,0},{3,1},{4,6},{5,7},{6,4},{7,5},{8,10},{9,11},{10,... | collective-permute-start | bytes 147464 | tf_op jit(solution)/shard_map/ppermute | solution.py:41

commit v21 on v18

--- a/solution.py
+++ b/solution.py
@@ -201,9 +201,11 @@
     ).astype(jnp.bfloat16)
     near = (local[:, None] == jnp.arange(img_dev)[None, :]).astype(jnp.bfloat16)
     query = pick_rows(near, query_img.reshape(img_dev, TOKS, -1)).reshape(rows_n, -1)
-    resid = jnp.take(resid_img.reshape(img_dev, TOKS, width), local, axis=0).reshape(
-        rows_n, width
-    )
+    per_image = resid_img.reshape(img_dev, 1, TOKS, width)
+    resid = jnp.broadcast_to(per_image[0], (views_n, TOKS, width))
+    for i in range(1, img_dev):
+        resid = jnp.where((local == i)[:, None, None], per_image[i], resid)
+    resid = resid.reshape(rows_n, width)
     term = jnp.dot(
         attend(query, keyval[0], keyval[1], views_n), cross_out, preferred_element_type=jnp.float32
     )

time: 45.9 us -> 45.6 us (level)
  local copies, waits for them, and re-layouts: 5.61 us -> 5.05 us
    gather x1 -> x0, local copies, waits for them, and re-layouts: 0.57 us -> none  [per_device(): jnp.take(resid_img.reshape(img_dev, TOKS, width), local, axis=0)]
  transfers between devices with their start and end apart: 17 -> 17, of which waited for: 8 -> 8; matrix products, arithmetic and copies ran while one was open for 22% -> 21% of each run, Pallas kernels for 0% -> 0%
where the time goes in v21:
time: 45.6 us; the launch traced here: 45.2 us
  starting transfers between devices  14.6 us (32%)
  waiting for transfers between devices  14.2 us (31%)
  other arithmetic  6.95 us (15%)
  local copies, waits for them, and re-layouts  5.05 us (11%)
  matrix products  3.57 us (8%)
  between operations  0.75 us (2%)
    ppermute x14, waiting for transfers between devices, swap(): return lax.ppermute(values, 'mp', pairs)  13 us
    ppermute x14, starting transfers between devices, swap(): return lax.ppermute(values, 'mp', pairs)  9.74 us
    ppermute x3, starting transfers between devices, pairs_shift(): lax.ppermute(values, 'pairs', [(i, (i + step) % owners_n) for i in range(...  4.9 us
    ppermute x3, waiting for transfers between devices, pairs_shift(): lax.ppermute(values, 'pairs', [(i, (i + step) % owners_n) for i in range(...  1.24 us
    convert_element_type x4, other arithmetic, layer_norm(): return (center * lax.rsqrt(spread + EPSILON) * gain).astype(jnp.bfloat16)  1.14 us
  transfers between devices with their start and end apart: 17, of which 8 were waited for; matrix products, arithmetic and copies ran while one was open for 21% of the time, Pallas kernels for 0%

profile of v21, /device:TPU:0, one launch (start us, length us, event | category | flops | bytes accessed | tf_op | source)
XLA Modules:
  0.0 45.2 jit_solution(18397413642625661768)
XLA Ops:
  0.0 0.5 %collective-permute-start.5 = (bf16[2,32,192]{2,1,0:T(8,128)(2,1)}, bf16[2,32,192]{2,1,0:T(8,128)(2,1)S(1)}, u32[]{:S(2)}, u32[]{:S(2)}) collective-permute-start(bf16[2,32,192]{2,1,0:T(8,128)(2,1)} %bitcast.76), channel_id=1, source_target_pairs={{0,1},{1,0},{2,3},{3,2},{4,5},{5,4},{6,7},{7,6},{8,9},{9,8},{10,11... | collective-permute-start | bytes 73736 | tf_op jit(solution)/shard_map/ppermute | solution.py:41
  0.5 2.6 %collective-permute-start.4 = (bf16[2,32,192]{2,1,0:T(8,128)(2,1)}, bf16[2,32,192]{2,1,0:T(8,128)(2,1)S(1)}, u32[]{:S(2)}, u32[]{:S(2)}) collective-permute-start(bf16[2,32,192]{2,1,0:T(8,128)(2,1)} %bitcast.77), channel_id=1, source_target_pairs={{0,2},{1,3},{2,0},{3,1},{4,6},{5,7},{6,4},{7,5},{8,10},{9,11},{10,... | collective-permute-start | bytes 73736 | tf_op jit(solution)/shard_map/ppermute | solution.py:41
  3.1 0.9 %reshape.497 = f32[12288]{0:T(1024)S(1)} reshape(bf16[64,192]{1,0:T(8,128)(2,1)} %param.16) | data formatting | bytes 73728 | tf_op jit(solution)/shard_map/reshape | solution.py:153
  4.0 0.8 %reshape.420 = f32[128]{0:T(128)S(1)} reshape(f32[2,64]{1,0:T(2,128)} %param.18) | data formatting | bytes 1024 | tf_op jit(solution)/shard_map/reshape | solution.py:155
  4.7 0.7 %convert_element_type.161 = f32[2,2]{1,0:T(2,128)S(1)} convert(s32[2,2]{1,0:T(2,128)} %param.17) | non-fusion elementwise | flops 4 | bytes 32 | tf_op jit(solution)/shard_map/convert_element_type | solution.py:154
  5.6 3.8 %collective-permute-start.2 = (f32[12420]{0:T(1024)S(1)}, f32[12420]{0:T(1024)S(1)}, u32[]{:S(2)}, u32[]{:S(2)}) collective-permute-start(f32[12420]{0:T(1024)S(1)} %concatenate.37), channel_id=1, source_target_pairs={{0,12},{4,0},{8,4},{12,8},{1,13},{5,1},{9,5},{13,9},{2,14},{6,2},{... | collective-permute-start | bytes 149048 | tf_op jit(solution)/shard_map/ppermute | solution.py:37
  9.5 1.1 %collective-permute-start = (f32[12420]{0:T(1024)S(1)}, f32[12420]{0:T(1024)S(1)}, u32[]{:S(2)}, u32[]{:S(2)}) collective-permute-start(f32[12420]{0:T(1024)S(1)} %concatenate.37), channel_id=1, source_target_pairs={{0,4},{4,8},{8,12},{12,0},{1,5},{5,9},{9,13},{13,1},{2,6},{6,10},{... | collective-permute-start | bytes 149048 | tf_op jit(solution)/shard_map/ppermute | solution.py:37
  10.6 0.8 %select_select_fusion.3 = (bf16[2,32,192]{2,1,0:T(8,128)(2,1)S(1)}, bf16[2,32,192]{2,1,0:T(8,128)(2,1)S(1)}, bf16[2,32,192]{2,1,0:T(8,128)(2,1)S(1)}, bf16[2,32,192]{2,1,0:T(8,128)(2,1)S(1)}) fusion(bf16[2,32,192]{2,1,0:T(8,128)(2,1)S(1)} %collective-permute-done.3, bf16[2,32,192]{2,1,0:T(8,128)(2,1)S(1)} %collective-permute-done.4, ...), kind=kLoop, calls=%fused_computation.102 | loop fusion | flops 147456 | bytes 196620 | tf_op jit(solution)/shard_map/jit(_where)/select_n | solution.py:91
  11.4 0.2 convert_reduce_fusion.1
  11.6 0.2 fusion.26
  11.8 0.8 %fusion.28 = bf16[64,768]{1,0:T(8,128)(2,1)S(1)} fusion(bf16[64,768]{1,0:T(8,128)(2,1)S(1)} %get-tuple-element.30, f32[768]{0:T(1024)} %param.19, f32[64]{0:T(128)S(1)} %add_rsqrt_fusion.3, f32[64]{0:T(128)S(1)} %broadcast_multiply_fusion.3), kind=kLoop, calls=%fused_computation.58 | loop fusion | flops 245760 | bytes 200192 | tf_op jit(solution)/shard_map/convert_element_type | solution.py:16
  12.6 0.4 fusion.6
  13.2 0.2 fusion.69
  13.4 0.1 convolution_multiply_fusion.1
  13.6 0.2 fusion.8
  14.0 0.2 convolution_convert_fusion.6
  14.4 1.2 %collective-permute-done.1 = f32[12420]{0:T(1024)S(1)} collective-permute-done((f32[12420]{0:T(1024)S(1)}, f32[12420]{0:T(1024)S(1)}, u32[]{:S(2)}, u32[]{:S(2)}) %collective-permute-start.1) | collective-permute-done | bytes 49712 | tf_op jit(solution)/shard_map/ppermute | solution.py:37
  15.7 0.2 pad_maximum_fusion
  16.5 0.1 add_reduce_fusion
  16.7 0.2 select_reduce_fusion
  16.9 0.2 convolution_convert_fusion.1
  17.1 0.1 reshape.427
  17.3 1.6 %collective-permute-start.7 = (bf16[32,768]{1,0:T(8,128)(2,1)S(1)}, bf16[32,768]{1,0:T(8,128)(2,1)S(1)}, u32[]{:S(2)}, u32[]{:S(2)}) collective-permute-start(bf16[32,768]{1,0:T(8,128)(2,1)S(1)} %add_convert_fusion.1), channel_id=1, source_target_pairs={{0,2},{1,3},{2,0},{3,1},{4,6},{5,7},{6,4},{7,5},{8,10},{9,11},{10,... | collective-permute-start | bytes 147464 | tf_op jit(solution)/shard_map/ppermute | solution.py:41
  18.9 0.1 maximum_select_fusion.1
  19.0 1.2 %collective-permute-start.10 = (bf16[4,32,384]{2,1,0:T(8,128)(2,1)S(1)}, bf16[4,32,384]{2,1,0:T(8,128)(2,1)S(1)}, u32[]{:S(2)}, u32[]{:S(2)}) collective-permute-start(bf16[4,32,384]{2,1,0:T(8,128)(2,1)S(1)} %maximum_select_fusion.1), channel_id=1, source_target_pairs={{0,2},{1,3},{2,0},{3,1},{4,6},{5,7},{6,4},{7,5},{8,10},{9,11},{10,... | collective-permute-start | bytes 294920 | tf_op jit(solution)/shard_map/ppermute | solution.py:41
  20.2 1.3 %collective-permute-done.7 = bf16[32,768]{1,0:T(8,128)(2,1)S(1)} collective-permute-done((bf16[32,768]{1,0:T(8,128)(2,1)S(1)}, bf16[32,768]{1,0:T(8,128)(2,1)S(1)}, u32[]{:S(2)}, u32[]{:S(2)}) %collective-permute-start.7) | collective-permute-done | bytes 49184 | tf_op jit(solution)/shard_map/ppermute | solution.py:41
  21.6 2.4 %collective-permute-done.10 = bf16[4,32,384]{2,1,0:T(8,128)(2,1)S(1)} collective-permute-done((bf16[4,32,384]{2,1,0:T(8,128)(2,1)S(1)}, bf16[4,32,384]{2,1,0:T(8,128)(2,1)S(1)}, u32[]{:S(2)}, u32[]{:S(2)}) %collective-permute-start.10) | collective-permute-done | bytes 98336 | tf_op jit(solution)/shard_map/ppermute | solution.py:41
  24.0 0.1 convert_reduce_fusion
  24.1 0.2 fusion.11
  24.3 0.1 fusion.13
  24.5 0.3 fusion.75
  24.9 0.1 reshape.534
  25.0 0.1 reshape.533
  25.2 0.1 fusion.65
  25.3 0.2 multiply_reduce_fusion.1
  25.6 0.2 copy-done.6
  25.8 0.2 convolution_convert_fusion.8
  26.0 0.1 reshape_reshape.3
  26.1 0.2 convolution_convert_fusion
  26.3 0.1 reshape_reshape_reshape.3
  26.5 0.2 convolution_multiply_fusion
  26.8 0.3 fusion.5
  27.2 0.1 reshape.429
  27.3 0.1 copy-done.4
  27.5 0.2 convolution_convert_fusion.3
  27.9 1.1 %collective-permute-done.11 = bf16[64,768]{1,0:T(8,128)(2,1)S(1)} collective-permute-done((bf16[64,768]{1,0:T(8,128)(2,1)S(1)}, bf16[64,768]{1,0:T(8,128)(2,1)S(1)}, u32[]{:S(2)}, u32[]{:S(2)}) %collective-permute-start.11) | collective-permute-done | bytes 98336 | tf_op jit(solution)/shard_map/ppermute | solution.py:41
  29.1 1.2 %collective-permute-start.12 = (bf16[64,768]{1,0:T(8,128)(2,1)S(1)}, bf16[64,768]{1,0:T(8,128)(2,1)S(1)}, u32[]{:S(2)}, u32[]{:S(2)}) collective-permute-start(bf16[64,768]{1,0:T(8,128)(2,1)S(1)} %add_convert_fusion), channel_id=1, source_target_pairs={{0,2},{1,3},{2,0},{3,1},{4,6},{5,7},{6,4},{7,5},{8,10},{9,11},{10,... | collective-permute-start | bytes 294920 | tf_op jit(solution)/shard_map/ppermute | solution.py:41
  30.3 0.1 fusion.44
  30.6 3.4 %collective-permute-done.12 = bf16[64,768]{1,0:T(8,128)(2,1)S(1)} collective-permute-done((bf16[64,768]{1,0:T(8,128)(2,1)S(1)}, bf16[64,768]{1,0:T(8,128)(2,1)S(1)}, u32[]{:S(2)}, u32[]{:S(2)}) %collective-permute-start.12) | collective-permute-done | bytes 98336 | tf_op jit(solution)/shard_map/ppermute | solution.py:41
  34.2 1.4 %collective-permute-done.13 = f32[64,768]{1,0:T(8,128)S(1)} collective-permute-done((f32[64,768]{1,0:T(8,128)S(1)}, f32[64,768]{1,0:T(8,128)S(1)}, u32[]{:S(2)}, u32[]{:S(2)}) %collective-permute-start.13) | collective-permute-done | bytes 196640 | tf_op jit(solution)/shard_map/ppermute | solution.py:41
  35.6 0.2 fusion.64
  35.8 0.2 multiply_reduce_fusion
  36.0 0.1 multiply_convert_fusion
  36.2 0.3 fusion.76
  36.5 0.8 %fusion.16 = bf16[128,768]{1,0:T(8,128)(2,1)S(1)} fusion(f32[128,768]{1,0:T(8,128)S(1)} %fusion.76), kind=kLoop, calls=%fused_computation.30 | loop fusion | flops 6389760 | bytes 589824 | tf_op jit(solution)/shard_map/convert_element_type | solution.py:218
  37.4 0.3 convolution_convert_fusion.2
  37.8 0.2 copy.71
  38.3 1.0 %collective-permute-start.16 = (bf16[128,192]{1,0:T(8,128)(2,1)S(1)}, bf16[128,192]{1,0:T(8,128)(2,1)S(1)}, u32[]{:S(2)}, u32[]{:S(2)}) collective-permute-start(bf16[128,192]{1,0:T(8,128)(2,1)S(1)} %select_bitcast_fusion), channel_id=1, source_target_pairs={{0,3},{1,2},{2,1},{3,0},{4,7},{5,6},{6,5},{7,4},{8,11},{9,10},{10,... | collective-permute-start | bytes 147464 | tf_op jit(solution)/shard_map/ppermute | solution.py:41
  39.3 0.4 collective-permute-start.14
  39.8 0.9 %collective-permute-start.15 = (bf16[128,192]{1,0:T(8,128)(2,1)S(1)}, bf16[128,192]{1,0:T(8,128)(2,1)S(1)}, u32[]{:S(2)}, u32[]{:S(2)}) collective-permute-start(bf16[128,192]{1,0:T(8,128)(2,1)S(1)} %select_bitcast_fusion.1), channel_id=1, source_target_pairs={{0,2},{1,3},{2,0},{3,1},{4,6},{5,7},{6,4},{7,5},{8,10},{9,11},{10,... | collective-permute-start | bytes 147464 | tf_op jit(solution)/shard_map/ppermute | solution.py:41
  40.8 1.7 %collective-permute-done.16 = bf16[128,192]{1,0:T(8,128)(2,1)S(1)} collective-permute-done((bf16[128,192]{1,0:T(8,128)(2,1)S(1)}, bf16[128,192]{1,0:T(8,128)(2,1)S(1)}, u32[]{:S(2)}, u32[]{:S(2)}) %collective-permute-start.16) | collective-permute-done | bytes 49184 | tf_op jit(solution)/shard_map/ppermute | solution.py:41
  42.5 1.7 %collective-permute-done.15 = bf16[128,192]{1,0:T(8,128)(2,1)S(1)} collective-permute-done((bf16[128,192]{1,0:T(8,128)(2,1)S(1)}, bf16[128,192]{1,0:T(8,128)(2,1)S(1)}, u32[]{:S(2)}, u32[]{:S(2)}) %collective-permute-start.15) | collective-permute-done | bytes 49184 | tf_op jit(solution)/shard_map/ppermute | solution.py:41
  44.2 0.1 add_add_fusion
  44.6 0.6 %pad_maximum_fusion.2 = bf16[64,192]{1,0:T(8,128)(2,1)} fusion(bf16[32,192]{1,0:T(8,128)(2,1)S(1)} %divide_convert_fusion.4, bf16[32,192]{1,0:T(8,128)(2,1)S(1)} %divide_convert_fusion.5), kind=kLoop, calls=%fused_computation.96 | loop fusion | flops 49152 | bytes 49152 | tf_op jit(solution)/shard_map/concatenate | solution.py:234
  (100 shorter events, 3.5 us)
Async XLA Ops:
  0.0 36.2 %copy-start = (bf16[768,768]{1,0:T(8,128)(2,1)S(1)}, bf16[768,768]{1,0:T(8,128)(2,1)}, u32[]{:S(2)}) copy-start(bf16[768,768]{1,0:T(8,128)(2,1)} %param.28) | copy-start | bytes 3538948
  0.0 12.6 %copy-start.2 = (bf16[3,768,192]{1,2,0:T(8,128)(2,1)S(1)}, bf16[3,768,192]{1,2,0:T(8,128)(2,1)}, u32[]{:S(2)}) copy-start(bf16[3,768,192]{1,2,0:T(8,128)(2,1)} %param.23) | copy-start | bytes 2654212
  0.0 9.5 %collective-permute-start.5 = (bf16[2,32,192]{2,1,0:T(8,128)(2,1)}, bf16[2,32,192]{2,1,0:T(8,128)(2,1)S(1)}, u32[]{:S(2)}, u32[]{:S(2)}) collective-permute-start(bf16[2,32,192]{2,1,0:T(8,128)(2,1)} %bitcast.76), channel_id=1, source_target_pairs={{0,1},{1,0},{2,3},{3,2},{4,5},{5,4},{6,7},{7,6},{8,9},{9,8},{10,11... | collective-permute-start | bytes 73736 | tf_op jit(solution)/shard_map/ppermute | solution.py:41
  0.5 10.1 %collective-permute-start.4 = (bf16[2,32,192]{2,1,0:T(8,128)(2,1)}, bf16[2,32,192]{2,1,0:T(8,128)(2,1)S(1)}, u32[]{:S(2)}, u32[]{:S(2)}) collective-permute-start(bf16[2,32,192]{2,1,0:T(8,128)(2,1)} %bitcast.77), channel_id=1, source_target_pairs={{0,2},{1,3},{2,0},{3,1},{4,6},{5,7},{6,4},{7,5},{8,10},{9,11},{10,... | collective-permute-start | bytes 73736 | tf_op jit(solution)/shard_map/ppermute | solution.py:41
  3.0 7.6 %collective-permute-start.3 = (bf16[2,32,192]{2,1,0:T(8,128)(2,1)}, bf16[2,32,192]{2,1,0:T(8,128)(2,1)S(1)}, u32[]{:S(2)}, u32[]{:S(2)}) collective-permute-start(bf16[2,32,192]{2,1,0:T(8,128)(2,1)} %bitcast.78), channel_id=1, source_target_pairs={{0,3},{1,2},{2,1},{3,0},{4,7},{5,6},{6,5},{7,4},{8,11},{9,10},{10,... | collective-permute-start | bytes 73736 | tf_op jit(solution)/shard_map/ppermute | solution.py:41
  5.6 8.7 %collective-permute-start.2 = (f32[12420]{0:T(1024)S(1)}, f32[12420]{0:T(1024)S(1)}, u32[]{:S(2)}, u32[]{:S(2)}) collective-permute-start(f32[12420]{0:T(1024)S(1)} %concatenate.37), channel_id=1, source_target_pairs={{0,12},{4,0},{8,4},{12,8},{1,13},{5,1},{9,5},{13,9},{2,14},{6,2},{... | collective-permute-start | bytes 149048 | tf_op jit(solution)/shard_map/ppermute | solution.py:37
  9.4 6.2 %collective-permute-start.1 = (f32[12420]{0:T(1024)S(1)}, f32[12420]{0:T(1024)S(1)}, u32[]{:S(2)}, u32[]{:S(2)}) collective-permute-start(f32[12420]{0:T(1024)S(1)} %concatenate.37), channel_id=1, source_target_pairs={{0,8},{4,12},{8,0},{12,4},{1,9},{5,13},{9,1},{13,5},{2,10},{6,14},... | collective-permute-start | bytes 149048 | tf_op jit(solution)/shard_map/ppermute | solution.py:37
  9.5 6.1 %collective-permute-start = (f32[12420]{0:T(1024)S(1)}, f32[12420]{0:T(1024)S(1)}, u32[]{:S(2)}, u32[]{:S(2)}) collective-permute-start(f32[12420]{0:T(1024)S(1)} %concatenate.37), channel_id=1, source_target_pairs={{0,4},{4,8},{8,12},{12,0},{1,5},{5,9},{9,13},{13,1},{2,6},{6,10},{... | collective-permute-start | bytes 149048 | tf_op jit(solution)/shard_map/ppermute | solution.py:37
  12.6 1.4 %copy-start.5 = (bf16[192,768]{1,0:T(8,128)(2,1)S(1)}, bf16[192,768]{1,0:T(8,128)(2,1)}, u32[]{:S(2)}) copy-start(bf16[192,768]{1,0:T(8,128)(2,1)} %param.24) | copy-start | bytes 884740
  14.2 3.1 %collective-permute-start.6 = (bf16[32,768]{1,0:T(8,128)(2,1)S(1)}, bf16[32,768]{1,0:T(8,128)(2,1)S(1)}, u32[]{:S(2)}, u32[]{:S(2)}) collective-permute-start(bf16[32,768]{1,0:T(8,128)(2,1)S(1)} %broadcast_select_fusion.5), channel_id=1, source_target_pairs={{0,1},{1,0},{2,3},{3,2},{4,5},{5,4},{6,7},{7,6},{8,9},{9,8},{10,11... | collective-permute-start | bytes 147464 | tf_op jit(solution)/shard_map/ppermute | solution.py:41
  14.4 10.0 %copy-start.7 = (f32[768]{0:T(1024)S(1)}, f32[768]{0:T(1024)}, u32[]{:S(2)}) copy-start(f32[768]{0:T(1024)} %param.21) | copy-start | bytes 9220
  15.9 8.6 %copy-start.3 = (bf16[2,768,192]{1,2,0:T(8,128)(2,1)S(1)}, bf16[2,768,192]{1,2,0:T(8,128)(2,1)}, u32[]{:S(2)}) copy-start(bf16[2,768,192]{1,2,0:T(8,128)(2,1)} %param.26) | copy-start | bytes 1769476
  17.2 1.7 %collective-permute-start.9 = (bf16[4,32,192]{2,1,0:T(8,128)(2,1)S(1)}, bf16[4,32,192]{2,1,0:T(8,128)(2,1)S(1)}, u32[]{:S(2)}, u32[]{:S(2)}) collective-permute-start(bf16[4,32,192]{2,1,0:T(8,128)(2,1)S(1)} %reshape.427), channel_id=1, source_target_pairs={{0,1},{1,0},{2,3},{3,2},{4,5},{5,4},{6,7},{7,6},{8,9},{9,8},{10,11... | collective-permute-start | bytes 147464 | tf_op jit(solution)/shard_map/ppermute | solution.py:41
  17.3 4.2 %collective-permute-start.7 = (bf16[32,768]{1,0:T(8,128)(2,1)S(1)}, bf16[32,768]{1,0:T(8,128)(2,1)S(1)}, u32[]{:S(2)}, u32[]{:S(2)}) collective-permute-start(bf16[32,768]{1,0:T(8,128)(2,1)S(1)} %add_convert_fusion.1), channel_id=1, source_target_pairs={{0,2},{1,3},{2,0},{3,1},{4,6},{5,7},{6,4},{7,5},{8,10},{9,11},{10,... | collective-permute-start | bytes 147464 | tf_op jit(solution)/shard_map/ppermute | solution.py:41
  19.0 5.0 %collective-permute-start.10 = (bf16[4,32,384]{2,1,0:T(8,128)(2,1)S(1)}, bf16[4,32,384]{2,1,0:T(8,128)(2,1)S(1)}, u32[]{:S(2)}, u32[]{:S(2)}) collective-permute-start(bf16[4,32,384]{2,1,0:T(8,128)(2,1)S(1)} %maximum_select_fusion.1), channel_id=1, source_target_pairs={{0,2},{1,3},{2,0},{3,1},{4,6},{5,7},{6,4},{7,5},{8,10},{9,11},{10,... | collective-permute-start | bytes 294920 | tf_op jit(solution)/shard_map/ppermute | solution.py:41
  21.5 3.6 %collective-permute-start.8 = (f32[32,768]{1,0:T(8,128)S(1)}, f32[32,768]{1,0:T(8,128)S(1)}, u32[]{:S(2)}, u32[]{:S(2)}) collective-permute-start(f32[32,768]{1,0:T(8,128)S(1)} %convert_add_fusion.2), channel_id=1, source_target_pairs={{0,1},{1,0},{2,3},{3,2},{4,5},{5,4},{6,7},{7,6},{8,9},{9,8},{10,11... | collective-permute-start | bytes 294920 | tf_op jit(solution)/shard_map/ppermute | solution.py:41
  24.8 0.7 %copy-start.8 = (f32[768]{0:T(1024)S(1)}, f32[768]{0:T(1024)}, u32[]{:S(2)}) copy-start(f32[768]{0:T(1024)} %param.20) | copy-start | bytes 9220
  24.8 1.0 %copy-start.6 = (bf16[768,192]{0,1:T(8,128)(2,1)S(1)}, bf16[768,192]{0,1:T(8,128)(2,1)}, u32[]{:S(2)}) copy-start(bf16[768,192]{0,1:T(8,128)(2,1)} %param.25) | copy-start | bytes 884740
  26.5 1.0 %copy-start.4 = (bf16[192,768]{1,0:T(8,128)(2,1)S(1)}, bf16[192,768]{1,0:T(8,128)(2,1)}, u32[]{:S(2)}) copy-start(bf16[192,768]{1,0:T(8,128)(2,1)} %param.27) | copy-start | bytes 884740
  27.7 1.4 %collective-permute-start.11 = (bf16[64,768]{1,0:T(8,128)(2,1)S(1)}, bf16[64,768]{1,0:T(8,128)(2,1)S(1)}, u32[]{:S(2)}, u32[]{:S(2)}) collective-permute-start(bf16[64,768]{1,0:T(8,128)(2,1)S(1)} %broadcast_select_fusion.2), channel_id=1, source_target_pairs={{0,1},{1,0},{2,3},{3,2},{4,5},{5,4},{6,7},{7,6},{8,9},{9,8},{10,11... | collective-permute-start | bytes 294920 | tf_op jit(solution)/shard_map/ppermute | solution.py:41
  29.1 4.9 %collective-permute-start.12 = (bf16[64,768]{1,0:T(8,128)(2,1)S(1)}, bf16[64,768]{1,0:T(8,128)(2,1)S(1)}, u32[]{:S(2)}, u32[]{:S(2)}) collective-permute-start(bf16[64,768]{1,0:T(8,128)(2,1)S(1)} %add_convert_fusion), channel_id=1, source_target_pairs={{0,2},{1,3},{2,0},{3,1},{4,6},{5,7},{6,4},{7,5},{8,10},{9,11},{10,... | collective-permute-start | bytes 294920 | tf_op jit(solution)/shard_map/ppermute | solution.py:41
  34.1 1.5 %collective-permute-start.13 = (f32[64,768]{1,0:T(8,128)S(1)}, f32[64,768]{1,0:T(8,128)S(1)}, u32[]{:S(2)}, u32[]{:S(2)}) collective-permute-start(f32[64,768]{1,0:T(8,128)S(1)} %convert_add_fusion.1), channel_id=1, source_target_pairs={{0,1},{1,0},{2,3},{3,2},{4,5},{5,4},{6,7},{7,6},{8,9},{9,8},{10,11... | collective-permute-start | bytes 589832 | tf_op jit(solution)/shard_map/ppermute | solution.py:41
  34.2 1.9 %copy-start.9 = (f32[768]{0:T(1024)S(1)}, f32[768]{0:T(1024)}, u32[]{:S(2)}) copy-start(f32[768]{0:T(1024)} %param.22) | copy-start | bytes 9220
  36.2 1.3 %copy-start.1 = (bf16[768,768]{1,0:T(8,128)(2,1)S(1)}, bf16[768,768]{1,0:T(8,128)(2,1)}, u32[]{:S(2)}) copy-start(bf16[768,768]{1,0:T(8,128)(2,1)} %param.29) | copy-start | bytes 3538948
  38.3 4.1 %collective-permute-start.16 = (bf16[128,192]{1,0:T(8,128)(2,1)S(1)}, bf16[128,192]{1,0:T(8,128)(2,1)S(1)}, u32[]{:S(2)}, u32[]{:S(2)}) collective-permute-start(bf16[128,192]{1,0:T(8,128)(2,1)S(1)} %select_bitcast_fusion), channel_id=1, source_target_pairs={{0,3},{1,2},{2,1},{3,0},{4,7},{5,6},{6,5},{7,4},{8,11},{9,10},{10,... | collective-permute-start | bytes 147464 | tf_op jit(solution)/shard_map/ppermute | solution.py:41
  39.3 3.2 %collective-permute-start.14 = (bf16[128,192]{1,0:T(8,128)(2,1)S(1)}, bf16[128,192]{1,0:T(8,128)(2,1)S(1)}, u32[]{:S(2)}, u32[]{:S(2)}) collective-permute-start(bf16[128,192]{1,0:T(8,128)(2,1)S(1)} %select_bitcast_fusion.2), channel_id=1, source_target_pairs={{0,1},{1,0},{2,3},{3,2},{4,5},{5,4},{6,7},{7,6},{8,9},{9,8},{10,11... | collective-permute-start | bytes 147464 | tf_op jit(solution)/shard_map/ppermute | solution.py:41
  39.8 4.4 %collective-permute-start.15 = (bf16[128,192]{1,0:T(8,128)(2,1)S(1)}, bf16[128,192]{1,0:T(8,128)(2,1)S(1)}, u32[]{:S(2)}, u32[]{:S(2)}) collective-permute-start(bf16[128,192]{1,0:T(8,128)(2,1)S(1)} %select_bitcast_fusion.1), channel_id=1, source_target_pairs={{0,2},{1,3},{2,0},{3,1},{4,6},{5,7},{6,4},{7,5},{8,10},{9,11},{10,... | collective-permute-start | bytes 147464 | tf_op jit(solution)/shard_map/ppermute | solution.py:41
